TPU v7x, 256 devices: a whole 4x4x8 slice. The times are simulated.
256 devices in a mesh: species: 4 (over z_lo), mode: 4 (over y), space: 16 (over x, z_hi, core).
Axes of the slice: x: 4, y: 4, z: 8 (z_hi: 2, z_lo: 4; z = z_hi * 4 + z_lo), core: 2. Of those that a mesh axis runs over, the one named last changes fastest.
Arguments:
- distribution: float32 [8, 1024, 16, 512], P('species', 'mode', 'space'), may hold values from -6 to 6
- kernel: bfloat16 [2, 120, 120, 120], P(None, 'mode'), may hold values from -0.046875 to 0.046875
- pair_kind: int32 [8, 8], replicated, may hold values from 0 to 1
- low_map: int32 [120], replicated, may hold values from 0 to 448, as said below
- thermal_speed: float32 [8], P('species'), may hold values from 0.5 to 1
- relax_rate: float32 [8], P('species'), may hold values from 2 to 8
Outputs:
- updated: float32 [8, 1024, 16, 512], P('species', 'mode', 'space')
Inputs may be any that keep to these rules, and one draw needn't show every extreme that they name: low_map lists each of the 120 modes whose degrees a, b, c sum to at most 7 exactly once, in some order; a mode's index is a * 8 * 8 + b * 8 + c.
All inputs are finite; a program needn't handle non-finite values.
Results may differ from a plain program's by a relative error of at most 0.0025.
Values may be sent and summed in bfloat16 or wider, within the bound.
No kernel may reach another device: no remote copies, remote signals or barrier semaphores. Data moves between devices by JAX's collectives and lax.ppermute only.
A program may use at most 128 MiB of HBM per device.

v0:
```python
import jax
import jax.numpy as jnp
from jax import lax
from jax.experimental import pallas as pl
from jax.sharding import PartitionSpec as P

NVY = 8
NVZ = 8
DEG = 7
NKIND = 2
NY = 256
NZ = 2
PAD = 128

nu_step = 0.0625
dt_step = 0.05
bound_x = 6.7
bound_y = 4.2
bound_z = 4.2

INTERPRET = False


def flux_from_padded(padded, axis_dim, first_degree):
    axis_count = padded.shape[axis_dim] - 2
    dims_shape = [1] * padded.ndim
    dims_shape[axis_dim] = axis_count
    degree = (first_degree + jnp.arange(axis_count)).astype(jnp.float32).reshape(dims_shape)
    below_part = lax.slice_in_dim(padded, 0, axis_count, axis=axis_dim)
    above_part = lax.slice_in_dim(padded, 2, axis_count + 2, axis=axis_dim)
    return jnp.sqrt(degree + 1.0) * above_part + jnp.sqrt(degree) * below_part


def degree_flux(phase_field, axis_dim):
    widths = [(0, 0)] * phase_field.ndim
    widths[axis_dim] = (1, 1)
    return flux_from_padded(jnp.pad(phase_field, widths), axis_dim, 0)


def rusanov(phase_field, up_field, down_field, up_flux, down_flux, speed_bound):
    return 0.5 * (up_flux - down_flux) - 0.5 * speed_bound * (
        up_field - 2.0 * phase_field + down_field
    )


def periodic_term(phase_field, axis_deg, axis_cell, speed_bound):
    flux_dir = degree_flux(phase_field, axis_deg)
    return rusanov(
        phase_field,
        jnp.roll(phase_field, -1, axis_cell),
        jnp.roll(phase_field, 1, axis_cell),
        jnp.roll(flux_dir, -1, axis_cell),
        jnp.roll(flux_dir, 1, axis_cell),
        speed_bound,
    )


def collide_body(k_ref, r_ref, l_ref, o_ref):
    def body(n, carry):
        z = jnp.dot(k_ref[n], r_ref[...], preferred_element_type=jnp.float32)
        o_ref[pl.ds(n, 1), :] = jnp.sum(z * l_ref[...], axis=0, keepdims=True)
        return carry

    lax.fori_loop(0, k_ref.shape[0], body, 0)


def collide_call(kcat, rhs, lmat):
    return pl.pallas_call(
        collide_body,
        out_shape=jax.ShapeDtypeStruct((kcat.shape[0], rhs.shape[1]), jnp.float32),
        interpret=INTERPRET,
    )(kcat, rhs, lmat)


def shift_permutes(values, axis, holders, count, toward):
    received = []
    for shift in range(1, count):
        if toward:
            pairs = [((h - shift) % count, h) for h in holders]
        else:
            pairs = [(h, (h + shift) % count) for h in holders]
        received.append((shift, lax.ppermute(values, axis, pairs)))
    return received


def per_device(distribution, kernel, pair_kind, low_map, thermal_speed, relax_rate):
    own_count, mode_count, row_count, plane_cells = distribution.shape
    per_vx = mode_count // (NVY * NVZ)
    mode_devs = lax.axis_size("mode")
    species_devs = lax.axis_size("species")
    space_devs = lax.axis_size("space")
    mode_id = lax.axis_index("mode")
    first_vx = mode_id * per_vx
    low_count = low_map.shape[0]
    out_rows = kernel.shape[1]
    species_all = own_count * species_devs

    phase_field = distribution.reshape(own_count, per_vx, NVY, NVZ, row_count, NZ, NY)
    below = lax.ppermute(
        phase_field[:, per_vx - 1 :], "mode", [(i, i + 1) for i in range(mode_devs - 1)]
    )
    above = lax.ppermute(phase_field[:, :1], "mode", [(i + 1, i) for i in range(mode_devs - 1)])
    flux_x = flux_from_padded(jnp.concatenate([below, phase_field, above], axis=1), 1, first_vx)
    up_part = 0.5 * flux_x - 0.5 * bound_x * phase_field
    down_part = -0.5 * flux_x - 0.5 * bound_x * phase_field
    from_next = lax.ppermute(
        up_part[:, :, :, :, :1], "space", [(i + 1, i) for i in range(space_devs - 1)]
    )
    from_prev = lax.ppermute(
        down_part[:, :, :, :, row_count - 1 :], "space", [(i, i + 1) for i in range(space_devs - 1)]
    )
    up_all = jnp.concatenate([up_part[:, :, :, :, 1:], from_next], axis=4)
    down_all = jnp.concatenate([from_prev, down_part[:, :, :, :, : row_count - 1]], axis=4)
    x_term = up_all + down_all + bound_x * phase_field
    y_term = periodic_term(phase_field, 2, 6, bound_y)
    z_term = periodic_term(phase_field, 3, 5, bound_z)
    stream = x_term + y_term + z_term
    advected = phase_field - nu_step * thermal_speed.reshape(own_count, 1, 1, 1, 1, 1, 1) * stream

    cell_count = row_count * plane_cells
    block_cells = cell_count // species_devs
    flat_dist = distribution.reshape(own_count, mode_count, cell_count)
    local_index = low_map - mode_id * mode_count
    owned = (local_index >= 0) & (local_index < mode_count)
    clipped = jnp.clip(local_index, 0, mode_count - 1)
    picked = jnp.where(owned[None, :, None], jnp.take(flat_dist, clipped, axis=1), 0.0).astype(
        jnp.bfloat16
    )
    picked = picked.reshape(own_count, low_count, species_devs, block_cells)
    spread = lax.all_to_all(picked, "species", 2, 0, tiled=True)
    holders = [h for h in range(mode_devs) if h * per_vx <= DEG]
    low_all = spread
    for _, got in shift_permutes(spread, "mode", holders, mode_devs, False):
        low_all = low_all + got
    low_all = low_all.reshape(species_all, low_count, block_cells).astype(jnp.float32)

    chooser = jnp.stack([(pair_kind == k).astype(jnp.float32) for k in range(NKIND)])
    partner = jnp.einsum("ksr,rlc->klsc", chooser, low_all, precision=lax.Precision.HIGHEST)
    part_hi = partner.astype(jnp.bfloat16)
    part_lo = (partner - part_hi.astype(jnp.float32)).astype(jnp.bfloat16)
    rhs = jnp.stack([piece for k in range(NKIND) for piece in (part_hi[k], part_lo[k])])
    rhs = jnp.pad(rhs, ((0, 0), (0, PAD - low_count), (0, 0), (0, 0)))
    rhs = rhs.reshape(2 * NKIND * PAD, species_all * block_cells)
    lmat = jnp.pad(jnp.moveaxis(low_all, 1, 0), ((0, PAD - low_count), (0, 0), (0, 0)))
    lmat = lmat.reshape(PAD, species_all * block_cells)
    kpad = jnp.pad(kernel, ((0, 0), (0, 0), (0, PAD - low_count), (0, PAD - low_count)))
    kcat = jnp.concatenate([kpad[k] for k in range(NKIND) for _ in range(2)], axis=-1)
    gained = collide_call(kcat, rhs, lmat)

    gained = gained.reshape(out_rows, species_devs, own_count, block_cells)
    gathered = lax.all_to_all(gained, "species", 1, 3, tiled=True)
    gathered = gathered.reshape(out_rows, own_count, cell_count)
    pieces = [None] * mode_devs
    pieces[0] = gathered
    for shift, got in shift_permutes(gathered, "mode", holders, mode_devs, True):
        pieces[shift] = got
    stacked = jnp.stack(pieces)
    by_source = jnp.take(stacked, (mode_id - jnp.arange(mode_devs)) % mode_devs, axis=0)
    all_gained = by_source.reshape(mode_devs * out_rows, own_count, cell_count)

    local_modes = mode_id * mode_count + jnp.arange(mode_count)
    match = low_map[None, :] == local_modes[:, None]
    inverse = jnp.argmax(match, axis=1)
    coll_low = jnp.moveaxis(jnp.take(all_gained, inverse, axis=0), 0, 1)
    vx_degree = first_vx + jnp.arange(per_vx)
    degree_total = (
        vx_degree[:, None, None] + jnp.arange(NVY)[None, :, None] + jnp.arange(NVZ)[None, None, :]
    ).reshape(1, mode_count, 1)
    collide = jnp.where(
        degree_total > DEG, -relax_rate.reshape(own_count, 1, 1) * flat_dist, coll_low
    )
    return advected.reshape(
        own_count, mode_count, row_count, plane_cells
    ) + dt_step * collide.reshape(own_count, mode_count, row_count, plane_cells)


def solution(mesh):
    in_specs = (
        P("species", "mode", "space", None),
        P(None, "mode", None, None),
        P(),
        P(),
        P("species"),
        P("species"),
    )
    out_specs = P("species", "mode", "space", None)
    return jax.shard_map(
        per_device, mesh=mesh, in_specs=in_specs, out_specs=out_specs, check_vma=False
    )
```

profile of v0, /device:TPU:2, one launch (start us, length us, event | category | flops | bytes accessed | tf_op | source)
XLA Modules:
  0.0 116.3 jit_solution(10913752298958969283)
XLA Ops:
  0.0 3.7 %reduce.18 = f32[2,256,512]{2,1,0:T(8,128)S(1)} reduce(f32[2,256,1,512]{3,2,1,0:T(1,128)} %param.6, f32[]{:T(128)} %constant.119), dimensions={2}, to_apply=%param.6.reduce_sub_computation | reduce | bytes 2097156 | tf_op args[0]
  4.5 4.2 %collective-permute-start.1 = (f32[2,1,8,8,1,2,256]{6,3,5,4,2,1,0:T(8,128)}, f32[2,1,8,8,1,2,256]{6,3,5,4,2,1,0:T(8,128)}, u32[]{:S(2)}, u32[]{:S(2)}) collective-permute-start(f32[2,1,8,8,1,2,256]{6,3,5,4,2,1,0:T(8,128)} %get-tuple-element.20), channel_id=1, source_target_pairs={{0,16},{16,32},{32,48},{1,17},{17,33},{33,49},{2,18},{18,34},{34,5... | collective-permute-start | bytes 786440 | tf_op jit(solution)/shard_map/ppermute | solution.py:99
  8.7 1.3 %collective-permute-start = (f32[2,1,8,8,1,2,256]{6,3,5,4,2,1,0:T(8,128)}, f32[2,1,8,8,1,2,256]{6,3,5,4,2,1,0:T(8,128)}, u32[]{:S(2)}, u32[]{:S(2)}) collective-permute-start(f32[2,1,8,8,1,2,256]{6,3,5,4,2,1,0:T(8,128)} %get-tuple-element.19), channel_id=1, source_target_pairs={{16,0},{32,16},{48,32},{17,1},{33,17},{49,33},{18,2},{34,18},{50,3... | collective-permute-start | bytes 786440 | tf_op jit(solution)/shard_map/ppermute | solution.py:102
  10.0 2.0 %copy.205 = bf16[2,256,1,512]{3,0,1,2:T(2,128)(2,1)S(1)} copy(f32[2,256,1,512]{3,2,1,0:T(1,128)} %param.6) | data formatting | bytes 1572864 | tf_op args[0]
  13.2 1.4 %fusion.26 = bf16[2,120,4,128]{3,0,1,2:T(2,128)(2,1)} fusion(pred[120]{0:T(512)(128)(4,1)S(1)} %get-tuple-element.9, pred[120]{0:T(512)(128)(4,1)S(1)} %get-tuple-element.39, bf16[120,2,512]{2,1,0:T(2,128)(2,1)S(1)} %gather_fusion), kind=kLoop, calls=%fused_computation.53 | loop fusion | flops 245760 | bytes 491760 | tf_op jit(solution)/shard_map/convert_element_type | solution.py:126
  14.6 5.9 %all-to-all-start = ((bf16[2,120,4,128]{3,0,1,2:T(2,128)(2,1)}), bf16[2,120,4,128]{3,0,1,2:T(2,128)(2,1)S(1)}, u32[]{:S(2)}, u32[]{:S(2)}) async-start(bf16[2,120,4,128]{3,0,1,2:T(2,128)(2,1)} %fusion.26), calls=%async_computation | async-start | bytes 491520 | tf_op jit(solution)/shard_map/all_to_all | solution.py:130
  20.5 1.2 %fusion.37 = (f32[2,4,8,8,1,2,1]{6,3,5,4,2,1,0:T(8,128)}, f32[2,4,8,8,1,2,1]{6,3,5,4,2,1,0:T(8,128)}) fusion(f32[2,4,8,8,1,2,256]{6,3,5,4,2,1,0:T(8,128)S(1)} %bitcast.78), kind=kLoop, calls=%fused_computation.97 | loop fusion | bytes 16384 | tf_op jit(solution)/shard_map/jit(_roll_static)/slice | solution.py:51
  21.7 1.7 %fusion.38 = (f32[2,4,8,8,1,2,255]{6,3,5,4,2,1,0:T(8,128)}, f32[2,4,8,8,1,2,255]{6,3,5,4,2,1,0:T(8,128)}) fusion(f32[2,4,8,8,1,2,256]{6,3,5,4,2,1,0:T(8,128)S(1)} %bitcast.79), kind=kLoop, calls=%fused_computation.98 | loop fusion | bytes 4177920 | tf_op jit(solution)/shard_map/jit(_roll_static)/slice | solution.py:51
  25.9 2.0 %pad_maximum_fusion.k_ref = bf16[30,128,512]{2,1,0:T(8,128)(2,1)} fusion(bf16[30,128,128]{2,1,0:T(8,128)(2,1)S(1)} %get-tuple-element.12, bf16[30,128,128]{2,1,0:T(8,128)(2,1)S(1)} %get-tuple-element.11), kind=kLoop, calls=%fused_computation.3 | loop fusion | flops 15728640 | bytes 5898240 | tf_op jit(solution)/shard_map/concatenate | solution.py:147
  28.3 3.1 %multiply_subtract_fusion = (f32[2,4,8,8,1,2,256]{6,3,5,4,2,1,0:T(8,128)}, f32[2,4,8,8,1,2,256]{6,3,5,4,2,1,0:T(8,128)}, f32[2,4,8,8,1,2,256]{6,3,5,4,2,1,0:T(8,128)S(1)}, f32[2,4,8,8,1,2,256]{6,3,5,4,2,1,0:T(8,128)S(1)}) fusion(f32[2,4,8,8,1,2,256]{6,3,5,4,2,1,0:T(8,128)S(1)} %bitcast.81, f32[2,1,8,8,1,2,256]{6,3,5,4,2,1,0:T(8,128)} %collective-permute-done.1, ...), kind=kLoop, calls=%fused_computation.43 | loop fusion | flops 4194304 | bytes 5770240 | tf_op jit(solution)/shard_map/sub | solution.py:105
  31.4 5.7 %collective-permute-start.2 = (f32[2,4,8,8,1,2,256]{6,3,5,4,2,1,0:T(8,128)}, f32[2,4,8,8,1,2,256]{6,3,5,4,2,1,0:T(8,128)}, u32[]{:S(2)}, u32[]{:S(2)}) collective-permute-start(f32[2,4,8,8,1,2,256]{6,3,5,4,2,1,0:T(8,128)} %get-tuple-element.14), channel_id=1, source_target_pairs={{1,0},{2,1},{3,2},{4,3},{5,4},{6,5},{7,6},{8,7},{9,8},{10,9},{11,1... | collective-permute-start | bytes 3145736 | tf_op jit(solution)/shard_map/ppermute | solution.py:106
  37.1 1.9 %collective-permute-start.3 = (f32[2,4,8,8,1,2,256]{6,3,5,4,2,1,0:T(8,128)}, f32[2,4,8,8,1,2,256]{6,3,5,4,2,1,0:T(8,128)}, u32[]{:S(2)}, u32[]{:S(2)}) collective-permute-start(f32[2,4,8,8,1,2,256]{6,3,5,4,2,1,0:T(8,128)} %get-tuple-element.13), channel_id=1, source_target_pairs={{0,1},{1,2},{2,3},{3,4},{4,5},{5,6},{6,7},{7,8},{8,9},{9,10},{10,1... | collective-permute-start | bytes 3145736 | tf_op jit(solution)/shard_map/ppermute | solution.py:109
  39.1 5.7 %collective-permute-start.6 = (bf16[8,120,1,128]{3,1,0,2:T(8,128)(2,1)S(1)}, bf16[8,120,1,128]{3,1,0,2:T(8,128)(2,1)S(1)}, u32[]{:S(2)}, u32[]{:S(2)}) collective-permute-start(bf16[8,120,1,128]{3,1,0,2:T(8,128)(2,1)S(1)} %bitcast.91), channel_id=1, source_target_pairs={{0,48},{16,0},{1,49},{17,1},{2,50},{18,2},{3,51},{19,3},{4,52},{20... | collective-permute-start | bytes 737288 | tf_op jit(solution)/shard_map/ppermute | solution.py:82
  44.8 1.3 %collective-permute-start.5 = (bf16[8,120,1,128]{3,1,0,2:T(8,128)(2,1)S(1)}, bf16[8,120,1,128]{3,1,0,2:T(8,128)(2,1)S(1)}, u32[]{:S(2)}, u32[]{:S(2)}) collective-permute-start(bf16[8,120,1,128]{3,1,0,2:T(8,128)(2,1)S(1)} %bitcast.92), channel_id=1, source_target_pairs={{0,32},{16,48},{1,33},{17,49},{2,34},{18,50},{3,35},{19,51},{4,36}... | collective-permute-start | bytes 737288 | tf_op jit(solution)/shard_map/ppermute | solution.py:82
  46.1 2.8 %collective-permute-start.4 = (bf16[8,120,1,128]{3,1,0,2:T(8,128)(2,1)S(1)}, bf16[8,120,1,128]{3,1,0,2:T(8,128)(2,1)S(1)}, u32[]{:S(2)}, u32[]{:S(2)}) collective-permute-start(bf16[8,120,1,128]{3,1,0,2:T(8,128)(2,1)S(1)} %bitcast.93), channel_id=1, source_target_pairs={{0,16},{16,32},{1,17},{17,33},{2,18},{18,34},{3,19},{19,35},{4,20}... | collective-permute-start | bytes 737288 | tf_op jit(solution)/shard_map/ppermute | solution.py:82
  48.9 1.7 %fusion.40 = (f32[2,4,8,8,1,2,255]{6,3,5,4,2,1,0:T(8,128)}, f32[2,4,8,8,1,2,255]{6,3,5,4,2,1,0:T(8,128)}) fusion(f32[2,4,8,8,1,2,256]{6,3,5,4,2,1,0:T(8,128)S(1)} %get-tuple-element.17), kind=kLoop, calls=%fused_computation.100 | loop fusion | bytes 4177920 | tf_op jit(solution)/shard_map/jit(_roll_static)/slice | solution.py:53
  50.6 5.5 %collective-permute-done.6 = bf16[8,120,1,128]{3,1,0,2:T(8,128)(2,1)S(1)} collective-permute-done((bf16[8,120,1,128]{3,1,0,2:T(8,128)(2,1)S(1)}, bf16[8,120,1,128]{3,1,0,2:T(8,128)(2,1)S(1)}, u32[]{:S(2)}, u32[]{:S(2)}) %collective-permute-start.6) | collective-permute-done | bytes 245792 | tf_op jit(solution)/shard_map/ppermute | solution.py:82
  56.1 1.3 %collective-permute-done.4 = bf16[8,120,1,128]{3,1,0,2:T(8,128)(2,1)S(1)} collective-permute-done((bf16[8,120,1,128]{3,1,0,2:T(8,128)(2,1)S(1)}, bf16[8,120,1,128]{3,1,0,2:T(8,128)(2,1)S(1)}, u32[]{:S(2)}, u32[]{:S(2)}) %collective-permute-start.4) | collective-permute-done | bytes 245792 | tf_op jit(solution)/shard_map/ppermute | solution.py:82
  58.4 1.3 %copy.204 = bf16[64,8,8,128]{3,1,2,0:T(8,128)(2,1)} copy(bf16[64,8,8,128]{3,2,1,0:T(8,128)(2,1)S(1)} %bitcast.84) | data formatting | bytes 2097152
  60.6 13.0 %shard_map.64 = f32[30,1024]{1,0:T(8,128)} custom-call(bf16[30,128,512]{2,1,0:T(8,128)(2,1)} %pad_maximum_fusion.k_ref, bf16[512,1024]{1,0:T(8,128)(2,1)} %bitcast.85, f32[128,1024]{1,0:T(8,128)} %copy_bitcast_fusion.2.l_ref), custom_call_target="tpu_custom_call" | custom-call | tf_op jit(solution)/shard_map/pallas_call | solution.py:68
  75.3 4.5 %all-to-all-start.1 = ((f32[30,4,2,128]{3,2,0,1:T(2,128)}), f32[30,4,2,128]{3,2,0,1:T(2,128)S(1)}, u32[]{:S(2)}, u32[]{:S(2)}) async-start(f32[30,4,2,128]{3,2,0,1:T(2,128)} %copy.180), calls=%async_computation.1 | async-start | bytes 245760 | tf_op jit(solution)/shard_map/all_to_all | solution.py:151
  79.9 1.2 fusion.39
  81.0 7.9 %all-to-all-done.1 = f32[30,4,2,128]{3,2,0,1:T(2,128)S(1)} async-done(((f32[30,4,2,128]{3,2,0,1:T(2,128)}), f32[30,4,2,128]{3,2,0,1:T(2,128)S(1)}, u32[]{:S(2)}, u32[]{:S(2)}) %all-to-all-start.1) | async-done | bytes 122912 | tf_op jit(solution)/shard_map/all_to_all | solution.py:151
  89.1 1.3 %collective-permute-start.9 = (f32[30,2,512]{2,1,0:T(2,128)S(1)}, f32[30,2,512]{2,1,0:T(2,128)S(1)}, u32[]{:S(2)}, u32[]{:S(2)}) collective-permute-start(f32[30,2,512]{2,1,0:T(2,128)S(1)} %reshape.477), channel_id=1, source_target_pairs={{16,0},{32,16},{17,1},{33,17},{18,2},{34,18},{19,3},{35,19},{20,4}... | collective-permute-start | bytes 368648 | tf_op jit(solution)/shard_map/ppermute | solution.py:82
  90.4 1.3 %collective-permute-start.8 = (f32[30,2,512]{2,1,0:T(2,128)S(1)}, f32[30,2,512]{2,1,0:T(2,128)S(1)}, u32[]{:S(2)}, u32[]{:S(2)}) collective-permute-start(f32[30,2,512]{2,1,0:T(2,128)S(1)} %reshape.477), channel_id=1, source_target_pairs={{32,0},{48,16},{33,1},{49,17},{34,2},{50,18},{35,3},{51,19},{36,4}... | collective-permute-start | bytes 368648 | tf_op jit(solution)/shard_map/ppermute | solution.py:82
  91.7 5.4 %collective-permute-start.7 = (f32[30,2,512]{2,1,0:T(2,128)S(1)}, f32[30,2,512]{2,1,0:T(2,128)S(1)}, u32[]{:S(2)}, u32[]{:S(2)}) collective-permute-start(f32[30,2,512]{2,1,0:T(2,128)S(1)} %reshape.477), channel_id=1, source_target_pairs={{48,0},{0,16},{49,1},{1,17},{50,2},{2,18},{51,3},{3,19},{52,4},{4,... | collective-permute-start | bytes 368648 | tf_op jit(solution)/shard_map/ppermute | solution.py:82
  98.3 2.0 %collective-permute-done.8 = f32[30,2,512]{2,1,0:T(2,128)S(1)} collective-permute-done((f32[30,2,512]{2,1,0:T(2,128)S(1)}, f32[30,2,512]{2,1,0:T(2,128)S(1)}, u32[]{:S(2)}, u32[]{:S(2)}) %collective-permute-start.8) | collective-permute-done | bytes 122912 | tf_op jit(solution)/shard_map/ppermute | solution.py:82
  100.3 2.6 %collective-permute-done.7 = f32[30,2,512]{2,1,0:T(2,128)S(1)} collective-permute-done((f32[30,2,512]{2,1,0:T(2,128)S(1)}, f32[30,2,512]{2,1,0:T(2,128)S(1)}, u32[]{:S(2)}, u32[]{:S(2)}) %collective-permute-start.7) | collective-permute-done | bytes 122912 | tf_op jit(solution)/shard_map/ppermute | solution.py:82
  104.5 1.8 %gather_fusion.2 = f32[256,2,512]{2,1,0:T(2,128)S(1)} fusion(f32[120,2,512]{2,1,0:T(2,128)S(1)} %bitcast_select_fusion.2, s32[1024]{0:T(1024)S(1)} %pad_clamp_fusion), kind=kCustom, calls=%fused_computation.2 | custom fusion | bytes 2098176 | tf_op jit(solution)/shard_map/jit(_take)/gather | solution.py:164
  106.3 5.1 %fusion.7 = f32[2,4,8,8,1,2,256]{6,3,5,4,2,1,0:T(8,128)S(1)} fusion(f32[2,4,8,8,1,2,256]{6,3,5,4,2,1,0:T(8,128)S(1)} %bitcast.82, f32[2,4,8,8,1,2,1]{6,3,5,4,2,1,0:T(8,128)} %get-tuple-element.30, f32[2,4,8,8,1,2,255]{6,3,5,4,2,1,0:T(8,128)} %get-tuple-element.32, f32[2,4,8,8,1,2,255]{6,3,5,4,2,1,0:T(8,128)} %get-tuple-element.31, ...), kind=kLoop, calls=%fused_computation.19 | loop fusion | flops 6815744 | bytes 10485768 | tf_op jit(solution)/shard_map/sub | solution.py:118
  111.4 2.8 %fusion.22 = f32[2,256,1,512]{3,0,1,2:T(2,128)S(1)} fusion(f32[2,256,512]{2,1,0:T(8,128)S(1)} %bitcast.83, f32[256,2,512]{2,1,0:T(2,128)S(1)} %gather_fusion.2, pred[256]{0:T(512)(128)(4,1)S(1)} %compare_and_fusion.3, pred[256]{0:T(512)(128)(4,1)S(1)} %gt.18, f32[2]{0:T(128)S(1)} %neg.4, f32[2,256,1,512]{3,2,1,0:T(1,128)S(1)} %copy-done), kind=kLoop, calls=%fused_computation.41 | loop fusion | flops 1310720 | bytes 4194824 | tf_op jit(solution)/shard_map/add | solution.py:172
  114.2 2.0 %copy.185 = f32[2,256,1,512]{3,2,1,0:T(1,128)} copy(f32[2,256,1,512]{3,0,1,2:T(2,128)S(1)} %fusion.22) | data formatting | bytes 2097152 | tf_op jit(solution)/shard_map/add | solution.py:172
  (64 shorter events, 11.2 us)
Async XLA Ops:
  0.0 12.1 %copy-start.4 = (s32[120]{0:T(128)S(1)}, s32[120]{0:T(128)}, u32[]{:S(2)}) copy-start(s32[120]{0:T(128)} %param.9) | copy-start | bytes 1444
  4.5 23.7 %collective-permute-start.1 = (f32[2,1,8,8,1,2,256]{6,3,5,4,2,1,0:T(8,128)}, f32[2,1,8,8,1,2,256]{6,3,5,4,2,1,0:T(8,128)}, u32[]{:S(2)}, u32[]{:S(2)}) collective-permute-start(f32[2,1,8,8,1,2,256]{6,3,5,4,2,1,0:T(8,128)} %get-tuple-element.20), channel_id=1, source_target_pairs={{0,16},{16,32},{32,48},{1,17},{17,33},{33,49},{2,18},{18,34},{34,5... | collective-permute-start | bytes 786440 | tf_op jit(solution)/shard_map/ppermute | solution.py:99
  8.7 19.5 %collective-permute-start = (f32[2,1,8,8,1,2,256]{6,3,5,4,2,1,0:T(8,128)}, f32[2,1,8,8,1,2,256]{6,3,5,4,2,1,0:T(8,128)}, u32[]{:S(2)}, u32[]{:S(2)}) collective-permute-start(f32[2,1,8,8,1,2,256]{6,3,5,4,2,1,0:T(8,128)} %get-tuple-element.19), channel_id=1, source_target_pairs={{16,0},{32,16},{48,32},{17,1},{33,17},{49,33},{18,2},{34,18},{50,3... | collective-permute-start | bytes 786440 | tf_op jit(solution)/shard_map/ppermute | solution.py:102
  14.6 24.5 %all-to-all-start = ((bf16[2,120,4,128]{3,0,1,2:T(2,128)(2,1)}), bf16[2,120,4,128]{3,0,1,2:T(2,128)(2,1)S(1)}, u32[]{:S(2)}, u32[]{:S(2)}) async-start(bf16[2,120,4,128]{3,0,1,2:T(2,128)(2,1)} %fusion.26), calls=%async_computation | async-start | bytes 491520 | tf_op jit(solution)/shard_map/all_to_all | solution.py:130
  20.5 4.7 %copy-start.5 = (f32[2]{0:T(128)S(1)}, f32[2]{0:T(128)}, u32[]{:S(2)}) copy-start(f32[2]{0:T(128)} %param.10) | copy-start | bytes 28
  20.5 4.7 %copy-start.2 = (bf16[2,30,120,120]{3,2,1,0:T(8,128)(2,1)S(1)}, bf16[2,30,120,120]{3,2,1,0:T(8,128)(2,1)}, u32[]{:S(2)}) copy-start(bf16[2,30,120,120]{3,2,1,0:T(8,128)(2,1)} %param.7) | copy-start | bytes 5184004
  23.3 2.4 %copy-start.3 = (s32[8,8]{1,0:T(8,128)S(1)}, s32[8,8]{1,0:T(8,128)}, u32[]{:S(2)}) copy-start(s32[8,8]{1,0:T(8,128)} %param.8) | copy-start | bytes 772
  25.1 3.1 %copy-start.6 = (f32[2]{0:T(128)S(1)}, f32[2]{0:T(128)}, u32[]{:S(2)}) copy-start(f32[2]{0:T(128)} %param.11) | copy-start | bytes 28
  31.4 74.9 %collective-permute-start.2 = (f32[2,4,8,8,1,2,256]{6,3,5,4,2,1,0:T(8,128)}, f32[2,4,8,8,1,2,256]{6,3,5,4,2,1,0:T(8,128)}, u32[]{:S(2)}, u32[]{:S(2)}) collective-permute-start(f32[2,4,8,8,1,2,256]{6,3,5,4,2,1,0:T(8,128)} %get-tuple-element.14), channel_id=1, source_target_pairs={{1,0},{2,1},{3,2},{4,3},{5,4},{6,5},{7,6},{8,7},{9,8},{10,9},{11,1... | collective-permute-start | bytes 3145736 | tf_op jit(solution)/shard_map/ppermute | solution.py:106
  37.1 69.1 %collective-permute-start.3 = (f32[2,4,8,8,1,2,256]{6,3,5,4,2,1,0:T(8,128)}, f32[2,4,8,8,1,2,256]{6,3,5,4,2,1,0:T(8,128)}, u32[]{:S(2)}, u32[]{:S(2)}) collective-permute-start(f32[2,4,8,8,1,2,256]{6,3,5,4,2,1,0:T(8,128)} %get-tuple-element.13), channel_id=1, source_target_pairs={{0,1},{1,2},{2,3},{3,4},{4,5},{5,6},{6,7},{7,8},{8,9},{9,10},{10,1... | collective-permute-start | bytes 3145736 | tf_op jit(solution)/shard_map/ppermute | solution.py:109
  39.1 17.0 %collective-permute-start.6 = (bf16[8,120,1,128]{3,1,0,2:T(8,128)(2,1)S(1)}, bf16[8,120,1,128]{3,1,0,2:T(8,128)(2,1)S(1)}, u32[]{:S(2)}, u32[]{:S(2)}) collective-permute-start(bf16[8,120,1,128]{3,1,0,2:T(8,128)(2,1)S(1)} %bitcast.91), channel_id=1, source_target_pairs={{0,48},{16,0},{1,49},{17,1},{2,50},{18,2},{3,51},{19,3},{4,52},{20... | collective-permute-start | bytes 737288 | tf_op jit(solution)/shard_map/ppermute | solution.py:82
  44.8 11.3 %collective-permute-start.5 = (bf16[8,120,1,128]{3,1,0,2:T(8,128)(2,1)S(1)}, bf16[8,120,1,128]{3,1,0,2:T(8,128)(2,1)S(1)}, u32[]{:S(2)}, u32[]{:S(2)}) collective-permute-start(bf16[8,120,1,128]{3,1,0,2:T(8,128)(2,1)S(1)} %bitcast.92), channel_id=1, source_target_pairs={{0,32},{16,48},{1,33},{17,49},{2,34},{18,50},{3,35},{19,51},{4,36}... | collective-permute-start | bytes 737288 | tf_op jit(solution)/shard_map/ppermute | solution.py:82
  46.1 11.3 %collective-permute-start.4 = (bf16[8,120,1,128]{3,1,0,2:T(8,128)(2,1)S(1)}, bf16[8,120,1,128]{3,1,0,2:T(8,128)(2,1)S(1)}, u32[]{:S(2)}, u32[]{:S(2)}) collective-permute-start(bf16[8,120,1,128]{3,1,0,2:T(8,128)(2,1)S(1)} %bitcast.93), channel_id=1, source_target_pairs={{0,16},{16,32},{1,17},{17,33},{2,18},{18,34},{3,19},{19,35},{4,20}... | collective-permute-start | bytes 737288 | tf_op jit(solution)/shard_map/ppermute | solution.py:82
  75.3 13.6 %all-to-all-start.1 = ((f32[30,4,2,128]{3,2,0,1:T(2,128)}), f32[30,4,2,128]{3,2,0,1:T(2,128)S(1)}, u32[]{:S(2)}, u32[]{:S(2)}) async-start(f32[30,4,2,128]{3,2,0,1:T(2,128)} %copy.180), calls=%async_computation.1 | async-start | bytes 245760 | tf_op jit(solution)/shard_map/all_to_all | solution.py:151
  89.1 9.2 %collective-permute-start.9 = (f32[30,2,512]{2,1,0:T(2,128)S(1)}, f32[30,2,512]{2,1,0:T(2,128)S(1)}, u32[]{:S(2)}, u32[]{:S(2)}) collective-permute-start(f32[30,2,512]{2,1,0:T(2,128)S(1)} %reshape.477), channel_id=1, source_target_pairs={{16,0},{32,16},{17,1},{33,17},{18,2},{34,18},{19,3},{35,19},{20,4}... | collective-permute-start | bytes 368648 | tf_op jit(solution)/shard_map/ppermute | solution.py:82
  90.4 9.9 %collective-permute-start.8 = (f32[30,2,512]{2,1,0:T(2,128)S(1)}, f32[30,2,512]{2,1,0:T(2,128)S(1)}, u32[]{:S(2)}, u32[]{:S(2)}) collective-permute-start(f32[30,2,512]{2,1,0:T(2,128)S(1)} %reshape.477), channel_id=1, source_target_pairs={{32,0},{48,16},{33,1},{49,17},{34,2},{50,18},{35,3},{51,19},{36,4}... | collective-permute-start | bytes 368648 | tf_op jit(solution)/shard_map/ppermute | solution.py:82
  91.7 11.2 %collective-permute-start.7 = (f32[30,2,512]{2,1,0:T(2,128)S(1)}, f32[30,2,512]{2,1,0:T(2,128)S(1)}, u32[]{:S(2)}, u32[]{:S(2)}) collective-permute-start(f32[30,2,512]{2,1,0:T(2,128)S(1)} %reshape.477), channel_id=1, source_target_pairs={{48,0},{0,16},{49,1},{1,17},{50,2},{2,18},{51,3},{3,19},{52,4},{4,... | collective-permute-start | bytes 368648 | tf_op jit(solution)/shard_map/ppermute | solution.py:82
  98.2 8.1 %copy-start.1 = (f32[2,4,8,8,1,1,256]{6,3,5,4,2,1,0:T(8,128)S(1)}, f32[2,4,8,8,1,1,256]{6,3,5,4,2,1,0:T(8,128)}, u32[]{:S(2)}) copy-start(f32[2,4,8,8,1,1,256]{6,3,5,4,2,1,0:T(8,128)} %get-tuple-element.23) | copy-start | bytes 1572868
  106.3 5.1 %copy-start = (f32[2,256,1,512]{3,2,1,0:T(1,128)S(1)}, f32[2,256,1,512]{3,2,1,0:T(1,128)}, u32[]{:S(2)}) copy-start(f32[2,256,1,512]{3,2,1,0:T(1,128)} %param.6) | copy-start | bytes 3145732
where the time goes:
time: 117 us; the launch traced here: 116 us
  starting transfers between devices  41.3 us (35%)
  local copies, waits for them, and re-layouts  21.3 us (18%)
  other arithmetic  20.6 us (18%)
  waiting for transfers between devices  19.3 us (16%)
  Pallas kernels  13 us (11%)
    ppermute x6, starting transfers between devices, shift_permutes(): received.append((shift, lax.ppermute(values, axis, pairs)))  17.7 us
    pallas_call x1, Pallas kernels, collide_call(): pl.pallas_call(collide_body, out_shape=jax.ShapeDtypeStruct((kcat.shape[0...  13 us
    ppermute x6, waiting for transfers between devices, shift_permutes(): received.append((shift, lax.ppermute(values, axis, pairs)))  11.4 us
    all_to_all x1, waiting for transfers between devices, per_device(): gathered = lax.all_to_all(gained, 'species', 1, 3, tiled=True)  7.91 us
    all_to_all x1, starting transfers between devices, per_device(): spread = lax.all_to_all(picked, 'species', 2, 0, tiled=True)  5.89 us
    ppermute x1, starting transfers between devices, per_device(): lax.ppermute(up_part[:, :, :, :, :1], 'space', [(i + 1, i) for i in range...  5.75 us
    sub x1, other arithmetic, per_device(): phase_field - nu_step * thermal_speed.reshape(own_count, 1, 1, 1, 1, 1, 1...  5.09 us
    all_to_all x1, starting transfers between devices, per_device(): gathered = lax.all_to_all(gained, 'species', 1, 3, tiled=True)  4.54 us
  transfers between devices with their start and end apart: 12, of which 5 were waited for; matrix products, arithmetic and copies ran while one was open for 24% of the time, Pallas kernels for 11%

commit v1 on v0

--- a/solution.py
+++ b/solution.py
@@ -81,6 +81,29 @@
             pairs = [(h, (h + shift) % count) for h in holders]
         received.append((shift, lax.ppermute(values, axis, pairs)))
     return received
+
+
+def species_exchange(values, split_axis, concat_axis):
+    count = lax.axis_size("species")
+    me = lax.axis_index("species")
+    pieces = [lax.dynamic_slice_in_dim(values, me, 1, axis=split_axis)]
+    for shift in range(1, count):
+        chunk = lax.dynamic_slice_in_dim(values, (me + shift) % count, 1, axis=split_axis)
+        pieces.append(
+            lax.ppermute(chunk, "species", [(i, (i + shift) % count) for i in range(count)])
+        )
+    stacked = jnp.stack(pieces)
+    by_source = jnp.take(stacked, (me - jnp.arange(count)) % count, axis=0)
+    by_source = jnp.moveaxis(by_source, 0, concat_axis)
+    shape = list(values.shape)
+    shape[split_axis] = 1
+    shape[concat_axis] *= count
+    merged = by_source.reshape(
+        by_source.shape[:concat_axis]
+        + (count * by_source.shape[concat_axis + 1],)
+        + by_source.shape[concat_axis + 2 :]
+    )
+    return merged.reshape(shape)
 
 
 def per_device(distribution, kernel, pair_kind, low_map, thermal_speed, relax_rate):
@@ -127,7 +150,7 @@
         jnp.bfloat16
     )
     picked = picked.reshape(own_count, low_count, species_devs, block_cells)
-    spread = lax.all_to_all(picked, "species", 2, 0, tiled=True)
+    spread = species_exchange(picked, 2, 0)
     holders = [h for h in range(mode_devs) if h * per_vx <= DEG]
     low_all = spread
     for _, got in shift_permutes(spread, "mode", holders, mode_devs, False):
@@ -148,7 +171,7 @@
     gained = collide_call(kcat, rhs, lmat)
 
     gained = gained.reshape(out_rows, species_devs, own_count, block_cells)
-    gathered = lax.all_to_all(gained, "species", 1, 3, tiled=True)
+    gathered = species_exchange(gained, 1, 3)
     gathered = gathered.reshape(out_rows, own_count, cell_count)
     pieces = [None] * mode_devs
     pieces[0] = gathered

time: 117 us -> 126 us (1.077)
  waiting for transfers between devices: 19.3 us -> 30.8 us
  starting transfers between devices: 41.3 us -> 38.6 us
  local copies, waits for them, and re-layouts: 21.3 us -> 23 us
  other arithmetic: 20.6 us -> 19.1 us
    ppermute x0 -> x6, waiting for transfers between devices: none -> 26.3 us  [species_exchange(): lax.ppermute(chunk, 'species', [(i, (i + shift) % count) for i in range(c...]
    all_to_all x2 -> x0, starting transfers between devices: 10.4 us -> none  [the longest x1 5.89 us: per_device(): spread = lax.all_to_all(picked, 'species', 2, 0, tiled=True)]
    ppermute x0 -> x6, starting transfers between devices: none -> 9.28 us  [species_exchange(): lax.ppermute(chunk, 'species', [(i, (i + shift) % count) for i in range(c...]
    all_to_all x2 -> x0, waiting for transfers between devices: 7.91 us -> none  [the longest x1 7.91 us: per_device(): gathered = lax.all_to_all(gained, 'species', 1, 3, tiled=True)]
    ppermute x6, waiting for transfers between devices: 11.4 us -> 4.44 us  [shift_permutes(): received.append((shift, lax.ppermute(values, axis, pairs)))]
    gather x0 -> x2, local copies, waits for them, and re-layouts: none -> 1.27 us  [species_exchange(): by_source = jnp.take(stacked, (me - jnp.arange(count)) % count, axis=0)]
    unnamed x17 -> x18, local copies, waits for them, and re-layouts: 3.52 us -> 4.39 us
  transfers between devices with their start and end apart: 12 -> 16, of which waited for: 5 -> 4; matrix products, arithmetic and copies ran while one was open for 24% -> 22% of each run, Pallas kernels for 11% -> 10%
where the time goes in v1:
time: 126 us; the launch traced here: 125 us
  starting transfers between devices  38.6 us (31%)
  waiting for transfers between devices  30.8 us (24%)
  local copies, waits for them, and re-layouts  23 us (18%)
  other arithmetic  19.1 us (15%)
  Pallas kernels  13 us (10%)
    ppermute x6, waiting for transfers between devices, species_exchange(): lax.ppermute(chunk, 'species', [(i, (i + shift) % count) for i in range(c...  26.3 us
    ppermute x6, starting transfers between devices, shift_permutes(): received.append((shift, lax.ppermute(values, axis, pairs)))  17.2 us
    pallas_call x1, Pallas kernels, collide_call(): pl.pallas_call(collide_body, out_shape=jax.ShapeDtypeStruct((kcat.shape[0...  13 us
    ppermute x6, starting transfers between devices, species_exchange(): lax.ppermute(chunk, 'species', [(i, (i + shift) % count) for i in range(c...  9.28 us
    sub x1, other arithmetic, per_device(): phase_field - nu_step * thermal_speed.reshape(own_count, 1, 1, 1, 1, 1, 1...  5.09 us
    ppermute x1, starting transfers between devices, per_device(): lax.ppermute(up_part[:, :, :, :, :1], 'space', [(i + 1, i) for i in range...  4.74 us
    ppermute x6, waiting for transfers between devices, shift_permutes(): received.append((shift, lax.ppermute(values, axis, pairs)))  4.44 us
    unnamed x18, local copies, waits for them, and re-layouts  4.39 us
  transfers between devices with their start and end apart: 16, of which 4 were waited for; matrix products, arithmetic and copies ran while one was open for 22% of the time, Pallas kernels for 10%

profile of v1, /device:TPU:2, one launch (start us, length us, event | category | flops | bytes accessed | tf_op | source)
XLA Modules:
  0.0 125.3 jit_solution(11530430849819231589)
XLA Ops:
  0.0 3.7 %reduce.18 = f32[2,256,512]{2,1,0:T(8,128)S(1)} reduce(f32[2,256,1,512]{3,2,1,0:T(1,128)} %param.6, f32[]{:T(128)} %constant.182), dimensions={2}, to_apply=%param.6.reduce_sub_computation | reduce | bytes 2097156 | tf_op args[0]
  4.6 4.2 %collective-permute-start.1 = (f32[2,1,8,8,1,2,256]{6,3,5,4,2,1,0:T(8,128)}, f32[2,1,8,8,1,2,256]{6,3,5,4,2,1,0:T(8,128)}, u32[]{:S(2)}, u32[]{:S(2)}) collective-permute-start(f32[2,1,8,8,1,2,256]{6,3,5,4,2,1,0:T(8,128)} %get-tuple-element.20), channel_id=1, source_target_pairs={{0,16},{16,32},{32,48},{1,17},{17,33},{33,49},{2,18},{18,34},{34,5... | collective-permute-start | bytes 786440 | tf_op jit(solution)/shard_map/ppermute | solution.py:122
  8.7 1.3 %collective-permute-start = (f32[2,1,8,8,1,2,256]{6,3,5,4,2,1,0:T(8,128)}, f32[2,1,8,8,1,2,256]{6,3,5,4,2,1,0:T(8,128)}, u32[]{:S(2)}, u32[]{:S(2)}) collective-permute-start(f32[2,1,8,8,1,2,256]{6,3,5,4,2,1,0:T(8,128)} %get-tuple-element.19), channel_id=1, source_target_pairs={{16,0},{32,16},{48,32},{17,1},{33,17},{49,33},{18,2},{34,18},{50,3... | collective-permute-start | bytes 786440 | tf_op jit(solution)/shard_map/ppermute | solution.py:125
  10.0 2.0 %copy.168 = bf16[2,256,1,512]{3,0,1,2:T(2,128)(2,1)S(1)} copy(f32[2,256,1,512]{3,2,1,0:T(1,128)} %param.6) | data formatting | bytes 1572864 | tf_op args[0]
  13.6 4.7 %collective-permute-start.6 = (bf16[2,120,1,128]{3,1,0,2:T(8,128)(2,1)S(1)}, bf16[2,120,1,128]{3,1,0,2:T(8,128)(2,1)S(1)}, u32[]{:S(2)}, u32[]{:S(2)}) collective-permute-start(bf16[2,120,1,128]{3,1,0,2:T(8,128)(2,1)S(1)} %get-tuple-element.38), channel_id=1, source_target_pairs={{0,192},{64,0},{128,64},{192,128},{1,193},{65,1},{129,65},{193,129... | collective-permute-start | bytes 184328 | tf_op jit(solution)/shard_map/ppermute | solution.py:93
  19.0 1.2 fusion.41
  20.2 1.7 %fusion.42 = (f32[2,4,8,8,1,2,255]{6,3,5,4,2,1,0:T(8,128)}, f32[2,4,8,8,1,2,255]{6,3,5,4,2,1,0:T(8,128)}) fusion(f32[2,4,8,8,1,2,256]{6,3,5,4,2,1,0:T(8,128)S(1)} %bitcast.95), kind=kLoop, calls=%fused_computation.126 | loop fusion | bytes 4177920 | tf_op jit(solution)/shard_map/jit(_roll_static)/slice | solution.py:51
  21.9 1.1 fusion.39
  24.9 2.1 %pad_maximum_fusion.k_ref = bf16[30,128,512]{2,1,0:T(8,128)(2,1)} fusion(bf16[30,128,128]{2,1,0:T(8,128)(2,1)S(1)} %get-tuple-element.12, bf16[30,128,128]{2,1,0:T(8,128)(2,1)S(1)} %get-tuple-element.11), kind=kLoop, calls=%fused_computation.5 | loop fusion | flops 15728640 | bytes 5898240 | tf_op jit(solution)/shard_map/concatenate | solution.py:170
  27.8 6.0 %collective-permute-start.9 = (bf16[8,120,1,128]{3,0,1,2:T(8,128)(2,1)S(1)}, bf16[8,120,1,128]{3,0,1,2:T(8,128)(2,1)S(1)}, u32[]{:S(2)}, u32[]{:S(2)}) collective-permute-start(bf16[8,120,1,128]{3,0,1,2:T(8,128)(2,1)S(1)} %copy_select_fusion.1), channel_id=1, source_target_pairs={{0,48},{16,0},{1,49},{17,1},{2,50},{18,2},{3,51},{19,3},{4,52},{20... | collective-permute-start | bytes 737288 | tf_op jit(solution)/shard_map/ppermute | solution.py:82
  33.8 1.3 %collective-permute-start.8 = (bf16[8,120,1,128]{3,0,1,2:T(8,128)(2,1)S(1)}, bf16[8,120,1,128]{3,0,1,2:T(8,128)(2,1)S(1)}, u32[]{:S(2)}, u32[]{:S(2)}) collective-permute-start(bf16[8,120,1,128]{3,0,1,2:T(8,128)(2,1)S(1)} %copy_select_fusion.1), channel_id=1, source_target_pairs={{0,32},{16,48},{1,33},{17,49},{2,34},{18,50},{3,35},{19,51},{4,36}... | collective-permute-start | bytes 737288 | tf_op jit(solution)/shard_map/ppermute | solution.py:82
  35.1 2.8 %collective-permute-start.7 = (bf16[8,120,1,128]{3,0,1,2:T(8,128)(2,1)S(1)}, bf16[8,120,1,128]{3,0,1,2:T(8,128)(2,1)S(1)}, u32[]{:S(2)}, u32[]{:S(2)}) collective-permute-start(bf16[8,120,1,128]{3,0,1,2:T(8,128)(2,1)S(1)} %copy_select_fusion.1), channel_id=1, source_target_pairs={{0,16},{16,32},{1,17},{17,33},{2,18},{18,34},{3,19},{19,35},{4,20}... | collective-permute-start | bytes 737288 | tf_op jit(solution)/shard_map/ppermute | solution.py:82
  37.9 3.1 %multiply_subtract_fusion = (f32[2,4,8,8,1,2,256]{6,3,5,4,2,1,0:T(8,128)}, f32[2,4,8,8,1,2,256]{6,3,5,4,2,1,0:T(8,128)}, f32[2,4,8,8,1,2,256]{6,3,5,4,2,1,0:T(8,128)S(1)}, f32[2,4,8,8,1,2,256]{6,3,5,4,2,1,0:T(8,128)S(1)}) fusion(f32[2,4,8,8,1,2,256]{6,3,5,4,2,1,0:T(8,128)S(1)} %bitcast.97, f32[2,1,8,8,1,2,256]{6,3,5,4,2,1,0:T(8,128)} %collective-permute-done.1, ...), kind=kLoop, calls=%fused_computation.45 | loop fusion | flops 4194304 | bytes 5770240 | tf_op jit(solution)/shard_map/sub | solution.py:128
  41.0 4.7 %collective-permute-start.2 = (f32[2,4,8,8,1,2,256]{6,3,5,4,2,1,0:T(8,128)}, f32[2,4,8,8,1,2,256]{6,3,5,4,2,1,0:T(8,128)}, u32[]{:S(2)}, u32[]{:S(2)}) collective-permute-start(f32[2,4,8,8,1,2,256]{6,3,5,4,2,1,0:T(8,128)} %get-tuple-element.14), channel_id=1, source_target_pairs={{1,0},{2,1},{3,2},{4,3},{5,4},{6,5},{7,6},{8,7},{9,8},{10,9},{11,1... | collective-permute-start | bytes 3145736 | tf_op jit(solution)/shard_map/ppermute | solution.py:129
  45.8 1.9 %collective-permute-start.3 = (f32[2,4,8,8,1,2,256]{6,3,5,4,2,1,0:T(8,128)}, f32[2,4,8,8,1,2,256]{6,3,5,4,2,1,0:T(8,128)}, u32[]{:S(2)}, u32[]{:S(2)}) collective-permute-start(f32[2,4,8,8,1,2,256]{6,3,5,4,2,1,0:T(8,128)} %get-tuple-element.13), channel_id=1, source_target_pairs={{0,1},{1,2},{2,3},{3,4},{4,5},{5,6},{6,7},{7,8},{8,9},{9,10},{10,1... | collective-permute-start | bytes 3145736 | tf_op jit(solution)/shard_map/ppermute | solution.py:132
  47.7 1.7 %fusion.44 = (f32[2,4,8,8,1,2,255]{6,3,5,4,2,1,0:T(8,128)}, f32[2,4,8,8,1,2,255]{6,3,5,4,2,1,0:T(8,128)}) fusion(f32[2,4,8,8,1,2,256]{6,3,5,4,2,1,0:T(8,128)S(1)} %get-tuple-element.17), kind=kLoop, calls=%fused_computation.128 | loop fusion | bytes 4177920 | tf_op jit(solution)/shard_map/jit(_roll_static)/slice | solution.py:53
  50.4 1.3 %copy.167 = bf16[64,8,8,128]{3,1,2,0:T(8,128)(2,1)} copy(bf16[64,8,8,128]{3,2,1,0:T(8,128)(2,1)S(1)} %bitcast.100) | data formatting | bytes 2097152
  52.6 13.0 %shard_map.64 = f32[30,1024]{1,0:T(8,128)} custom-call(bf16[30,128,512]{2,1,0:T(8,128)(2,1)} %pad_maximum_fusion.k_ref, bf16[512,1024]{1,0:T(8,128)(2,1)} %bitcast.101, f32[128,1024]{1,0:T(8,128)} %bitcast.106), custom_call_target="tpu_custom_call" | custom-call | tf_op jit(solution)/shard_map/pallas_call | solution.py:68
  66.7 3.1 %collective-permute-start.12 = (f32[30,1,2,128]{3,2,0,1:T(2,128)S(1)}, f32[30,1,2,128]{3,2,0,1:T(2,128)S(1)}, u32[]{:S(2)}, u32[]{:S(2)}) collective-permute-start(f32[30,1,2,128]{3,2,0,1:T(2,128)S(1)} %get-tuple-element.44), channel_id=1, source_target_pairs={{0,192},{64,0},{128,64},{192,128},{1,193},{65,1},{129,65},{193,129... | collective-permute-start | bytes 92168 | tf_op jit(solution)/shard_map/ppermute | solution.py:93
  70.6 1.1 fusion.43
  71.7 18.8 %collective-permute-done.12 = f32[30,1,2,128]{3,2,0,1:T(2,128)S(1)} collective-permute-done((f32[30,1,2,128]{3,2,0,1:T(2,128)S(1)}, f32[30,1,2,128]{3,2,0,1:T(2,128)S(1)}, u32[]{:S(2)}, u32[]{:S(2)}) %collective-permute-start.12) | collective-permute-done | bytes 30752 | tf_op jit(solution)/shard_map/ppermute | solution.py:93
  90.5 7.6 %collective-permute-done.11 = f32[30,1,2,128]{3,2,0,1:T(2,128)S(1)} collective-permute-done((f32[30,1,2,128]{3,2,0,1:T(2,128)S(1)}, f32[30,1,2,128]{3,2,0,1:T(2,128)S(1)}, u32[]{:S(2)}, u32[]{:S(2)}) %collective-permute-start.11) | collective-permute-done | bytes 30752 | tf_op jit(solution)/shard_map/ppermute | solution.py:93
  99.1 1.3 %collective-permute-start.15 = (f32[30,2,512]{2,1,0:T(2,128)S(1)}, f32[30,2,512]{2,1,0:T(2,128)S(1)}, u32[]{:S(2)}, u32[]{:S(2)}) collective-permute-start(f32[30,2,512]{2,1,0:T(2,128)S(1)} %reshape_reshape.3), channel_id=1, source_target_pairs={{16,0},{32,16},{17,1},{33,17},{18,2},{34,18},{19,3},{35,19},{20,4}... | collective-permute-start | bytes 368648 | tf_op jit(solution)/shard_map/ppermute | solution.py:82
  100.4 1.3 %collective-permute-start.14 = (f32[30,2,512]{2,1,0:T(2,128)S(1)}, f32[30,2,512]{2,1,0:T(2,128)S(1)}, u32[]{:S(2)}, u32[]{:S(2)}) collective-permute-start(f32[30,2,512]{2,1,0:T(2,128)S(1)} %reshape_reshape.3), channel_id=1, source_target_pairs={{32,0},{48,16},{33,1},{49,17},{34,2},{50,18},{35,3},{51,19},{36,4}... | collective-permute-start | bytes 368648 | tf_op jit(solution)/shard_map/ppermute | solution.py:82
  101.7 4.6 %collective-permute-start.13 = (f32[30,2,512]{2,1,0:T(2,128)S(1)}, f32[30,2,512]{2,1,0:T(2,128)S(1)}, u32[]{:S(2)}, u32[]{:S(2)}) collective-permute-start(f32[30,2,512]{2,1,0:T(2,128)S(1)} %reshape_reshape.3), channel_id=1, source_target_pairs={{48,0},{0,16},{49,1},{1,17},{50,2},{2,18},{51,3},{3,19},{52,4},{4,... | collective-permute-start | bytes 368648 | tf_op jit(solution)/shard_map/ppermute | solution.py:82
  106.2 1.1 fusion.40
  107.5 1.6 %collective-permute-done.14 = f32[30,2,512]{2,1,0:T(2,128)S(1)} collective-permute-done((f32[30,2,512]{2,1,0:T(2,128)S(1)}, f32[30,2,512]{2,1,0:T(2,128)S(1)}, u32[]{:S(2)}, u32[]{:S(2)}) %collective-permute-start.14) | collective-permute-done | bytes 122912 | tf_op jit(solution)/shard_map/ppermute | solution.py:82
  109.1 2.8 %collective-permute-done.13 = f32[30,2,512]{2,1,0:T(2,128)S(1)} collective-permute-done((f32[30,2,512]{2,1,0:T(2,128)S(1)}, f32[30,2,512]{2,1,0:T(2,128)S(1)}, u32[]{:S(2)}, u32[]{:S(2)}) %collective-permute-start.13) | collective-permute-done | bytes 122912 | tf_op jit(solution)/shard_map/ppermute | solution.py:82
  113.5 1.8 %gather_fusion.4 = f32[256,2,512]{2,1,0:T(2,128)S(1)} fusion(f32[120,2,512]{2,1,0:T(2,128)S(1)} %bitcast_select_fusion.1, s32[1024]{0:T(1024)S(1)} %pad_clamp_fusion), kind=kCustom, calls=%fused_computation.4 | custom fusion | bytes 2098176 | tf_op jit(solution)/shard_map/jit(_take)/gather | solution.py:187
  115.3 5.1 %fusion.7 = f32[2,4,8,8,1,2,256]{6,3,5,4,2,1,0:T(8,128)S(1)} fusion(f32[2,4,8,8,1,2,256]{6,3,5,4,2,1,0:T(8,128)S(1)} %bitcast.98, f32[2,4,8,8,1,2,1]{6,3,5,4,2,1,0:T(8,128)} %get-tuple-element.30, f32[2,4,8,8,1,2,255]{6,3,5,4,2,1,0:T(8,128)} %get-tuple-element.32, f32[2,4,8,8,1,2,255]{6,3,5,4,2,1,0:T(8,128)} %get-tuple-element.31, ...), kind=kLoop, calls=%fused_computation.21 | loop fusion | flops 6815744 | bytes 10485768 | tf_op jit(solution)/shard_map/sub | solution.py:141
  120.4 2.8 %fusion.22 = f32[2,256,1,512]{3,0,1,2:T(2,128)S(1)} fusion(f32[2,256,512]{2,1,0:T(8,128)S(1)} %bitcast.99, f32[256,2,512]{2,1,0:T(2,128)S(1)} %gather_fusion.4, pred[256]{0:T(512)(128)(4,1)S(1)} %compare_and_fusion.4, pred[256]{0:T(512)(128)(4,1)S(1)} %gt.18, f32[2]{0:T(128)S(1)} %neg.4, f32[2,256,1,512]{3,2,1,0:T(1,128)S(1)} %copy-done), kind=kLoop, calls=%fused_computation.43 | loop fusion | flops 1310720 | bytes 4194824 | tf_op jit(solution)/shard_map/add | solution.py:195
  123.3 2.0 %copy.145 = f32[2,256,1,512]{3,2,1,0:T(1,128)} copy(f32[2,256,1,512]{3,0,1,2:T(2,128)S(1)} %fusion.22) | data formatting | bytes 2097152 | tf_op jit(solution)/shard_map/add | solution.py:195
  (85 shorter events, 12.0 us)
Async XLA Ops:
  0.0 12.1 %copy-start.4 = (s32[120]{0:T(128)S(1)}, s32[120]{0:T(128)}, u32[]{:S(2)}) copy-start(s32[120]{0:T(128)} %param.9) | copy-start | bytes 1444
  4.6 33.3 %collective-permute-start.1 = (f32[2,1,8,8,1,2,256]{6,3,5,4,2,1,0:T(8,128)}, f32[2,1,8,8,1,2,256]{6,3,5,4,2,1,0:T(8,128)}, u32[]{:S(2)}, u32[]{:S(2)}) collective-permute-start(f32[2,1,8,8,1,2,256]{6,3,5,4,2,1,0:T(8,128)} %get-tuple-element.20), channel_id=1, source_target_pairs={{0,16},{16,32},{32,48},{1,17},{17,33},{33,49},{2,18},{18,34},{34,5... | collective-permute-start | bytes 786440 | tf_op jit(solution)/shard_map/ppermute | solution.py:122
  8.7 29.1 %collective-permute-start = (f32[2,1,8,8,1,2,256]{6,3,5,4,2,1,0:T(8,128)}, f32[2,1,8,8,1,2,256]{6,3,5,4,2,1,0:T(8,128)}, u32[]{:S(2)}, u32[]{:S(2)}) collective-permute-start(f32[2,1,8,8,1,2,256]{6,3,5,4,2,1,0:T(8,128)} %get-tuple-element.19), channel_id=1, source_target_pairs={{16,0},{32,16},{48,32},{17,1},{33,17},{49,33},{18,2},{34,18},{50,3... | collective-permute-start | bytes 786440 | tf_op jit(solution)/shard_map/ppermute | solution.py:125
  13.6 13.4 %collective-permute-start.6 = (bf16[2,120,1,128]{3,1,0,2:T(8,128)(2,1)S(1)}, bf16[2,120,1,128]{3,1,0,2:T(8,128)(2,1)S(1)}, u32[]{:S(2)}, u32[]{:S(2)}) collective-permute-start(bf16[2,120,1,128]{3,1,0,2:T(8,128)(2,1)S(1)} %get-tuple-element.38), channel_id=1, source_target_pairs={{0,192},{64,0},{128,64},{192,128},{1,193},{65,1},{129,65},{193,129... | collective-permute-start | bytes 184328 | tf_op jit(solution)/shard_map/ppermute | solution.py:93
  18.3 8.7 %collective-permute-start.5 = (bf16[2,120,1,128]{3,1,0,2:T(8,128)(2,1)S(1)}, bf16[2,120,1,128]{3,1,0,2:T(8,128)(2,1)S(1)}, u32[]{:S(2)}, u32[]{:S(2)}) collective-permute-start(bf16[2,120,1,128]{3,1,0,2:T(8,128)(2,1)S(1)} %get-tuple-element.39), channel_id=1, source_target_pairs={{0,128},{64,192},{128,0},{192,64},{1,129},{65,193},{129,1},{193,65... | collective-permute-start | bytes 184328 | tf_op jit(solution)/shard_map/ppermute | solution.py:93
  18.3 8.7 %collective-permute-start.4 = (bf16[2,120,1,128]{3,1,0,2:T(8,128)(2,1)S(1)}, bf16[2,120,1,128]{3,1,0,2:T(8,128)(2,1)S(1)}, u32[]{:S(2)}, u32[]{:S(2)}) collective-permute-start(bf16[2,120,1,128]{3,1,0,2:T(8,128)(2,1)S(1)} %get-tuple-element.40), channel_id=1, source_target_pairs={{0,64},{64,128},{128,192},{192,0},{1,65},{65,129},{129,193},{193,1... | collective-permute-start | bytes 184328 | tf_op jit(solution)/shard_map/ppermute | solution.py:93
  19.0 4.7 %copy-start.5 = (f32[2]{0:T(128)S(1)}, f32[2]{0:T(128)}, u32[]{:S(2)}) copy-start(f32[2]{0:T(128)} %param.10) | copy-start | bytes 28
  19.0 4.7 %copy-start.2 = (bf16[2,30,120,120]{3,2,1,0:T(8,128)(2,1)S(1)}, bf16[2,30,120,120]{3,2,1,0:T(8,128)(2,1)}, u32[]{:S(2)}) copy-start(bf16[2,30,120,120]{3,2,1,0:T(8,128)(2,1)} %param.7) | copy-start | bytes 5184004
  21.9 2.4 %copy-start.3 = (s32[8,8]{1,0:T(8,128)S(1)}, s32[8,8]{1,0:T(8,128)}, u32[]{:S(2)}) copy-start(s32[8,8]{1,0:T(8,128)} %param.8) | copy-start | bytes 772
  21.9 3.0 %copy-start.6 = (f32[2]{0:T(128)S(1)}, f32[2]{0:T(128)}, u32[]{:S(2)}) copy-start(f32[2]{0:T(128)} %param.11) | copy-start | bytes 28
  27.8 21.6 %collective-permute-start.9 = (bf16[8,120,1,128]{3,0,1,2:T(8,128)(2,1)S(1)}, bf16[8,120,1,128]{3,0,1,2:T(8,128)(2,1)S(1)}, u32[]{:S(2)}, u32[]{:S(2)}) collective-permute-start(bf16[8,120,1,128]{3,0,1,2:T(8,128)(2,1)S(1)} %copy_select_fusion.1), channel_id=1, source_target_pairs={{0,48},{16,0},{1,49},{17,1},{2,50},{18,2},{3,51},{19,3},{4,52},{20... | collective-permute-start | bytes 737288 | tf_op jit(solution)/shard_map/ppermute | solution.py:82
  33.8 15.6 %collective-permute-start.8 = (bf16[8,120,1,128]{3,0,1,2:T(8,128)(2,1)S(1)}, bf16[8,120,1,128]{3,0,1,2:T(8,128)(2,1)S(1)}, u32[]{:S(2)}, u32[]{:S(2)}) collective-permute-start(bf16[8,120,1,128]{3,0,1,2:T(8,128)(2,1)S(1)} %copy_select_fusion.1), channel_id=1, source_target_pairs={{0,32},{16,48},{1,33},{17,49},{2,34},{18,50},{3,35},{19,51},{4,36}... | collective-permute-start | bytes 737288 | tf_op jit(solution)/shard_map/ppermute | solution.py:82
  35.1 14.3 %collective-permute-start.7 = (bf16[8,120,1,128]{3,0,1,2:T(8,128)(2,1)S(1)}, bf16[8,120,1,128]{3,0,1,2:T(8,128)(2,1)S(1)}, u32[]{:S(2)}, u32[]{:S(2)}) collective-permute-start(bf16[8,120,1,128]{3,0,1,2:T(8,128)(2,1)S(1)} %copy_select_fusion.1), channel_id=1, source_target_pairs={{0,16},{16,32},{1,17},{17,33},{2,18},{18,34},{3,19},{19,35},{4,20}... | collective-permute-start | bytes 737288 | tf_op jit(solution)/shard_map/ppermute | solution.py:82
  41.0 74.3 %collective-permute-start.2 = (f32[2,4,8,8,1,2,256]{6,3,5,4,2,1,0:T(8,128)}, f32[2,4,8,8,1,2,256]{6,3,5,4,2,1,0:T(8,128)}, u32[]{:S(2)}, u32[]{:S(2)}) collective-permute-start(f32[2,4,8,8,1,2,256]{6,3,5,4,2,1,0:T(8,128)} %get-tuple-element.14), channel_id=1, source_target_pairs={{1,0},{2,1},{3,2},{4,3},{5,4},{6,5},{7,6},{8,7},{9,8},{10,9},{11,1... | collective-permute-start | bytes 3145736 | tf_op jit(solution)/shard_map/ppermute | solution.py:129
  45.8 69.6 %collective-permute-start.3 = (f32[2,4,8,8,1,2,256]{6,3,5,4,2,1,0:T(8,128)}, f32[2,4,8,8,1,2,256]{6,3,5,4,2,1,0:T(8,128)}, u32[]{:S(2)}, u32[]{:S(2)}) collective-permute-start(f32[2,4,8,8,1,2,256]{6,3,5,4,2,1,0:T(8,128)} %get-tuple-element.13), channel_id=1, source_target_pairs={{0,1},{1,2},{2,3},{3,4},{4,5},{5,6},{6,7},{7,8},{8,9},{9,10},{10,1... | collective-permute-start | bytes 3145736 | tf_op jit(solution)/shard_map/ppermute | solution.py:132
  66.7 23.8 %collective-permute-start.12 = (f32[30,1,2,128]{3,2,0,1:T(2,128)S(1)}, f32[30,1,2,128]{3,2,0,1:T(2,128)S(1)}, u32[]{:S(2)}, u32[]{:S(2)}) collective-permute-start(f32[30,1,2,128]{3,2,0,1:T(2,128)S(1)} %get-tuple-element.44), channel_id=1, source_target_pairs={{0,192},{64,0},{128,64},{192,128},{1,193},{65,1},{129,65},{193,129... | collective-permute-start | bytes 92168 | tf_op jit(solution)/shard_map/ppermute | solution.py:93
  69.7 28.3 %collective-permute-start.11 = (f32[30,1,2,128]{3,2,0,1:T(2,128)S(1)}, f32[30,1,2,128]{3,2,0,1:T(2,128)S(1)}, u32[]{:S(2)}, u32[]{:S(2)}) collective-permute-start(f32[30,1,2,128]{3,2,0,1:T(2,128)S(1)} %get-tuple-element.42), channel_id=1, source_target_pairs={{0,128},{64,192},{128,0},{192,64},{1,129},{65,193},{129,1},{193,65... | collective-permute-start | bytes 92168 | tf_op jit(solution)/shard_map/ppermute | solution.py:93
  70.3 27.7 %collective-permute-start.10 = (f32[30,1,2,128]{3,2,0,1:T(2,128)S(1)}, f32[30,1,2,128]{3,2,0,1:T(2,128)S(1)}, u32[]{:S(2)}, u32[]{:S(2)}) collective-permute-start(f32[30,1,2,128]{3,2,0,1:T(2,128)S(1)} %get-tuple-element.43), channel_id=1, source_target_pairs={{0,64},{64,128},{128,192},{192,0},{1,65},{65,129},{129,193},{193,1... | collective-permute-start | bytes 92168 | tf_op jit(solution)/shard_map/ppermute | solution.py:93
  99.1 8.4 %collective-permute-start.15 = (f32[30,2,512]{2,1,0:T(2,128)S(1)}, f32[30,2,512]{2,1,0:T(2,128)S(1)}, u32[]{:S(2)}, u32[]{:S(2)}) collective-permute-start(f32[30,2,512]{2,1,0:T(2,128)S(1)} %reshape_reshape.3), channel_id=1, source_target_pairs={{16,0},{32,16},{17,1},{33,17},{18,2},{34,18},{19,3},{35,19},{20,4}... | collective-permute-start | bytes 368648 | tf_op jit(solution)/shard_map/ppermute | solution.py:82
  100.4 8.7 %collective-permute-start.14 = (f32[30,2,512]{2,1,0:T(2,128)S(1)}, f32[30,2,512]{2,1,0:T(2,128)S(1)}, u32[]{:S(2)}, u32[]{:S(2)}) collective-permute-start(f32[30,2,512]{2,1,0:T(2,128)S(1)} %reshape_reshape.3), channel_id=1, source_target_pairs={{32,0},{48,16},{33,1},{49,17},{34,2},{50,18},{35,3},{51,19},{36,4}... | collective-permute-start | bytes 368648 | tf_op jit(solution)/shard_map/ppermute | solution.py:82
  101.7 10.2 %collective-permute-start.13 = (f32[30,2,512]{2,1,0:T(2,128)S(1)}, f32[30,2,512]{2,1,0:T(2,128)S(1)}, u32[]{:S(2)}, u32[]{:S(2)}) collective-permute-start(f32[30,2,512]{2,1,0:T(2,128)S(1)} %reshape_reshape.3), channel_id=1, source_target_pairs={{48,0},{0,16},{49,1},{1,17},{50,2},{2,18},{51,3},{3,19},{52,4},{4,... | collective-permute-start | bytes 368648 | tf_op jit(solution)/shard_map/ppermute | solution.py:82
  107.4 7.9 %copy-start.1 = (f32[2,4,8,8,1,1,256]{6,3,5,4,2,1,0:T(8,128)S(1)}, f32[2,4,8,8,1,1,256]{6,3,5,4,2,1,0:T(8,128)}, u32[]{:S(2)}) copy-start(f32[2,4,8,8,1,1,256]{6,3,5,4,2,1,0:T(8,128)} %get-tuple-element.23) | copy-start | bytes 1572868
  115.3 5.1 %copy-start = (f32[2,256,1,512]{3,2,1,0:T(1,128)S(1)}, f32[2,256,1,512]{3,2,1,0:T(1,128)}, u32[]{:S(2)}) copy-start(f32[2,256,1,512]{3,2,1,0:T(1,128)} %param.6) | copy-start | bytes 3145732

commit v2 on v0

--- a/solution.py
+++ b/solution.py
@@ -11,6 +11,7 @@
 NY = 256
 NZ = 2
 PAD = 128
+ROW_CHUNK = 10
 
 nu_step = 0.0625
 dt_step = 0.05
@@ -56,12 +57,19 @@
 
 
 def collide_body(k_ref, r_ref, l_ref, o_ref):
-    def body(n, carry):
-        z = jnp.dot(k_ref[n], r_ref[...], preferred_element_type=jnp.float32)
-        o_ref[pl.ds(n, 1), :] = jnp.sum(z * l_ref[...], axis=0, keepdims=True)
+    rows, depth, width = k_ref.shape
+    chunk = ROW_CHUNK
+
+    def body(step, carry):
+        first = step * chunk
+        block = k_ref[pl.ds(first, chunk)].reshape(chunk * depth, width)
+        z = jnp.dot(block, r_ref[...], preferred_element_type=jnp.float32)
+        for i in range(chunk):
+            part = z[i * depth : (i + 1) * depth] * l_ref[...]
+            o_ref[pl.ds(first + i, 1), :] = jnp.sum(part, axis=0, keepdims=True)
         return carry
 
-    lax.fori_loop(0, k_ref.shape[0], body, 0)
+    lax.fori_loop(0, rows // chunk, body, 0)
 
 
 def collide_call(kcat, rhs, lmat):

time: 117 us -> 117 us (level)
  waiting for transfers between devices: 19.3 us -> 24.6 us
  Pallas kernels: 13 us -> 7.81 us
    all_to_all x1, waiting for transfers between devices: 7.91 us -> 13.2 us  [per_device(): gathered = lax.all_to_all(gained, 'species', 1, 3, tiled=True)]
    pallas_call x1, Pallas kernels: 13 us -> 7.81 us  [collide_call(): pl.pallas_call(collide_body, out_shape=jax.ShapeDtypeStruct((kcat.shape[0...]
  transfers between devices with their start and end apart: 12 -> 12, of which waited for: 5 -> 5; matrix products, arithmetic and copies ran while one was open for 24% -> 24% of each run, Pallas kernels for 11% -> 7%
where the time goes in v2:
time: 117 us; the launch traced here: 116 us
  starting transfers between devices  41.4 us (35%)
  waiting for transfers between devices  24.6 us (21%)
  local copies, waits for them, and re-layouts  21.3 us (18%)
  other arithmetic  20.6 us (18%)
  Pallas kernels  7.81 us (7%)
    ppermute x6, starting transfers between devices, shift_permutes(): received.append((shift, lax.ppermute(values, axis, pairs)))  17.8 us
    all_to_all x1, waiting for transfers between devices, per_device(): gathered = lax.all_to_all(gained, 'species', 1, 3, tiled=True)  13.2 us
    ppermute x6, waiting for transfers between devices, shift_permutes(): received.append((shift, lax.ppermute(values, axis, pairs)))  11.4 us
    pallas_call x1, Pallas kernels, collide_call(): pl.pallas_call(collide_body, out_shape=jax.ShapeDtypeStruct((kcat.shape[0...  7.81 us
    all_to_all x1, starting transfers between devices, per_device(): spread = lax.all_to_all(picked, 'species', 2, 0, tiled=True)  5.89 us
    ppermute x1, starting transfers between devices, per_device(): lax.ppermute(up_part[:, :, :, :, :1], 'space', [(i + 1, i) for i in range...  5.75 us
    sub x1, other arithmetic, per_device(): phase_field - nu_step * thermal_speed.reshape(own_count, 1, 1, 1, 1, 1, 1...  5.09 us
    all_to_all x1, starting transfers between devices, per_device(): gathered = lax.all_to_all(gained, 'species', 1, 3, tiled=True)  4.53 us
  transfers between devices with their start and end apart: 12, of which 5 were waited for; matrix products, arithmetic and copies ran while one was open for 24% of the time, Pallas kernels for 7%

profile of v2, /device:TPU:2, one launch (start us, length us, event | category | flops | bytes accessed | tf_op | source)
XLA Modules:
  0.0 116.4 jit_solution(16913203471403821101)
XLA Ops:
  0.0 3.7 %reduce.18 = f32[2,256,512]{2,1,0:T(8,128)S(1)} reduce(f32[2,256,1,512]{3,2,1,0:T(1,128)} %param.6, f32[]{:T(128)} %constant.119), dimensions={2}, to_apply=%param.6.reduce_sub_computation | reduce | bytes 2097156 | tf_op args[0]
  4.5 4.2 %collective-permute-start.1 = (f32[2,1,8,8,1,2,256]{6,3,5,4,2,1,0:T(8,128)}, f32[2,1,8,8,1,2,256]{6,3,5,4,2,1,0:T(8,128)}, u32[]{:S(2)}, u32[]{:S(2)}) collective-permute-start(f32[2,1,8,8,1,2,256]{6,3,5,4,2,1,0:T(8,128)} %get-tuple-element.20), channel_id=1, source_target_pairs={{0,16},{16,32},{32,48},{1,17},{17,33},{33,49},{2,18},{18,34},{34,5... | collective-permute-start | bytes 786440 | tf_op jit(solution)/shard_map/ppermute | solution.py:107
  8.7 1.3 %collective-permute-start = (f32[2,1,8,8,1,2,256]{6,3,5,4,2,1,0:T(8,128)}, f32[2,1,8,8,1,2,256]{6,3,5,4,2,1,0:T(8,128)}, u32[]{:S(2)}, u32[]{:S(2)}) collective-permute-start(f32[2,1,8,8,1,2,256]{6,3,5,4,2,1,0:T(8,128)} %get-tuple-element.19), channel_id=1, source_target_pairs={{16,0},{32,16},{48,32},{17,1},{33,17},{49,33},{18,2},{34,18},{50,3... | collective-permute-start | bytes 786440 | tf_op jit(solution)/shard_map/ppermute | solution.py:110
  10.0 2.0 %copy.205 = bf16[2,256,1,512]{3,0,1,2:T(2,128)(2,1)S(1)} copy(f32[2,256,1,512]{3,2,1,0:T(1,128)} %param.6) | data formatting | bytes 1572864 | tf_op args[0]
  13.2 1.4 %fusion.26 = bf16[2,120,4,128]{3,0,1,2:T(2,128)(2,1)} fusion(pred[120]{0:T(512)(128)(4,1)S(1)} %get-tuple-element.9, pred[120]{0:T(512)(128)(4,1)S(1)} %get-tuple-element.39, bf16[120,2,512]{2,1,0:T(2,128)(2,1)S(1)} %gather_fusion), kind=kLoop, calls=%fused_computation.53 | loop fusion | flops 245760 | bytes 491760 | tf_op jit(solution)/shard_map/convert_element_type | solution.py:134
  14.6 5.9 %all-to-all-start = ((bf16[2,120,4,128]{3,0,1,2:T(2,128)(2,1)}), bf16[2,120,4,128]{3,0,1,2:T(2,128)(2,1)S(1)}, u32[]{:S(2)}, u32[]{:S(2)}) async-start(bf16[2,120,4,128]{3,0,1,2:T(2,128)(2,1)} %fusion.26), calls=%async_computation | async-start | bytes 491520 | tf_op jit(solution)/shard_map/all_to_all | solution.py:138
  20.5 1.2 %fusion.37 = (f32[2,4,8,8,1,2,1]{6,3,5,4,2,1,0:T(8,128)}, f32[2,4,8,8,1,2,1]{6,3,5,4,2,1,0:T(8,128)}) fusion(f32[2,4,8,8,1,2,256]{6,3,5,4,2,1,0:T(8,128)S(1)} %bitcast.78), kind=kLoop, calls=%fused_computation.97 | loop fusion | bytes 16384 | tf_op jit(solution)/shard_map/jit(_roll_static)/slice | solution.py:52
  21.7 1.7 %fusion.38 = (f32[2,4,8,8,1,2,255]{6,3,5,4,2,1,0:T(8,128)}, f32[2,4,8,8,1,2,255]{6,3,5,4,2,1,0:T(8,128)}) fusion(f32[2,4,8,8,1,2,256]{6,3,5,4,2,1,0:T(8,128)S(1)} %bitcast.79), kind=kLoop, calls=%fused_computation.98 | loop fusion | bytes 4177920 | tf_op jit(solution)/shard_map/jit(_roll_static)/slice | solution.py:52
  25.9 2.0 %pad_maximum_fusion.k_ref = bf16[30,128,512]{2,1,0:T(8,128)(2,1)} fusion(bf16[30,128,128]{2,1,0:T(8,128)(2,1)S(1)} %get-tuple-element.12, bf16[30,128,128]{2,1,0:T(8,128)(2,1)S(1)} %get-tuple-element.11), kind=kLoop, calls=%fused_computation.3 | loop fusion | flops 15728640 | bytes 5898240 | tf_op jit(solution)/shard_map/concatenate | solution.py:155
  28.3 3.1 %multiply_subtract_fusion = (f32[2,4,8,8,1,2,256]{6,3,5,4,2,1,0:T(8,128)}, f32[2,4,8,8,1,2,256]{6,3,5,4,2,1,0:T(8,128)}, f32[2,4,8,8,1,2,256]{6,3,5,4,2,1,0:T(8,128)S(1)}, f32[2,4,8,8,1,2,256]{6,3,5,4,2,1,0:T(8,128)S(1)}) fusion(f32[2,4,8,8,1,2,256]{6,3,5,4,2,1,0:T(8,128)S(1)} %bitcast.81, f32[2,1,8,8,1,2,256]{6,3,5,4,2,1,0:T(8,128)} %collective-permute-done.1, ...), kind=kLoop, calls=%fused_computation.43 | loop fusion | flops 4194304 | bytes 5770240 | tf_op jit(solution)/shard_map/sub | solution.py:113
  31.4 5.7 %collective-permute-start.2 = (f32[2,4,8,8,1,2,256]{6,3,5,4,2,1,0:T(8,128)}, f32[2,4,8,8,1,2,256]{6,3,5,4,2,1,0:T(8,128)}, u32[]{:S(2)}, u32[]{:S(2)}) collective-permute-start(f32[2,4,8,8,1,2,256]{6,3,5,4,2,1,0:T(8,128)} %get-tuple-element.14), channel_id=1, source_target_pairs={{1,0},{2,1},{3,2},{4,3},{5,4},{6,5},{7,6},{8,7},{9,8},{10,9},{11,1... | collective-permute-start | bytes 3145736 | tf_op jit(solution)/shard_map/ppermute | solution.py:114
  37.1 1.9 %collective-permute-start.3 = (f32[2,4,8,8,1,2,256]{6,3,5,4,2,1,0:T(8,128)}, f32[2,4,8,8,1,2,256]{6,3,5,4,2,1,0:T(8,128)}, u32[]{:S(2)}, u32[]{:S(2)}) collective-permute-start(f32[2,4,8,8,1,2,256]{6,3,5,4,2,1,0:T(8,128)} %get-tuple-element.13), channel_id=1, source_target_pairs={{0,1},{1,2},{2,3},{3,4},{4,5},{5,6},{6,7},{7,8},{8,9},{9,10},{10,1... | collective-permute-start | bytes 3145736 | tf_op jit(solution)/shard_map/ppermute | solution.py:117
  39.1 5.7 %collective-permute-start.6 = (bf16[8,120,1,128]{3,1,0,2:T(8,128)(2,1)S(1)}, bf16[8,120,1,128]{3,1,0,2:T(8,128)(2,1)S(1)}, u32[]{:S(2)}, u32[]{:S(2)}) collective-permute-start(bf16[8,120,1,128]{3,1,0,2:T(8,128)(2,1)S(1)} %bitcast.91), channel_id=1, source_target_pairs={{0,48},{16,0},{1,49},{17,1},{2,50},{18,2},{3,51},{19,3},{4,52},{20... | collective-permute-start | bytes 737288 | tf_op jit(solution)/shard_map/ppermute | solution.py:90
  44.8 1.3 %collective-permute-start.5 = (bf16[8,120,1,128]{3,1,0,2:T(8,128)(2,1)S(1)}, bf16[8,120,1,128]{3,1,0,2:T(8,128)(2,1)S(1)}, u32[]{:S(2)}, u32[]{:S(2)}) collective-permute-start(bf16[8,120,1,128]{3,1,0,2:T(8,128)(2,1)S(1)} %bitcast.92), channel_id=1, source_target_pairs={{0,32},{16,48},{1,33},{17,49},{2,34},{18,50},{3,35},{19,51},{4,36}... | collective-permute-start | bytes 737288 | tf_op jit(solution)/shard_map/ppermute | solution.py:90
  46.1 2.8 %collective-permute-start.4 = (bf16[8,120,1,128]{3,1,0,2:T(8,128)(2,1)S(1)}, bf16[8,120,1,128]{3,1,0,2:T(8,128)(2,1)S(1)}, u32[]{:S(2)}, u32[]{:S(2)}) collective-permute-start(bf16[8,120,1,128]{3,1,0,2:T(8,128)(2,1)S(1)} %bitcast.93), channel_id=1, source_target_pairs={{0,16},{16,32},{1,17},{17,33},{2,18},{18,34},{3,19},{19,35},{4,20}... | collective-permute-start | bytes 737288 | tf_op jit(solution)/shard_map/ppermute | solution.py:90
  48.9 1.7 %fusion.40 = (f32[2,4,8,8,1,2,255]{6,3,5,4,2,1,0:T(8,128)}, f32[2,4,8,8,1,2,255]{6,3,5,4,2,1,0:T(8,128)}) fusion(f32[2,4,8,8,1,2,256]{6,3,5,4,2,1,0:T(8,128)S(1)} %get-tuple-element.17), kind=kLoop, calls=%fused_computation.100 | loop fusion | bytes 4177920 | tf_op jit(solution)/shard_map/jit(_roll_static)/slice | solution.py:54
  50.6 5.5 %collective-permute-done.6 = bf16[8,120,1,128]{3,1,0,2:T(8,128)(2,1)S(1)} collective-permute-done((bf16[8,120,1,128]{3,1,0,2:T(8,128)(2,1)S(1)}, bf16[8,120,1,128]{3,1,0,2:T(8,128)(2,1)S(1)}, u32[]{:S(2)}, u32[]{:S(2)}) %collective-permute-start.6) | collective-permute-done | bytes 245792 | tf_op jit(solution)/shard_map/ppermute | solution.py:90
  56.1 1.3 %collective-permute-done.4 = bf16[8,120,1,128]{3,1,0,2:T(8,128)(2,1)S(1)} collective-permute-done((bf16[8,120,1,128]{3,1,0,2:T(8,128)(2,1)S(1)}, bf16[8,120,1,128]{3,1,0,2:T(8,128)(2,1)S(1)}, u32[]{:S(2)}, u32[]{:S(2)}) %collective-permute-start.4) | collective-permute-done | bytes 245792 | tf_op jit(solution)/shard_map/ppermute | solution.py:90
  58.4 1.3 %copy.204 = bf16[64,8,8,128]{3,1,2,0:T(8,128)(2,1)} copy(bf16[64,8,8,128]{3,2,1,0:T(8,128)(2,1)S(1)} %bitcast.84) | data formatting | bytes 2097152
  60.6 7.8 %shard_map.64 = f32[30,1024]{1,0:T(8,128)} custom-call(bf16[30,128,512]{2,1,0:T(8,128)(2,1)} %pad_maximum_fusion.k_ref, bf16[512,1024]{1,0:T(8,128)(2,1)} %bitcast.85, f32[128,1024]{1,0:T(8,128)} %copy_bitcast_fusion.2.l_ref), custom_call_target="tpu_custom_call" | custom-call | tf_op jit(solution)/shard_map/pallas_call | solution.py:76
  70.1 4.5 %all-to-all-start.1 = ((f32[30,4,2,128]{3,2,0,1:T(2,128)}), f32[30,4,2,128]{3,2,0,1:T(2,128)S(1)}, u32[]{:S(2)}, u32[]{:S(2)}) async-start(f32[30,4,2,128]{3,2,0,1:T(2,128)} %copy.180), calls=%async_computation.1 | async-start | bytes 245760 | tf_op jit(solution)/shard_map/all_to_all | solution.py:159
  74.6 1.2 fusion.39
  75.8 13.2 %all-to-all-done.1 = f32[30,4,2,128]{3,2,0,1:T(2,128)S(1)} async-done(((f32[30,4,2,128]{3,2,0,1:T(2,128)}), f32[30,4,2,128]{3,2,0,1:T(2,128)S(1)}, u32[]{:S(2)}, u32[]{:S(2)}) %all-to-all-start.1) | async-done | bytes 122912 | tf_op jit(solution)/shard_map/all_to_all | solution.py:159
  89.1 1.3 %collective-permute-start.9 = (f32[30,2,512]{2,1,0:T(2,128)S(1)}, f32[30,2,512]{2,1,0:T(2,128)S(1)}, u32[]{:S(2)}, u32[]{:S(2)}) collective-permute-start(f32[30,2,512]{2,1,0:T(2,128)S(1)} %reshape.477), channel_id=1, source_target_pairs={{16,0},{32,16},{17,1},{33,17},{18,2},{34,18},{19,3},{35,19},{20,4}... | collective-permute-start | bytes 368648 | tf_op jit(solution)/shard_map/ppermute | solution.py:90
  90.4 1.3 %collective-permute-start.8 = (f32[30,2,512]{2,1,0:T(2,128)S(1)}, f32[30,2,512]{2,1,0:T(2,128)S(1)}, u32[]{:S(2)}, u32[]{:S(2)}) collective-permute-start(f32[30,2,512]{2,1,0:T(2,128)S(1)} %reshape.477), channel_id=1, source_target_pairs={{32,0},{48,16},{33,1},{49,17},{34,2},{50,18},{35,3},{51,19},{36,4}... | collective-permute-start | bytes 368648 | tf_op jit(solution)/shard_map/ppermute | solution.py:90
  91.7 5.5 %collective-permute-start.7 = (f32[30,2,512]{2,1,0:T(2,128)S(1)}, f32[30,2,512]{2,1,0:T(2,128)S(1)}, u32[]{:S(2)}, u32[]{:S(2)}) collective-permute-start(f32[30,2,512]{2,1,0:T(2,128)S(1)} %reshape.477), channel_id=1, source_target_pairs={{48,0},{0,16},{49,1},{1,17},{50,2},{2,18},{51,3},{3,19},{52,4},{4,... | collective-permute-start | bytes 368648 | tf_op jit(solution)/shard_map/ppermute | solution.py:90
  98.4 2.0 %collective-permute-done.8 = f32[30,2,512]{2,1,0:T(2,128)S(1)} collective-permute-done((f32[30,2,512]{2,1,0:T(2,128)S(1)}, f32[30,2,512]{2,1,0:T(2,128)S(1)}, u32[]{:S(2)}, u32[]{:S(2)}) %collective-permute-start.8) | collective-permute-done | bytes 122912 | tf_op jit(solution)/shard_map/ppermute | solution.py:90
  100.4 2.6 %collective-permute-done.7 = f32[30,2,512]{2,1,0:T(2,128)S(1)} collective-permute-done((f32[30,2,512]{2,1,0:T(2,128)S(1)}, f32[30,2,512]{2,1,0:T(2,128)S(1)}, u32[]{:S(2)}, u32[]{:S(2)}) %collective-permute-start.7) | collective-permute-done | bytes 122912 | tf_op jit(solution)/shard_map/ppermute | solution.py:90
  104.6 1.8 %gather_fusion.2 = f32[256,2,512]{2,1,0:T(2,128)S(1)} fusion(f32[120,2,512]{2,1,0:T(2,128)S(1)} %bitcast_select_fusion.2, s32[1024]{0:T(1024)S(1)} %pad_clamp_fusion), kind=kCustom, calls=%fused_computation.2 | custom fusion | bytes 2098176 | tf_op jit(solution)/shard_map/jit(_take)/gather | solution.py:172
  106.4 5.1 %fusion.7 = f32[2,4,8,8,1,2,256]{6,3,5,4,2,1,0:T(8,128)S(1)} fusion(f32[2,4,8,8,1,2,256]{6,3,5,4,2,1,0:T(8,128)S(1)} %bitcast.82, f32[2,4,8,8,1,2,1]{6,3,5,4,2,1,0:T(8,128)} %get-tuple-element.30, f32[2,4,8,8,1,2,255]{6,3,5,4,2,1,0:T(8,128)} %get-tuple-element.32, f32[2,4,8,8,1,2,255]{6,3,5,4,2,1,0:T(8,128)} %get-tuple-element.31, ...), kind=kLoop, calls=%fused_computation.19 | loop fusion | flops 6815744 | bytes 10485768 | tf_op jit(solution)/shard_map/sub | solution.py:126
  111.5 2.8 %fusion.22 = f32[2,256,1,512]{3,0,1,2:T(2,128)S(1)} fusion(f32[2,256,512]{2,1,0:T(8,128)S(1)} %bitcast.83, f32[256,2,512]{2,1,0:T(2,128)S(1)} %gather_fusion.2, pred[256]{0:T(512)(128)(4,1)S(1)} %compare_and_fusion.3, pred[256]{0:T(512)(128)(4,1)S(1)} %gt.18, f32[2]{0:T(128)S(1)} %neg.4, f32[2,256,1,512]{3,2,1,0:T(1,128)S(1)} %copy-done), kind=kLoop, calls=%fused_computation.41 | loop fusion | flops 1310720 | bytes 4194824 | tf_op jit(solution)/shard_map/add | solution.py:180
  114.3 2.0 %copy.185 = f32[2,256,1,512]{3,2,1,0:T(1,128)} copy(f32[2,256,1,512]{3,0,1,2:T(2,128)S(1)} %fusion.22) | data formatting | bytes 2097152 | tf_op jit(solution)/shard_map/add | solution.py:180
  (64 shorter events, 11.2 us)
Async XLA Ops:
  0.0 12.1 %copy-start.4 = (s32[120]{0:T(128)S(1)}, s32[120]{0:T(128)}, u32[]{:S(2)}) copy-start(s32[120]{0:T(128)} %param.9) | copy-start | bytes 1444
  4.5 23.7 %collective-permute-start.1 = (f32[2,1,8,8,1,2,256]{6,3,5,4,2,1,0:T(8,128)}, f32[2,1,8,8,1,2,256]{6,3,5,4,2,1,0:T(8,128)}, u32[]{:S(2)}, u32[]{:S(2)}) collective-permute-start(f32[2,1,8,8,1,2,256]{6,3,5,4,2,1,0:T(8,128)} %get-tuple-element.20), channel_id=1, source_target_pairs={{0,16},{16,32},{32,48},{1,17},{17,33},{33,49},{2,18},{18,34},{34,5... | collective-permute-start | bytes 786440 | tf_op jit(solution)/shard_map/ppermute | solution.py:107
  8.7 19.5 %collective-permute-start = (f32[2,1,8,8,1,2,256]{6,3,5,4,2,1,0:T(8,128)}, f32[2,1,8,8,1,2,256]{6,3,5,4,2,1,0:T(8,128)}, u32[]{:S(2)}, u32[]{:S(2)}) collective-permute-start(f32[2,1,8,8,1,2,256]{6,3,5,4,2,1,0:T(8,128)} %get-tuple-element.19), channel_id=1, source_target_pairs={{16,0},{32,16},{48,32},{17,1},{33,17},{49,33},{18,2},{34,18},{50,3... | collective-permute-start | bytes 786440 | tf_op jit(solution)/shard_map/ppermute | solution.py:110
  14.6 24.5 %all-to-all-start = ((bf16[2,120,4,128]{3,0,1,2:T(2,128)(2,1)}), bf16[2,120,4,128]{3,0,1,2:T(2,128)(2,1)S(1)}, u32[]{:S(2)}, u32[]{:S(2)}) async-start(bf16[2,120,4,128]{3,0,1,2:T(2,128)(2,1)} %fusion.26), calls=%async_computation | async-start | bytes 491520 | tf_op jit(solution)/shard_map/all_to_all | solution.py:138
  20.5 4.7 %copy-start.5 = (f32[2]{0:T(128)S(1)}, f32[2]{0:T(128)}, u32[]{:S(2)}) copy-start(f32[2]{0:T(128)} %param.10) | copy-start | bytes 28
  20.5 4.7 %copy-start.2 = (bf16[2,30,120,120]{3,2,1,0:T(8,128)(2,1)S(1)}, bf16[2,30,120,120]{3,2,1,0:T(8,128)(2,1)}, u32[]{:S(2)}) copy-start(bf16[2,30,120,120]{3,2,1,0:T(8,128)(2,1)} %param.7) | copy-start | bytes 5184004
  23.3 2.4 %copy-start.3 = (s32[8,8]{1,0:T(8,128)S(1)}, s32[8,8]{1,0:T(8,128)}, u32[]{:S(2)}) copy-start(s32[8,8]{1,0:T(8,128)} %param.8) | copy-start | bytes 772
  25.1 3.1 %copy-start.6 = (f32[2]{0:T(128)S(1)}, f32[2]{0:T(128)}, u32[]{:S(2)}) copy-start(f32[2]{0:T(128)} %param.11) | copy-start | bytes 28
  31.4 75.0 %collective-permute-start.2 = (f32[2,4,8,8,1,2,256]{6,3,5,4,2,1,0:T(8,128)}, f32[2,4,8,8,1,2,256]{6,3,5,4,2,1,0:T(8,128)}, u32[]{:S(2)}, u32[]{:S(2)}) collective-permute-start(f32[2,4,8,8,1,2,256]{6,3,5,4,2,1,0:T(8,128)} %get-tuple-element.14), channel_id=1, source_target_pairs={{1,0},{2,1},{3,2},{4,3},{5,4},{6,5},{7,6},{8,7},{9,8},{10,9},{11,1... | collective-permute-start | bytes 3145736 | tf_op jit(solution)/shard_map/ppermute | solution.py:114
  37.1 69.2 %collective-permute-start.3 = (f32[2,4,8,8,1,2,256]{6,3,5,4,2,1,0:T(8,128)}, f32[2,4,8,8,1,2,256]{6,3,5,4,2,1,0:T(8,128)}, u32[]{:S(2)}, u32[]{:S(2)}) collective-permute-start(f32[2,4,8,8,1,2,256]{6,3,5,4,2,1,0:T(8,128)} %get-tuple-element.13), channel_id=1, source_target_pairs={{0,1},{1,2},{2,3},{3,4},{4,5},{5,6},{6,7},{7,8},{8,9},{9,10},{10,1... | collective-permute-start | bytes 3145736 | tf_op jit(solution)/shard_map/ppermute | solution.py:117
  39.1 17.0 %collective-permute-start.6 = (bf16[8,120,1,128]{3,1,0,2:T(8,128)(2,1)S(1)}, bf16[8,120,1,128]{3,1,0,2:T(8,128)(2,1)S(1)}, u32[]{:S(2)}, u32[]{:S(2)}) collective-permute-start(bf16[8,120,1,128]{3,1,0,2:T(8,128)(2,1)S(1)} %bitcast.91), channel_id=1, source_target_pairs={{0,48},{16,0},{1,49},{17,1},{2,50},{18,2},{3,51},{19,3},{4,52},{20... | collective-permute-start | bytes 737288 | tf_op jit(solution)/shard_map/ppermute | solution.py:90
  44.8 11.3 %collective-permute-start.5 = (bf16[8,120,1,128]{3,1,0,2:T(8,128)(2,1)S(1)}, bf16[8,120,1,128]{3,1,0,2:T(8,128)(2,1)S(1)}, u32[]{:S(2)}, u32[]{:S(2)}) collective-permute-start(bf16[8,120,1,128]{3,1,0,2:T(8,128)(2,1)S(1)} %bitcast.92), channel_id=1, source_target_pairs={{0,32},{16,48},{1,33},{17,49},{2,34},{18,50},{3,35},{19,51},{4,36}... | collective-permute-start | bytes 737288 | tf_op jit(solution)/shard_map/ppermute | solution.py:90
  46.1 11.3 %collective-permute-start.4 = (bf16[8,120,1,128]{3,1,0,2:T(8,128)(2,1)S(1)}, bf16[8,120,1,128]{3,1,0,2:T(8,128)(2,1)S(1)}, u32[]{:S(2)}, u32[]{:S(2)}) collective-permute-start(bf16[8,120,1,128]{3,1,0,2:T(8,128)(2,1)S(1)} %bitcast.93), channel_id=1, source_target_pairs={{0,16},{16,32},{1,17},{17,33},{2,18},{18,34},{3,19},{19,35},{4,20}... | collective-permute-start | bytes 737288 | tf_op jit(solution)/shard_map/ppermute | solution.py:90
  70.1 18.8 %all-to-all-start.1 = ((f32[30,4,2,128]{3,2,0,1:T(2,128)}), f32[30,4,2,128]{3,2,0,1:T(2,128)S(1)}, u32[]{:S(2)}, u32[]{:S(2)}) async-start(f32[30,4,2,128]{3,2,0,1:T(2,128)} %copy.180), calls=%async_computation.1 | async-start | bytes 245760 | tf_op jit(solution)/shard_map/all_to_all | solution.py:159
  89.1 9.3 %collective-permute-start.9 = (f32[30,2,512]{2,1,0:T(2,128)S(1)}, f32[30,2,512]{2,1,0:T(2,128)S(1)}, u32[]{:S(2)}, u32[]{:S(2)}) collective-permute-start(f32[30,2,512]{2,1,0:T(2,128)S(1)} %reshape.477), channel_id=1, source_target_pairs={{16,0},{32,16},{17,1},{33,17},{18,2},{34,18},{19,3},{35,19},{20,4}... | collective-permute-start | bytes 368648 | tf_op jit(solution)/shard_map/ppermute | solution.py:90
  90.4 10.0 %collective-permute-start.8 = (f32[30,2,512]{2,1,0:T(2,128)S(1)}, f32[30,2,512]{2,1,0:T(2,128)S(1)}, u32[]{:S(2)}, u32[]{:S(2)}) collective-permute-start(f32[30,2,512]{2,1,0:T(2,128)S(1)} %reshape.477), channel_id=1, source_target_pairs={{32,0},{48,16},{33,1},{49,17},{34,2},{50,18},{35,3},{51,19},{36,4}... | collective-permute-start | bytes 368648 | tf_op jit(solution)/shard_map/ppermute | solution.py:90
  91.7 11.3 %collective-permute-start.7 = (f32[30,2,512]{2,1,0:T(2,128)S(1)}, f32[30,2,512]{2,1,0:T(2,128)S(1)}, u32[]{:S(2)}, u32[]{:S(2)}) collective-permute-start(f32[30,2,512]{2,1,0:T(2,128)S(1)} %reshape.477), channel_id=1, source_target_pairs={{48,0},{0,16},{49,1},{1,17},{50,2},{2,18},{51,3},{3,19},{52,4},{4,... | collective-permute-start | bytes 368648 | tf_op jit(solution)/shard_map/ppermute | solution.py:90
  98.3 8.1 %copy-start.1 = (f32[2,4,8,8,1,1,256]{6,3,5,4,2,1,0:T(8,128)S(1)}, f32[2,4,8,8,1,1,256]{6,3,5,4,2,1,0:T(8,128)}, u32[]{:S(2)}) copy-start(f32[2,4,8,8,1,1,256]{6,3,5,4,2,1,0:T(8,128)} %get-tuple-element.23) | copy-start | bytes 1572868
  106.4 5.1 %copy-start = (f32[2,256,1,512]{3,2,1,0:T(1,128)S(1)}, f32[2,256,1,512]{3,2,1,0:T(1,128)}, u32[]{:S(2)}) copy-start(f32[2,256,1,512]{3,2,1,0:T(1,128)} %param.6) | copy-start | bytes 3145732

commit v3 on v2

--- a/solution.py
+++ b/solution.py
@@ -155,16 +155,15 @@
     kcat = jnp.concatenate([kpad[k] for k in range(NKIND) for _ in range(2)], axis=-1)
     gained = collide_call(kcat, rhs, lmat)
 
-    gained = gained.reshape(out_rows, species_devs, own_count, block_cells)
-    gathered = lax.all_to_all(gained, "species", 1, 3, tiled=True)
-    gathered = gathered.reshape(out_rows, own_count, cell_count)
-    pieces = [None] * mode_devs
-    pieces[0] = gathered
-    for shift, got in shift_permutes(gathered, "mode", holders, mode_devs, True):
-        pieces[shift] = got
-    stacked = jnp.stack(pieces)
-    by_source = jnp.take(stacked, (mode_id - jnp.arange(mode_devs)) % mode_devs, axis=0)
-    all_gained = by_source.reshape(mode_devs * out_rows, own_count, cell_count)
+    gained = gained.reshape(out_rows, species_devs, 1, own_count, block_cells)
+    gained = jnp.broadcast_to(
+        gained, (out_rows, species_devs, mode_devs, own_count, block_cells)
+    ).reshape(out_rows, species_devs * mode_devs, own_count, block_cells)
+    gathered = lax.all_to_all(gained, ("species", "mode"), 1, 1, tiled=True)
+    gathered = gathered.reshape(out_rows, species_devs, mode_devs, own_count, block_cells)
+    all_gained = jnp.transpose(gathered, (2, 0, 3, 1, 4)).reshape(
+        mode_devs * out_rows, own_count, cell_count
+    )
 
     local_modes = mode_id * mode_count + jnp.arange(mode_count)
     match = low_map[None, :] == local_modes[:, None]

time: 117 us -> 111 us (0.949)
  starting transfers between devices: 41.4 us -> 36.7 us
  waiting for transfers between devices: 24.6 us -> 21.9 us
  local copies, waits for them, and re-layouts: 21.3 us -> 23.1 us
  other arithmetic: 20.6 us -> 19.3 us
    ppermute x6 -> x3, starting transfers between devices: 17.8 us -> 9.79 us  [shift_permutes(): received.append((shift, lax.ppermute(values, axis, pairs)))]
    ppermute x6 -> x3, waiting for transfers between devices: 11.4 us -> 7.37 us  [shift_permutes(): received.append((shift, lax.ppermute(values, axis, pairs)))]
    all_to_all x1, starting transfers between devices: 4.53 us -> 8.56 us  [per_device(): gathered = lax.all_to_all(gained, ('species', 'mode'), 1, 1, tiled=True)]
    sub x1, other arithmetic: 5.09 us -> 2.81 us  [per_device(): phase_field - nu_step * thermal_speed.reshape(own_count, 1, 1, 1, 1, 1, 1...]
    broadcast_in_dim x2 -> x3, local copies, waits for them, and re-layouts: 0.16 us -> 1.95 us  [per_device(): jnp.broadcast_to(gained, (out_rows, species_devs, mode_devs, own_count, b...]
    squeeze x1, local copies, waits for them, and re-layouts: 0.53 us -> 2.01 us  [per_device(): kpad[k]]
    all_to_all x1, waiting for transfers between devices: 13.2 us -> 14.5 us  [per_device(): gathered = lax.all_to_all(gained, ('species', 'mode'), 1, 1, tiled=True)]
    slice x2, local copies, waits for them, and re-layouts: 2.88 us -> 1.53 us  [periodic_term(): jnp.roll(flux_dir, 1, axis_cell)]
  transfers between devices with their start and end apart: 12 -> 9, of which waited for: 5 -> 3; matrix products, arithmetic and copies ran while one was open for 24% -> 25% of each run, Pallas kernels for 7% -> 7%
where the time goes in v3:
time: 111 us; the launch traced here: 110 us
  starting transfers between devices  36.7 us (33%)
  local copies, waits for them, and re-layouts  23.1 us (21%)
  waiting for transfers between devices  21.9 us (20%)
  other arithmetic  19.3 us (17%)
  Pallas kernels  7.81 us (7%)
    all_to_all x1, waiting for transfers between devices, per_device(): gathered = lax.all_to_all(gained, ('species', 'mode'), 1, 1, tiled=True)  14.5 us
    ppermute x3, starting transfers between devices, shift_permutes(): received.append((shift, lax.ppermute(values, axis, pairs)))  9.79 us
    all_to_all x1, starting transfers between devices, per_device(): gathered = lax.all_to_all(gained, ('species', 'mode'), 1, 1, tiled=True)  8.56 us
    pallas_call x1, Pallas kernels, collide_call(): pl.pallas_call(collide_body, out_shape=jax.ShapeDtypeStruct((kcat.shape[0...  7.81 us
    ppermute x3, waiting for transfers between devices, shift_permutes(): received.append((shift, lax.ppermute(values, axis, pairs)))  7.37 us
    all_to_all x1, starting transfers between devices, per_device(): spread = lax.all_to_all(picked, 'species', 2, 0, tiled=True)  5.89 us
    ppermute x1, starting transfers between devices, per_device(): lax.ppermute(up_part[:, :, :, :, :1], 'space', [(i + 1, i) for i in range...  5.74 us
    unnamed x31, local copies, waits for them, and re-layouts  4.81 us
  transfers between devices with their start and end apart: 9, of which 3 were waited for; matrix products, arithmetic and copies ran while one was open for 25% of the time, Pallas kernels for 7%

profile of v3, /device:TPU:2, one launch (start us, length us, event | category | flops | bytes accessed | tf_op | source)
XLA Modules:
  0.0 109.5 jit_solution(4494914008457471181)
XLA Ops:
  0.0 3.7 %reduce.18 = f32[2,256,512]{2,1,0:T(8,128)S(1)} reduce(f32[2,256,1,512]{3,2,1,0:T(1,128)} %param.6, f32[]{:T(128)} %constant.93), dimensions={2}, to_apply=%param.6.reduce_sub_computation | reduce | bytes 2097156 | tf_op args[0]
  3.8 3.5 %collective-permute-start.1 = (f32[2,1,8,8,1,2,256]{6,3,5,4,2,1,0:T(8,128)S(1)}, f32[2,1,8,8,1,2,256]{6,3,5,4,2,1,0:T(8,128)S(1)}, u32[]{:S(2)}, u32[]{:S(2)}) collective-permute-start(f32[2,1,8,8,1,2,256]{6,3,5,4,2,1,0:T(8,128)S(1)} %get-tuple-element.20), channel_id=1, source_target_pairs={{0,16},{16,32},{32,48},{1,17},{17,33},{33,49},{2,18},{18,34},{34,5... | collective-permute-start | bytes 786440 | tf_op jit(solution)/shard_map/ppermute | solution.py:107
  7.3 1.3 %collective-permute-start = (f32[2,1,8,8,1,2,256]{6,3,5,4,2,1,0:T(8,128)S(1)}, f32[2,1,8,8,1,2,256]{6,3,5,4,2,1,0:T(8,128)S(1)}, u32[]{:S(2)}, u32[]{:S(2)}) collective-permute-start(f32[2,1,8,8,1,2,256]{6,3,5,4,2,1,0:T(8,128)S(1)} %get-tuple-element.19), channel_id=1, source_target_pairs={{16,0},{32,16},{48,32},{17,1},{33,17},{49,33},{18,2},{34,18},{50,3... | collective-permute-start | bytes 786440 | tf_op jit(solution)/shard_map/ppermute | solution.py:110
  8.6 2.0 %copy.207 = bf16[2,256,1,512]{3,0,1,2:T(2,128)(2,1)S(1)} copy(f32[2,256,1,512]{3,2,1,0:T(1,128)} %param.6) | data formatting | bytes 1572864 | tf_op args[0]
  10.7 1.1 gather_fusion
  11.8 1.3 %fusion.26 = bf16[2,120,4,128]{3,0,1,2:T(2,128)(2,1)} fusion(pred[120]{0:T(512)(128)(4,1)S(1)} %get-tuple-element.9, pred[120]{0:T(512)(128)(4,1)S(1)} %get-tuple-element.39, bf16[120,2,512]{2,1,0:T(2,128)(2,1)S(1)} %gather_fusion), kind=kLoop, calls=%fused_computation.52 | loop fusion | flops 245760 | bytes 491760 | tf_op jit(solution)/shard_map/convert_element_type | solution.py:134
  13.1 5.9 %all-to-all-start = ((bf16[2,120,4,128]{3,0,1,2:T(2,128)(2,1)}), bf16[2,120,4,128]{3,0,1,2:T(2,128)(2,1)S(1)}, u32[]{:S(2)}, u32[]{:S(2)}) async-start(bf16[2,120,4,128]{3,0,1,2:T(2,128)(2,1)} %fusion.26), calls=%async_computation | async-start | bytes 491520 | tf_op jit(solution)/shard_map/all_to_all | solution.py:138
  19.0 1.2 %fusion.34 = (f32[2,4,8,8,1,2,1]{6,3,5,4,2,1,0:T(8,128)}, f32[2,4,8,8,1,2,1]{6,3,5,4,2,1,0:T(8,128)}) fusion(f32[2,4,8,8,1,2,256]{6,3,5,4,2,1,0:T(8,128)S(1)} %bitcast.69), kind=kLoop, calls=%fused_computation.81 | loop fusion | bytes 16384 | tf_op jit(solution)/shard_map/jit(_roll_static)/slice | solution.py:52
  20.2 1.3 %fusion.35 = (f32[2,4,8,8,1,2,255]{6,3,5,4,2,1,0:T(8,128)S(1)}, f32[2,4,8,8,1,2,255]{6,3,5,4,2,1,0:T(8,128)}) fusion(f32[2,4,8,8,1,2,256]{6,3,5,4,2,1,0:T(8,128)S(1)} %bitcast.70), kind=kLoop, calls=%fused_computation.82 | loop fusion | bytes 4177920 | tf_op jit(solution)/shard_map/jit(_roll_static)/slice | solution.py:52
  21.5 1.1 %fusion.32 = (f32[2,4,8,8,1,1,256]{6,3,5,4,2,1,0:T(8,128)}, f32[2,4,8,8,1,1,256]{6,3,5,4,2,1,0:T(8,128)}) fusion(f32[2,4,8,8,1,2,256]{6,3,5,4,2,1,0:T(8,128)S(1)} %bitcast.71), kind=kLoop, calls=%fused_computation.79 | loop fusion | bytes 2097152 | tf_op jit(solution)/shard_map/jit(_roll_static)/slice | solution.py:51
  23.3 2.0 %fusion.23 = (bf16[30,128,128]{2,1,0:T(8,128)(2,1)S(1)}, bf16[30,128,128]{2,1,0:T(8,128)(2,1)S(1)}) fusion(bf16[2,30,120,120]{3,2,1,0:T(8,128)(2,1)} %param.7), kind=kLoop, calls=%fused_computation.44 | loop fusion | bytes 3694080 | tf_op jit(solution)/shard_map/squeeze | solution.py:155
  25.5 2.0 %pad_maximum_fusion.k_ref = bf16[30,128,512]{2,1,0:T(8,128)(2,1)} fusion(bf16[30,128,128]{2,1,0:T(8,128)(2,1)S(1)} %get-tuple-element.12, bf16[30,128,128]{2,1,0:T(8,128)(2,1)S(1)} %get-tuple-element.11), kind=kLoop, calls=%fused_computation.2 | loop fusion | flops 15728640 | bytes 5898240 | tf_op jit(solution)/shard_map/concatenate | solution.py:155
  28.5 3.3 %multiply_subtract_fusion = (f32[2,4,8,8,1,2,256]{6,3,5,4,2,1,0:T(8,128)}, f32[2,4,8,8,1,2,256]{6,3,5,4,2,1,0:T(8,128)}, f32[2,4,8,8,1,2,256]{6,3,5,4,2,1,0:T(8,128)S(1)}, f32[2,4,8,8,1,2,256]{6,3,5,4,2,1,0:T(8,128)}) fusion(f32[2,4,8,8,1,2,256]{6,3,5,4,2,1,0:T(8,128)S(1)} %bitcast.72, f32[2,1,8,8,1,2,256]{6,3,5,4,2,1,0:T(8,128)} %copy-done.8, ...), kind=kLoop, calls=%fused_computation.42 | loop fusion | flops 4194304 | bytes 5770240 | tf_op jit(solution)/shard_map/sub | solution.py:113
  31.8 5.7 %collective-permute-start.2 = (f32[2,4,8,8,1,2,256]{6,3,5,4,2,1,0:T(8,128)}, f32[2,4,8,8,1,2,256]{6,3,5,4,2,1,0:T(8,128)}, u32[]{:S(2)}, u32[]{:S(2)}) collective-permute-start(f32[2,4,8,8,1,2,256]{6,3,5,4,2,1,0:T(8,128)} %get-tuple-element.14), channel_id=1, source_target_pairs={{1,0},{2,1},{3,2},{4,3},{5,4},{6,5},{7,6},{8,7},{9,8},{10,9},{11,1... | collective-permute-start | bytes 3145736 | tf_op jit(solution)/shard_map/ppermute | solution.py:114
  37.6 1.9 %collective-permute-start.3 = (f32[2,4,8,8,1,2,256]{6,3,5,4,2,1,0:T(8,128)}, f32[2,4,8,8,1,2,256]{6,3,5,4,2,1,0:T(8,128)}, u32[]{:S(2)}, u32[]{:S(2)}) collective-permute-start(f32[2,4,8,8,1,2,256]{6,3,5,4,2,1,0:T(8,128)} %get-tuple-element.13), channel_id=1, source_target_pairs={{0,1},{1,2},{2,3},{3,4},{4,5},{5,6},{6,7},{7,8},{8,9},{9,10},{10,1... | collective-permute-start | bytes 3145736 | tf_op jit(solution)/shard_map/ppermute | solution.py:117
  39.6 5.7 %collective-permute-start.6 = (bf16[8,120,1,128]{3,1,0,2:T(8,128)(2,1)S(1)}, bf16[8,120,1,128]{3,1,0,2:T(8,128)(2,1)S(1)}, u32[]{:S(2)}, u32[]{:S(2)}) collective-permute-start(bf16[8,120,1,128]{3,1,0,2:T(8,128)(2,1)S(1)} %bitcast.82), channel_id=1, source_target_pairs={{0,48},{16,0},{1,49},{17,1},{2,50},{18,2},{3,51},{19,3},{4,52},{20... | collective-permute-start | bytes 737288 | tf_op jit(solution)/shard_map/ppermute | solution.py:90
  45.3 1.3 %collective-permute-start.5 = (bf16[8,120,1,128]{3,1,0,2:T(8,128)(2,1)S(1)}, bf16[8,120,1,128]{3,1,0,2:T(8,128)(2,1)S(1)}, u32[]{:S(2)}, u32[]{:S(2)}) collective-permute-start(bf16[8,120,1,128]{3,1,0,2:T(8,128)(2,1)S(1)} %bitcast.83), channel_id=1, source_target_pairs={{0,32},{16,48},{1,33},{17,49},{2,34},{18,50},{3,35},{19,51},{4,36}... | collective-permute-start | bytes 737288 | tf_op jit(solution)/shard_map/ppermute | solution.py:90
  46.6 2.8 %collective-permute-start.4 = (bf16[8,120,1,128]{3,1,0,2:T(8,128)(2,1)S(1)}, bf16[8,120,1,128]{3,1,0,2:T(8,128)(2,1)S(1)}, u32[]{:S(2)}, u32[]{:S(2)}) collective-permute-start(bf16[8,120,1,128]{3,1,0,2:T(8,128)(2,1)S(1)} %bitcast.84), channel_id=1, source_target_pairs={{0,16},{16,32},{1,17},{17,33},{2,18},{18,34},{3,19},{19,35},{4,20}... | collective-permute-start | bytes 737288 | tf_op jit(solution)/shard_map/ppermute | solution.py:90
  49.4 1.2 %fusion.36 = (f32[2,4,8,8,1,2,1]{6,3,5,4,2,1,0:T(8,128)}, f32[2,4,8,8,1,2,1]{6,3,5,4,2,1,0:T(8,128)}) fusion(f32[2,4,8,8,1,2,256]{6,3,5,4,2,1,0:T(8,128)S(1)} %get-tuple-element.17), kind=kLoop, calls=%fused_computation.83 | loop fusion | bytes 16384 | tf_op jit(solution)/shard_map/jit(_roll_static)/slice | solution.py:54
  50.6 6.0 %collective-permute-done.6 = bf16[8,120,1,128]{3,1,0,2:T(8,128)(2,1)S(1)} collective-permute-done((bf16[8,120,1,128]{3,1,0,2:T(8,128)(2,1)S(1)}, bf16[8,120,1,128]{3,1,0,2:T(8,128)(2,1)S(1)}, u32[]{:S(2)}, u32[]{:S(2)}) %collective-permute-start.6) | collective-permute-done | bytes 245792 | tf_op jit(solution)/shard_map/ppermute | solution.py:90
  56.6 1.3 %collective-permute-done.4 = bf16[8,120,1,128]{3,1,0,2:T(8,128)(2,1)S(1)} collective-permute-done((bf16[8,120,1,128]{3,1,0,2:T(8,128)(2,1)S(1)}, bf16[8,120,1,128]{3,1,0,2:T(8,128)(2,1)S(1)}, u32[]{:S(2)}, u32[]{:S(2)}) %collective-permute-start.4) | collective-permute-done | bytes 245792 | tf_op jit(solution)/shard_map/ppermute | solution.py:90
  58.9 1.2 %copy.206 = bf16[64,8,8,128]{3,1,2,0:T(8,128)(2,1)} copy(bf16[64,8,8,128]{3,2,1,0:T(8,128)(2,1)S(1)} %bitcast.75) | data formatting | bytes 2097152
  61.0 7.8 %shard_map.64 = f32[30,1024]{1,0:T(8,128)} custom-call(bf16[30,128,512]{2,1,0:T(8,128)(2,1)} %pad_maximum_fusion.k_ref, bf16[512,1024]{1,0:T(8,128)(2,1)} %bitcast.76, f32[128,1024]{1,0:T(8,128)} %copy_bitcast_fusion.2.l_ref), custom_call_target="tpu_custom_call" | custom-call | tf_op jit(solution)/shard_map/pallas_call | solution.py:76
  68.8 1.0 broadcast_in_dim.64
  70.8 8.6 %all-to-all-start.1 = ((f32[30,16,2,128]{3,2,0,1:T(2,128)}), f32[30,16,2,128]{3,2,0,1:T(2,128)}, u32[]{:S(2)}, u32[]{:S(2)}) async-start(f32[30,16,2,128]{3,2,0,1:T(2,128)} %bitcast.79), calls=%async_computation.1 | async-start | bytes 983040 | tf_op jit(solution)/shard_map/all_to_all | solution.py:162
  79.4 1.4 %fusion.33 = (f32[2,4,8,8,1,1,256]{6,3,5,4,2,1,0:T(8,128)S(1)}, f32[2,4,8,8,1,1,256]{6,3,5,4,2,1,0:T(8,128)S(1)}) fusion(f32[2,4,8,8,1,2,256]{6,3,5,4,2,1,0:T(8,128)} %get-tuple-element.18), kind=kLoop, calls=%fused_computation.80 | loop fusion | bytes 2097152 | tf_op jit(solution)/shard_map/jit(_roll_static)/slice | solution.py:53
  81.8 2.8 %fusion.7 = f32[2,4,8,8,1,2,256]{6,3,5,4,2,1,0:T(8,128)S(1)} fusion(f32[2,4,8,8,1,2,256]{6,3,5,4,2,1,0:T(8,128)S(1)} %bitcast.73, f32[2,4,8,8,1,2,1]{6,3,5,4,2,1,0:T(8,128)S(1)} %copy-done.7, f32[2,4,8,8,1,2,255]{6,3,5,4,2,1,0:T(8,128)S(1)} %get-tuple-element.32, f32[2,4,8,8,1,2,255]{6,3,5,4,2,1,0:T(8,128)S(1)} %get-tuple-element.31, ...), kind=kLoop, calls=%fused_computation.18 | loop fusion | flops 6815744 | bytes 10485768 | tf_op jit(solution)/shard_map/sub | solution.py:126
  84.7 14.5 %all-to-all-done.1 = f32[30,16,2,128]{3,2,0,1:T(2,128)} async-done(((f32[30,16,2,128]{3,2,0,1:T(2,128)}), f32[30,16,2,128]{3,2,0,1:T(2,128)}, u32[]{:S(2)}, u32[]{:S(2)}) %all-to-all-start.1) | async-done | bytes 491552 | tf_op jit(solution)/shard_map/all_to_all | solution.py:162
  99.2 1.1 copy.181
  100.8 2.7 %gather_fusion.1 = f32[256,2,512]{2,1,0:T(2,128)} fusion(f32[120,2,512]{2,1,0:T(2,128)S(1)} %reshape.447, s32[1024]{0:T(1024)S(1)} %pad_clamp_fusion), kind=kCustom, calls=%fused_computation.1 | custom fusion | bytes 2098176 | tf_op jit(solution)/shard_map/jit(_take)/gather | solution.py:171
  103.4 4.0 %fusion.22 = f32[2,256,1,512]{3,0,1,2:T(2,128)S(1)} fusion(f32[2,256,512]{2,1,0:T(8,128)S(1)} %bitcast.74, f32[256,2,512]{2,1,0:T(2,128)} %gather_fusion.1, pred[256]{0:T(512)(128)(4,1)S(1)} %compare_and_fusion.2, pred[256]{0:T(512)(128)(4,1)S(1)} %gt.18, f32[2]{0:T(128)S(1)} %neg.4, f32[2,256,1,512]{3,2,1,0:T(1,128)S(1)} %copy-done), kind=kLoop, calls=%fused_computation.40 | loop fusion | flops 1310720 | bytes 4194824 | tf_op jit(solution)/shard_map/add | solution.py:179
  107.5 2.0 %copy.185 = f32[2,256,1,512]{3,2,1,0:T(1,128)} copy(f32[2,256,1,512]{3,0,1,2:T(2,128)S(1)} %fusion.22) | data formatting | bytes 2097152 | tf_op jit(solution)/shard_map/add | solution.py:179
  (64 shorter events, 6.0 us)
Async XLA Ops:
  0.0 10.6 %copy-start.11 = (s32[120]{0:T(128)S(1)}, s32[120]{0:T(128)}, u32[]{:S(2)}) copy-start(s32[120]{0:T(128)} %param.9) | copy-start | bytes 1444
  3.8 23.9 %collective-permute-start.1 = (f32[2,1,8,8,1,2,256]{6,3,5,4,2,1,0:T(8,128)S(1)}, f32[2,1,8,8,1,2,256]{6,3,5,4,2,1,0:T(8,128)S(1)}, u32[]{:S(2)}, u32[]{:S(2)}) collective-permute-start(f32[2,1,8,8,1,2,256]{6,3,5,4,2,1,0:T(8,128)S(1)} %get-tuple-element.20), channel_id=1, source_target_pairs={{0,16},{16,32},{32,48},{1,17},{17,33},{33,49},{2,18},{18,34},{34,5... | collective-permute-start | bytes 786440 | tf_op jit(solution)/shard_map/ppermute | solution.py:107
  7.3 20.5 %collective-permute-start = (f32[2,1,8,8,1,2,256]{6,3,5,4,2,1,0:T(8,128)S(1)}, f32[2,1,8,8,1,2,256]{6,3,5,4,2,1,0:T(8,128)S(1)}, u32[]{:S(2)}, u32[]{:S(2)}) collective-permute-start(f32[2,1,8,8,1,2,256]{6,3,5,4,2,1,0:T(8,128)S(1)} %get-tuple-element.19), channel_id=1, source_target_pairs={{16,0},{32,16},{48,32},{17,1},{33,17},{49,33},{18,2},{34,18},{50,3... | collective-permute-start | bytes 786440 | tf_op jit(solution)/shard_map/ppermute | solution.py:110
  13.1 26.4 %all-to-all-start = ((bf16[2,120,4,128]{3,0,1,2:T(2,128)(2,1)}), bf16[2,120,4,128]{3,0,1,2:T(2,128)(2,1)S(1)}, u32[]{:S(2)}, u32[]{:S(2)}) async-start(bf16[2,120,4,128]{3,0,1,2:T(2,128)(2,1)} %fusion.26), calls=%async_computation | async-start | bytes 491520 | tf_op jit(solution)/shard_map/all_to_all | solution.py:138
  19.0 4.3 %copy-start.12 = (f32[2]{0:T(128)S(1)}, f32[2]{0:T(128)}, u32[]{:S(2)}) copy-start(f32[2]{0:T(128)} %param.10) | copy-start | bytes 28
  21.5 3.8 %copy-start.10 = (s32[8,8]{1,0:T(8,128)S(1)}, s32[8,8]{1,0:T(8,128)}, u32[]{:S(2)}) copy-start(s32[8,8]{1,0:T(8,128)} %param.8) | copy-start | bytes 772
  23.3 4.4 %copy-start.13 = (f32[2]{0:T(128)S(1)}, f32[2]{0:T(128)}, u32[]{:S(2)}) copy-start(f32[2]{0:T(128)} %param.11) | copy-start | bytes 28
  27.7 0.7 copy-start.8
  27.7 0.8 copy-start.9
  31.8 49.4 %collective-permute-start.2 = (f32[2,4,8,8,1,2,256]{6,3,5,4,2,1,0:T(8,128)}, f32[2,4,8,8,1,2,256]{6,3,5,4,2,1,0:T(8,128)}, u32[]{:S(2)}, u32[]{:S(2)}) collective-permute-start(f32[2,4,8,8,1,2,256]{6,3,5,4,2,1,0:T(8,128)} %get-tuple-element.14), channel_id=1, source_target_pairs={{1,0},{2,1},{3,2},{4,3},{5,4},{6,5},{7,6},{8,7},{9,8},{10,9},{11,1... | collective-permute-start | bytes 3145736 | tf_op jit(solution)/shard_map/ppermute | solution.py:114
  37.6 43.7 %collective-permute-start.3 = (f32[2,4,8,8,1,2,256]{6,3,5,4,2,1,0:T(8,128)}, f32[2,4,8,8,1,2,256]{6,3,5,4,2,1,0:T(8,128)}, u32[]{:S(2)}, u32[]{:S(2)}) collective-permute-start(f32[2,4,8,8,1,2,256]{6,3,5,4,2,1,0:T(8,128)} %get-tuple-element.13), channel_id=1, source_target_pairs={{0,1},{1,2},{2,3},{3,4},{4,5},{5,6},{6,7},{7,8},{8,9},{9,10},{10,1... | collective-permute-start | bytes 3145736 | tf_op jit(solution)/shard_map/ppermute | solution.py:117
  39.6 17.0 %collective-permute-start.6 = (bf16[8,120,1,128]{3,1,0,2:T(8,128)(2,1)S(1)}, bf16[8,120,1,128]{3,1,0,2:T(8,128)(2,1)S(1)}, u32[]{:S(2)}, u32[]{:S(2)}) collective-permute-start(bf16[8,120,1,128]{3,1,0,2:T(8,128)(2,1)S(1)} %bitcast.82), channel_id=1, source_target_pairs={{0,48},{16,0},{1,49},{17,1},{2,50},{18,2},{3,51},{19,3},{4,52},{20... | collective-permute-start | bytes 737288 | tf_op jit(solution)/shard_map/ppermute | solution.py:90
  45.3 11.3 %collective-permute-start.5 = (bf16[8,120,1,128]{3,1,0,2:T(8,128)(2,1)S(1)}, bf16[8,120,1,128]{3,1,0,2:T(8,128)(2,1)S(1)}, u32[]{:S(2)}, u32[]{:S(2)}) collective-permute-start(bf16[8,120,1,128]{3,1,0,2:T(8,128)(2,1)S(1)} %bitcast.83), channel_id=1, source_target_pairs={{0,32},{16,48},{1,33},{17,49},{2,34},{18,50},{3,35},{19,51},{4,36}... | collective-permute-start | bytes 737288 | tf_op jit(solution)/shard_map/ppermute | solution.py:90
  46.6 11.3 %collective-permute-start.4 = (bf16[8,120,1,128]{3,1,0,2:T(8,128)(2,1)S(1)}, bf16[8,120,1,128]{3,1,0,2:T(8,128)(2,1)S(1)}, u32[]{:S(2)}, u32[]{:S(2)}) collective-permute-start(bf16[8,120,1,128]{3,1,0,2:T(8,128)(2,1)S(1)} %bitcast.84), channel_id=1, source_target_pairs={{0,16},{16,32},{1,17},{17,33},{2,18},{18,34},{3,19},{19,35},{4,20}... | collective-permute-start | bytes 737288 | tf_op jit(solution)/shard_map/ppermute | solution.py:90
  70.8 28.4 %all-to-all-start.1 = ((f32[30,16,2,128]{3,2,0,1:T(2,128)}), f32[30,16,2,128]{3,2,0,1:T(2,128)}, u32[]{:S(2)}, u32[]{:S(2)}) async-start(f32[30,16,2,128]{3,2,0,1:T(2,128)} %bitcast.79), calls=%async_computation.1 | async-start | bytes 983040 | tf_op jit(solution)/shard_map/all_to_all | solution.py:162
  79.4 1.9 %copy-start.1 = (f32[2,4,8,8,1,2,255]{6,3,5,4,2,1,0:T(8,128)S(1)}, f32[2,4,8,8,1,2,255]{6,3,5,4,2,1,0:T(8,128)}, u32[]{:S(2)}) copy-start(f32[2,4,8,8,1,2,255]{6,3,5,4,2,1,0:T(8,128)} %get-tuple-element.28) | copy-start | bytes 3133444
  79.4 1.9 %copy-start.2 = (f32[2,4,8,8,1,2,1]{6,3,5,4,2,1,0:T(8,128)S(1)}, f32[2,4,8,8,1,2,1]{6,3,5,4,2,1,0:T(8,128)}, u32[]{:S(2)}) copy-start(f32[2,4,8,8,1,2,1]{6,3,5,4,2,1,0:T(8,128)} %get-tuple-element.25) | copy-start | bytes 12292
  79.4 1.9 %copy-start.3 = (f32[2,4,8,8,1,2,1]{6,3,5,4,2,1,0:T(8,128)S(1)}, f32[2,4,8,8,1,2,1]{6,3,5,4,2,1,0:T(8,128)}, u32[]{:S(2)}) copy-start(f32[2,4,8,8,1,2,1]{6,3,5,4,2,1,0:T(8,128)} %get-tuple-element.26) | copy-start | bytes 12292
  79.4 2.0 %copy-start.4 = (f32[2,4,8,8,1,1,256]{6,3,5,4,2,1,0:T(8,128)S(1)}, f32[2,4,8,8,1,1,256]{6,3,5,4,2,1,0:T(8,128)}, u32[]{:S(2)}) copy-start(f32[2,4,8,8,1,1,256]{6,3,5,4,2,1,0:T(8,128)} %get-tuple-element.21) | copy-start | bytes 1572868
  79.4 2.1 %copy-start.5 = (f32[2,4,8,8,1,1,256]{6,3,5,4,2,1,0:T(8,128)S(1)}, f32[2,4,8,8,1,1,256]{6,3,5,4,2,1,0:T(8,128)}, u32[]{:S(2)}) copy-start(f32[2,4,8,8,1,1,256]{6,3,5,4,2,1,0:T(8,128)} %get-tuple-element.22) | copy-start | bytes 1572868
  79.4 2.3 %copy-start.6 = (f32[2,4,8,8,1,2,1]{6,3,5,4,2,1,0:T(8,128)S(1)}, f32[2,4,8,8,1,2,1]{6,3,5,4,2,1,0:T(8,128)}, u32[]{:S(2)}) copy-start(f32[2,4,8,8,1,2,1]{6,3,5,4,2,1,0:T(8,128)} %get-tuple-element.29) | copy-start | bytes 12292
  79.4 2.4 %copy-start.7 = (f32[2,4,8,8,1,2,1]{6,3,5,4,2,1,0:T(8,128)S(1)}, f32[2,4,8,8,1,2,1]{6,3,5,4,2,1,0:T(8,128)}, u32[]{:S(2)}) copy-start(f32[2,4,8,8,1,2,1]{6,3,5,4,2,1,0:T(8,128)} %get-tuple-element.30) | copy-start | bytes 12292
  84.7 18.8 %copy-start = (f32[2,256,1,512]{3,2,1,0:T(1,128)S(1)}, f32[2,256,1,512]{3,2,1,0:T(1,128)}, u32[]{:S(2)}) copy-start(f32[2,256,1,512]{3,2,1,0:T(1,128)} %param.6) | copy-start | bytes 3145732

commit v4 on v3

--- a/solution.py
+++ b/solution.py
@@ -159,7 +159,8 @@
     gained = jnp.broadcast_to(
         gained, (out_rows, species_devs, mode_devs, own_count, block_cells)
     ).reshape(out_rows, species_devs * mode_devs, own_count, block_cells)
-    gathered = lax.all_to_all(gained, ("species", "mode"), 1, 1, tiled=True)
+    gathered = lax.all_to_all(gained.astype(jnp.bfloat16), ("species", "mode"), 1, 1, tiled=True)
+    gathered = gathered.astype(jnp.float32)
     gathered = gathered.reshape(out_rows, species_devs, mode_devs, own_count, block_cells)
     all_gained = jnp.transpose(gathered, (2, 0, 3, 1, 4)).reshape(
         mode_devs * out_rows, own_count, cell_count

time: 111 us -> 108 us (0.973)
  local copies, waits for them, and re-layouts: 23.1 us -> 19.5 us
  other arithmetic: 19.3 us -> 21.2 us
  waiting for transfers between devices: 21.9 us -> 20.1 us
    sub x1, other arithmetic: 2.81 us -> 5.08 us  [per_device(): phase_field - nu_step * thermal_speed.reshape(own_count, 1, 1, 1, 1, 1, 1...]
    all_to_all x1, waiting for transfers between devices: 14.5 us -> 12.8 us  [per_device(): lax.all_to_all(gained.astype(jnp.bfloat16), ('species', 'mode'), 1, 1, ti...]
    squeeze x1, local copies, waits for them, and re-layouts: 2.01 us -> 0.53 us  [per_device(): kpad[k]]
    slice x2, local copies, waits for them, and re-layouts: 1.53 us -> 2.91 us  [periodic_term(): jnp.roll(flux_dir, 1, axis_cell)]
    unnamed x31 -> x17, local copies, waits for them, and re-layouts: 4.81 us -> 3.47 us
    add x1, other arithmetic: 4.05 us -> 2.84 us  [per_device(): advected.reshape(own_count, mode_count, row_count, plane_cells)]
    broadcast_in_dim x3 -> x1, local copies, waits for them, and re-layouts: 1.95 us -> 0.83 us  [per_device(): jnp.broadcast_to(gained, (out_rows, species_devs, mode_devs, own_count, b...]
where the time goes in v4:
time: 108 us; the launch traced here: 107 us
  starting transfers between devices  37.3 us (35%)
  other arithmetic  21.2 us (20%)
  waiting for transfers between devices  20.1 us (19%)
  local copies, waits for them, and re-layouts  19.5 us (18%)
  Pallas kernels  7.8 us (7%)
    all_to_all x1, waiting for transfers between devices, per_device(): lax.all_to_all(gained.astype(jnp.bfloat16), ('species', 'mode'), 1, 1, ti...  12.8 us
    ppermute x3, starting transfers between devices, shift_permutes(): received.append((shift, lax.ppermute(values, axis, pairs)))  9.8 us
    all_to_all x1, starting transfers between devices, per_device(): lax.all_to_all(gained.astype(jnp.bfloat16), ('species', 'mode'), 1, 1, ti...  8.5 us
    pallas_call x1, Pallas kernels, collide_call(): pl.pallas_call(collide_body, out_shape=jax.ShapeDtypeStruct((kcat.shape[0...  7.8 us
    ppermute x3, waiting for transfers between devices, shift_permutes(): received.append((shift, lax.ppermute(values, axis, pairs)))  7.35 us
    all_to_all x1, starting transfers between devices, per_device(): spread = lax.all_to_all(picked, 'species', 2, 0, tiled=True)  5.89 us
    ppermute x1, starting transfers between devices, per_device(): lax.ppermute(up_part[:, :, :, :, :1], 'space', [(i + 1, i) for i in range...  5.75 us
    sub x1, other arithmetic, per_device(): phase_field - nu_step * thermal_speed.reshape(own_count, 1, 1, 1, 1, 1, 1...  5.08 us
  transfers between devices with their start and end apart: 9, of which 3 were waited for; matrix products, arithmetic and copies ran while one was open for 25% of the time, Pallas kernels for 7%

profile of v4, /device:TPU:2, one launch (start us, length us, event | category | flops | bytes accessed | tf_op | source)
XLA Modules:
  0.0 106.5 jit_solution(3047047694877895915)
XLA Ops:
  0.0 3.7 %reduce.18 = f32[2,256,512]{2,1,0:T(8,128)S(1)} reduce(f32[2,256,1,512]{3,2,1,0:T(1,128)} %param.6, f32[]{:T(128)} %constant.93), dimensions={2}, to_apply=%param.6.reduce_sub_computation | reduce | bytes 2097156 | tf_op args[0]
  3.7 0.8 fusion.31
  4.6 4.2 %collective-permute-start.1 = (f32[2,1,8,8,1,2,256]{6,3,5,4,2,1,0:T(8,128)}, f32[2,1,8,8,1,2,256]{6,3,5,4,2,1,0:T(8,128)}, u32[]{:S(2)}, u32[]{:S(2)}) collective-permute-start(f32[2,1,8,8,1,2,256]{6,3,5,4,2,1,0:T(8,128)} %get-tuple-element.20), channel_id=1, source_target_pairs={{0,16},{16,32},{32,48},{1,17},{17,33},{33,49},{2,18},{18,34},{34,5... | collective-permute-start | bytes 786440 | tf_op jit(solution)/shard_map/ppermute | solution.py:107
  8.7 1.3 %collective-permute-start = (f32[2,1,8,8,1,2,256]{6,3,5,4,2,1,0:T(8,128)}, f32[2,1,8,8,1,2,256]{6,3,5,4,2,1,0:T(8,128)}, u32[]{:S(2)}, u32[]{:S(2)}) collective-permute-start(f32[2,1,8,8,1,2,256]{6,3,5,4,2,1,0:T(8,128)} %get-tuple-element.19), channel_id=1, source_target_pairs={{16,0},{32,16},{48,32},{17,1},{33,17},{49,33},{18,2},{34,18},{50,3... | collective-permute-start | bytes 786440 | tf_op jit(solution)/shard_map/ppermute | solution.py:110
  10.0 2.0 %copy.207 = bf16[2,256,1,512]{3,0,1,2:T(2,128)(2,1)S(1)} copy(f32[2,256,1,512]{3,2,1,0:T(1,128)} %param.6) | data formatting | bytes 1572864 | tf_op args[0]
  12.1 1.1 %gather_fusion = bf16[120,2,512]{2,1,0:T(2,128)(2,1)S(1)} fusion(bf16[2,256,512]{2,0,1:T(2,128)(2,1)S(1)} %bitcast.80, s32[1024]{0:T(1024)S(1)} %pad_clamp_fusion.1), kind=kCustom, calls=%fused_computation | custom fusion | bytes 492000 | tf_op jit(solution)/shard_map/jit(_take)/gather | solution.py:134
  13.2 1.4 %fusion.26 = bf16[2,120,4,128]{3,0,1,2:T(2,128)(2,1)} fusion(pred[120]{0:T(512)(128)(4,1)S(1)} %get-tuple-element.9, pred[120]{0:T(512)(128)(4,1)S(1)} %get-tuple-element.39, bf16[120,2,512]{2,1,0:T(2,128)(2,1)S(1)} %gather_fusion), kind=kLoop, calls=%fused_computation.52 | loop fusion | flops 245760 | bytes 491760 | tf_op jit(solution)/shard_map/convert_element_type | solution.py:134
  14.6 5.9 %all-to-all-start = ((bf16[2,120,4,128]{3,0,1,2:T(2,128)(2,1)}), bf16[2,120,4,128]{3,0,1,2:T(2,128)(2,1)S(1)}, u32[]{:S(2)}, u32[]{:S(2)}) async-start(bf16[2,120,4,128]{3,0,1,2:T(2,128)(2,1)} %fusion.26), calls=%async_computation | async-start | bytes 491520 | tf_op jit(solution)/shard_map/all_to_all | solution.py:138
  20.5 1.1 %fusion.34 = (f32[2,4,8,8,1,2,1]{6,3,5,4,2,1,0:T(8,128)}, f32[2,4,8,8,1,2,1]{6,3,5,4,2,1,0:T(8,128)}) fusion(f32[2,4,8,8,1,2,256]{6,3,5,4,2,1,0:T(8,128)S(1)} %bitcast.70), kind=kLoop, calls=%fused_computation.82 | loop fusion | bytes 16384 | tf_op jit(solution)/shard_map/jit(_roll_static)/slice | solution.py:52
  21.6 1.7 %fusion.35 = (f32[2,4,8,8,1,2,255]{6,3,5,4,2,1,0:T(8,128)}, f32[2,4,8,8,1,2,255]{6,3,5,4,2,1,0:T(8,128)}) fusion(f32[2,4,8,8,1,2,256]{6,3,5,4,2,1,0:T(8,128)S(1)} %bitcast.71), kind=kLoop, calls=%fused_computation.83 | loop fusion | bytes 4177920 | tf_op jit(solution)/shard_map/jit(_roll_static)/slice | solution.py:52
  23.3 1.1 %fusion.32 = (f32[2,4,8,8,1,1,256]{6,3,5,4,2,1,0:T(8,128)}, f32[2,4,8,8,1,1,256]{6,3,5,4,2,1,0:T(8,128)}) fusion(f32[2,4,8,8,1,2,256]{6,3,5,4,2,1,0:T(8,128)S(1)} %bitcast.72), kind=kLoop, calls=%fused_computation.80 | loop fusion | bytes 2097152 | tf_op jit(solution)/shard_map/jit(_roll_static)/slice | solution.py:51
  25.8 2.0 %pad_maximum_fusion.k_ref = bf16[30,128,512]{2,1,0:T(8,128)(2,1)} fusion(bf16[30,128,128]{2,1,0:T(8,128)(2,1)S(1)} %get-tuple-element.12, bf16[30,128,128]{2,1,0:T(8,128)(2,1)S(1)} %get-tuple-element.11), kind=kLoop, calls=%fused_computation.2 | loop fusion | flops 15728640 | bytes 5898240 | tf_op jit(solution)/shard_map/concatenate | solution.py:155
  28.0 3.2 %multiply_subtract_fusion = (f32[2,4,8,8,1,2,256]{6,3,5,4,2,1,0:T(8,128)}, f32[2,4,8,8,1,2,256]{6,3,5,4,2,1,0:T(8,128)}, f32[2,4,8,8,1,2,256]{6,3,5,4,2,1,0:T(8,128)S(1)}, f32[2,4,8,8,1,2,256]{6,3,5,4,2,1,0:T(8,128)S(1)}) fusion(f32[2,4,8,8,1,2,256]{6,3,5,4,2,1,0:T(8,128)S(1)} %bitcast.73, f32[2,1,8,8,1,2,256]{6,3,5,4,2,1,0:T(8,128)} %collective-permute-done.1, ...), kind=kLoop, calls=%fused_computation.42 | loop fusion | flops 4194304 | bytes 5770240 | tf_op jit(solution)/shard_map/sub | solution.py:113
  31.2 5.7 %collective-permute-start.2 = (f32[2,4,8,8,1,2,256]{6,3,5,4,2,1,0:T(8,128)}, f32[2,4,8,8,1,2,256]{6,3,5,4,2,1,0:T(8,128)}, u32[]{:S(2)}, u32[]{:S(2)}) collective-permute-start(f32[2,4,8,8,1,2,256]{6,3,5,4,2,1,0:T(8,128)} %get-tuple-element.14), channel_id=1, source_target_pairs={{1,0},{2,1},{3,2},{4,3},{5,4},{6,5},{7,6},{8,7},{9,8},{10,9},{11,1... | collective-permute-start | bytes 3145736 | tf_op jit(solution)/shard_map/ppermute | solution.py:114
  37.0 1.9 %collective-permute-start.3 = (f32[2,4,8,8,1,2,256]{6,3,5,4,2,1,0:T(8,128)}, f32[2,4,8,8,1,2,256]{6,3,5,4,2,1,0:T(8,128)}, u32[]{:S(2)}, u32[]{:S(2)}) collective-permute-start(f32[2,4,8,8,1,2,256]{6,3,5,4,2,1,0:T(8,128)} %get-tuple-element.13), channel_id=1, source_target_pairs={{0,1},{1,2},{2,3},{3,4},{4,5},{5,6},{6,7},{7,8},{8,9},{9,10},{10,1... | collective-permute-start | bytes 3145736 | tf_op jit(solution)/shard_map/ppermute | solution.py:117
  39.0 5.7 %collective-permute-start.6 = (bf16[8,120,1,128]{3,1,0,2:T(8,128)(2,1)S(1)}, bf16[8,120,1,128]{3,1,0,2:T(8,128)(2,1)S(1)}, u32[]{:S(2)}, u32[]{:S(2)}) collective-permute-start(bf16[8,120,1,128]{3,1,0,2:T(8,128)(2,1)S(1)} %bitcast.81), channel_id=1, source_target_pairs={{0,48},{16,0},{1,49},{17,1},{2,50},{18,2},{3,51},{19,3},{4,52},{20... | collective-permute-start | bytes 737288 | tf_op jit(solution)/shard_map/ppermute | solution.py:90
  44.7 1.3 %collective-permute-start.5 = (bf16[8,120,1,128]{3,1,0,2:T(8,128)(2,1)S(1)}, bf16[8,120,1,128]{3,1,0,2:T(8,128)(2,1)S(1)}, u32[]{:S(2)}, u32[]{:S(2)}) collective-permute-start(bf16[8,120,1,128]{3,1,0,2:T(8,128)(2,1)S(1)} %bitcast.82), channel_id=1, source_target_pairs={{0,32},{16,48},{1,33},{17,49},{2,34},{18,50},{3,35},{19,51},{4,36}... | collective-permute-start | bytes 737288 | tf_op jit(solution)/shard_map/ppermute | solution.py:90
  46.0 2.8 %collective-permute-start.4 = (bf16[8,120,1,128]{3,1,0,2:T(8,128)(2,1)S(1)}, bf16[8,120,1,128]{3,1,0,2:T(8,128)(2,1)S(1)}, u32[]{:S(2)}, u32[]{:S(2)}) collective-permute-start(bf16[8,120,1,128]{3,1,0,2:T(8,128)(2,1)S(1)} %bitcast.83), channel_id=1, source_target_pairs={{0,16},{16,32},{1,17},{17,33},{2,18},{18,34},{3,19},{19,35},{4,20}... | collective-permute-start | bytes 737288 | tf_op jit(solution)/shard_map/ppermute | solution.py:90
  48.8 1.2 %fusion.36 = (f32[2,4,8,8,1,2,1]{6,3,5,4,2,1,0:T(8,128)}, f32[2,4,8,8,1,2,1]{6,3,5,4,2,1,0:T(8,128)}) fusion(f32[2,4,8,8,1,2,256]{6,3,5,4,2,1,0:T(8,128)S(1)} %get-tuple-element.17), kind=kLoop, calls=%fused_computation.84 | loop fusion | bytes 16384 | tf_op jit(solution)/shard_map/jit(_roll_static)/slice | solution.py:54
  50.0 6.0 %collective-permute-done.6 = bf16[8,120,1,128]{3,1,0,2:T(8,128)(2,1)S(1)} collective-permute-done((bf16[8,120,1,128]{3,1,0,2:T(8,128)(2,1)S(1)}, bf16[8,120,1,128]{3,1,0,2:T(8,128)(2,1)S(1)}, u32[]{:S(2)}, u32[]{:S(2)}) %collective-permute-start.6) | collective-permute-done | bytes 245792 | tf_op jit(solution)/shard_map/ppermute | solution.py:90
  56.0 1.3 %collective-permute-done.4 = bf16[8,120,1,128]{3,1,0,2:T(8,128)(2,1)S(1)} collective-permute-done((bf16[8,120,1,128]{3,1,0,2:T(8,128)(2,1)S(1)}, bf16[8,120,1,128]{3,1,0,2:T(8,128)(2,1)S(1)}, u32[]{:S(2)}, u32[]{:S(2)}) %collective-permute-start.4) | collective-permute-done | bytes 245792 | tf_op jit(solution)/shard_map/ppermute | solution.py:90
  58.3 1.2 %copy.206 = bf16[64,8,8,128]{3,1,2,0:T(8,128)(2,1)} copy(bf16[64,8,8,128]{3,2,1,0:T(8,128)(2,1)S(1)} %bitcast.76) | data formatting | bytes 2097152
  60.4 7.8 %shard_map.64 = f32[30,1024]{1,0:T(8,128)} custom-call(bf16[30,128,512]{2,1,0:T(8,128)(2,1)} %pad_maximum_fusion.k_ref, bf16[512,1024]{1,0:T(8,128)(2,1)} %bitcast.77, f32[128,1024]{1,0:T(8,128)} %copy_bitcast_fusion.2.l_ref), custom_call_target="tpu_custom_call" | custom-call | tf_op jit(solution)/shard_map/pallas_call | solution.py:76
  68.2 0.9 convert_element_type.77
  70.0 8.5 %all-to-all-start.1 = ((bf16[30,16,2,128]{3,2,0,1:T(2,128)(2,1)}), bf16[30,16,2,128]{3,2,0,1:T(2,128)(2,1)S(1)}, u32[]{:S(2)}, u32[]{:S(2)}) async-start(bf16[30,16,2,128]{3,2,0,1:T(2,128)(2,1)} %bitcast.85), calls=%async_computation.1 | async-start | bytes 491520 | tf_op jit(solution)/shard_map/all_to_all | solution.py:162
  78.5 1.1 %fusion.33 = (f32[2,4,8,8,1,1,256]{6,3,5,4,2,1,0:T(8,128)}, f32[2,4,8,8,1,1,256]{6,3,5,4,2,1,0:T(8,128)}) fusion(f32[2,4,8,8,1,2,256]{6,3,5,4,2,1,0:T(8,128)S(1)} %get-tuple-element.18), kind=kLoop, calls=%fused_computation.81 | loop fusion | bytes 2097152 | tf_op jit(solution)/shard_map/jit(_roll_static)/slice | solution.py:53
  79.6 1.7 %fusion.37 = (f32[2,4,8,8,1,2,255]{6,3,5,4,2,1,0:T(8,128)}, f32[2,4,8,8,1,2,255]{6,3,5,4,2,1,0:T(8,128)}) fusion(f32[2,4,8,8,1,2,256]{6,3,5,4,2,1,0:T(8,128)S(1)} %get-tuple-element.17), kind=kLoop, calls=%fused_computation.85 | loop fusion | bytes 4177920 | tf_op jit(solution)/shard_map/jit(_roll_static)/slice | solution.py:54
  81.3 12.8 %all-to-all-done.1 = bf16[30,16,2,128]{3,2,0,1:T(2,128)(2,1)S(1)} async-done(((bf16[30,16,2,128]{3,2,0,1:T(2,128)(2,1)}), bf16[30,16,2,128]{3,2,0,1:T(2,128)(2,1)S(1)}, u32[]{:S(2)}, u32[]{:S(2)}) %all-to-all-start.1) | async-done | bytes 245792 | tf_op jit(solution)/shard_map/all_to_all | solution.py:162
  94.7 1.8 %gather_fusion.1 = f32[256,2,512]{2,1,0:T(2,128)S(1)} fusion(f32[120,2,512]{2,1,0:T(2,128)S(1)} %reshape.456, s32[1024]{0:T(1024)S(1)} %pad_clamp_fusion), kind=kCustom, calls=%fused_computation.1 | custom fusion | bytes 2098176 | tf_op jit(solution)/shard_map/jit(_take)/gather | solution.py:172
  96.5 5.1 %fusion.7 = f32[2,4,8,8,1,2,256]{6,3,5,4,2,1,0:T(8,128)S(1)} fusion(f32[2,4,8,8,1,2,256]{6,3,5,4,2,1,0:T(8,128)S(1)} %bitcast.74, f32[2,4,8,8,1,2,1]{6,3,5,4,2,1,0:T(8,128)} %get-tuple-element.30, f32[2,4,8,8,1,2,255]{6,3,5,4,2,1,0:T(8,128)} %get-tuple-element.32, f32[2,4,8,8,1,2,255]{6,3,5,4,2,1,0:T(8,128)} %get-tuple-element.31, ...), kind=kLoop, calls=%fused_computation.18 | loop fusion | flops 6815744 | bytes 10485768 | tf_op jit(solution)/shard_map/sub | solution.py:126
  101.6 2.8 %fusion.22 = f32[2,256,1,512]{3,0,1,2:T(2,128)S(1)} fusion(f32[2,256,512]{2,1,0:T(8,128)S(1)} %bitcast.75, f32[256,2,512]{2,1,0:T(2,128)S(1)} %gather_fusion.1, pred[256]{0:T(512)(128)(4,1)S(1)} %compare_and_fusion.2, pred[256]{0:T(512)(128)(4,1)S(1)} %gt.18, f32[2]{0:T(128)S(1)} %neg.4, f32[2,256,1,512]{3,2,1,0:T(1,128)S(1)} %copy-done), kind=kLoop, calls=%fused_computation.40 | loop fusion | flops 1310720 | bytes 4194824 | tf_op jit(solution)/shard_map/add | solution.py:180
  104.5 2.0 %copy.185 = f32[2,256,1,512]{3,2,1,0:T(1,128)} copy(f32[2,256,1,512]{3,0,1,2:T(2,128)S(1)} %fusion.22) | data formatting | bytes 2097152 | tf_op jit(solution)/shard_map/add | solution.py:180
  (52 shorter events, 4.9 us)
Async XLA Ops:
  0.0 12.1 %copy-start.4 = (s32[120]{0:T(128)S(1)}, s32[120]{0:T(128)}, u32[]{:S(2)}) copy-start(s32[120]{0:T(128)} %param.9) | copy-start | bytes 1444
  4.6 23.5 %collective-permute-start.1 = (f32[2,1,8,8,1,2,256]{6,3,5,4,2,1,0:T(8,128)}, f32[2,1,8,8,1,2,256]{6,3,5,4,2,1,0:T(8,128)}, u32[]{:S(2)}, u32[]{:S(2)}) collective-permute-start(f32[2,1,8,8,1,2,256]{6,3,5,4,2,1,0:T(8,128)} %get-tuple-element.20), channel_id=1, source_target_pairs={{0,16},{16,32},{32,48},{1,17},{17,33},{33,49},{2,18},{18,34},{34,5... | collective-permute-start | bytes 786440 | tf_op jit(solution)/shard_map/ppermute | solution.py:107
  8.7 19.3 %collective-permute-start = (f32[2,1,8,8,1,2,256]{6,3,5,4,2,1,0:T(8,128)}, f32[2,1,8,8,1,2,256]{6,3,5,4,2,1,0:T(8,128)}, u32[]{:S(2)}, u32[]{:S(2)}) collective-permute-start(f32[2,1,8,8,1,2,256]{6,3,5,4,2,1,0:T(8,128)} %get-tuple-element.19), channel_id=1, source_target_pairs={{16,0},{32,16},{48,32},{17,1},{33,17},{49,33},{18,2},{34,18},{50,3... | collective-permute-start | bytes 786440 | tf_op jit(solution)/shard_map/ppermute | solution.py:110
  14.6 24.4 %all-to-all-start = ((bf16[2,120,4,128]{3,0,1,2:T(2,128)(2,1)}), bf16[2,120,4,128]{3,0,1,2:T(2,128)(2,1)S(1)}, u32[]{:S(2)}, u32[]{:S(2)}) async-start(bf16[2,120,4,128]{3,0,1,2:T(2,128)(2,1)} %fusion.26), calls=%async_computation | async-start | bytes 491520 | tf_op jit(solution)/shard_map/all_to_all | solution.py:138
  20.5 4.6 %copy-start.5 = (f32[2]{0:T(128)S(1)}, f32[2]{0:T(128)}, u32[]{:S(2)}) copy-start(f32[2]{0:T(128)} %param.10) | copy-start | bytes 28
  20.5 4.6 %copy-start.2 = (bf16[2,30,120,120]{3,2,1,0:T(8,128)(2,1)S(1)}, bf16[2,30,120,120]{3,2,1,0:T(8,128)(2,1)}, u32[]{:S(2)}) copy-start(bf16[2,30,120,120]{3,2,1,0:T(8,128)(2,1)} %param.7) | copy-start | bytes 5184004
  23.3 2.4 %copy-start.3 = (s32[8,8]{1,0:T(8,128)S(1)}, s32[8,8]{1,0:T(8,128)}, u32[]{:S(2)}) copy-start(s32[8,8]{1,0:T(8,128)} %param.8) | copy-start | bytes 772
  25.1 2.9 %copy-start.6 = (f32[2]{0:T(128)S(1)}, f32[2]{0:T(128)}, u32[]{:S(2)}) copy-start(f32[2]{0:T(128)} %param.11) | copy-start | bytes 28
  31.2 65.2 %collective-permute-start.2 = (f32[2,4,8,8,1,2,256]{6,3,5,4,2,1,0:T(8,128)}, f32[2,4,8,8,1,2,256]{6,3,5,4,2,1,0:T(8,128)}, u32[]{:S(2)}, u32[]{:S(2)}) collective-permute-start(f32[2,4,8,8,1,2,256]{6,3,5,4,2,1,0:T(8,128)} %get-tuple-element.14), channel_id=1, source_target_pairs={{1,0},{2,1},{3,2},{4,3},{5,4},{6,5},{7,6},{8,7},{9,8},{10,9},{11,1... | collective-permute-start | bytes 3145736 | tf_op jit(solution)/shard_map/ppermute | solution.py:114
  37.0 59.5 %collective-permute-start.3 = (f32[2,4,8,8,1,2,256]{6,3,5,4,2,1,0:T(8,128)}, f32[2,4,8,8,1,2,256]{6,3,5,4,2,1,0:T(8,128)}, u32[]{:S(2)}, u32[]{:S(2)}) collective-permute-start(f32[2,4,8,8,1,2,256]{6,3,5,4,2,1,0:T(8,128)} %get-tuple-element.13), channel_id=1, source_target_pairs={{0,1},{1,2},{2,3},{3,4},{4,5},{5,6},{6,7},{7,8},{8,9},{9,10},{10,1... | collective-permute-start | bytes 3145736 | tf_op jit(solution)/shard_map/ppermute | solution.py:117
  39.0 17.0 %collective-permute-start.6 = (bf16[8,120,1,128]{3,1,0,2:T(8,128)(2,1)S(1)}, bf16[8,120,1,128]{3,1,0,2:T(8,128)(2,1)S(1)}, u32[]{:S(2)}, u32[]{:S(2)}) collective-permute-start(bf16[8,120,1,128]{3,1,0,2:T(8,128)(2,1)S(1)} %bitcast.81), channel_id=1, source_target_pairs={{0,48},{16,0},{1,49},{17,1},{2,50},{18,2},{3,51},{19,3},{4,52},{20... | collective-permute-start | bytes 737288 | tf_op jit(solution)/shard_map/ppermute | solution.py:90
  44.7 11.3 %collective-permute-start.5 = (bf16[8,120,1,128]{3,1,0,2:T(8,128)(2,1)S(1)}, bf16[8,120,1,128]{3,1,0,2:T(8,128)(2,1)S(1)}, u32[]{:S(2)}, u32[]{:S(2)}) collective-permute-start(bf16[8,120,1,128]{3,1,0,2:T(8,128)(2,1)S(1)} %bitcast.82), channel_id=1, source_target_pairs={{0,32},{16,48},{1,33},{17,49},{2,34},{18,50},{3,35},{19,51},{4,36}... | collective-permute-start | bytes 737288 | tf_op jit(solution)/shard_map/ppermute | solution.py:90
  46.0 11.3 %collective-permute-start.4 = (bf16[8,120,1,128]{3,1,0,2:T(8,128)(2,1)S(1)}, bf16[8,120,1,128]{3,1,0,2:T(8,128)(2,1)S(1)}, u32[]{:S(2)}, u32[]{:S(2)}) collective-permute-start(bf16[8,120,1,128]{3,1,0,2:T(8,128)(2,1)S(1)} %bitcast.83), channel_id=1, source_target_pairs={{0,16},{16,32},{1,17},{17,33},{2,18},{18,34},{3,19},{19,35},{4,20}... | collective-permute-start | bytes 737288 | tf_op jit(solution)/shard_map/ppermute | solution.py:90
  70.0 24.1 %all-to-all-start.1 = ((bf16[30,16,2,128]{3,2,0,1:T(2,128)(2,1)}), bf16[30,16,2,128]{3,2,0,1:T(2,128)(2,1)S(1)}, u32[]{:S(2)}, u32[]{:S(2)}) async-start(bf16[30,16,2,128]{3,2,0,1:T(2,128)(2,1)} %bitcast.85), calls=%async_computation.1 | async-start | bytes 491520 | tf_op jit(solution)/shard_map/all_to_all | solution.py:162
  79.6 16.9 %copy-start.1 = (f32[2,4,8,8,1,2,1]{6,3,5,4,2,1,0:T(8,128)S(1)}, f32[2,4,8,8,1,2,1]{6,3,5,4,2,1,0:T(8,128)}, u32[]{:S(2)}) copy-start(f32[2,4,8,8,1,2,1]{6,3,5,4,2,1,0:T(8,128)} %get-tuple-element.25) | copy-start | bytes 12292
  96.5 5.1 %copy-start = (f32[2,256,1,512]{3,2,1,0:T(1,128)S(1)}, f32[2,256,1,512]{3,2,1,0:T(1,128)}, u32[]{:S(2)}) copy-start(f32[2,256,1,512]{3,2,1,0:T(1,128)} %param.6) | copy-start | bytes 3145732

commit v5 on v4

--- a/solution.py
+++ b/solution.py
@@ -155,6 +155,7 @@
     kcat = jnp.concatenate([kpad[k] for k in range(NKIND) for _ in range(2)], axis=-1)
     gained = collide_call(kcat, rhs, lmat)
 
+    advected, gained = lax.optimization_barrier((advected, gained))
     gained = gained.reshape(out_rows, species_devs, 1, own_count, block_cells)
     gained = jnp.broadcast_to(
         gained, (out_rows, species_devs, mode_devs, own_count, block_cells)

time: 108 us -> 124 us (1.15)
  starting transfers between devices: 37.3 us -> 47.3 us
  local copies, waits for them, and re-layouts: 19.5 us -> 22.4 us
  other arithmetic: 21.2 us -> 22.6 us
  waiting for transfers between devices: 20.1 us -> 21.4 us
    all_to_all x1, starting transfers between devices: 8.5 us -> 18.3 us  [per_device(): lax.all_to_all(gained.astype(jnp.bfloat16), ('species', 'mode'), 1, 1, ti...]
    ppermute x1, waiting for transfers between devices: 0.01 us -> 3.69 us  [per_device(): lax.ppermute(down_part[:, :, :, :, row_count - 1:], 'space', [(i, i + 1)...]
    all_to_all x1, waiting for transfers between devices: 12.8 us -> 10.5 us  [per_device(): lax.all_to_all(gained.astype(jnp.bfloat16), ('species', 'mode'), 1, 1, ti...]
    squeeze x1, local copies, waits for them, and re-layouts: 0.53 us -> 2.78 us  [per_device(): kpad[k]]
    concatenate x1, other arithmetic: 2.03 us -> 3.55 us  [per_device(): jnp.concatenate([kpad[k] for k in range(NKIND) for _ in range(2)], axis=-1)]
    unnamed x17 -> x15, local copies, waits for them, and re-layouts: 3.47 us -> 3.49 us
  transfers between devices with their start and end apart: 9 -> 9, of which waited for: 3 -> 4; matrix products, arithmetic and copies ran while one was open for 25% -> 21% of each run, Pallas kernels for 7% -> 6%
where the time goes in v5:
time: 124 us; the launch traced here: 122 us
  starting transfers between devices  47.3 us (38%)
  other arithmetic  22.6 us (18%)
  local copies, waits for them, and re-layouts  22.4 us (18%)
  waiting for transfers between devices  21.4 us (17%)
  Pallas kernels  7.8 us (6%)
    all_to_all x1, starting transfers between devices, per_device(): lax.all_to_all(gained.astype(jnp.bfloat16), ('species', 'mode'), 1, 1, ti...  18.3 us
    all_to_all x1, waiting for transfers between devices, per_device(): lax.all_to_all(gained.astype(jnp.bfloat16), ('species', 'mode'), 1, 1, ti...  10.5 us
    ppermute x3, starting transfers between devices, shift_permutes(): received.append((shift, lax.ppermute(values, axis, pairs)))  9.96 us
    pallas_call x1, Pallas kernels, collide_call(): pl.pallas_call(collide_body, out_shape=jax.ShapeDtypeStruct((kcat.shape[0...  7.8 us
    ppermute x3, waiting for transfers between devices, shift_permutes(): received.append((shift, lax.ppermute(values, axis, pairs)))  7.24 us
    all_to_all x1, starting transfers between devices, per_device(): spread = lax.all_to_all(picked, 'species', 2, 0, tiled=True)  5.89 us
    ppermute x1, starting transfers between devices, per_device(): lax.ppermute(up_part[:, :, :, :, :1], 'space', [(i + 1, i) for i in range...  5.73 us
    sub x1, other arithmetic, per_device(): phase_field - nu_step * thermal_speed.reshape(own_count, 1, 1, 1, 1, 1, 1...  4.89 us
  transfers between devices with their start and end apart: 9, of which 4 were waited for; matrix products, arithmetic and copies ran while one was open for 21% of the time, Pallas kernels for 6%

profile of v5, /device:TPU:2, one launch (start us, length us, event | category | flops | bytes accessed | tf_op | source)
XLA Modules:
  0.0 122.2 jit_solution(4472325577172960056)
XLA Ops:
  0.0 3.7 %reduce.18 = f32[2,256,512]{2,1,0:T(8,128)S(1)} reduce(f32[2,256,1,512]{3,2,1,0:T(1,128)} %param.6, f32[]{:T(128)} %constant.93), dimensions={2}, to_apply=%param.6.reduce_sub_computation | reduce | bytes 2097156 | tf_op args[0]
  4.6 4.2 %collective-permute-start.1 = (f32[2,1,8,8,1,2,256]{6,3,5,4,2,1,0:T(8,128)}, f32[2,1,8,8,1,2,256]{6,3,5,4,2,1,0:T(8,128)}, u32[]{:S(2)}, u32[]{:S(2)}) collective-permute-start(f32[2,1,8,8,1,2,256]{6,3,5,4,2,1,0:T(8,128)} %get-tuple-element.24), channel_id=1, source_target_pairs={{0,16},{16,32},{32,48},{1,17},{17,33},{33,49},{2,18},{18,34},{34,5... | collective-permute-start | bytes 786440 | tf_op jit(solution)/shard_map/ppermute | solution.py:107
  8.8 1.3 %collective-permute-start = (f32[2,1,8,8,1,2,256]{6,3,5,4,2,1,0:T(8,128)}, f32[2,1,8,8,1,2,256]{6,3,5,4,2,1,0:T(8,128)}, u32[]{:S(2)}, u32[]{:S(2)}) collective-permute-start(f32[2,1,8,8,1,2,256]{6,3,5,4,2,1,0:T(8,128)} %get-tuple-element.23), channel_id=1, source_target_pairs={{16,0},{32,16},{48,32},{17,1},{33,17},{49,33},{18,2},{34,18},{50,3... | collective-permute-start | bytes 786440 | tf_op jit(solution)/shard_map/ppermute | solution.py:110
  10.1 2.0 %copy.207 = bf16[2,256,1,512]{3,0,1,2:T(2,128)(2,1)S(1)} copy(f32[2,256,1,512]{3,2,1,0:T(1,128)} %param.6) | data formatting | bytes 1572864 | tf_op args[0]
  12.2 1.1 gather_fusion
  13.3 1.4 %fusion.26 = bf16[2,120,4,128]{3,0,1,2:T(2,128)(2,1)} fusion(pred[120]{0:T(512)(128)(4,1)S(1)} %get-tuple-element.13, pred[120]{0:T(512)(128)(4,1)S(1)} %get-tuple-element.43, bf16[120,2,512]{2,1,0:T(2,128)(2,1)S(1)} %gather_fusion), kind=kLoop, calls=%fused_computation.52 | loop fusion | flops 245760 | bytes 491760 | tf_op jit(solution)/shard_map/convert_element_type | solution.py:134
  14.6 5.9 %all-to-all-start = ((bf16[2,120,4,128]{3,0,1,2:T(2,128)(2,1)}), bf16[2,120,4,128]{3,0,1,2:T(2,128)(2,1)S(1)}, u32[]{:S(2)}, u32[]{:S(2)}) async-start(bf16[2,120,4,128]{3,0,1,2:T(2,128)(2,1)} %fusion.26), calls=%async_computation | async-start | bytes 491520 | tf_op jit(solution)/shard_map/all_to_all | solution.py:138
  20.5 1.2 fusion.34
  21.7 1.4 %fusion.35 = (f32[2,4,8,8,1,2,255]{6,3,5,4,2,1,0:T(8,128)S(1)}, f32[2,4,8,8,1,2,255]{6,3,5,4,2,1,0:T(8,128)}) fusion(f32[2,4,8,8,1,2,256]{6,3,5,4,2,1,0:T(8,128)S(1)} %bitcast.71), kind=kLoop, calls=%fused_computation.83 | loop fusion | bytes 4177920 | tf_op jit(solution)/shard_map/jit(_roll_static)/slice | solution.py:52
  23.1 2.8 %fusion.23 = (bf16[30,128,128]{2,1,0:T(8,128)(2,1)S(1)}, bf16[30,128,128]{2,1,0:T(8,128)(2,1)}) fusion(bf16[2,30,120,120]{3,2,1,0:T(8,128)(2,1)} %param.7), kind=kLoop, calls=%fused_computation.44 | loop fusion | bytes 3694080 | tf_op jit(solution)/shard_map/squeeze | solution.py:155
  26.9 3.5 %pad_maximum_fusion.k_ref = bf16[30,128,512]{2,1,0:T(8,128)(2,1)} fusion(bf16[30,128,128]{2,1,0:T(8,128)(2,1)} %get-tuple-element.16, bf16[30,128,128]{2,1,0:T(8,128)(2,1)S(1)} %get-tuple-element.15), kind=kLoop, calls=%fused_computation.2 | loop fusion | flops 15728640 | bytes 5898240 | tf_op jit(solution)/shard_map/concatenate | solution.py:155
  30.4 1.2 fusion.32
  31.6 3.0 %multiply_subtract_fusion = (f32[2,4,8,8,1,2,256]{6,3,5,4,2,1,0:T(8,128)}, f32[2,4,8,8,1,2,256]{6,3,5,4,2,1,0:T(8,128)}, f32[2,4,8,8,1,2,256]{6,3,5,4,2,1,0:T(8,128)S(1)}, f32[2,4,8,8,1,2,256]{6,3,5,4,2,1,0:T(8,128)S(1)}) fusion(f32[2,4,8,8,1,2,256]{6,3,5,4,2,1,0:T(8,128)S(1)} %bitcast.73, f32[2,1,8,8,1,2,256]{6,3,5,4,2,1,0:T(8,128)} %collective-permute-done.1, ...), kind=kLoop, calls=%fused_computation.42 | loop fusion | flops 4194304 | bytes 5770240 | tf_op jit(solution)/shard_map/sub | solution.py:113
  34.6 1.1 fusion.36
  35.7 5.7 %collective-permute-start.2 = (f32[2,4,8,8,1,2,256]{6,3,5,4,2,1,0:T(8,128)}, f32[2,4,8,8,1,2,256]{6,3,5,4,2,1,0:T(8,128)}, u32[]{:S(2)}, u32[]{:S(2)}) collective-permute-start(f32[2,4,8,8,1,2,256]{6,3,5,4,2,1,0:T(8,128)} %get-tuple-element.18), channel_id=1, source_target_pairs={{1,0},{2,1},{3,2},{4,3},{5,4},{6,5},{7,6},{8,7},{9,8},{10,9},{11,1... | collective-permute-start | bytes 3145736 | tf_op jit(solution)/shard_map/ppermute | solution.py:114
  41.5 1.9 %collective-permute-start.3 = (f32[2,4,8,8,1,2,256]{6,3,5,4,2,1,0:T(8,128)}, f32[2,4,8,8,1,2,256]{6,3,5,4,2,1,0:T(8,128)}, u32[]{:S(2)}, u32[]{:S(2)}) collective-permute-start(f32[2,4,8,8,1,2,256]{6,3,5,4,2,1,0:T(8,128)} %get-tuple-element.17), channel_id=1, source_target_pairs={{0,1},{1,2},{2,3},{3,4},{4,5},{5,6},{6,7},{7,8},{8,9},{9,10},{10,1... | collective-permute-start | bytes 3145736 | tf_op jit(solution)/shard_map/ppermute | solution.py:117
  43.4 1.7 %fusion.37 = (f32[2,4,8,8,1,2,255]{6,3,5,4,2,1,0:T(8,128)}, f32[2,4,8,8,1,2,255]{6,3,5,4,2,1,0:T(8,128)}) fusion(f32[2,4,8,8,1,2,256]{6,3,5,4,2,1,0:T(8,128)S(1)} %get-tuple-element.21), kind=kLoop, calls=%fused_computation.85 | loop fusion | bytes 4177920 | tf_op jit(solution)/shard_map/jit(_roll_static)/slice | solution.py:54
  45.2 5.7 %collective-permute-start.6 = (bf16[8,120,1,128]{3,1,0,2:T(8,128)(2,1)S(1)}, bf16[8,120,1,128]{3,1,0,2:T(8,128)(2,1)S(1)}, u32[]{:S(2)}, u32[]{:S(2)}) collective-permute-start(bf16[8,120,1,128]{3,1,0,2:T(8,128)(2,1)S(1)} %bitcast.81), channel_id=1, source_target_pairs={{0,48},{16,0},{1,49},{17,1},{2,50},{18,2},{3,51},{19,3},{4,52},{20... | collective-permute-start | bytes 737288 | tf_op jit(solution)/shard_map/ppermute | solution.py:90
  50.9 1.3 %collective-permute-start.5 = (bf16[8,120,1,128]{3,1,0,2:T(8,128)(2,1)S(1)}, bf16[8,120,1,128]{3,1,0,2:T(8,128)(2,1)S(1)}, u32[]{:S(2)}, u32[]{:S(2)}) collective-permute-start(bf16[8,120,1,128]{3,1,0,2:T(8,128)(2,1)S(1)} %bitcast.82), channel_id=1, source_target_pairs={{0,32},{16,48},{1,33},{17,49},{2,34},{18,50},{3,35},{19,51},{4,36}... | collective-permute-start | bytes 737288 | tf_op jit(solution)/shard_map/ppermute | solution.py:90
  52.2 3.0 %collective-permute-start.4 = (bf16[8,120,1,128]{3,1,0,2:T(8,128)(2,1)S(1)}, bf16[8,120,1,128]{3,1,0,2:T(8,128)(2,1)S(1)}, u32[]{:S(2)}, u32[]{:S(2)}) collective-permute-start(bf16[8,120,1,128]{3,1,0,2:T(8,128)(2,1)S(1)} %bitcast.83), channel_id=1, source_target_pairs={{0,16},{16,32},{1,17},{17,33},{2,18},{18,34},{3,19},{19,35},{4,20}... | collective-permute-start | bytes 737288 | tf_op jit(solution)/shard_map/ppermute | solution.py:90
  55.1 1.1 fusion.33
  56.3 5.9 %collective-permute-done.6 = bf16[8,120,1,128]{3,1,0,2:T(8,128)(2,1)S(1)} collective-permute-done((bf16[8,120,1,128]{3,1,0,2:T(8,128)(2,1)S(1)}, bf16[8,120,1,128]{3,1,0,2:T(8,128)(2,1)S(1)}, u32[]{:S(2)}, u32[]{:S(2)}) %collective-permute-start.6) | collective-permute-done | bytes 245792 | tf_op jit(solution)/shard_map/ppermute | solution.py:90
  62.2 1.3 %collective-permute-done.4 = bf16[8,120,1,128]{3,1,0,2:T(8,128)(2,1)S(1)} collective-permute-done((bf16[8,120,1,128]{3,1,0,2:T(8,128)(2,1)S(1)}, bf16[8,120,1,128]{3,1,0,2:T(8,128)(2,1)S(1)}, u32[]{:S(2)}, u32[]{:S(2)}) %collective-permute-start.4) | collective-permute-done | bytes 245792 | tf_op jit(solution)/shard_map/ppermute | solution.py:90
  64.5 1.3 %copy.206 = bf16[64,8,8,128]{3,1,2,0:T(8,128)(2,1)} copy(bf16[64,8,8,128]{3,2,1,0:T(8,128)(2,1)S(1)} %bitcast.76) | data formatting | bytes 2097152
  66.6 7.8 %shard_map.64 = f32[30,1024]{1,0:T(8,128)} custom-call(bf16[30,128,512]{2,1,0:T(8,128)(2,1)} %pad_maximum_fusion.k_ref, bf16[512,1024]{1,0:T(8,128)(2,1)} %bitcast.77, f32[128,1024]{1,0:T(8,128)} %copy_bitcast_fusion.2.l_ref), custom_call_target="tpu_custom_call" | custom-call | tf_op jit(solution)/shard_map/pallas_call | solution.py:76
  74.4 3.7 %collective-permute-done.3 = f32[2,4,8,8,1,2,256]{6,3,5,4,2,1,0:T(8,128)} collective-permute-done((f32[2,4,8,8,1,2,256]{6,3,5,4,2,1,0:T(8,128)}, f32[2,4,8,8,1,2,256]{6,3,5,4,2,1,0:T(8,128)}, u32[]{:S(2)}, u32[]{:S(2)}) %collective-permute-start.3) | collective-permute-done | bytes 1048608 | tf_op jit(solution)/shard_map/ppermute | solution.py:117
  78.1 4.9 %fusion.7 = f32[2,4,8,8,1,2,256]{6,3,5,4,2,1,0:T(8,128)S(1)} fusion(f32[2,4,8,8,1,2,256]{6,3,5,4,2,1,0:T(8,128)S(1)} %bitcast.74, f32[2,4,8,8,1,2,1]{6,3,5,4,2,1,0:T(8,128)} %get-tuple-element.34, f32[2,4,8,8,1,2,255]{6,3,5,4,2,1,0:T(8,128)} %get-tuple-element.36, f32[2,4,8,8,1,2,255]{6,3,5,4,2,1,0:T(8,128)} %get-tuple-element.35, ...), kind=kLoop, calls=%fused_computation.18 | loop fusion | flops 6815744 | bytes 10485768 | tf_op jit(solution)/shard_map/sub | solution.py:126
  83.9 18.3 %all-to-all-start.1 = ((bf16[30,16,2,128]{3,2,0,1:T(2,128)(2,1)}), bf16[30,16,2,128]{3,2,0,1:T(2,128)(2,1)S(1)}, u32[]{:S(2)}, u32[]{:S(2)}) async-start(bf16[30,16,2,128]{3,2,0,1:T(2,128)(2,1)} %bitcast.17), calls=%async_computation.1 | async-start | bytes 491520 | tf_op jit(solution)/shard_map/all_to_all | solution.py:163
  102.3 10.5 %all-to-all-done.1 = bf16[30,16,2,128]{3,2,0,1:T(2,128)(2,1)S(1)} async-done(((bf16[30,16,2,128]{3,2,0,1:T(2,128)(2,1)}), bf16[30,16,2,128]{3,2,0,1:T(2,128)(2,1)S(1)}, u32[]{:S(2)}, u32[]{:S(2)}) %all-to-all-start.1) | async-done | bytes 245792 | tf_op jit(solution)/shard_map/all_to_all | solution.py:163
  113.4 2.7 %gather_fusion.1 = f32[256,2,512]{2,1,0:T(2,128)} fusion(f32[120,2,512]{2,1,0:T(2,128)S(1)} %reshape.456, s32[1024]{0:T(1024)S(1)} %pad_clamp_fusion), kind=kCustom, calls=%fused_computation.1 | custom fusion | bytes 2098176 | tf_op jit(solution)/shard_map/jit(_take)/gather | solution.py:173
  116.1 4.0 %fusion.22 = f32[2,256,1,512]{3,0,1,2:T(2,128)S(1)} fusion(f32[2,256,512]{2,1,0:T(8,128)S(1)} %bitcast.75, f32[256,2,512]{2,1,0:T(2,128)} %gather_fusion.1, pred[256]{0:T(512)(128)(4,1)S(1)} %compare_and_fusion, pred[256]{0:T(512)(128)(4,1)S(1)} %gt.18, f32[2]{0:T(128)S(1)} %neg.4, f32[2,256,1,512]{3,2,1,0:T(1,128)S(1)} %copy-done), kind=kLoop, calls=%fused_computation.40 | loop fusion | flops 1310720 | bytes 4194824 | tf_op jit(solution)/shard_map/add | solution.py:181
  120.1 2.0 %copy.185 = f32[2,256,1,512]{3,2,1,0:T(1,128)} copy(f32[2,256,1,512]{3,0,1,2:T(2,128)S(1)} %fusion.22) | data formatting | bytes 2097152 | tf_op jit(solution)/shard_map/add | solution.py:181
  (50 shorter events, 5.2 us)
Async XLA Ops:
  0.0 12.1 %copy-start.3 = (s32[120]{0:T(128)S(1)}, s32[120]{0:T(128)}, u32[]{:S(2)}) copy-start(s32[120]{0:T(128)} %param.9) | copy-start | bytes 1444
  4.6 27.0 %collective-permute-start.1 = (f32[2,1,8,8,1,2,256]{6,3,5,4,2,1,0:T(8,128)}, f32[2,1,8,8,1,2,256]{6,3,5,4,2,1,0:T(8,128)}, u32[]{:S(2)}, u32[]{:S(2)}) collective-permute-start(f32[2,1,8,8,1,2,256]{6,3,5,4,2,1,0:T(8,128)} %get-tuple-element.24), channel_id=1, source_target_pairs={{0,16},{16,32},{32,48},{1,17},{17,33},{33,49},{2,18},{18,34},{34,5... | collective-permute-start | bytes 786440 | tf_op jit(solution)/shard_map/ppermute | solution.py:107
  8.8 22.8 %collective-permute-start = (f32[2,1,8,8,1,2,256]{6,3,5,4,2,1,0:T(8,128)}, f32[2,1,8,8,1,2,256]{6,3,5,4,2,1,0:T(8,128)}, u32[]{:S(2)}, u32[]{:S(2)}) collective-permute-start(f32[2,1,8,8,1,2,256]{6,3,5,4,2,1,0:T(8,128)} %get-tuple-element.23), channel_id=1, source_target_pairs={{16,0},{32,16},{48,32},{17,1},{33,17},{49,33},{18,2},{34,18},{50,3... | collective-permute-start | bytes 786440 | tf_op jit(solution)/shard_map/ppermute | solution.py:110
  12.1 11.0 %copy-start.4 = (f32[2]{0:T(128)S(1)}, f32[2]{0:T(128)}, u32[]{:S(2)}) copy-start(f32[2]{0:T(128)} %param.10) | copy-start | bytes 28
  14.6 30.5 %all-to-all-start = ((bf16[2,120,4,128]{3,0,1,2:T(2,128)(2,1)}), bf16[2,120,4,128]{3,0,1,2:T(2,128)(2,1)S(1)}, u32[]{:S(2)}, u32[]{:S(2)}) async-start(bf16[2,120,4,128]{3,0,1,2:T(2,128)(2,1)} %fusion.26), calls=%async_computation | async-start | bytes 491520 | tf_op jit(solution)/shard_map/all_to_all | solution.py:138
  21.7 4.2 %copy-start.2 = (s32[8,8]{1,0:T(8,128)S(1)}, s32[8,8]{1,0:T(8,128)}, u32[]{:S(2)}) copy-start(s32[8,8]{1,0:T(8,128)} %param.8) | copy-start | bytes 772
  21.7 5.2 %copy-start.5 = (f32[2]{0:T(128)S(1)}, f32[2]{0:T(128)}, u32[]{:S(2)}) copy-start(f32[2]{0:T(128)} %param.11) | copy-start | bytes 28
  35.7 38.7 %collective-permute-start.2 = (f32[2,4,8,8,1,2,256]{6,3,5,4,2,1,0:T(8,128)}, f32[2,4,8,8,1,2,256]{6,3,5,4,2,1,0:T(8,128)}, u32[]{:S(2)}, u32[]{:S(2)}) collective-permute-start(f32[2,4,8,8,1,2,256]{6,3,5,4,2,1,0:T(8,128)} %get-tuple-element.18), channel_id=1, source_target_pairs={{1,0},{2,1},{3,2},{4,3},{5,4},{6,5},{7,6},{8,7},{9,8},{10,9},{11,1... | collective-permute-start | bytes 3145736 | tf_op jit(solution)/shard_map/ppermute | solution.py:114
  41.5 36.6 %collective-permute-start.3 = (f32[2,4,8,8,1,2,256]{6,3,5,4,2,1,0:T(8,128)}, f32[2,4,8,8,1,2,256]{6,3,5,4,2,1,0:T(8,128)}, u32[]{:S(2)}, u32[]{:S(2)}) collective-permute-start(f32[2,4,8,8,1,2,256]{6,3,5,4,2,1,0:T(8,128)} %get-tuple-element.17), channel_id=1, source_target_pairs={{0,1},{1,2},{2,3},{3,4},{4,5},{5,6},{6,7},{7,8},{8,9},{9,10},{10,1... | collective-permute-start | bytes 3145736 | tf_op jit(solution)/shard_map/ppermute | solution.py:117
  45.2 17.0 %collective-permute-start.6 = (bf16[8,120,1,128]{3,1,0,2:T(8,128)(2,1)S(1)}, bf16[8,120,1,128]{3,1,0,2:T(8,128)(2,1)S(1)}, u32[]{:S(2)}, u32[]{:S(2)}) collective-permute-start(bf16[8,120,1,128]{3,1,0,2:T(8,128)(2,1)S(1)} %bitcast.81), channel_id=1, source_target_pairs={{0,48},{16,0},{1,49},{17,1},{2,50},{18,2},{3,51},{19,3},{4,52},{20... | collective-permute-start | bytes 737288 | tf_op jit(solution)/shard_map/ppermute | solution.py:90
  50.9 11.3 %collective-permute-start.5 = (bf16[8,120,1,128]{3,1,0,2:T(8,128)(2,1)S(1)}, bf16[8,120,1,128]{3,1,0,2:T(8,128)(2,1)S(1)}, u32[]{:S(2)}, u32[]{:S(2)}) collective-permute-start(bf16[8,120,1,128]{3,1,0,2:T(8,128)(2,1)S(1)} %bitcast.82), channel_id=1, source_target_pairs={{0,32},{16,48},{1,33},{17,49},{2,34},{18,50},{3,35},{19,51},{4,36}... | collective-permute-start | bytes 737288 | tf_op jit(solution)/shard_map/ppermute | solution.py:90
  52.2 11.3 %collective-permute-start.4 = (bf16[8,120,1,128]{3,1,0,2:T(8,128)(2,1)S(1)}, bf16[8,120,1,128]{3,1,0,2:T(8,128)(2,1)S(1)}, u32[]{:S(2)}, u32[]{:S(2)}) collective-permute-start(bf16[8,120,1,128]{3,1,0,2:T(8,128)(2,1)S(1)} %bitcast.83), channel_id=1, source_target_pairs={{0,16},{16,32},{1,17},{17,33},{2,18},{18,34},{3,19},{19,35},{4,20}... | collective-permute-start | bytes 737288 | tf_op jit(solution)/shard_map/ppermute | solution.py:90
  78.1 4.9 %copy-start.1 = (f32[30,1024]{1,0:T(8,128)S(1)}, f32[30,1024]{1,0:T(8,128)}, u32[]{:S(2)}) copy-start(f32[30,1024]{1,0:T(8,128)} %shard_map.64) | copy-start | bytes 368644
  83.0 33.0 %copy-start = (f32[2,256,1,512]{3,2,1,0:T(1,128)S(1)}, f32[2,256,1,512]{3,2,1,0:T(1,128)}, u32[]{:S(2)}) copy-start(f32[2,256,1,512]{3,2,1,0:T(1,128)} %param.6) | copy-start | bytes 3145732
  83.9 28.8 %all-to-all-start.1 = ((bf16[30,16,2,128]{3,2,0,1:T(2,128)(2,1)}), bf16[30,16,2,128]{3,2,0,1:T(2,128)(2,1)S(1)}, u32[]{:S(2)}, u32[]{:S(2)}) async-start(bf16[30,16,2,128]{3,2,0,1:T(2,128)(2,1)} %bitcast.17), calls=%async_computation.1 | async-start | bytes 491520 | tf_op jit(solution)/shard_map/all_to_all | solution.py:163

commit v6 on v4

--- a/solution.py
+++ b/solution.py
@@ -134,13 +134,14 @@
     picked = jnp.where(owned[None, :, None], jnp.take(flat_dist, clipped, axis=1), 0.0).astype(
         jnp.bfloat16
     )
-    picked = picked.reshape(own_count, low_count, species_devs, block_cells)
-    spread = lax.all_to_all(picked, "species", 2, 0, tiled=True)
-    holders = [h for h in range(mode_devs) if h * per_vx <= DEG]
-    low_all = spread
-    for _, got in shift_permutes(spread, "mode", holders, mode_devs, False):
-        low_all = low_all + got
-    low_all = low_all.reshape(species_all, low_count, block_cells).astype(jnp.float32)
+    picked = picked.reshape(own_count, low_count, species_devs, 1, block_cells)
+    picked = jnp.broadcast_to(
+        picked, (own_count, low_count, species_devs, mode_devs, block_cells)
+    ).reshape(own_count, low_count, species_devs * mode_devs, block_cells)
+    spread = lax.all_to_all(picked, ("species", "mode"), 2, 2, tiled=True)
+    spread = spread.reshape(own_count, low_count, species_devs, mode_devs, block_cells)
+    spread = jnp.sum(spread.astype(jnp.float32), axis=3)
+    low_all = jnp.transpose(spread, (2, 0, 1, 3)).reshape(species_all, low_count, block_cells)
 
     chooser = jnp.stack([(pair_kind == k).astype(jnp.float32) for k in range(NKIND)])
     partner = jnp.einsum("ksr,rlc->klsc", chooser, low_all, precision=lax.Precision.HIGHEST)

time: 108 us -> 130 us (1.20)
  the two profiles are of different devices: /device:TPU:2 before, /device:TPU:130 now
where the time goes in v6:
time: 130 us; the launch traced here: 129 us
  waiting for transfers between devices  41.1 us (32%)
  starting transfers between devices  34.9 us (27%)
  local copies, waits for them, and re-layouts  23.6 us (18%)
  other arithmetic  21 us (16%)
  Pallas kernels  7.8 us (6%)
    all_to_all x1, waiting for transfers between devices, per_device(): spread = lax.all_to_all(picked, ('species', 'mode'), 2, 2, tiled=True)  36 us
    all_to_all x1, starting transfers between devices, per_device(): lax.all_to_all(gained.astype(jnp.bfloat16), ('species', 'mode'), 1, 1, ti...  18.1 us
    pallas_call x1, Pallas kernels, collide_call(): pl.pallas_call(collide_body, out_shape=jax.ShapeDtypeStruct((kcat.shape[0...  7.8 us
    all_to_all x1, starting transfers between devices, per_device(): spread = lax.all_to_all(picked, ('species', 'mode'), 2, 2, tiled=True)  7.68 us
    all_to_all x1, waiting for transfers between devices, per_device(): lax.all_to_all(gained.astype(jnp.bfloat16), ('species', 'mode'), 1, 1, ti...  5.12 us
    sub x1, other arithmetic, per_device(): phase_field - nu_step * thermal_speed.reshape(own_count, 1, 1, 1, 1, 1, 1...  4.59 us
    unnamed x16, local copies, waits for them, and re-layouts  4.37 us
    add x1, other arithmetic, per_device(): advected.reshape(own_count, mode_count, row_count, plane_cells)  4.05 us
  transfers between devices with their start and end apart: 6, of which 2 were waited for; matrix products, arithmetic and copies ran while one was open for 24% of the time, Pallas kernels for 6%

profile of v6, /device:TPU:130, one launch (start us, length us, event | category | flops | bytes accessed | tf_op | source)
XLA Modules:
  0.0 129.4 jit_solution(5379342693065986964)
XLA Ops:
  0.0 3.7 %reduce.18 = f32[2,256,512]{2,1,0:T(8,128)S(1)} reduce(f32[2,256,1,512]{3,2,1,0:T(1,128)} %param.6, f32[]{:T(128)} %constant.92), dimensions={2}, to_apply=%param.6.reduce_sub_computation | reduce | bytes 2097156 | tf_op args[0]
  3.7 0.9 fusion.29
  4.6 3.5 %collective-permute-start.1 = (f32[2,1,8,8,1,2,256]{6,3,5,4,2,1,0:T(8,128)}, f32[2,1,8,8,1,2,256]{6,3,5,4,2,1,0:T(8,128)S(1)}, u32[]{:S(2)}, u32[]{:S(2)}) collective-permute-start(f32[2,1,8,8,1,2,256]{6,3,5,4,2,1,0:T(8,128)} %get-tuple-element.20), channel_id=1, source_target_pairs={{0,16},{16,32},{32,48},{1,17},{17,33},{33,49},{2,18},{18,34},{34,5... | collective-permute-start | bytes 786440 | tf_op jit(solution)/shard_map/ppermute | solution.py:107
  8.1 1.3 collective-permute-start
  9.4 2.0 %copy.201 = bf16[2,256,1,512]{3,0,1,2:T(2,128)(2,1)S(1)} copy(f32[2,256,1,512]{3,2,1,0:T(1,128)} %param.6) | data formatting | bytes 1572864 | tf_op args[0]
  11.5 1.1 gather_fusion
  13.1 1.1 broadcast_in_dim.67
  14.2 7.7 %all-to-all-start = ((bf16[2,120,16,128]{3,1,0,2:T(8,128)(2,1)}), bf16[2,120,16,128]{3,1,0,2:T(8,128)(2,1)}, u32[]{:S(2)}, u32[]{:S(2)}) async-start(bf16[2,120,16,128]{3,1,0,2:T(8,128)(2,1)} %bitcast.5), calls=%async_computation | async-start | bytes 1966080 | tf_op jit(solution)/shard_map/all_to_all | solution.py:141
  21.9 1.2 fusion.32
  23.1 0.6 iota_reduce_fusion
  23.8 2.8 %fusion.23 = (bf16[30,128,128]{2,1,0:T(8,128)(2,1)S(1)}, bf16[30,128,128]{2,1,0:T(8,128)(2,1)}) fusion(bf16[2,30,120,120]{3,2,1,0:T(8,128)(2,1)} %param.7), kind=kLoop, calls=%fused_computation.45 | loop fusion | bytes 3694080 | tf_op jit(solution)/shard_map/squeeze | solution.py:156
  26.9 1.4 %fusion.33 = (f32[2,4,8,8,1,2,255]{6,3,5,4,2,1,0:T(8,128)S(1)}, f32[2,4,8,8,1,2,255]{6,3,5,4,2,1,0:T(8,128)}) fusion(f32[2,4,8,8,1,2,256]{6,3,5,4,2,1,0:T(8,128)S(1)} %bitcast.63), kind=kLoop, calls=%fused_computation.81 | loop fusion | bytes 4177920 | tf_op jit(solution)/shard_map/jit(_roll_static)/slice | solution.py:52
  28.2 2.0 %pad_maximum_fusion.k_ref = bf16[30,128,512]{2,1,0:T(8,128)(2,1)} fusion(bf16[30,128,128]{2,1,0:T(8,128)(2,1)S(1)} %copy-done.1, bf16[30,128,128]{2,1,0:T(8,128)(2,1)S(1)} %get-tuple-element.11), kind=kLoop, calls=%fused_computation.2 | loop fusion | flops 15728640 | bytes 5898240 | tf_op jit(solution)/shard_map/concatenate | solution.py:156
  30.3 1.1 fusion.30
  31.4 2.9 %multiply_subtract_fusion = (f32[2,4,8,8,1,2,256]{6,3,5,4,2,1,0:T(8,128)}, f32[2,4,8,8,1,2,256]{6,3,5,4,2,1,0:T(8,128)}, f32[2,4,8,8,1,2,256]{6,3,5,4,2,1,0:T(8,128)S(1)}, f32[2,4,8,8,1,2,256]{6,3,5,4,2,1,0:T(8,128)S(1)}) fusion(f32[2,4,8,8,1,2,256]{6,3,5,4,2,1,0:T(8,128)S(1)} %bitcast.65, f32[2,1,8,8,1,2,256]{6,3,5,4,2,1,0:T(8,128)S(1)} %collective-permute-done.1, ...), kind=kLoop, calls=%fused_computation.43 | loop fusion | flops 4194304 | bytes 5770240 | tf_op jit(solution)/shard_map/sub | solution.py:113
  34.3 1.9 %collective-permute-start.2 = (f32[2,4,8,8,1,2,256]{6,3,5,4,2,1,0:T(8,128)}, f32[2,4,8,8,1,2,256]{6,3,5,4,2,1,0:T(8,128)}, u32[]{:S(2)}, u32[]{:S(2)}) collective-permute-start(f32[2,4,8,8,1,2,256]{6,3,5,4,2,1,0:T(8,128)} %get-tuple-element.14), channel_id=1, source_target_pairs={{1,0},{2,1},{3,2},{4,3},{5,4},{6,5},{7,6},{8,7},{9,8},{10,9},{11,1... | collective-permute-start | bytes 3145736 | tf_op jit(solution)/shard_map/ppermute | solution.py:114
  36.2 2.4 %collective-permute-start.3 = (f32[2,4,8,8,1,2,256]{6,3,5,4,2,1,0:T(8,128)}, f32[2,4,8,8,1,2,256]{6,3,5,4,2,1,0:T(8,128)}, u32[]{:S(2)}, u32[]{:S(2)}) collective-permute-start(f32[2,4,8,8,1,2,256]{6,3,5,4,2,1,0:T(8,128)} %get-tuple-element.13), channel_id=1, source_target_pairs={{0,1},{1,2},{2,3},{3,4},{4,5},{5,6},{6,7},{7,8},{8,9},{9,10},{10,1... | collective-permute-start | bytes 3145736 | tf_op jit(solution)/shard_map/ppermute | solution.py:117
  38.6 1.1 fusion.34
  39.8 1.7 %fusion.35 = (f32[2,4,8,8,1,2,255]{6,3,5,4,2,1,0:T(8,128)}, f32[2,4,8,8,1,2,255]{6,3,5,4,2,1,0:T(8,128)}) fusion(f32[2,4,8,8,1,2,256]{6,3,5,4,2,1,0:T(8,128)S(1)} %get-tuple-element.17), kind=kLoop, calls=%fused_computation.83 | loop fusion | bytes 4177920 | tf_op jit(solution)/shard_map/jit(_roll_static)/slice | solution.py:54
  41.5 36.0 %all-to-all-done = bf16[2,120,16,128]{3,1,0,2:T(8,128)(2,1)} async-done(((bf16[2,120,16,128]{3,1,0,2:T(8,128)(2,1)}), bf16[2,120,16,128]{3,1,0,2:T(8,128)(2,1)}, u32[]{:S(2)}, u32[]{:S(2)}) %all-to-all-start) | async-done | bytes 983072 | tf_op jit(solution)/shard_map/all_to_all | solution.py:141
  77.5 1.4 %convert_reduce_fusion = f32[2,120,4,128]{3,1,0,2:T(8,128)S(1)} fusion(bf16[2,120,16,128]{3,1,0,2:T(8,128)(2,1)} %all-to-all-done), kind=kLoop, calls=%fused_computation.5 | loop fusion | flops 860160 | bytes 1474560 | tf_op jit(solution)/shard_map/reduce_sum | solution.py:143
  80.1 1.2 copy.200
  81.5 0.9 copy.202
  82.4 7.8 %shard_map.64 = f32[30,1024]{1,0:T(8,128)} custom-call(bf16[30,128,512]{2,1,0:T(8,128)(2,1)} %pad_maximum_fusion.k_ref, bf16[512,1024]{1,0:T(8,128)(2,1)} %bitcast.71, f32[128,1024]{1,0:T(8,128)} %bitcast.73), custom_call_target="tpu_custom_call" | custom-call | tf_op jit(solution)/shard_map/pallas_call | solution.py:76
  90.2 0.9 convert_element_type.87
  91.2 0.8 broadcast_in_dim.68
  92.0 18.1 %all-to-all-start.1 = ((bf16[30,16,2,128]{3,2,0,1:T(2,128)(2,1)}), bf16[30,16,2,128]{3,2,0,1:T(2,128)(2,1)S(1)}, u32[]{:S(2)}, u32[]{:S(2)}) async-start(bf16[30,16,2,128]{3,2,0,1:T(2,128)(2,1)} %bitcast.77), calls=%async_computation.1 | async-start | bytes 491520 | tf_op jit(solution)/shard_map/all_to_all | solution.py:163
  110.3 4.6 %fusion.7 = f32[2,4,8,8,1,2,256]{6,3,5,4,2,1,0:T(8,128)S(1)} fusion(f32[2,4,8,8,1,2,256]{6,3,5,4,2,1,0:T(8,128)S(1)} %bitcast.66, f32[2,4,8,8,1,2,1]{6,3,5,4,2,1,0:T(8,128)} %get-tuple-element.30, f32[2,4,8,8,1,2,255]{6,3,5,4,2,1,0:T(8,128)} %get-tuple-element.32, f32[2,4,8,8,1,2,255]{6,3,5,4,2,1,0:T(8,128)} %get-tuple-element.31, ...), kind=kLoop, calls=%fused_computation.19 | loop fusion | flops 6815744 | bytes 10485768 | tf_op jit(solution)/shard_map/sub | solution.py:126
  114.9 5.1 %all-to-all-done.1 = bf16[30,16,2,128]{3,2,0,1:T(2,128)(2,1)S(1)} async-done(((bf16[30,16,2,128]{3,2,0,1:T(2,128)(2,1)}), bf16[30,16,2,128]{3,2,0,1:T(2,128)(2,1)S(1)}, u32[]{:S(2)}, u32[]{:S(2)}) %all-to-all-start.1) | async-done | bytes 245792 | tf_op jit(solution)/shard_map/all_to_all | solution.py:163
  120.6 2.7 %gather_fusion.1 = f32[256,2,512]{2,1,0:T(2,128)} fusion(f32[120,2,512]{2,1,0:T(2,128)S(1)} %reshape.465, s32[1024]{0:T(1024)S(1)} %pad_clamp_fusion), kind=kCustom, calls=%fused_computation.1 | custom fusion | bytes 2098176 | tf_op jit(solution)/shard_map/jit(_take)/gather | solution.py:173
  123.3 4.0 %fusion.22 = f32[2,256,1,512]{3,0,1,2:T(2,128)S(1)} fusion(f32[2,256,512]{2,1,0:T(8,128)S(1)} %bitcast.69, f32[256,2,512]{2,1,0:T(2,128)} %gather_fusion.1, pred[256]{0:T(512)(128)(4,1)S(1)} %compare_and_fusion.2, pred[256]{0:T(512)(128)(4,1)S(1)} %gt.18, f32[2]{0:T(128)S(1)} %neg.4, f32[2,256,1,512]{3,2,1,0:T(1,128)S(1)} %copy-done), kind=kLoop, calls=%fused_computation.41 | loop fusion | flops 1310720 | bytes 4194824 | tf_op jit(solution)/shard_map/add | solution.py:181
  127.3 2.0 %copy.180 = f32[2,256,1,512]{3,2,1,0:T(1,128)} copy(f32[2,256,1,512]{3,0,1,2:T(2,128)S(1)} %fusion.22) | data formatting | bytes 2097152 | tf_op jit(solution)/shard_map/add | solution.py:181
  (48 shorter events, 3.0 us)
Async XLA Ops:
  0.0 11.5 %copy-start.3 = (s32[120]{0:T(128)S(1)}, s32[120]{0:T(128)}, u32[]{:S(2)}) copy-start(s32[120]{0:T(128)} %param.9) | copy-start | bytes 1444
  4.6 26.8 %collective-permute-start.1 = (f32[2,1,8,8,1,2,256]{6,3,5,4,2,1,0:T(8,128)}, f32[2,1,8,8,1,2,256]{6,3,5,4,2,1,0:T(8,128)S(1)}, u32[]{:S(2)}, u32[]{:S(2)}) collective-permute-start(f32[2,1,8,8,1,2,256]{6,3,5,4,2,1,0:T(8,128)} %get-tuple-element.20), channel_id=1, source_target_pairs={{0,16},{16,32},{32,48},{1,17},{17,33},{33,49},{2,18},{18,34},{34,5... | collective-permute-start | bytes 786440 | tf_op jit(solution)/shard_map/ppermute | solution.py:107
  8.1 23.3 %collective-permute-start = (f32[2,1,8,8,1,2,256]{6,3,5,4,2,1,0:T(8,128)}, f32[2,1,8,8,1,2,256]{6,3,5,4,2,1,0:T(8,128)}, u32[]{:S(2)}, u32[]{:S(2)}) collective-permute-start(f32[2,1,8,8,1,2,256]{6,3,5,4,2,1,0:T(8,128)} %get-tuple-element.19), channel_id=1, source_target_pairs={{16,0},{32,16},{48,32},{17,1},{33,17},{49,33},{18,2},{34,18},{50,3... | collective-permute-start | bytes 786440 | tf_op jit(solution)/shard_map/ppermute | solution.py:110
  11.4 12.3 %copy-start.4 = (f32[2]{0:T(128)S(1)}, f32[2]{0:T(128)}, u32[]{:S(2)}) copy-start(f32[2]{0:T(128)} %param.10) | copy-start | bytes 28
  14.2 12.4 %copy-start.2 = (s32[8,8]{1,0:T(8,128)S(1)}, s32[8,8]{1,0:T(8,128)}, u32[]{:S(2)}) copy-start(s32[8,8]{1,0:T(8,128)} %param.8) | copy-start | bytes 772
  14.2 12.7 %copy-start.5 = (f32[2]{0:T(128)S(1)}, f32[2]{0:T(128)}, u32[]{:S(2)}) copy-start(f32[2]{0:T(128)} %param.11) | copy-start | bytes 28
  14.2 63.3 %all-to-all-start = ((bf16[2,120,16,128]{3,1,0,2:T(8,128)(2,1)}), bf16[2,120,16,128]{3,1,0,2:T(8,128)(2,1)}, u32[]{:S(2)}, u32[]{:S(2)}) async-start(bf16[2,120,16,128]{3,1,0,2:T(8,128)(2,1)} %bitcast.5), calls=%async_computation | async-start | bytes 1966080 | tf_op jit(solution)/shard_map/all_to_all | solution.py:141
  26.9 1.4 %copy-start.1 = (bf16[30,128,128]{2,1,0:T(8,128)(2,1)S(1)}, bf16[30,128,128]{2,1,0:T(8,128)(2,1)}, u32[]{:S(2)}) copy-start(bf16[30,128,128]{2,1,0:T(8,128)(2,1)} %get-tuple-element.12) | copy-start | bytes 2949124
  34.3 75.9 %collective-permute-start.2 = (f32[2,4,8,8,1,2,256]{6,3,5,4,2,1,0:T(8,128)}, f32[2,4,8,8,1,2,256]{6,3,5,4,2,1,0:T(8,128)}, u32[]{:S(2)}, u32[]{:S(2)}) collective-permute-start(f32[2,4,8,8,1,2,256]{6,3,5,4,2,1,0:T(8,128)} %get-tuple-element.14), channel_id=1, source_target_pairs={{1,0},{2,1},{3,2},{4,3},{5,4},{6,5},{7,6},{8,7},{9,8},{10,9},{11,1... | collective-permute-start | bytes 3145736 | tf_op jit(solution)/shard_map/ppermute | solution.py:114
  36.2 74.0 %collective-permute-start.3 = (f32[2,4,8,8,1,2,256]{6,3,5,4,2,1,0:T(8,128)}, f32[2,4,8,8,1,2,256]{6,3,5,4,2,1,0:T(8,128)}, u32[]{:S(2)}, u32[]{:S(2)}) collective-permute-start(f32[2,4,8,8,1,2,256]{6,3,5,4,2,1,0:T(8,128)} %get-tuple-element.13), channel_id=1, source_target_pairs={{0,1},{1,2},{2,3},{3,4},{4,5},{5,6},{6,7},{7,8},{8,9},{9,10},{10,1... | collective-permute-start | bytes 3145736 | tf_op jit(solution)/shard_map/ppermute | solution.py:117
  92.0 28.0 %all-to-all-start.1 = ((bf16[30,16,2,128]{3,2,0,1:T(2,128)(2,1)}), bf16[30,16,2,128]{3,2,0,1:T(2,128)(2,1)S(1)}, u32[]{:S(2)}, u32[]{:S(2)}) async-start(bf16[30,16,2,128]{3,2,0,1:T(2,128)(2,1)} %bitcast.77), calls=%async_computation.1 | async-start | bytes 491520 | tf_op jit(solution)/shard_map/all_to_all | solution.py:163
  114.9 8.4 %copy-start = (f32[2,256,1,512]{3,2,1,0:T(1,128)S(1)}, f32[2,256,1,512]{3,2,1,0:T(1,128)}, u32[]{:S(2)}) copy-start(f32[2,256,1,512]{3,2,1,0:T(1,128)} %param.6) | copy-start | bytes 3145732

commit v7 on v4

--- a/solution.py
+++ b/solution.py
@@ -144,15 +144,12 @@
 
     chooser = jnp.stack([(pair_kind == k).astype(jnp.float32) for k in range(NKIND)])
     partner = jnp.einsum("ksr,rlc->klsc", chooser, low_all, precision=lax.Precision.HIGHEST)
-    part_hi = partner.astype(jnp.bfloat16)
-    part_lo = (partner - part_hi.astype(jnp.float32)).astype(jnp.bfloat16)
-    rhs = jnp.stack([piece for k in range(NKIND) for piece in (part_hi[k], part_lo[k])])
-    rhs = jnp.pad(rhs, ((0, 0), (0, PAD - low_count), (0, 0), (0, 0)))
-    rhs = rhs.reshape(2 * NKIND * PAD, species_all * block_cells)
+    rhs = jnp.pad(partner.astype(jnp.bfloat16), ((0, 0), (0, PAD - low_count), (0, 0), (0, 0)))
+    rhs = rhs.reshape(NKIND * PAD, species_all * block_cells)
     lmat = jnp.pad(jnp.moveaxis(low_all, 1, 0), ((0, PAD - low_count), (0, 0), (0, 0)))
     lmat = lmat.reshape(PAD, species_all * block_cells)
     kpad = jnp.pad(kernel, ((0, 0), (0, 0), (0, PAD - low_count), (0, PAD - low_count)))
-    kcat = jnp.concatenate([kpad[k] for k in range(NKIND) for _ in range(2)], axis=-1)
+    kcat = jnp.concatenate([kpad[k] for k in range(NKIND)], axis=-1)
     gained = collide_call(kcat, rhs, lmat)
 
     gained = gained.reshape(out_rows, species_devs, 1, own_count, block_cells)

time: 108 us -> 110 us (1.019)
  local copies, waits for them, and re-layouts: 19.5 us -> 23.8 us
  waiting for transfers between devices: 20.1 us -> 23.1 us
  Pallas kernels: 7.8 us -> 5.03 us
  starting transfers between devices: 37.3 us -> 34.7 us
    pallas_call x1, Pallas kernels: 7.8 us -> 5.03 us  [collide_call(): pl.pallas_call(collide_body, out_shape=jax.ShapeDtypeStruct((kcat.shape[0...]
    ppermute x3, starting transfers between devices: 9.8 us -> 7.63 us  [shift_permutes(): received.append((shift, lax.ppermute(values, axis, pairs)))]
    reshape x2, local copies, waits for them, and re-layouts: 0.49 us -> 2.32 us  [per_device(): jnp.transpose(gathered, (2, 0, 3, 1, 4))]
    all_to_all x1, waiting for transfers between devices: 12.8 us -> 14.5 us  [per_device(): lax.all_to_all(gained.astype(jnp.bfloat16), ('species', 'mode'), 1, 1, ti...]
    squeeze x1, local copies, waits for them, and re-layouts: 0.53 us -> 2.01 us  [per_device(): kcat = jnp.concatenate([kpad[k] for k in range(NKIND)], axis=-1)]
    ppermute x3, waiting for transfers between devices: 7.35 us -> 8.67 us  [shift_permutes(): received.append((shift, lax.ppermute(values, axis, pairs)))]
    all_to_all x1, starting transfers between devices: 8.5 us -> 7.2 us  [per_device(): lax.all_to_all(gained.astype(jnp.bfloat16), ('species', 'mode'), 1, 1, ti...]
    slice x1, local copies, waits for them, and re-layouts: 1.08 us -> 2.35 us  [periodic_term(): jnp.roll(flux_dir, -1, axis_cell)]
  transfers between devices with their start and end apart: 9 -> 9, of which waited for: 3 -> 3; matrix products, arithmetic and copies ran while one was open for 25% -> 27% of each run, Pallas kernels for 7% -> 5%
where the time goes in v7:
time: 110 us; the launch traced here: 108 us
  starting transfers between devices  34.7 us (32%)
  local copies, waits for them, and re-layouts  23.8 us (22%)
  waiting for transfers between devices  23.1 us (21%)
  other arithmetic  20.6 us (19%)
  Pallas kernels  5.03 us (5%)
    all_to_all x1, waiting for transfers between devices, per_device(): lax.all_to_all(gained.astype(jnp.bfloat16), ('species', 'mode'), 1, 1, ti...  14.5 us
    ppermute x3, waiting for transfers between devices, shift_permutes(): received.append((shift, lax.ppermute(values, axis, pairs)))  8.67 us
    ppermute x3, starting transfers between devices, shift_permutes(): received.append((shift, lax.ppermute(values, axis, pairs)))  7.63 us
    all_to_all x1, starting transfers between devices, per_device(): lax.all_to_all(gained.astype(jnp.bfloat16), ('species', 'mode'), 1, 1, ti...  7.2 us
    all_to_all x1, starting transfers between devices, per_device(): spread = lax.all_to_all(picked, 'species', 2, 0, tiled=True)  5.89 us
    ppermute x1, starting transfers between devices, per_device(): lax.ppermute(up_part[:, :, :, :, :1], 'space', [(i + 1, i) for i in range...  5.45 us
    ppermute x1, starting transfers between devices, per_device(): lax.ppermute(phase_field[:, per_vx - 1:], 'mode', [(i, i + 1) for i in ra...  5.28 us
    sub x1, other arithmetic, per_device(): phase_field - nu_step * thermal_speed.reshape(own_count, 1, 1, 1, 1, 1, 1...  5.08 us
  transfers between devices with their start and end apart: 9, of which 3 were waited for; matrix products, arithmetic and copies ran while one was open for 27% of the time, Pallas kernels for 5%

profile of v7, /device:TPU:2, one launch (start us, length us, event | category | flops | bytes accessed | tf_op | source)
XLA Modules:
  0.0 107.8 jit_solution(4041448592551961953)
XLA Ops:
  0.0 3.8 %reduce.18 = f32[2,256,512]{2,1,0:T(8,128)S(1)} reduce(f32[2,256,1,512]{3,2,1,0:T(1,128)} %param.6, f32[]{:T(128)} %constant.93), dimensions={2}, to_apply=%param.6.reduce_sub_computation | reduce | bytes 2097156 | tf_op args[0]
  4.6 1.3 %collective-permute-start = (f32[2,1,8,8,1,2,256]{6,3,5,4,2,1,0:T(8,128)}, f32[2,1,8,8,1,2,256]{6,3,5,4,2,1,0:T(8,128)S(1)}, u32[]{:S(2)}, u32[]{:S(2)}) collective-permute-start(f32[2,1,8,8,1,2,256]{6,3,5,4,2,1,0:T(8,128)} %get-tuple-element.17), channel_id=1, source_target_pairs={{16,0},{32,16},{48,32},{17,1},{33,17},{49,33},{18,2},{34,18},{50,3... | collective-permute-start | bytes 786440 | tf_op jit(solution)/shard_map/ppermute | solution.py:110
  5.9 5.3 %collective-permute-start.1 = (f32[2,1,8,8,1,2,256]{6,3,5,4,2,1,0:T(8,128)}, f32[2,1,8,8,1,2,256]{6,3,5,4,2,1,0:T(8,128)}, u32[]{:S(2)}, u32[]{:S(2)}) collective-permute-start(f32[2,1,8,8,1,2,256]{6,3,5,4,2,1,0:T(8,128)} %get-tuple-element.18), channel_id=1, source_target_pairs={{0,16},{16,32},{32,48},{1,17},{17,33},{33,49},{2,18},{18,34},{34,5... | collective-permute-start | bytes 786440 | tf_op jit(solution)/shard_map/ppermute | solution.py:107
  12.1 1.1 %gather_fusion = bf16[120,2,512]{2,1,0:T(2,128)(2,1)S(1)} fusion(bf16[2,256,512]{2,0,1:T(2,128)(2,1)S(1)} %bitcast.78, s32[1024]{0:T(1024)S(1)} %pad_clamp_fusion.1), kind=kCustom, calls=%fused_computation | custom fusion | bytes 492000 | tf_op jit(solution)/shard_map/jit(_take)/gather | solution.py:134
  13.2 1.4 %fusion.27 = bf16[2,120,4,128]{3,0,1,2:T(2,128)(2,1)} fusion(pred[120]{0:T(512)(128)(4,1)S(1)} %get-tuple-element.7, pred[120]{0:T(512)(128)(4,1)S(1)} %get-tuple-element.33, bf16[120,2,512]{2,1,0:T(2,128)(2,1)S(1)} %gather_fusion), kind=kLoop, calls=%fused_computation.51 | loop fusion | flops 245760 | bytes 491760 | tf_op jit(solution)/shard_map/convert_element_type | solution.py:134
  14.5 5.9 %all-to-all-start = ((bf16[2,120,4,128]{3,0,1,2:T(2,128)(2,1)}), bf16[2,120,4,128]{3,0,1,2:T(2,128)(2,1)S(1)}, u32[]{:S(2)}, u32[]{:S(2)}) async-start(bf16[2,120,4,128]{3,0,1,2:T(2,128)(2,1)} %fusion.27), calls=%async_computation | async-start | bytes 491520 | tf_op jit(solution)/shard_map/all_to_all | solution.py:138
  20.4 1.7 %fusion.36 = (f32[2,4,8,8,1,2,255]{6,3,5,4,2,1,0:T(8,128)}, f32[2,4,8,8,1,2,255]{6,3,5,4,2,1,0:T(8,128)}) fusion(f32[2,4,8,8,1,2,256]{6,3,5,4,2,1,0:T(8,128)S(1)} %bitcast.68), kind=kLoop, calls=%fused_computation.82 | loop fusion | bytes 4177920 | tf_op jit(solution)/shard_map/jit(_roll_static)/slice | solution.py:52
  22.1 1.1 %fusion.33 = (f32[2,4,8,8,1,1,256]{6,3,5,4,2,1,0:T(8,128)}, f32[2,4,8,8,1,1,256]{6,3,5,4,2,1,0:T(8,128)}) fusion(f32[2,4,8,8,1,2,256]{6,3,5,4,2,1,0:T(8,128)S(1)} %bitcast.69), kind=kLoop, calls=%fused_computation.79 | loop fusion | bytes 2097152 | tf_op jit(solution)/shard_map/jit(_roll_static)/slice | solution.py:51
  23.3 1.1 %fusion.35 = (f32[2,4,8,8,1,2,1]{6,3,5,4,2,1,0:T(8,128)}, f32[2,4,8,8,1,2,1]{6,3,5,4,2,1,0:T(8,128)}) fusion(f32[2,4,8,8,1,2,256]{6,3,5,4,2,1,0:T(8,128)S(1)} %bitcast.70), kind=kLoop, calls=%fused_computation.81 | loop fusion | bytes 16384 | tf_op jit(solution)/shard_map/jit(_roll_static)/slice | solution.py:52
  25.1 2.0 %fusion.24 = (bf16[30,128,128]{2,1,0:T(8,128)(2,1)S(1)}, bf16[30,128,128]{2,1,0:T(8,128)(2,1)S(1)}) fusion(bf16[2,30,120,120]{3,2,1,0:T(8,128)(2,1)} %param.7), kind=kLoop, calls=%fused_computation.44 | loop fusion | bytes 3694080 | tf_op jit(solution)/shard_map/squeeze | solution.py:152
  27.3 1.5 %pad_maximum_fusion.k_ref = bf16[30,128,256]{2,1,0:T(8,128)(2,1)} fusion(bf16[30,128,128]{2,1,0:T(8,128)(2,1)S(1)} %get-tuple-element.10, bf16[30,128,128]{2,1,0:T(8,128)(2,1)S(1)} %get-tuple-element.9), kind=kLoop, calls=%fused_computation.4 | loop fusion | flops 3932160 | bytes 3932160 | tf_op jit(solution)/shard_map/concatenate | solution.py:152
  29.7 3.2 %multiply_subtract_fusion = (f32[2,4,8,8,1,2,256]{6,3,5,4,2,1,0:T(8,128)}, f32[2,4,8,8,1,2,256]{6,3,5,4,2,1,0:T(8,128)}, f32[2,4,8,8,1,2,256]{6,3,5,4,2,1,0:T(8,128)S(1)}, f32[2,4,8,8,1,2,256]{6,3,5,4,2,1,0:T(8,128)}) fusion(f32[2,4,8,8,1,2,256]{6,3,5,4,2,1,0:T(8,128)S(1)} %bitcast.71, f32[2,1,8,8,1,2,256]{6,3,5,4,2,1,0:T(8,128)} %collective-permute-done.1, ...), kind=kLoop, calls=%fused_computation.42 | loop fusion | flops 4194304 | bytes 5770240 | tf_op jit(solution)/shard_map/sub | solution.py:113
  32.9 5.4 %collective-permute-start.2 = (f32[2,4,8,8,1,2,256]{6,3,5,4,2,1,0:T(8,128)}, f32[2,4,8,8,1,2,256]{6,3,5,4,2,1,0:T(8,128)}, u32[]{:S(2)}, u32[]{:S(2)}) collective-permute-start(f32[2,4,8,8,1,2,256]{6,3,5,4,2,1,0:T(8,128)} %get-tuple-element.12), channel_id=1, source_target_pairs={{1,0},{2,1},{3,2},{4,3},{5,4},{6,5},{7,6},{8,7},{9,8},{10,9},{11,1... | collective-permute-start | bytes 3145736 | tf_op jit(solution)/shard_map/ppermute | solution.py:114
  38.4 1.9 %collective-permute-start.3 = (f32[2,4,8,8,1,2,256]{6,3,5,4,2,1,0:T(8,128)}, f32[2,4,8,8,1,2,256]{6,3,5,4,2,1,0:T(8,128)}, u32[]{:S(2)}, u32[]{:S(2)}) collective-permute-start(f32[2,4,8,8,1,2,256]{6,3,5,4,2,1,0:T(8,128)} %get-tuple-element.11), channel_id=1, source_target_pairs={{0,1},{1,2},{2,3},{3,4},{4,5},{5,6},{6,7},{7,8},{8,9},{9,10},{10,1... | collective-permute-start | bytes 3145736 | tf_op jit(solution)/shard_map/ppermute | solution.py:117
  40.4 2.8 %collective-permute-start.4 = (bf16[8,120,1,128]{3,1,0,2:T(8,128)(2,1)S(1)}, bf16[8,120,1,128]{3,1,0,2:T(8,128)(2,1)S(1)}, u32[]{:S(2)}, u32[]{:S(2)}) collective-permute-start(bf16[8,120,1,128]{3,1,0,2:T(8,128)(2,1)S(1)} %bitcast.79), channel_id=1, source_target_pairs={{0,16},{16,32},{1,17},{17,33},{2,18},{18,34},{3,19},{19,35},{4,20}... | collective-permute-start | bytes 737288 | tf_op jit(solution)/shard_map/ppermute | solution.py:90
  43.2 2.9 %collective-permute-start.5 = (bf16[8,120,1,128]{3,1,0,2:T(8,128)(2,1)S(1)}, bf16[8,120,1,128]{3,1,0,2:T(8,128)(2,1)S(1)}, u32[]{:S(2)}, u32[]{:S(2)}) collective-permute-start(bf16[8,120,1,128]{3,1,0,2:T(8,128)(2,1)S(1)} %bitcast.80), channel_id=1, source_target_pairs={{0,32},{16,48},{1,33},{17,49},{2,34},{18,50},{3,35},{19,51},{4,36}... | collective-permute-start | bytes 737288 | tf_op jit(solution)/shard_map/ppermute | solution.py:90
  46.1 1.9 %collective-permute-start.6 = (bf16[8,120,1,128]{3,1,0,2:T(8,128)(2,1)S(1)}, bf16[8,120,1,128]{3,1,0,2:T(8,128)(2,1)S(1)}, u32[]{:S(2)}, u32[]{:S(2)}) collective-permute-start(bf16[8,120,1,128]{3,1,0,2:T(8,128)(2,1)S(1)} %bitcast.81), channel_id=1, source_target_pairs={{0,48},{16,0},{1,49},{17,1},{2,50},{18,2},{3,51},{19,3},{4,52},{20... | collective-permute-start | bytes 737288 | tf_op jit(solution)/shard_map/ppermute | solution.py:90
  48.0 1.1 %fusion.37 = (f32[2,4,8,8,1,2,1]{6,3,5,4,2,1,0:T(8,128)}, f32[2,4,8,8,1,2,1]{6,3,5,4,2,1,0:T(8,128)}) fusion(f32[2,4,8,8,1,2,256]{6,3,5,4,2,1,0:T(8,128)S(1)} %get-tuple-element.15), kind=kLoop, calls=%fused_computation.83 | loop fusion | bytes 16384 | tf_op jit(solution)/shard_map/jit(_roll_static)/slice | solution.py:54
  49.2 5.3 %collective-permute-done.5 = bf16[8,120,1,128]{3,1,0,2:T(8,128)(2,1)S(1)} collective-permute-done((bf16[8,120,1,128]{3,1,0,2:T(8,128)(2,1)S(1)}, bf16[8,120,1,128]{3,1,0,2:T(8,128)(2,1)S(1)}, u32[]{:S(2)}, u32[]{:S(2)}) %collective-permute-start.5) | collective-permute-done | bytes 245792 | tf_op jit(solution)/shard_map/ppermute | solution.py:90
  54.5 3.3 %collective-permute-done.6 = bf16[8,120,1,128]{3,1,0,2:T(8,128)(2,1)S(1)} collective-permute-done((bf16[8,120,1,128]{3,1,0,2:T(8,128)(2,1)S(1)}, bf16[8,120,1,128]{3,1,0,2:T(8,128)(2,1)S(1)}, u32[]{:S(2)}, u32[]{:S(2)}) %collective-permute-start.6) | collective-permute-done | bytes 245792 | tf_op jit(solution)/shard_map/ppermute | solution.py:90
  58.3 0.9 copy.205
  60.1 5.0 %shard_map.64 = f32[30,1024]{1,0:T(8,128)} custom-call(bf16[30,128,256]{2,1,0:T(8,128)(2,1)} %pad_maximum_fusion.k_ref, bf16[256,1024]{1,0:T(8,128)(2,1)} %bitcast.77, f32[128,1024]{1,0:T(8,128)} %copy_bitcast_fusion.2.l_ref), custom_call_target="tpu_custom_call" | custom-call | tf_op jit(solution)/shard_map/pallas_call | solution.py:76
  66.9 7.2 %all-to-all-start.1 = ((bf16[30,16,2,128]{3,2,0,1:T(2,128)(2,1)}), bf16[30,16,2,128]{3,2,0,1:T(2,128)(2,1)S(1)}, u32[]{:S(2)}, u32[]{:S(2)}) async-start(bf16[30,16,2,128]{3,2,0,1:T(2,128)(2,1)} %bitcast.83), calls=%async_computation.1 | async-start | bytes 491520 | tf_op jit(solution)/shard_map/all_to_all | solution.py:159
  74.1 2.3 %fusion.34 = (f32[2,4,8,8,1,1,256]{6,3,5,4,2,1,0:T(8,128)}, f32[2,4,8,8,1,1,256]{6,3,5,4,2,1,0:T(8,128)}) fusion(f32[2,4,8,8,1,2,256]{6,3,5,4,2,1,0:T(8,128)} %get-tuple-element.16), kind=kLoop, calls=%fused_computation.80 | loop fusion | bytes 2097152 | tf_op jit(solution)/shard_map/jit(_roll_static)/slice | solution.py:53
  76.5 1.7 %fusion.38 = (f32[2,4,8,8,1,2,255]{6,3,5,4,2,1,0:T(8,128)}, f32[2,4,8,8,1,2,255]{6,3,5,4,2,1,0:T(8,128)}) fusion(f32[2,4,8,8,1,2,256]{6,3,5,4,2,1,0:T(8,128)S(1)} %get-tuple-element.15), kind=kLoop, calls=%fused_computation.84 | loop fusion | bytes 4177920 | tf_op jit(solution)/shard_map/jit(_roll_static)/slice | solution.py:54
  78.2 14.5 %all-to-all-done.1 = bf16[30,16,2,128]{3,2,0,1:T(2,128)(2,1)S(1)} async-done(((bf16[30,16,2,128]{3,2,0,1:T(2,128)(2,1)}), bf16[30,16,2,128]{3,2,0,1:T(2,128)(2,1)S(1)}, u32[]{:S(2)}, u32[]{:S(2)}) %all-to-all-start.1) | async-done | bytes 245792 | tf_op jit(solution)/shard_map/all_to_all | solution.py:159
  92.7 0.9 copy.189
  93.7 1.4 %reshape.456 = f32[120,2,512]{2,1,0:T(2,128)S(1)} reshape(f32[4,30,2,4,128]{4,3,2,1,0:T(4,128)} %copy.189) | data formatting | bytes 983040 | tf_op jit(solution)/shard_map/reshape | solution.py:162
  95.1 2.7 %gather_fusion.1 = f32[256,2,512]{2,1,0:T(2,128)} fusion(f32[120,2,512]{2,1,0:T(2,128)S(1)} %reshape.456, s32[1024]{0:T(1024)S(1)} %pad_clamp_fusion), kind=kCustom, calls=%fused_computation.1 | custom fusion | bytes 2098176 | tf_op jit(solution)/shard_map/jit(_take)/gather | solution.py:169
  97.8 5.1 %fusion.8 = f32[2,4,8,8,1,2,256]{6,3,5,4,2,1,0:T(8,128)S(1)} fusion(f32[2,4,8,8,1,2,256]{6,3,5,4,2,1,0:T(8,128)S(1)} %bitcast.72, f32[2,4,8,8,1,2,1]{6,3,5,4,2,1,0:T(8,128)} %get-tuple-element.28, f32[2,4,8,8,1,2,255]{6,3,5,4,2,1,0:T(8,128)} %get-tuple-element.30, f32[2,4,8,8,1,2,255]{6,3,5,4,2,1,0:T(8,128)} %get-tuple-element.29, ...), kind=kLoop, calls=%fused_computation.19 | loop fusion | flops 6815744 | bytes 10485768 | tf_op jit(solution)/shard_map/sub | solution.py:126
  102.9 2.8 %fusion.23 = f32[2,256,1,512]{3,0,1,2:T(2,128)S(1)} fusion(f32[2,256,512]{2,1,0:T(8,128)S(1)} %bitcast.73, f32[256,2,512]{2,1,0:T(2,128)S(1)} %copy-done.1, pred[256]{0:T(512)(128)(4,1)S(1)} %compare_and_fusion.2, pred[256]{0:T(512)(128)(4,1)S(1)} %gt.18, f32[2]{0:T(128)S(1)} %neg.4, f32[2,256,1,512]{3,2,1,0:T(1,128)S(1)} %copy-done), kind=kLoop, calls=%fused_computation.40 | loop fusion | flops 1310720 | bytes 4194824 | tf_op jit(solution)/shard_map/add | solution.py:177
  105.7 2.0 %copy.185 = f32[2,256,1,512]{3,2,1,0:T(1,128)} copy(f32[2,256,1,512]{3,0,1,2:T(2,128)S(1)} %fusion.23) | data formatting | bytes 2097152 | tf_op jit(solution)/shard_map/add | solution.py:177
  (52 shorter events, 6.5 us)
Async XLA Ops:
  0.0 11.2 %copy-start = (f32[2,256,1,512]{3,2,1,0:T(1,128)S(1)}, f32[2,256,1,512]{3,2,1,0:T(1,128)}, u32[]{:S(2)}) copy-start(f32[2,256,1,512]{3,2,1,0:T(1,128)} %param.6) | copy-start | bytes 3145732
  0.0 12.0 %copy-start.5 = (s32[120]{0:T(128)S(1)}, s32[120]{0:T(128)}, u32[]{:S(2)}) copy-start(s32[120]{0:T(128)} %param.9) | copy-start | bytes 1444
  4.6 24.3 %collective-permute-start = (f32[2,1,8,8,1,2,256]{6,3,5,4,2,1,0:T(8,128)}, f32[2,1,8,8,1,2,256]{6,3,5,4,2,1,0:T(8,128)S(1)}, u32[]{:S(2)}, u32[]{:S(2)}) collective-permute-start(f32[2,1,8,8,1,2,256]{6,3,5,4,2,1,0:T(8,128)} %get-tuple-element.17), channel_id=1, source_target_pairs={{16,0},{32,16},{48,32},{17,1},{33,17},{49,33},{18,2},{34,18},{50,3... | collective-permute-start | bytes 786440 | tf_op jit(solution)/shard_map/ppermute | solution.py:110
  5.9 23.1 %collective-permute-start.1 = (f32[2,1,8,8,1,2,256]{6,3,5,4,2,1,0:T(8,128)}, f32[2,1,8,8,1,2,256]{6,3,5,4,2,1,0:T(8,128)}, u32[]{:S(2)}, u32[]{:S(2)}) collective-permute-start(f32[2,1,8,8,1,2,256]{6,3,5,4,2,1,0:T(8,128)} %get-tuple-element.18), channel_id=1, source_target_pairs={{0,16},{16,32},{32,48},{1,17},{17,33},{33,49},{2,18},{18,34},{34,5... | collective-permute-start | bytes 786440 | tf_op jit(solution)/shard_map/ppermute | solution.py:107
  14.5 25.8 %all-to-all-start = ((bf16[2,120,4,128]{3,0,1,2:T(2,128)(2,1)}), bf16[2,120,4,128]{3,0,1,2:T(2,128)(2,1)S(1)}, u32[]{:S(2)}, u32[]{:S(2)}) async-start(bf16[2,120,4,128]{3,0,1,2:T(2,128)(2,1)} %fusion.27), calls=%async_computation | async-start | bytes 491520 | tf_op jit(solution)/shard_map/all_to_all | solution.py:138
  22.1 2.9 %copy-start.6 = (f32[2]{0:T(128)S(1)}, f32[2]{0:T(128)}, u32[]{:S(2)}) copy-start(f32[2]{0:T(128)} %param.10) | copy-start | bytes 28
  22.1 3.0 %copy-start.4 = (s32[8,8]{1,0:T(8,128)S(1)}, s32[8,8]{1,0:T(8,128)}, u32[]{:S(2)}) copy-start(s32[8,8]{1,0:T(8,128)} %param.8) | copy-start | bytes 772
  27.3 1.7 %copy-start.7 = (f32[2]{0:T(128)S(1)}, f32[2]{0:T(128)}, u32[]{:S(2)}) copy-start(f32[2]{0:T(128)} %param.11) | copy-start | bytes 28
  29.0 0.7 copy-start.3
  32.9 64.8 %collective-permute-start.2 = (f32[2,4,8,8,1,2,256]{6,3,5,4,2,1,0:T(8,128)}, f32[2,4,8,8,1,2,256]{6,3,5,4,2,1,0:T(8,128)}, u32[]{:S(2)}, u32[]{:S(2)}) collective-permute-start(f32[2,4,8,8,1,2,256]{6,3,5,4,2,1,0:T(8,128)} %get-tuple-element.12), channel_id=1, source_target_pairs={{1,0},{2,1},{3,2},{4,3},{5,4},{6,5},{7,6},{8,7},{9,8},{10,9},{11,1... | collective-permute-start | bytes 3145736 | tf_op jit(solution)/shard_map/ppermute | solution.py:114
  38.4 59.4 %collective-permute-start.3 = (f32[2,4,8,8,1,2,256]{6,3,5,4,2,1,0:T(8,128)}, f32[2,4,8,8,1,2,256]{6,3,5,4,2,1,0:T(8,128)}, u32[]{:S(2)}, u32[]{:S(2)}) collective-permute-start(f32[2,4,8,8,1,2,256]{6,3,5,4,2,1,0:T(8,128)} %get-tuple-element.11), channel_id=1, source_target_pairs={{0,1},{1,2},{2,3},{3,4},{4,5},{5,6},{6,7},{7,8},{8,9},{9,10},{10,1... | collective-permute-start | bytes 3145736 | tf_op jit(solution)/shard_map/ppermute | solution.py:117
  40.4 8.8 %collective-permute-start.4 = (bf16[8,120,1,128]{3,1,0,2:T(8,128)(2,1)S(1)}, bf16[8,120,1,128]{3,1,0,2:T(8,128)(2,1)S(1)}, u32[]{:S(2)}, u32[]{:S(2)}) collective-permute-start(bf16[8,120,1,128]{3,1,0,2:T(8,128)(2,1)S(1)} %bitcast.79), channel_id=1, source_target_pairs={{0,16},{16,32},{1,17},{17,33},{2,18},{18,34},{3,19},{19,35},{4,20}... | collective-permute-start | bytes 737288 | tf_op jit(solution)/shard_map/ppermute | solution.py:90
  43.2 11.3 %collective-permute-start.5 = (bf16[8,120,1,128]{3,1,0,2:T(8,128)(2,1)S(1)}, bf16[8,120,1,128]{3,1,0,2:T(8,128)(2,1)S(1)}, u32[]{:S(2)}, u32[]{:S(2)}) collective-permute-start(bf16[8,120,1,128]{3,1,0,2:T(8,128)(2,1)S(1)} %bitcast.80), channel_id=1, source_target_pairs={{0,32},{16,48},{1,33},{17,49},{2,34},{18,50},{3,35},{19,51},{4,36}... | collective-permute-start | bytes 737288 | tf_op jit(solution)/shard_map/ppermute | solution.py:90
  46.1 11.7 %collective-permute-start.6 = (bf16[8,120,1,128]{3,1,0,2:T(8,128)(2,1)S(1)}, bf16[8,120,1,128]{3,1,0,2:T(8,128)(2,1)S(1)}, u32[]{:S(2)}, u32[]{:S(2)}) collective-permute-start(bf16[8,120,1,128]{3,1,0,2:T(8,128)(2,1)S(1)} %bitcast.81), channel_id=1, source_target_pairs={{0,48},{16,0},{1,49},{17,1},{2,50},{18,2},{3,51},{19,3},{4,52},{20... | collective-permute-start | bytes 737288 | tf_op jit(solution)/shard_map/ppermute | solution.py:90
  66.9 25.7 %all-to-all-start.1 = ((bf16[30,16,2,128]{3,2,0,1:T(2,128)(2,1)}), bf16[30,16,2,128]{3,2,0,1:T(2,128)(2,1)S(1)}, u32[]{:S(2)}, u32[]{:S(2)}) async-start(bf16[30,16,2,128]{3,2,0,1:T(2,128)(2,1)} %bitcast.83), calls=%async_computation.1 | async-start | bytes 491520 | tf_op jit(solution)/shard_map/all_to_all | solution.py:159
  92.7 5.0 %copy-start.2 = (f32[2,4,8,8,1,1,256]{6,3,5,4,2,1,0:T(8,128)S(1)}, f32[2,4,8,8,1,1,256]{6,3,5,4,2,1,0:T(8,128)}, u32[]{:S(2)}) copy-start(f32[2,4,8,8,1,1,256]{6,3,5,4,2,1,0:T(8,128)} %get-tuple-element.19) | copy-start | bytes 1572868
  97.8 5.1 %copy-start.1 = (f32[256,2,512]{2,1,0:T(2,128)S(1)}, f32[256,2,512]{2,1,0:T(2,128)}, u32[]{:S(2)}) copy-start(f32[256,2,512]{2,1,0:T(2,128)} %gather_fusion.1) | copy-start | bytes 3145732

commit v8 on v4

--- a/solution.py
+++ b/solution.py
@@ -2,6 +2,7 @@
 import jax.numpy as jnp
 from jax import lax
 from jax.experimental import pallas as pl
+from jax.experimental.pallas import tpu as pltpu
 from jax.sharding import PartitionSpec as P
 
 NVY = 8
@@ -78,6 +79,55 @@
         out_shape=jax.ShapeDtypeStruct((kcat.shape[0], rhs.shape[1]), jnp.float32),
         interpret=INTERPRET,
     )(kcat, rhs, lmat)
+
+
+def stream_body(speed_ref, phi_ref, next_ref, prev_ref, o_ref):
+    rows, cells = phi_ref.shape[1], phi_ref.shape[2]
+    row = lax.broadcasted_iota(jnp.int32, (rows, cells), 0)
+    lane = lax.broadcasted_iota(jnp.int32, (rows, cells), 1)
+    deg_b = ((row // NVZ) % NVY).astype(jnp.float32)
+    deg_c = (row % NVZ).astype(jnp.float32)
+    ypos = lane % NY
+
+    def y_up(v):
+        return jnp.where(ypos == NY - 1, pltpu.roll(v, NY - 1, 1), pltpu.roll(v, cells - 1, 1))
+
+    def y_down(v):
+        return jnp.where(ypos == 0, pltpu.roll(v, cells - NY + 1, 1), pltpu.roll(v, 1, 1))
+
+    def z_up(v):
+        return pltpu.roll(v, cells - NY, 1)
+
+    def z_down(v):
+        return pltpu.roll(v, NY, 1)
+
+    for s in range(phi_ref.shape[0]):
+        x = phi_ref[s]
+        flux_y = jnp.sqrt(deg_b + 1.0) * jnp.where(
+            deg_b < NVY - 1, pltpu.roll(x, rows - NVZ, 0), 0.0
+        ) + jnp.sqrt(deg_b) * jnp.where(deg_b > 0, pltpu.roll(x, NVZ, 0), 0.0)
+        flux_z = jnp.sqrt(deg_c + 1.0) * jnp.where(
+            deg_c < NVZ - 1, pltpu.roll(x, rows - 1, 0), 0.0
+        ) + jnp.sqrt(deg_c) * jnp.where(deg_c > 0, pltpu.roll(x, 1, 0), 0.0)
+        y_term = 0.5 * (y_up(flux_y) - y_down(flux_y)) - 0.5 * bound_y * (
+            y_up(x) - 2.0 * x + y_down(x)
+        )
+        z_term = 0.5 * (z_up(flux_z) - z_down(flux_z)) - 0.5 * bound_z * (
+            z_up(x) - 2.0 * x + z_down(x)
+        )
+        x_term = next_ref[s] + prev_ref[s] + bound_x * x
+        o_ref[s] = x - nu_step * speed_ref[s] * (x_term + y_term + z_term)
+
+
+def stream_call(speed, phi, from_next, from_prev):
+    vmem = pl.BlockSpec(memory_space=pltpu.VMEM)
+    return pl.pallas_call(
+        stream_body,
+        out_shape=jax.ShapeDtypeStruct(phi.shape, jnp.float32),
+        in_specs=[pl.BlockSpec(memory_space=pltpu.SMEM), vmem, vmem, vmem],
+        out_specs=vmem,
+        interpret=INTERPRET,
+    )(speed, phi, from_next, from_prev)
 
 
 def shift_permutes(values, axis, holders, count, toward):
@@ -103,31 +153,26 @@
     out_rows = kernel.shape[1]
     species_all = own_count * species_devs
 
-    phase_field = distribution.reshape(own_count, per_vx, NVY, NVZ, row_count, NZ, NY)
+    cell_count = row_count * plane_cells
+    flat_dist = distribution.reshape(own_count, mode_count, cell_count)
+    plane = NVY * NVZ
     below = lax.ppermute(
-        phase_field[:, per_vx - 1 :], "mode", [(i, i + 1) for i in range(mode_devs - 1)]
-    )
-    above = lax.ppermute(phase_field[:, :1], "mode", [(i + 1, i) for i in range(mode_devs - 1)])
-    flux_x = flux_from_padded(jnp.concatenate([below, phase_field, above], axis=1), 1, first_vx)
-    up_part = 0.5 * flux_x - 0.5 * bound_x * phase_field
-    down_part = -0.5 * flux_x - 0.5 * bound_x * phase_field
-    from_next = lax.ppermute(
-        up_part[:, :, :, :, :1], "space", [(i + 1, i) for i in range(space_devs - 1)]
-    )
-    from_prev = lax.ppermute(
-        down_part[:, :, :, :, row_count - 1 :], "space", [(i, i + 1) for i in range(space_devs - 1)]
-    )
-    up_all = jnp.concatenate([up_part[:, :, :, :, 1:], from_next], axis=4)
-    down_all = jnp.concatenate([from_prev, down_part[:, :, :, :, : row_count - 1]], axis=4)
-    x_term = up_all + down_all + bound_x * phase_field
-    y_term = periodic_term(phase_field, 2, 6, bound_y)
-    z_term = periodic_term(phase_field, 3, 5, bound_z)
-    stream = x_term + y_term + z_term
-    advected = phase_field - nu_step * thermal_speed.reshape(own_count, 1, 1, 1, 1, 1, 1) * stream
-
-    cell_count = row_count * plane_cells
+        flat_dist[:, mode_count - plane :], "mode", [(i, i + 1) for i in range(mode_devs - 1)]
+    )
+    above = lax.ppermute(flat_dist[:, :plane], "mode", [(i + 1, i) for i in range(mode_devs - 1)])
+    padded = jnp.concatenate([below, flat_dist, above], axis=1)
+    degree_a = (first_vx + jnp.arange(mode_count) // plane).astype(jnp.float32).reshape(1, -1, 1)
+    flux_x = (
+        jnp.sqrt(degree_a + 1.0) * padded[:, 2 * plane :]
+        + jnp.sqrt(degree_a) * padded[:, : mode_count]
+    )
+    up_part = 0.5 * flux_x - 0.5 * bound_x * flat_dist
+    down_part = -0.5 * flux_x - 0.5 * bound_x * flat_dist
+    from_next = lax.ppermute(up_part, "space", [(i + 1, i) for i in range(space_devs - 1)])
+    from_prev = lax.ppermute(down_part, "space", [(i, i + 1) for i in range(space_devs - 1)])
+    advected = stream_call(thermal_speed, flat_dist, from_next, from_prev)
+
     block_cells = cell_count // species_devs
-    flat_dist = distribution.reshape(own_count, mode_count, cell_count)
     local_index = low_map - mode_id * mode_count
     owned = (local_index >= 0) & (local_index < mode_count)
     clipped = jnp.clip(local_index, 0, mode_count - 1)

time: 108 us -> 109 us (level)
  waiting for transfers between devices: 20.1 us -> 38.5 us
  other arithmetic: 21.2 us -> 11.6 us
  local copies, waits for them, and re-layouts: 19.5 us -> 12.6 us
  starting transfers between devices: 37.3 us -> 31.5 us
  Pallas kernels: 7.8 us -> 12.8 us
    all_to_all x1, waiting for transfers between devices: 12.8 us -> 33.8 us  [per_device(): lax.all_to_all(gained.astype(jnp.bfloat16), ('species', 'mode'), 1, 1, ti...]
    slice x7 -> x1, local copies, waits for them, and re-layouts: 8.75 us -> 0.91 us  [per_device(): flat_dist[:, :plane]]
    ppermute x3, waiting for transfers between devices: 7.35 us -> 0.01 us  [shift_permutes(): received.append((shift, lax.ppermute(values, axis, pairs)))]
    sub x2 -> x1, other arithmetic: 8.27 us -> 2.73 us  [per_device(): down_part = -0.5 * flux_x - 0.5 * bound_x * flat_dist]
    pallas_call x0 -> x1, Pallas kernels: none -> 4.97 us  [stream_call(): pl.pallas_call(stream_body, out_shape=jax.ShapeDtypeStruct(phi.shape, jnp...]
    all_to_all x1, waiting for transfers between devices: 0.01 us -> 4.7 us  [per_device(): spread = lax.all_to_all(picked, 'species', 2, 0, tiled=True)]
    unnamed x1 -> x0, other arithmetic: 3.72 us -> none
    ppermute x4, starting transfers between devices: 13.1 us -> 9.98 us  [the longest x1 4.19 us: per_device(): lax.ppermute(flat_dist[:, mode_count - plane:], 'mode', [(i, i + 1) for i...]
  transfers between devices with their start and end apart: 9 -> 9, of which waited for: 3 -> 2; matrix products, arithmetic and copies ran while one was open for 25% -> 17% of each run, Pallas kernels for 7% -> 7%
where the time goes in v8:
time: 109 us; the launch traced here: 108 us
  waiting for transfers between devices  38.5 us (35%)
  starting transfers between devices  31.5 us (29%)
  Pallas kernels  12.8 us (12%)
  local copies, waits for them, and re-layouts  12.6 us (12%)
  other arithmetic  11.6 us (11%)
    all_to_all x1, waiting for transfers between devices, per_device(): lax.all_to_all(gained.astype(jnp.bfloat16), ('species', 'mode'), 1, 1, ti...  33.8 us
    ppermute x3, starting transfers between devices, shift_permutes(): received.append((shift, lax.ppermute(values, axis, pairs)))  9.78 us
    pallas_call x1, Pallas kernels, collide_call(): pl.pallas_call(collide_body, out_shape=jax.ShapeDtypeStruct((kcat.shape[0...  7.81 us
    all_to_all x1, starting transfers between devices, per_device(): spread = lax.all_to_all(picked, 'species', 2, 0, tiled=True)  5.89 us
    all_to_all x1, starting transfers between devices, per_device(): lax.all_to_all(gained.astype(jnp.bfloat16), ('species', 'mode'), 1, 1, ti...  5.86 us
    pallas_call x1, Pallas kernels, stream_call(): pl.pallas_call(stream_body, out_shape=jax.ShapeDtypeStruct(phi.shape, jnp...  4.97 us
    all_to_all x1, waiting for transfers between devices, per_device(): spread = lax.all_to_all(picked, 'species', 2, 0, tiled=True)  4.7 us
    ppermute x1, starting transfers between devices, per_device(): lax.ppermute(flat_dist[:, mode_count - plane:], 'mode', [(i, i + 1) for i...  4.19 us
  transfers between devices with their start and end apart: 9, of which 2 were waited for; matrix products, arithmetic and copies ran while one was open for 17% of the time, Pallas kernels for 7%

profile of v8, /device:TPU:2, one launch (start us, length us, event | category | flops | bytes accessed | tf_op | source)
XLA Modules:
  0.0 107.6 jit_solution(2927974573402029250)
XLA Ops:
  0.0 1.4 %copy.81 = f32[2,256,1,512]{3,1,2,0:T(8,128)S(1)} copy(f32[2,256,1,512]{3,2,1,0:T(1,128)} %param.6) | data formatting | bytes 2097152
  1.5 0.9 fusion.17
  2.4 4.2 %collective-permute-start.1 = (f32[2,64,512]{2,1,0:T(8,128)}, f32[2,64,512]{2,1,0:T(8,128)}, u32[]{:S(2)}, u32[]{:S(2)}) collective-permute-start(f32[2,64,512]{2,1,0:T(8,128)} %get-tuple-element.16), channel_id=1, source_target_pairs={{0,16},{16,32},{32,48},{1,17},{17,33},{33,49},{2,18},{18,34},{34,5... | collective-permute-start | bytes 786440 | tf_op jit(solution)/shard_map/ppermute | solution.py:159
  6.6 1.3 %collective-permute-start = (f32[2,64,512]{2,1,0:T(8,128)}, f32[2,64,512]{2,1,0:T(8,128)}, u32[]{:S(2)}, u32[]{:S(2)}) collective-permute-start(f32[2,64,512]{2,1,0:T(8,128)} %get-tuple-element.15), channel_id=1, source_target_pairs={{16,0},{32,16},{48,32},{17,1},{33,17},{49,33},{18,2},{34,18},{50,3... | collective-permute-start | bytes 786440 | tf_op jit(solution)/shard_map/ppermute | solution.py:162
  7.8 0.8 copy.45
  8.7 1.8 %gather_fusion = bf16[120,2,512]{2,1,0:T(2,128)(2,1)} fusion(bf16[2,256,512]{2,0,1:T(2,128)(2,1)S(1)} %copy.45, s32[1024]{0:T(1024)S(1)} %pad_clamp_fusion.1), kind=kCustom, calls=%fused_computation | custom fusion | bytes 492000 | tf_op jit(solution)/shard_map/jit(_take)/gather | solution.py:179
  10.5 2.3 %fusion.9 = bf16[2,120,4,128]{3,0,1,2:T(2,128)(2,1)} fusion(pred[120]{0:T(512)(128)(4,1)S(1)} %get-tuple-element.9, pred[120]{0:T(512)(128)(4,1)S(1)} %get-tuple-element.23, bf16[120,2,512]{2,1,0:T(2,128)(2,1)} %gather_fusion), kind=kLoop, calls=%fused_computation.28 | loop fusion | flops 245760 | bytes 491760 | tf_op jit(solution)/shard_map/convert_element_type | solution.py:179
  12.8 5.9 %all-to-all-start = ((bf16[2,120,4,128]{3,0,1,2:T(2,128)(2,1)}), bf16[2,120,4,128]{3,0,1,2:T(2,128)(2,1)S(1)}, u32[]{:S(2)}, u32[]{:S(2)}) async-start(bf16[2,120,4,128]{3,0,1,2:T(2,128)(2,1)} %fusion.9), calls=%async_computation | async-start | bytes 491520 | tf_op jit(solution)/shard_map/all_to_all | solution.py:183
  18.7 0.5 fusion.6
  19.4 2.0 %pad_maximum_fusion.k_ref = bf16[30,128,512]{2,1,0:T(8,128)(2,1)} fusion(bf16[30,128,128]{2,1,0:T(8,128)(2,1)S(1)} %get-tuple-element.12, bf16[30,128,128]{2,1,0:T(8,128)(2,1)S(1)} %get-tuple-element.11), kind=kLoop, calls=%fused_computation.2 | loop fusion | flops 15728640 | bytes 5898240 | tf_op jit(solution)/shard_map/concatenate | solution.py:200
  21.6 0.7 iota_reduce_fusion
  22.2 4.7 %all-to-all-done = bf16[2,120,4,128]{3,0,1,2:T(2,128)(2,1)S(1)} async-done(((bf16[2,120,4,128]{3,0,1,2:T(2,128)(2,1)}), bf16[2,120,4,128]{3,0,1,2:T(2,128)(2,1)S(1)}, u32[]{:S(2)}, u32[]{:S(2)}) %all-to-all-start) | async-done | bytes 245792 | tf_op jit(solution)/shard_map/all_to_all | solution.py:183
  27.0 5.7 %collective-permute-start.6 = (bf16[8,120,1,128]{3,1,0,2:T(8,128)(2,1)S(1)}, bf16[8,120,1,128]{3,1,0,2:T(8,128)(2,1)S(1)}, u32[]{:S(2)}, u32[]{:S(2)}) collective-permute-start(bf16[8,120,1,128]{3,1,0,2:T(8,128)(2,1)S(1)} %bitcast.75), channel_id=1, source_target_pairs={{0,48},{16,0},{1,49},{17,1},{2,50},{18,2},{3,51},{19,3},{4,52},{20... | collective-permute-start | bytes 737288 | tf_op jit(solution)/shard_map/ppermute | solution.py:140
  32.7 1.3 %collective-permute-start.5 = (bf16[8,120,1,128]{3,1,0,2:T(8,128)(2,1)S(1)}, bf16[8,120,1,128]{3,1,0,2:T(8,128)(2,1)S(1)}, u32[]{:S(2)}, u32[]{:S(2)}) collective-permute-start(bf16[8,120,1,128]{3,1,0,2:T(8,128)(2,1)S(1)} %bitcast.76), channel_id=1, source_target_pairs={{0,32},{16,48},{1,33},{17,49},{2,34},{18,50},{3,35},{19,51},{4,36}... | collective-permute-start | bytes 737288 | tf_op jit(solution)/shard_map/ppermute | solution.py:140
  34.0 2.8 %collective-permute-start.4 = (bf16[8,120,1,128]{3,1,0,2:T(8,128)(2,1)S(1)}, bf16[8,120,1,128]{3,1,0,2:T(8,128)(2,1)S(1)}, u32[]{:S(2)}, u32[]{:S(2)}) collective-permute-start(bf16[8,120,1,128]{3,1,0,2:T(8,128)(2,1)S(1)} %bitcast.77), channel_id=1, source_target_pairs={{0,16},{16,32},{1,17},{17,33},{2,18},{18,34},{3,19},{19,35},{4,20}... | collective-permute-start | bytes 737288 | tf_op jit(solution)/shard_map/ppermute | solution.py:140
  36.8 2.7 %multiply_subtract_fusion = (f32[2,256,512]{2,1,0:T(8,128)}, f32[2,256,512]{2,1,0:T(8,128)}) fusion(f32[2,256,512]{2,1,0:T(8,128)S(1)} %bitcast.69, f32[2,64,512]{2,1,0:T(8,128)} %collective-permute-done.1, f32[256]{0:T(256)S(1)} %get-tuple-element.25, f32[2,64,512]{2,1,0:T(8,128)} %collective-permute-done, f32[256]{0:T(256)S(1)} %get-tuple-element.24), kind=kLoop, calls=%fused_computation.18 | loop fusion | flops 2621440 | bytes 3672064 | tf_op jit(solution)/shard_map/sub | solution.py:170
  39.5 2.6 %collective-permute-start.2 = (f32[2,256,512]{2,1,0:T(8,128)}, f32[2,256,512]{2,1,0:T(8,128)}, u32[]{:S(2)}, u32[]{:S(2)}) collective-permute-start(f32[2,256,512]{2,1,0:T(8,128)} %get-tuple-element.14), channel_id=1, source_target_pairs={{1,0},{2,1},{3,2},{4,3},{5,4},{6,5},{7,6},{8,7},{9,8},{10,9},{11,1... | collective-permute-start | bytes 3145736 | tf_op jit(solution)/shard_map/ppermute | solution.py:171
  42.1 1.9 %collective-permute-start.3 = (f32[2,256,512]{2,1,0:T(8,128)}, f32[2,256,512]{2,1,0:T(8,128)}, u32[]{:S(2)}, u32[]{:S(2)}) collective-permute-start(f32[2,256,512]{2,1,0:T(8,128)} %get-tuple-element.13), channel_id=1, source_target_pairs={{0,1},{1,2},{2,3},{3,4},{4,5},{5,6},{6,7},{7,8},{8,9},{9,10},{10,1... | collective-permute-start | bytes 3145736 | tf_op jit(solution)/shard_map/ppermute | solution.py:172
  44.1 0.3 subtract_convert_fusion
  44.6 0.2 pad_maximum_fusion.3
  45.1 1.4 %copy.80 = bf16[64,8,8,128]{3,1,2,0:T(8,128)(2,1)} copy(bf16[64,8,8,128]{3,2,1,0:T(8,128)(2,1)S(1)} %bitcast.71) | data formatting | bytes 2097152
  46.4 0.8 copy_bitcast_fusion.2.l_ref
  47.3 7.8 %shard_map.65 = f32[30,1024]{1,0:T(8,128)} custom-call(bf16[30,128,512]{2,1,0:T(8,128)(2,1)} %pad_maximum_fusion.k_ref, bf16[512,1024]{1,0:T(8,128)(2,1)} %bitcast.72, f32[128,1024]{1,0:T(8,128)} %copy_bitcast_fusion.2.l_ref), custom_call_target="tpu_custom_call" | custom-call | tf_op jit(solution)/shard_map/pallas_call | solution.py:77
  55.1 0.9 convert_element_type.48
  56.1 0.8 broadcast_in_dim.62
  56.9 5.9 %all-to-all-start.1 = ((bf16[30,16,2,128]{3,2,0,1:T(2,128)(2,1)}), bf16[30,16,2,128]{3,2,0,1:T(2,128)(2,1)S(1)}, u32[]{:S(2)}, u32[]{:S(2)}) async-start(bf16[30,16,2,128]{3,2,0,1:T(2,128)(2,1)} %bitcast.15), calls=%async_computation.1 | async-start | bytes 491520 | tf_op jit(solution)/shard_map/all_to_all | solution.py:207
  62.8 33.8 %all-to-all-done.1 = bf16[30,16,2,128]{3,2,0,1:T(2,128)(2,1)S(1)} async-done(((bf16[30,16,2,128]{3,2,0,1:T(2,128)(2,1)}), bf16[30,16,2,128]{3,2,0,1:T(2,128)(2,1)S(1)}, u32[]{:S(2)}, u32[]{:S(2)}) %all-to-all-start.1) | async-done | bytes 245792 | tf_op jit(solution)/shard_map/all_to_all | solution.py:207
  96.8 0.4 reshape.159
  97.2 1.8 %gather_fusion.1 = f32[256,2,512]{2,1,0:T(2,128)S(1)} fusion(f32[120,2,512]{2,1,0:T(2,128)S(1)} %reshape.159, s32[1024]{0:T(1024)S(1)} %pad_clamp_fusion), kind=kCustom, calls=%fused_computation.1 | custom fusion | bytes 2098176 | tf_op jit(solution)/shard_map/jit(_take)/gather | solution.py:217
  99.0 5.0 %shard_map.64 = f32[2,256,512]{2,1,0:T(8,128)} custom-call(f32[2]{0:T(128)} %speed_ref.1, f32[2,256,512]{2,1,0:T(8,128)} %bitcast.70, f32[2,256,512]{2,1,0:T(8,128)} %collective-permute-done.2.next_ref, f32[2,256,512]{2,1,0:T(8,128)} %collective-permute-done.3.prev_ref), custom_call_target="tpu_custom_call" | custom-call | tf_op jit(solution)/shard_map/pallas_call | solution.py:124
  103.9 1.6 %fusion.5 = f32[2,256,1,512]{3,1,0,2:T(8,128)S(1)} fusion(f32[2,256,512]{2,1,0:T(8,128)} %shard_map.64, f32[256,2,512]{2,1,0:T(2,128)S(1)} %gather_fusion.1, f32[2]{0:T(128)S(1)} %neg.4, pred[256]{0:T(512)(128)(4,1)S(1)} %compare_and_fusion.2, pred[256]{0:T(512)(128)(4,1)S(1)} %gt.18, f32[2,256,1,512]{3,2,1,0:T(1,128)S(1)} %copy-done.1), kind=kLoop, calls=%fused_computation.16 | loop fusion | flops 1310720 | bytes 4194824 | tf_op jit(solution)/shard_map/add | solution.py:225
  105.6 2.0 %copy.56 = f32[2,256,1,512]{3,2,1,0:T(1,128)} copy(f32[2,256,1,512]{3,1,0,2:T(8,128)S(1)} %fusion.5) | data formatting | bytes 2097152 | tf_op jit(solution)/shard_map/add | solution.py:225
  (42 shorter events, 1.2 us)
Async XLA Ops:
  0.0 8.7 %copy-start.4 = (s32[120]{0:T(128)S(1)}, s32[120]{0:T(128)}, u32[]{:S(2)}) copy-start(s32[120]{0:T(128)} %param.9) | copy-start | bytes 1444
  0.0 18.7 %copy-start.2 = (bf16[2,30,120,120]{3,2,1,0:T(8,128)(2,1)S(1)}, bf16[2,30,120,120]{3,2,1,0:T(8,128)(2,1)}, u32[]{:S(2)}) copy-start(bf16[2,30,120,120]{3,2,1,0:T(8,128)(2,1)} %param.7) | copy-start | bytes 5184004
  1.4 35.3 %copy-start = (f32[2,256,1,512]{3,1,2,0:T(8,128)}, f32[2,256,1,512]{3,1,2,0:T(8,128)S(1)}, u32[]{:S(2)}) copy-start(f32[2,256,1,512]{3,1,2,0:T(8,128)S(1)} %copy.81) | copy-start | bytes 3145732
  1.4 17.8 %copy-start.3 = (s32[8,8]{1,0:T(8,128)S(1)}, s32[8,8]{1,0:T(8,128)}, u32[]{:S(2)}) copy-start(s32[8,8]{1,0:T(8,128)} %param.8) | copy-start | bytes 772
  2.4 34.4 %collective-permute-start.1 = (f32[2,64,512]{2,1,0:T(8,128)}, f32[2,64,512]{2,1,0:T(8,128)}, u32[]{:S(2)}, u32[]{:S(2)}) collective-permute-start(f32[2,64,512]{2,1,0:T(8,128)} %get-tuple-element.16), channel_id=1, source_target_pairs={{0,16},{16,32},{32,48},{1,17},{17,33},{33,49},{2,18},{18,34},{34,5... | collective-permute-start | bytes 786440 | tf_op jit(solution)/shard_map/ppermute | solution.py:159
  6.6 30.2 %collective-permute-start = (f32[2,64,512]{2,1,0:T(8,128)}, f32[2,64,512]{2,1,0:T(8,128)}, u32[]{:S(2)}, u32[]{:S(2)}) collective-permute-start(f32[2,64,512]{2,1,0:T(8,128)} %get-tuple-element.15), channel_id=1, source_target_pairs={{16,0},{32,16},{48,32},{17,1},{33,17},{49,33},{18,2},{34,18},{50,3... | collective-permute-start | bytes 786440 | tf_op jit(solution)/shard_map/ppermute | solution.py:162
  12.8 14.1 %all-to-all-start = ((bf16[2,120,4,128]{3,0,1,2:T(2,128)(2,1)}), bf16[2,120,4,128]{3,0,1,2:T(2,128)(2,1)S(1)}, u32[]{:S(2)}, u32[]{:S(2)}) async-start(bf16[2,120,4,128]{3,0,1,2:T(2,128)(2,1)} %fusion.9), calls=%async_computation | async-start | bytes 491520 | tf_op jit(solution)/shard_map/all_to_all | solution.py:183
  18.7 2.8 %copy-start.5 = (f32[2]{0:T(128)S(1)}, f32[2]{0:T(128)}, u32[]{:S(2)}) copy-start(f32[2]{0:T(128)} %param.11) | copy-start | bytes 28
  27.0 17.1 %collective-permute-start.6 = (bf16[8,120,1,128]{3,1,0,2:T(8,128)(2,1)S(1)}, bf16[8,120,1,128]{3,1,0,2:T(8,128)(2,1)S(1)}, u32[]{:S(2)}, u32[]{:S(2)}) collective-permute-start(bf16[8,120,1,128]{3,1,0,2:T(8,128)(2,1)S(1)} %bitcast.75), channel_id=1, source_target_pairs={{0,48},{16,0},{1,49},{17,1},{2,50},{18,2},{3,51},{19,3},{4,52},{20... | collective-permute-start | bytes 737288 | tf_op jit(solution)/shard_map/ppermute | solution.py:140
  32.7 11.4 %collective-permute-start.5 = (bf16[8,120,1,128]{3,1,0,2:T(8,128)(2,1)S(1)}, bf16[8,120,1,128]{3,1,0,2:T(8,128)(2,1)S(1)}, u32[]{:S(2)}, u32[]{:S(2)}) collective-permute-start(bf16[8,120,1,128]{3,1,0,2:T(8,128)(2,1)S(1)} %bitcast.76), channel_id=1, source_target_pairs={{0,32},{16,48},{1,33},{17,49},{2,34},{18,50},{3,35},{19,51},{4,36}... | collective-permute-start | bytes 737288 | tf_op jit(solution)/shard_map/ppermute | solution.py:140
  34.0 10.1 %collective-permute-start.4 = (bf16[8,120,1,128]{3,1,0,2:T(8,128)(2,1)S(1)}, bf16[8,120,1,128]{3,1,0,2:T(8,128)(2,1)S(1)}, u32[]{:S(2)}, u32[]{:S(2)}) collective-permute-start(bf16[8,120,1,128]{3,1,0,2:T(8,128)(2,1)S(1)} %bitcast.77), channel_id=1, source_target_pairs={{0,16},{16,32},{1,17},{17,33},{2,18},{18,34},{3,19},{19,35},{4,20}... | collective-permute-start | bytes 737288 | tf_op jit(solution)/shard_map/ppermute | solution.py:140
  39.5 59.4 %collective-permute-start.2 = (f32[2,256,512]{2,1,0:T(8,128)}, f32[2,256,512]{2,1,0:T(8,128)}, u32[]{:S(2)}, u32[]{:S(2)}) collective-permute-start(f32[2,256,512]{2,1,0:T(8,128)} %get-tuple-element.14), channel_id=1, source_target_pairs={{1,0},{2,1},{3,2},{4,3},{5,4},{6,5},{7,6},{8,7},{9,8},{10,9},{11,1... | collective-permute-start | bytes 3145736 | tf_op jit(solution)/shard_map/ppermute | solution.py:171
  42.1 56.8 %collective-permute-start.3 = (f32[2,256,512]{2,1,0:T(8,128)}, f32[2,256,512]{2,1,0:T(8,128)}, u32[]{:S(2)}, u32[]{:S(2)}) collective-permute-start(f32[2,256,512]{2,1,0:T(8,128)} %get-tuple-element.13), channel_id=1, source_target_pairs={{0,1},{1,2},{2,3},{3,4},{4,5},{5,6},{6,7},{7,8},{8,9},{9,10},{10,1... | collective-permute-start | bytes 3145736 | tf_op jit(solution)/shard_map/ppermute | solution.py:172
  56.9 39.7 %all-to-all-start.1 = ((bf16[30,16,2,128]{3,2,0,1:T(2,128)(2,1)}), bf16[30,16,2,128]{3,2,0,1:T(2,128)(2,1)S(1)}, u32[]{:S(2)}, u32[]{:S(2)}) async-start(bf16[30,16,2,128]{3,2,0,1:T(2,128)(2,1)} %bitcast.15), calls=%async_computation.1 | async-start | bytes 491520 | tf_op jit(solution)/shard_map/all_to_all | solution.py:207
  96.7 7.3 %copy-start.1 = (f32[2,256,1,512]{3,2,1,0:T(1,128)S(1)}, f32[2,256,1,512]{3,2,1,0:T(1,128)}, u32[]{:S(2)}) copy-start(f32[2,256,1,512]{3,2,1,0:T(1,128)} %param.6) | copy-start | bytes 3145732

commit v9 on v4

--- a/solution.py
+++ b/solution.py
@@ -112,11 +112,15 @@
     up_part = 0.5 * flux_x - 0.5 * bound_x * phase_field
     down_part = -0.5 * flux_x - 0.5 * bound_x * phase_field
     from_next = lax.ppermute(
-        up_part[:, :, :, :, :1], "space", [(i + 1, i) for i in range(space_devs - 1)]
-    )
+        up_part[:, :, :, :, :1].astype(jnp.float16),
+        "space",
+        [(i + 1, i) for i in range(space_devs - 1)],
+    ).astype(jnp.float32)
     from_prev = lax.ppermute(
-        down_part[:, :, :, :, row_count - 1 :], "space", [(i, i + 1) for i in range(space_devs - 1)]
-    )
+        down_part[:, :, :, :, row_count - 1 :].astype(jnp.float16),
+        "space",
+        [(i, i + 1) for i in range(space_devs - 1)],
+    ).astype(jnp.float32)
     up_all = jnp.concatenate([up_part[:, :, :, :, 1:], from_next], axis=4)
     down_all = jnp.concatenate([from_prev, down_part[:, :, :, :, : row_count - 1]], axis=4)
     x_term = up_all + down_all + bound_x * phase_field

time: 108 us -> 102 us (0.944)
  waiting for transfers between devices: 20.1 us -> 10.3 us
  starting transfers between devices: 37.3 us -> 40.4 us
  local copies, waits for them, and re-layouts: 19.5 us -> 20.9 us
    all_to_all x1, waiting for transfers between devices: 12.8 us -> 5.38 us  [per_device(): lax.all_to_all(gained.astype(jnp.bfloat16), ('species', 'mode'), 1, 1, ti...]
    sub x1 -> x0, other arithmetic: 3.19 us -> none  [per_device(): down_part = -0.5 * flux_x - 0.5 * bound_x * phase_field]
    convert_element_type x0 -> x1, other arithmetic: none -> 2.89 us  [per_device(): up_part[:, :, :, :, :1].astype(jnp.float16)]
    ppermute x2, starting transfers between devices: 7.67 us -> 10.4 us  [the longest x1 8.45 us: per_device(): lax.ppermute(up_part[:, :, :, :, :1].astype(jnp.float16), 'space', [(i +...]
    ppermute x3, waiting for transfers between devices: 7.35 us -> 4.96 us  [shift_permutes(): received.append((shift, lax.ppermute(values, axis, pairs)))]
    squeeze x1, local copies, waits for them, and re-layouts: 0.53 us -> 2.02 us  [per_device(): kpad[k]]
    add x1, other arithmetic: 2.84 us -> 4.05 us  [per_device(): advected.reshape(own_count, mode_count, row_count, plane_cells)]
    unnamed x17 -> x15, local copies, waits for them, and re-layouts: 3.47 us -> 3.5 us
  transfers between devices with their start and end apart: 9 -> 9, of which waited for: 3 -> 3; matrix products, arithmetic and copies ran while one was open for 25% -> 28% of each run, Pallas kernels for 7% -> 8%
where the time goes in v9:
time: 102 us; the launch traced here: 101 us
  starting transfers between devices  40.4 us (40%)
  other arithmetic  21.3 us (21%)
  local copies, waits for them, and re-layouts  20.9 us (20%)
  waiting for transfers between devices  10.3 us (10%)
  Pallas kernels  7.91 us (8%)
    ppermute x3, starting transfers between devices, shift_permutes(): received.append((shift, lax.ppermute(values, axis, pairs)))  10.1 us
    all_to_all x1, starting transfers between devices, per_device(): lax.all_to_all(gained.astype(jnp.bfloat16), ('species', 'mode'), 1, 1, ti...  8.59 us
    ppermute x1, starting transfers between devices, per_device(): lax.ppermute(up_part[:, :, :, :, :1].astype(jnp.float16), 'space', [(i +...  8.45 us
    pallas_call x1, Pallas kernels, collide_call(): pl.pallas_call(collide_body, out_shape=jax.ShapeDtypeStruct((kcat.shape[0...  7.91 us
    all_to_all x1, starting transfers between devices, per_device(): spread = lax.all_to_all(picked, 'species', 2, 0, tiled=True)  5.89 us
    all_to_all x1, waiting for transfers between devices, per_device(): lax.all_to_all(gained.astype(jnp.bfloat16), ('species', 'mode'), 1, 1, ti...  5.38 us
    ppermute x3, waiting for transfers between devices, shift_permutes(): received.append((shift, lax.ppermute(values, axis, pairs)))  4.96 us
    sub x1, other arithmetic, per_device(): phase_field - nu_step * thermal_speed.reshape(own_count, 1, 1, 1, 1, 1, 1...  4.3 us
  transfers between devices with their start and end apart: 9, of which 3 were waited for; matrix products, arithmetic and copies ran while one was open for 28% of the time, Pallas kernels for 8%

profile of v9, /device:TPU:2, one launch (start us, length us, event | category | flops | bytes accessed | tf_op | source)
XLA Modules:
  0.0 101.5 jit_solution(7033591285534496142)
XLA Ops:
  0.0 3.7 %reduce.18 = f32[2,256,512]{2,1,0:T(8,128)S(1)} reduce(f32[2,256,1,512]{3,2,1,0:T(1,128)} %param.6, f32[]{:T(128)} %constant.93), dimensions={2}, to_apply=%param.6.reduce_sub_computation | reduce | bytes 2097156 | tf_op args[0]
  3.7 0.8 fusion.31
  4.6 4.2 %collective-permute-start.1 = (f32[2,1,8,8,1,2,256]{6,3,5,4,2,1,0:T(8,128)}, f32[2,1,8,8,1,2,256]{6,3,5,4,2,1,0:T(8,128)}, u32[]{:S(2)}, u32[]{:S(2)}) collective-permute-start(f32[2,1,8,8,1,2,256]{6,3,5,4,2,1,0:T(8,128)} %get-tuple-element.20), channel_id=1, source_target_pairs={{0,16},{16,32},{32,48},{1,17},{17,33},{33,49},{2,18},{18,34},{34,5... | collective-permute-start | bytes 786440 | tf_op jit(solution)/shard_map/ppermute | solution.py:107
  8.7 1.3 %collective-permute-start = (f32[2,1,8,8,1,2,256]{6,3,5,4,2,1,0:T(8,128)}, f32[2,1,8,8,1,2,256]{6,3,5,4,2,1,0:T(8,128)}, u32[]{:S(2)}, u32[]{:S(2)}) collective-permute-start(f32[2,1,8,8,1,2,256]{6,3,5,4,2,1,0:T(8,128)} %get-tuple-element.19), channel_id=1, source_target_pairs={{16,0},{32,16},{48,32},{17,1},{33,17},{49,33},{18,2},{34,18},{50,3... | collective-permute-start | bytes 786440 | tf_op jit(solution)/shard_map/ppermute | solution.py:110
  10.0 2.0 %copy.207 = bf16[2,256,1,512]{3,0,1,2:T(2,128)(2,1)S(1)} copy(f32[2,256,1,512]{3,2,1,0:T(1,128)} %param.6) | data formatting | bytes 1572864 | tf_op args[0]
  12.1 1.1 %gather_fusion = bf16[120,2,512]{2,1,0:T(2,128)(2,1)S(1)} fusion(bf16[2,256,512]{2,0,1:T(2,128)(2,1)S(1)} %bitcast.80, s32[1024]{0:T(1024)S(1)} %pad_clamp_fusion.1), kind=kCustom, calls=%fused_computation | custom fusion | bytes 492000 | tf_op jit(solution)/shard_map/jit(_take)/gather | solution.py:138
  13.2 1.4 %fusion.26 = bf16[2,120,4,128]{3,0,1,2:T(2,128)(2,1)} fusion(pred[120]{0:T(512)(128)(4,1)S(1)} %get-tuple-element.9, pred[120]{0:T(512)(128)(4,1)S(1)} %get-tuple-element.39, bf16[120,2,512]{2,1,0:T(2,128)(2,1)S(1)} %gather_fusion), kind=kLoop, calls=%fused_computation.52 | loop fusion | flops 245760 | bytes 491760 | tf_op jit(solution)/shard_map/convert_element_type | solution.py:138
  14.6 5.9 %all-to-all-start = ((bf16[2,120,4,128]{3,0,1,2:T(2,128)(2,1)}), bf16[2,120,4,128]{3,0,1,2:T(2,128)(2,1)S(1)}, u32[]{:S(2)}, u32[]{:S(2)}) async-start(bf16[2,120,4,128]{3,0,1,2:T(2,128)(2,1)} %fusion.26), calls=%async_computation | async-start | bytes 491520 | tf_op jit(solution)/shard_map/all_to_all | solution.py:142
  20.5 1.2 %fusion.34 = (f32[2,4,8,8,1,2,1]{6,3,5,4,2,1,0:T(8,128)}, f32[2,4,8,8,1,2,1]{6,3,5,4,2,1,0:T(8,128)}) fusion(f32[2,4,8,8,1,2,256]{6,3,5,4,2,1,0:T(8,128)S(1)} %bitcast.70), kind=kLoop, calls=%fused_computation.82 | loop fusion | bytes 16384 | tf_op jit(solution)/shard_map/jit(_roll_static)/slice | solution.py:52
  21.7 1.7 %fusion.35 = (f32[2,4,8,8,1,2,255]{6,3,5,4,2,1,0:T(8,128)}, f32[2,4,8,8,1,2,255]{6,3,5,4,2,1,0:T(8,128)}) fusion(f32[2,4,8,8,1,2,256]{6,3,5,4,2,1,0:T(8,128)S(1)} %bitcast.71), kind=kLoop, calls=%fused_computation.83 | loop fusion | bytes 4177920 | tf_op jit(solution)/shard_map/jit(_roll_static)/slice | solution.py:52
  24.2 2.0 %fusion.23 = (bf16[30,128,128]{2,1,0:T(8,128)(2,1)S(1)}, bf16[30,128,128]{2,1,0:T(8,128)(2,1)S(1)}) fusion(bf16[2,30,120,120]{3,2,1,0:T(8,128)(2,1)} %param.7), kind=kLoop, calls=%fused_computation.44 | loop fusion | bytes 3694080 | tf_op jit(solution)/shard_map/squeeze | solution.py:159
  26.5 2.0 %pad_maximum_fusion.k_ref = bf16[30,128,512]{2,1,0:T(8,128)(2,1)} fusion(bf16[30,128,128]{2,1,0:T(8,128)(2,1)S(1)} %get-tuple-element.12, bf16[30,128,128]{2,1,0:T(8,128)(2,1)S(1)} %get-tuple-element.11), kind=kLoop, calls=%fused_computation.2 | loop fusion | flops 15728640 | bytes 5898240 | tf_op jit(solution)/shard_map/concatenate | solution.py:159
  28.5 1.1 %fusion.32 = (f32[2,4,8,8,1,1,256]{6,3,5,4,2,1,0:T(8,128)}, f32[2,4,8,8,1,1,256]{6,3,5,4,2,1,0:T(8,128)}) fusion(f32[2,4,8,8,1,2,256]{6,3,5,4,2,1,0:T(8,128)S(1)} %bitcast.72), kind=kLoop, calls=%fused_computation.80 | loop fusion | bytes 2097152 | tf_op jit(solution)/shard_map/jit(_roll_static)/slice | solution.py:51
  29.6 2.9 %subtract_convert_fusion.1 = (f16[2,4,8,8,1,2,256]{6,3,5,4,2,1,0:T(8,128)(2,1)}, f16[2,4,8,8,1,2,256]{6,3,5,4,2,1,0:T(8,128)(2,1)}, f32[2,4,8,8,1,2,256]{6,3,5,4,2,1,0:T(8,128)S(1)}, f32[2,4,8,8,1,2,256]{6,3,5,4,2,1,0:T(8,128)S(1)}) fusion(f32[2,4,8,8,1,2,256]{6,3,5,4,2,1,0:T(8,128)S(1)} %bitcast.73, f32[2,1,8,8,1,2,256]{6,3,5,4,2,1,0:T(8,128)} %collective-permute-done.1, ...), kind=kLoop, calls=%fused_computation.43 | loop fusion | flops 4718592 | bytes 4721664 | tf_op jit(solution)/shard_map/convert_element_type | solution.py:115
  32.5 1.9 %collective-permute-start.3 = (f16[2,4,8,8,1,2,256]{6,3,5,4,2,1,0:T(8,128)(2,1)}, f16[2,4,8,8,1,2,256]{6,3,5,4,2,1,0:T(8,128)(2,1)}, u32[]{:S(2)}, u32[]{:S(2)}) collective-permute-start(f16[2,4,8,8,1,2,256]{6,3,5,4,2,1,0:T(8,128)(2,1)} %get-tuple-element.14), channel_id=1, source_target_pairs={{0,1},{1,2},{2,3},{3,4},{4,5},{5,6},{6,7},{7,8},{8,9},{9,10},{10,1... | collective-permute-start | bytes 1572872 | tf_op jit(solution)/shard_map/ppermute | solution.py:119
  34.4 8.4 %collective-permute-start.2 = (f16[2,4,8,8,1,2,256]{6,3,5,4,2,1,0:T(8,128)(2,1)}, f16[2,4,8,8,1,2,256]{6,3,5,4,2,1,0:T(8,128)(2,1)}, u32[]{:S(2)}, u32[]{:S(2)}) collective-permute-start(f16[2,4,8,8,1,2,256]{6,3,5,4,2,1,0:T(8,128)(2,1)} %get-tuple-element.13), channel_id=1, source_target_pairs={{1,0},{2,1},{3,2},{4,3},{5,4},{6,5},{7,6},{8,7},{9,8},{10,9},{11,1... | collective-permute-start | bytes 1572872 | tf_op jit(solution)/shard_map/ppermute | solution.py:114
  42.9 1.7 %fusion.37 = (f32[2,4,8,8,1,2,255]{6,3,5,4,2,1,0:T(8,128)}, f32[2,4,8,8,1,2,255]{6,3,5,4,2,1,0:T(8,128)}) fusion(f32[2,4,8,8,1,2,256]{6,3,5,4,2,1,0:T(8,128)S(1)} %get-tuple-element.17), kind=kLoop, calls=%fused_computation.85 | loop fusion | bytes 4177920 | tf_op jit(solution)/shard_map/jit(_roll_static)/slice | solution.py:54
  44.6 6.0 %collective-permute-start.6 = (bf16[8,120,1,128]{3,1,0,2:T(8,128)(2,1)S(1)}, bf16[8,120,1,128]{3,1,0,2:T(8,128)(2,1)S(1)}, u32[]{:S(2)}, u32[]{:S(2)}) collective-permute-start(bf16[8,120,1,128]{3,1,0,2:T(8,128)(2,1)S(1)} %bitcast.81), channel_id=1, source_target_pairs={{0,48},{16,0},{1,49},{17,1},{2,50},{18,2},{3,51},{19,3},{4,52},{20... | collective-permute-start | bytes 737288 | tf_op jit(solution)/shard_map/ppermute | solution.py:90
  50.6 1.3 %collective-permute-start.5 = (bf16[8,120,1,128]{3,1,0,2:T(8,128)(2,1)S(1)}, bf16[8,120,1,128]{3,1,0,2:T(8,128)(2,1)S(1)}, u32[]{:S(2)}, u32[]{:S(2)}) collective-permute-start(bf16[8,120,1,128]{3,1,0,2:T(8,128)(2,1)S(1)} %bitcast.82), channel_id=1, source_target_pairs={{0,32},{16,48},{1,33},{17,49},{2,34},{18,50},{3,35},{19,51},{4,36}... | collective-permute-start | bytes 737288 | tf_op jit(solution)/shard_map/ppermute | solution.py:90
  52.0 2.8 %collective-permute-start.4 = (bf16[8,120,1,128]{3,1,0,2:T(8,128)(2,1)S(1)}, bf16[8,120,1,128]{3,1,0,2:T(8,128)(2,1)S(1)}, u32[]{:S(2)}, u32[]{:S(2)}) collective-permute-start(bf16[8,120,1,128]{3,1,0,2:T(8,128)(2,1)S(1)} %bitcast.83), channel_id=1, source_target_pairs={{0,16},{16,32},{1,17},{17,33},{2,18},{18,34},{3,19},{19,35},{4,20}... | collective-permute-start | bytes 737288 | tf_op jit(solution)/shard_map/ppermute | solution.py:90
  54.7 1.2 %fusion.36 = (f32[2,4,8,8,1,2,1]{6,3,5,4,2,1,0:T(8,128)}, f32[2,4,8,8,1,2,1]{6,3,5,4,2,1,0:T(8,128)}) fusion(f32[2,4,8,8,1,2,256]{6,3,5,4,2,1,0:T(8,128)S(1)} %get-tuple-element.17), kind=kLoop, calls=%fused_computation.84 | loop fusion | bytes 16384 | tf_op jit(solution)/shard_map/jit(_roll_static)/slice | solution.py:54
  55.9 3.7 %collective-permute-done.6 = bf16[8,120,1,128]{3,1,0,2:T(8,128)(2,1)S(1)} collective-permute-done((bf16[8,120,1,128]{3,1,0,2:T(8,128)(2,1)S(1)}, bf16[8,120,1,128]{3,1,0,2:T(8,128)(2,1)S(1)}, u32[]{:S(2)}, u32[]{:S(2)}) %collective-permute-start.6) | collective-permute-done | bytes 245792 | tf_op jit(solution)/shard_map/ppermute | solution.py:90
  59.5 1.3 %collective-permute-done.4 = bf16[8,120,1,128]{3,1,0,2:T(8,128)(2,1)S(1)} collective-permute-done((bf16[8,120,1,128]{3,1,0,2:T(8,128)(2,1)S(1)}, bf16[8,120,1,128]{3,1,0,2:T(8,128)(2,1)S(1)}, u32[]{:S(2)}, u32[]{:S(2)}) %collective-permute-start.4) | collective-permute-done | bytes 245792 | tf_op jit(solution)/shard_map/ppermute | solution.py:90
  61.8 1.3 %copy.206 = bf16[64,8,8,128]{3,1,2,0:T(8,128)(2,1)} copy(bf16[64,8,8,128]{3,2,1,0:T(8,128)(2,1)S(1)} %bitcast.76) | data formatting | bytes 2097152
  63.9 7.9 %shard_map.64 = f32[30,1024]{1,0:T(8,128)} custom-call(bf16[30,128,512]{2,1,0:T(8,128)(2,1)} %pad_maximum_fusion.k_ref, bf16[512,1024]{1,0:T(8,128)(2,1)} %bitcast.77, f32[128,1024]{1,0:T(8,128)} %copy_bitcast_fusion.2.l_ref), custom_call_target="tpu_custom_call" | custom-call | tf_op jit(solution)/shard_map/pallas_call | solution.py:76
  71.9 0.9 convert_element_type.93
  73.7 8.6 %all-to-all-start.1 = ((bf16[30,16,2,128]{3,2,0,1:T(2,128)(2,1)}), bf16[30,16,2,128]{3,2,0,1:T(2,128)(2,1)S(1)}, u32[]{:S(2)}, u32[]{:S(2)}) async-start(bf16[30,16,2,128]{3,2,0,1:T(2,128)(2,1)} %bitcast.85), calls=%async_computation.1 | async-start | bytes 491520 | tf_op jit(solution)/shard_map/all_to_all | solution.py:166
  82.4 4.3 %fusion.7 = f32[2,4,8,8,1,2,256]{6,3,5,4,2,1,0:T(8,128)S(1)} fusion(f32[2,4,8,8,1,2,256]{6,3,5,4,2,1,0:T(8,128)S(1)} %bitcast.74, f32[2,4,8,8,1,2,1]{6,3,5,4,2,1,0:T(8,128)} %get-tuple-element.30, f32[2,4,8,8,1,2,255]{6,3,5,4,2,1,0:T(8,128)} %get-tuple-element.32, f32[2,4,8,8,1,2,255]{6,3,5,4,2,1,0:T(8,128)} %get-tuple-element.31, ...), kind=kLoop, calls=%fused_computation.18 | loop fusion | flops 7340032 | bytes 9437192 | tf_op jit(solution)/shard_map/sub | solution.py:130
  86.7 5.4 %all-to-all-done.1 = bf16[30,16,2,128]{3,2,0,1:T(2,128)(2,1)S(1)} async-done(((bf16[30,16,2,128]{3,2,0,1:T(2,128)(2,1)}), bf16[30,16,2,128]{3,2,0,1:T(2,128)(2,1)S(1)}, u32[]{:S(2)}, u32[]{:S(2)}) %all-to-all-start.1) | async-done | bytes 245792 | tf_op jit(solution)/shard_map/all_to_all | solution.py:166
  92.7 2.7 %gather_fusion.1 = f32[256,2,512]{2,1,0:T(2,128)} fusion(f32[120,2,512]{2,1,0:T(2,128)S(1)} %reshape.456, s32[1024]{0:T(1024)S(1)} %pad_clamp_fusion), kind=kCustom, calls=%fused_computation.1 | custom fusion | bytes 2098176 | tf_op jit(solution)/shard_map/jit(_take)/gather | solution.py:176
  95.4 4.0 %fusion.22 = f32[2,256,1,512]{3,0,1,2:T(2,128)S(1)} fusion(f32[2,256,512]{2,1,0:T(8,128)S(1)} %bitcast.75, f32[256,2,512]{2,1,0:T(2,128)} %gather_fusion.1, pred[256]{0:T(512)(128)(4,1)S(1)} %compare_and_fusion.2, pred[256]{0:T(512)(128)(4,1)S(1)} %gt.18, f32[2]{0:T(128)S(1)} %neg.4, f32[2,256,1,512]{3,2,1,0:T(1,128)S(1)} %copy-done), kind=kLoop, calls=%fused_computation.40 | loop fusion | flops 1310720 | bytes 4194824 | tf_op jit(solution)/shard_map/add | solution.py:184
  99.4 2.0 %copy.185 = f32[2,256,1,512]{3,2,1,0:T(1,128)} copy(f32[2,256,1,512]{3,0,1,2:T(2,128)S(1)} %fusion.22) | data formatting | bytes 2097152 | tf_op jit(solution)/shard_map/add | solution.py:184
  (50 shorter events, 4.5 us)
Async XLA Ops:
  0.0 12.1 %copy-start.3 = (s32[120]{0:T(128)S(1)}, s32[120]{0:T(128)}, u32[]{:S(2)}) copy-start(s32[120]{0:T(128)} %param.9) | copy-start | bytes 1444
  4.6 25.1 %collective-permute-start.1 = (f32[2,1,8,8,1,2,256]{6,3,5,4,2,1,0:T(8,128)}, f32[2,1,8,8,1,2,256]{6,3,5,4,2,1,0:T(8,128)}, u32[]{:S(2)}, u32[]{:S(2)}) collective-permute-start(f32[2,1,8,8,1,2,256]{6,3,5,4,2,1,0:T(8,128)} %get-tuple-element.20), channel_id=1, source_target_pairs={{0,16},{16,32},{32,48},{1,17},{17,33},{33,49},{2,18},{18,34},{34,5... | collective-permute-start | bytes 786440 | tf_op jit(solution)/shard_map/ppermute | solution.py:107
  8.7 20.9 %collective-permute-start = (f32[2,1,8,8,1,2,256]{6,3,5,4,2,1,0:T(8,128)}, f32[2,1,8,8,1,2,256]{6,3,5,4,2,1,0:T(8,128)}, u32[]{:S(2)}, u32[]{:S(2)}) collective-permute-start(f32[2,1,8,8,1,2,256]{6,3,5,4,2,1,0:T(8,128)} %get-tuple-element.19), channel_id=1, source_target_pairs={{16,0},{32,16},{48,32},{17,1},{33,17},{49,33},{18,2},{34,18},{50,3... | collective-permute-start | bytes 786440 | tf_op jit(solution)/shard_map/ppermute | solution.py:110
  12.1 12.1 %copy-start.4 = (f32[2]{0:T(128)S(1)}, f32[2]{0:T(128)}, u32[]{:S(2)}) copy-start(f32[2]{0:T(128)} %param.10) | copy-start | bytes 28
  14.6 30.0 %all-to-all-start = ((bf16[2,120,4,128]{3,0,1,2:T(2,128)(2,1)}), bf16[2,120,4,128]{3,0,1,2:T(2,128)(2,1)S(1)}, u32[]{:S(2)}, u32[]{:S(2)}) async-start(bf16[2,120,4,128]{3,0,1,2:T(2,128)(2,1)} %fusion.26), calls=%async_computation | async-start | bytes 491520 | tf_op jit(solution)/shard_map/all_to_all | solution.py:142
  21.7 4.5 %copy-start.2 = (s32[8,8]{1,0:T(8,128)S(1)}, s32[8,8]{1,0:T(8,128)}, u32[]{:S(2)}) copy-start(s32[8,8]{1,0:T(8,128)} %param.8) | copy-start | bytes 772
  21.7 4.8 %copy-start.5 = (f32[2]{0:T(128)S(1)}, f32[2]{0:T(128)}, u32[]{:S(2)}) copy-start(f32[2]{0:T(128)} %param.11) | copy-start | bytes 28
  32.5 49.9 %collective-permute-start.3 = (f16[2,4,8,8,1,2,256]{6,3,5,4,2,1,0:T(8,128)(2,1)}, f16[2,4,8,8,1,2,256]{6,3,5,4,2,1,0:T(8,128)(2,1)}, u32[]{:S(2)}, u32[]{:S(2)}) collective-permute-start(f16[2,4,8,8,1,2,256]{6,3,5,4,2,1,0:T(8,128)(2,1)} %get-tuple-element.14), channel_id=1, source_target_pairs={{0,1},{1,2},{2,3},{3,4},{4,5},{5,6},{6,7},{7,8},{8,9},{9,10},{10,1... | collective-permute-start | bytes 1572872 | tf_op jit(solution)/shard_map/ppermute | solution.py:119
  34.4 48.0 %collective-permute-start.2 = (f16[2,4,8,8,1,2,256]{6,3,5,4,2,1,0:T(8,128)(2,1)}, f16[2,4,8,8,1,2,256]{6,3,5,4,2,1,0:T(8,128)(2,1)}, u32[]{:S(2)}, u32[]{:S(2)}) collective-permute-start(f16[2,4,8,8,1,2,256]{6,3,5,4,2,1,0:T(8,128)(2,1)} %get-tuple-element.13), channel_id=1, source_target_pairs={{1,0},{2,1},{3,2},{4,3},{5,4},{6,5},{7,6},{8,7},{9,8},{10,9},{11,1... | collective-permute-start | bytes 1572872 | tf_op jit(solution)/shard_map/ppermute | solution.py:114
  44.6 14.9 %collective-permute-start.6 = (bf16[8,120,1,128]{3,1,0,2:T(8,128)(2,1)S(1)}, bf16[8,120,1,128]{3,1,0,2:T(8,128)(2,1)S(1)}, u32[]{:S(2)}, u32[]{:S(2)}) collective-permute-start(bf16[8,120,1,128]{3,1,0,2:T(8,128)(2,1)S(1)} %bitcast.81), channel_id=1, source_target_pairs={{0,48},{16,0},{1,49},{17,1},{2,50},{18,2},{3,51},{19,3},{4,52},{20... | collective-permute-start | bytes 737288 | tf_op jit(solution)/shard_map/ppermute | solution.py:90
  50.6 8.9 %collective-permute-start.5 = (bf16[8,120,1,128]{3,1,0,2:T(8,128)(2,1)S(1)}, bf16[8,120,1,128]{3,1,0,2:T(8,128)(2,1)S(1)}, u32[]{:S(2)}, u32[]{:S(2)}) collective-permute-start(bf16[8,120,1,128]{3,1,0,2:T(8,128)(2,1)S(1)} %bitcast.82), channel_id=1, source_target_pairs={{0,32},{16,48},{1,33},{17,49},{2,34},{18,50},{3,35},{19,51},{4,36}... | collective-permute-start | bytes 737288 | tf_op jit(solution)/shard_map/ppermute | solution.py:90
  52.0 8.9 %collective-permute-start.4 = (bf16[8,120,1,128]{3,1,0,2:T(8,128)(2,1)S(1)}, bf16[8,120,1,128]{3,1,0,2:T(8,128)(2,1)S(1)}, u32[]{:S(2)}, u32[]{:S(2)}) collective-permute-start(bf16[8,120,1,128]{3,1,0,2:T(8,128)(2,1)S(1)} %bitcast.83), channel_id=1, source_target_pairs={{0,16},{16,32},{1,17},{17,33},{2,18},{18,34},{3,19},{19,35},{4,20}... | collective-permute-start | bytes 737288 | tf_op jit(solution)/shard_map/ppermute | solution.py:90
  63.9 18.5 %copy-start.1 = (f32[2,4,8,8,1,2,255]{6,3,5,4,2,1,0:T(8,128)S(1)}, f32[2,4,8,8,1,2,255]{6,3,5,4,2,1,0:T(8,128)}, u32[]{:S(2)}) copy-start(f32[2,4,8,8,1,2,255]{6,3,5,4,2,1,0:T(8,128)} %get-tuple-element.27) | copy-start | bytes 3133444
  73.7 18.4 %all-to-all-start.1 = ((bf16[30,16,2,128]{3,2,0,1:T(2,128)(2,1)}), bf16[30,16,2,128]{3,2,0,1:T(2,128)(2,1)S(1)}, u32[]{:S(2)}, u32[]{:S(2)}) async-start(bf16[30,16,2,128]{3,2,0,1:T(2,128)(2,1)} %bitcast.85), calls=%async_computation.1 | async-start | bytes 491520 | tf_op jit(solution)/shard_map/all_to_all | solution.py:166
  86.7 8.7 %copy-start = (f32[2,256,1,512]{3,2,1,0:T(1,128)S(1)}, f32[2,256,1,512]{3,2,1,0:T(1,128)}, u32[]{:S(2)}) copy-start(f32[2,256,1,512]{3,2,1,0:T(1,128)} %param.6) | copy-start | bytes 3145732

commit v10 on v9

--- a/solution.py
+++ b/solution.py
@@ -103,6 +103,18 @@
     out_rows = kernel.shape[1]
     species_all = own_count * species_devs
 
+    cell_count = row_count * plane_cells
+    block_cells = cell_count // species_devs
+    flat_dist = distribution.reshape(own_count, mode_count, cell_count)
+    local_index = low_map - mode_id * mode_count
+    owned = (local_index >= 0) & (local_index < mode_count)
+    clipped = jnp.clip(local_index, 0, mode_count - 1)
+    picked = jnp.where(owned[None, :, None], jnp.take(flat_dist, clipped, axis=1), 0.0).astype(
+        jnp.bfloat16
+    )
+    picked = picked.reshape(own_count, low_count, species_devs, block_cells)
+    picked, distribution = lax.optimization_barrier((picked, distribution))
+    spread = lax.all_to_all(picked, "species", 2, 0, tiled=True)
     phase_field = distribution.reshape(own_count, per_vx, NVY, NVZ, row_count, NZ, NY)
     below = lax.ppermute(
         phase_field[:, per_vx - 1 :], "mode", [(i, i + 1) for i in range(mode_devs - 1)]
@@ -129,17 +141,6 @@
     stream = x_term + y_term + z_term
     advected = phase_field - nu_step * thermal_speed.reshape(own_count, 1, 1, 1, 1, 1, 1) * stream
 
-    cell_count = row_count * plane_cells
-    block_cells = cell_count // species_devs
-    flat_dist = distribution.reshape(own_count, mode_count, cell_count)
-    local_index = low_map - mode_id * mode_count
-    owned = (local_index >= 0) & (local_index < mode_count)
-    clipped = jnp.clip(local_index, 0, mode_count - 1)
-    picked = jnp.where(owned[None, :, None], jnp.take(flat_dist, clipped, axis=1), 0.0).astype(
-        jnp.bfloat16
-    )
-    picked = picked.reshape(own_count, low_count, species_devs, block_cells)
-    spread = lax.all_to_all(picked, "species", 2, 0, tiled=True)
     holders = [h for h in range(mode_devs) if h * per_vx <= DEG]
     low_all = spread
     for _, got in shift_permutes(spread, "mode", holders, mode_devs, False):

time: 102 us -> 103 us (level)
    optimization_barrier x0 -> x1, other arithmetic: none -> 3.72 us  [per_device(): picked, distribution = lax.optimization_barrier((picked, distribution))]
    unnamed x1 -> x0, other arithmetic: 3.72 us -> none
  transfers between devices with their start and end apart: 9 -> 9, of which waited for: 3 -> 3; matrix products, arithmetic and copies ran while one was open for 28% -> 24% of each run, Pallas kernels for 8% -> 8%
where the time goes in v10:
time: 103 us; the launch traced here: 102 us
  starting transfers between devices  40.4 us (39%)
  other arithmetic  22 us (21%)
  local copies, waits for them, and re-layouts  20.9 us (20%)
  waiting for transfers between devices  10.4 us (10%)
  Pallas kernels  7.91 us (8%)
    ppermute x3, starting transfers between devices, shift_permutes(): received.append((shift, lax.ppermute(values, axis, pairs)))  10.1 us
    all_to_all x1, starting transfers between devices, per_device(): lax.all_to_all(gained.astype(jnp.bfloat16), ('species', 'mode'), 1, 1, ti...  8.59 us
    ppermute x1, starting transfers between devices, per_device(): lax.ppermute(up_part[:, :, :, :, :1].astype(jnp.float16), 'space', [(i +...  8.45 us
    pallas_call x1, Pallas kernels, collide_call(): pl.pallas_call(collide_body, out_shape=jax.ShapeDtypeStruct((kcat.shape[0...  7.91 us
    all_to_all x1, starting transfers between devices, per_device(): spread = lax.all_to_all(picked, 'species', 2, 0, tiled=True)  5.91 us
    all_to_all x1, waiting for transfers between devices, per_device(): lax.all_to_all(gained.astype(jnp.bfloat16), ('species', 'mode'), 1, 1, ti...  5.38 us
    ppermute x3, waiting for transfers between devices, shift_permutes(): received.append((shift, lax.ppermute(values, axis, pairs)))  4.96 us
    sub x1, other arithmetic, per_device(): phase_field - nu_step * thermal_speed.reshape(own_count, 1, 1, 1, 1, 1, 1...  4.3 us
  transfers between devices with their start and end apart: 9, of which 3 were waited for; matrix products, arithmetic and copies ran while one was open for 24% of the time, Pallas kernels for 8%

profile of v10, /device:TPU:2, one launch (start us, length us, event | category | flops | bytes accessed | tf_op | source)
XLA Modules:
  0.0 102.1 jit_solution(17704377209647352858)
XLA Ops:
  0.0 2.0 %copy.207 = bf16[2,256,1,512]{3,0,1,2:T(2,128)(2,1)S(1)} copy(f32[2,256,1,512]{3,2,1,0:T(1,128)} %param.6) | data formatting | bytes 1572864 | tf_op args[0]
  2.7 1.1 %gather_fusion = bf16[120,2,512]{2,1,0:T(2,128)(2,1)S(1)} fusion(bf16[2,256,512]{2,0,1:T(2,128)(2,1)S(1)} %bitcast.80, s32[1024]{0:T(1024)S(1)} %pad_clamp_fusion.1), kind=kCustom, calls=%fused_computation | custom fusion | bytes 492000 | tf_op jit(solution)/shard_map/jit(_take)/gather | solution.py:112
  3.8 1.4 %fusion.26 = bf16[2,120,4,128]{3,0,1,2:T(2,128)(2,1)} fusion(pred[120]{0:T(512)(128)(4,1)S(1)} %get-tuple-element.13, pred[120]{0:T(512)(128)(4,1)S(1)} %get-tuple-element.43, bf16[120,2,512]{2,1,0:T(2,128)(2,1)S(1)} %gather_fusion), kind=kLoop, calls=%fused_computation.52 | loop fusion | flops 245760 | bytes 491760 | tf_op jit(solution)/shard_map/convert_element_type | solution.py:112
  5.2 3.7 %reduce.18 = f32[2,256,512]{2,1,0:T(8,128)S(1)} reduce(f32[2,256,1,512]{3,2,1,0:T(1,128)} %param.6, f32[]{:T(128)} %constant.93), dimensions={2}, to_apply=%get-tuple-element.8.reduce_sub_computation | reduce | bytes 2097156 | tf_op jit(solution)/shard_map/optimization_barrier | solution.py:116
  8.9 0.8 fusion.31
  9.7 4.2 %collective-permute-start.1 = (f32[2,1,8,8,1,2,256]{6,3,5,4,2,1,0:T(8,128)}, f32[2,1,8,8,1,2,256]{6,3,5,4,2,1,0:T(8,128)}, u32[]{:S(2)}, u32[]{:S(2)}) collective-permute-start(f32[2,1,8,8,1,2,256]{6,3,5,4,2,1,0:T(8,128)} %get-tuple-element.24), channel_id=1, source_target_pairs={{0,16},{16,32},{32,48},{1,17},{17,33},{33,49},{2,18},{18,34},{34,5... | collective-permute-start | bytes 786440 | tf_op jit(solution)/shard_map/ppermute | solution.py:119
  13.9 1.3 %collective-permute-start = (f32[2,1,8,8,1,2,256]{6,3,5,4,2,1,0:T(8,128)}, f32[2,1,8,8,1,2,256]{6,3,5,4,2,1,0:T(8,128)}, u32[]{:S(2)}, u32[]{:S(2)}) collective-permute-start(f32[2,1,8,8,1,2,256]{6,3,5,4,2,1,0:T(8,128)} %get-tuple-element.23), channel_id=1, source_target_pairs={{16,0},{32,16},{48,32},{17,1},{33,17},{49,33},{18,2},{34,18},{50,3... | collective-permute-start | bytes 786440 | tf_op jit(solution)/shard_map/ppermute | solution.py:122
  15.2 5.9 %all-to-all-start = ((bf16[2,120,4,128]{3,0,1,2:T(2,128)(2,1)}), bf16[2,120,4,128]{3,0,1,2:T(2,128)(2,1)S(1)}, u32[]{:S(2)}, u32[]{:S(2)}) async-start(bf16[2,120,4,128]{3,0,1,2:T(2,128)(2,1)} %fusion.26), calls=%async_computation | async-start | bytes 491520 | tf_op jit(solution)/shard_map/all_to_all | solution.py:117
  21.1 1.2 %fusion.34 = (f32[2,4,8,8,1,2,1]{6,3,5,4,2,1,0:T(8,128)}, f32[2,4,8,8,1,2,1]{6,3,5,4,2,1,0:T(8,128)}) fusion(f32[2,4,8,8,1,2,256]{6,3,5,4,2,1,0:T(8,128)S(1)} %bitcast.70), kind=kLoop, calls=%fused_computation.82 | loop fusion | bytes 16384 | tf_op jit(solution)/shard_map/jit(_roll_static)/slice | solution.py:52
  22.4 1.7 %fusion.35 = (f32[2,4,8,8,1,2,255]{6,3,5,4,2,1,0:T(8,128)}, f32[2,4,8,8,1,2,255]{6,3,5,4,2,1,0:T(8,128)}) fusion(f32[2,4,8,8,1,2,256]{6,3,5,4,2,1,0:T(8,128)S(1)} %bitcast.71), kind=kLoop, calls=%fused_computation.83 | loop fusion | bytes 4177920 | tf_op jit(solution)/shard_map/jit(_roll_static)/slice | solution.py:52
  24.8 2.0 %fusion.23 = (bf16[30,128,128]{2,1,0:T(8,128)(2,1)S(1)}, bf16[30,128,128]{2,1,0:T(8,128)(2,1)S(1)}) fusion(bf16[2,30,120,120]{3,2,1,0:T(8,128)(2,1)} %param.7), kind=kLoop, calls=%fused_computation.44 | loop fusion | bytes 3694080 | tf_op jit(solution)/shard_map/squeeze | solution.py:160
  27.1 2.0 %pad_maximum_fusion.k_ref = bf16[30,128,512]{2,1,0:T(8,128)(2,1)} fusion(bf16[30,128,128]{2,1,0:T(8,128)(2,1)S(1)} %get-tuple-element.16, bf16[30,128,128]{2,1,0:T(8,128)(2,1)S(1)} %get-tuple-element.15), kind=kLoop, calls=%fused_computation.2 | loop fusion | flops 15728640 | bytes 5898240 | tf_op jit(solution)/shard_map/concatenate | solution.py:160
  29.2 1.1 %fusion.32 = (f32[2,4,8,8,1,1,256]{6,3,5,4,2,1,0:T(8,128)}, f32[2,4,8,8,1,1,256]{6,3,5,4,2,1,0:T(8,128)}) fusion(f32[2,4,8,8,1,2,256]{6,3,5,4,2,1,0:T(8,128)S(1)} %bitcast.72), kind=kLoop, calls=%fused_computation.80 | loop fusion | bytes 2097152 | tf_op jit(solution)/shard_map/jit(_roll_static)/slice | solution.py:51
  30.3 2.9 %subtract_convert_fusion.1 = (f16[2,4,8,8,1,2,256]{6,3,5,4,2,1,0:T(8,128)(2,1)}, f16[2,4,8,8,1,2,256]{6,3,5,4,2,1,0:T(8,128)(2,1)}, f32[2,4,8,8,1,2,256]{6,3,5,4,2,1,0:T(8,128)S(1)}, f32[2,4,8,8,1,2,256]{6,3,5,4,2,1,0:T(8,128)S(1)}) fusion(f32[2,4,8,8,1,2,256]{6,3,5,4,2,1,0:T(8,128)S(1)} %bitcast.73, f32[2,1,8,8,1,2,256]{6,3,5,4,2,1,0:T(8,128)} %collective-permute-done.1, ...), kind=kLoop, calls=%fused_computation.43 | loop fusion | flops 4718592 | bytes 4721664 | tf_op jit(solution)/shard_map/convert_element_type | solution.py:127
  33.2 1.9 %collective-permute-start.3 = (f16[2,4,8,8,1,2,256]{6,3,5,4,2,1,0:T(8,128)(2,1)}, f16[2,4,8,8,1,2,256]{6,3,5,4,2,1,0:T(8,128)(2,1)}, u32[]{:S(2)}, u32[]{:S(2)}) collective-permute-start(f16[2,4,8,8,1,2,256]{6,3,5,4,2,1,0:T(8,128)(2,1)} %get-tuple-element.18), channel_id=1, source_target_pairs={{0,1},{1,2},{2,3},{3,4},{4,5},{5,6},{6,7},{7,8},{8,9},{9,10},{10,1... | collective-permute-start | bytes 1572872 | tf_op jit(solution)/shard_map/ppermute | solution.py:131
  35.1 8.4 %collective-permute-start.2 = (f16[2,4,8,8,1,2,256]{6,3,5,4,2,1,0:T(8,128)(2,1)}, f16[2,4,8,8,1,2,256]{6,3,5,4,2,1,0:T(8,128)(2,1)}, u32[]{:S(2)}, u32[]{:S(2)}) collective-permute-start(f16[2,4,8,8,1,2,256]{6,3,5,4,2,1,0:T(8,128)(2,1)} %get-tuple-element.17), channel_id=1, source_target_pairs={{1,0},{2,1},{3,2},{4,3},{5,4},{6,5},{7,6},{8,7},{9,8},{10,9},{11,1... | collective-permute-start | bytes 1572872 | tf_op jit(solution)/shard_map/ppermute | solution.py:126
  43.5 1.7 %fusion.37 = (f32[2,4,8,8,1,2,255]{6,3,5,4,2,1,0:T(8,128)}, f32[2,4,8,8,1,2,255]{6,3,5,4,2,1,0:T(8,128)}) fusion(f32[2,4,8,8,1,2,256]{6,3,5,4,2,1,0:T(8,128)S(1)} %get-tuple-element.21), kind=kLoop, calls=%fused_computation.85 | loop fusion | bytes 4177920 | tf_op jit(solution)/shard_map/jit(_roll_static)/slice | solution.py:54
  45.3 6.0 %collective-permute-start.6 = (bf16[8,120,1,128]{3,1,0,2:T(8,128)(2,1)S(1)}, bf16[8,120,1,128]{3,1,0,2:T(8,128)(2,1)S(1)}, u32[]{:S(2)}, u32[]{:S(2)}) collective-permute-start(bf16[8,120,1,128]{3,1,0,2:T(8,128)(2,1)S(1)} %bitcast.81), channel_id=1, source_target_pairs={{0,48},{16,0},{1,49},{17,1},{2,50},{18,2},{3,51},{19,3},{4,52},{20... | collective-permute-start | bytes 737288 | tf_op jit(solution)/shard_map/ppermute | solution.py:90
  51.3 1.3 %collective-permute-start.5 = (bf16[8,120,1,128]{3,1,0,2:T(8,128)(2,1)S(1)}, bf16[8,120,1,128]{3,1,0,2:T(8,128)(2,1)S(1)}, u32[]{:S(2)}, u32[]{:S(2)}) collective-permute-start(bf16[8,120,1,128]{3,1,0,2:T(8,128)(2,1)S(1)} %bitcast.82), channel_id=1, source_target_pairs={{0,32},{16,48},{1,33},{17,49},{2,34},{18,50},{3,35},{19,51},{4,36}... | collective-permute-start | bytes 737288 | tf_op jit(solution)/shard_map/ppermute | solution.py:90
  52.6 2.8 %collective-permute-start.4 = (bf16[8,120,1,128]{3,1,0,2:T(8,128)(2,1)S(1)}, bf16[8,120,1,128]{3,1,0,2:T(8,128)(2,1)S(1)}, u32[]{:S(2)}, u32[]{:S(2)}) collective-permute-start(bf16[8,120,1,128]{3,1,0,2:T(8,128)(2,1)S(1)} %bitcast.83), channel_id=1, source_target_pairs={{0,16},{16,32},{1,17},{17,33},{2,18},{18,34},{3,19},{19,35},{4,20}... | collective-permute-start | bytes 737288 | tf_op jit(solution)/shard_map/ppermute | solution.py:90
  55.4 1.2 %fusion.36 = (f32[2,4,8,8,1,2,1]{6,3,5,4,2,1,0:T(8,128)}, f32[2,4,8,8,1,2,1]{6,3,5,4,2,1,0:T(8,128)}) fusion(f32[2,4,8,8,1,2,256]{6,3,5,4,2,1,0:T(8,128)S(1)} %get-tuple-element.21), kind=kLoop, calls=%fused_computation.84 | loop fusion | bytes 16384 | tf_op jit(solution)/shard_map/jit(_roll_static)/slice | solution.py:54
  56.5 3.7 %collective-permute-done.6 = bf16[8,120,1,128]{3,1,0,2:T(8,128)(2,1)S(1)} collective-permute-done((bf16[8,120,1,128]{3,1,0,2:T(8,128)(2,1)S(1)}, bf16[8,120,1,128]{3,1,0,2:T(8,128)(2,1)S(1)}, u32[]{:S(2)}, u32[]{:S(2)}) %collective-permute-start.6) | collective-permute-done | bytes 245792 | tf_op jit(solution)/shard_map/ppermute | solution.py:90
  60.2 1.3 %collective-permute-done.4 = bf16[8,120,1,128]{3,1,0,2:T(8,128)(2,1)S(1)} collective-permute-done((bf16[8,120,1,128]{3,1,0,2:T(8,128)(2,1)S(1)}, bf16[8,120,1,128]{3,1,0,2:T(8,128)(2,1)S(1)}, u32[]{:S(2)}, u32[]{:S(2)}) %collective-permute-start.4) | collective-permute-done | bytes 245792 | tf_op jit(solution)/shard_map/ppermute | solution.py:90
  62.5 1.3 %copy.206 = bf16[64,8,8,128]{3,1,2,0:T(8,128)(2,1)} copy(bf16[64,8,8,128]{3,2,1,0:T(8,128)(2,1)S(1)} %bitcast.76) | data formatting | bytes 2097152
  64.6 7.9 %shard_map.64 = f32[30,1024]{1,0:T(8,128)} custom-call(bf16[30,128,512]{2,1,0:T(8,128)(2,1)} %pad_maximum_fusion.k_ref, bf16[512,1024]{1,0:T(8,128)(2,1)} %bitcast.77, f32[128,1024]{1,0:T(8,128)} %copy_bitcast_fusion.2.l_ref), custom_call_target="tpu_custom_call" | custom-call | tf_op jit(solution)/shard_map/pallas_call | solution.py:76
  72.5 0.9 convert_element_type.93
  74.3 8.6 %all-to-all-start.1 = ((bf16[30,16,2,128]{3,2,0,1:T(2,128)(2,1)}), bf16[30,16,2,128]{3,2,0,1:T(2,128)(2,1)S(1)}, u32[]{:S(2)}, u32[]{:S(2)}) async-start(bf16[30,16,2,128]{3,2,0,1:T(2,128)(2,1)} %bitcast.85), calls=%async_computation.1 | async-start | bytes 491520 | tf_op jit(solution)/shard_map/all_to_all | solution.py:167
  83.1 4.3 %fusion.7 = f32[2,4,8,8,1,2,256]{6,3,5,4,2,1,0:T(8,128)S(1)} fusion(f32[2,4,8,8,1,2,256]{6,3,5,4,2,1,0:T(8,128)S(1)} %bitcast.74, f32[2,4,8,8,1,2,1]{6,3,5,4,2,1,0:T(8,128)} %get-tuple-element.34, f32[2,4,8,8,1,2,255]{6,3,5,4,2,1,0:T(8,128)} %get-tuple-element.36, f32[2,4,8,8,1,2,255]{6,3,5,4,2,1,0:T(8,128)} %get-tuple-element.35, ...), kind=kLoop, calls=%fused_computation.18 | loop fusion | flops 7340032 | bytes 9437192 | tf_op jit(solution)/shard_map/sub | solution.py:142
  87.4 5.4 %all-to-all-done.1 = bf16[30,16,2,128]{3,2,0,1:T(2,128)(2,1)S(1)} async-done(((bf16[30,16,2,128]{3,2,0,1:T(2,128)(2,1)}), bf16[30,16,2,128]{3,2,0,1:T(2,128)(2,1)S(1)}, u32[]{:S(2)}, u32[]{:S(2)}) %all-to-all-start.1) | async-done | bytes 245792 | tf_op jit(solution)/shard_map/all_to_all | solution.py:167
  93.4 2.7 %gather_fusion.1 = f32[256,2,512]{2,1,0:T(2,128)} fusion(f32[120,2,512]{2,1,0:T(2,128)S(1)} %reshape.456, s32[1024]{0:T(1024)S(1)} %pad_clamp_fusion), kind=kCustom, calls=%fused_computation.1 | custom fusion | bytes 2098176 | tf_op jit(solution)/shard_map/jit(_take)/gather | solution.py:177
  96.0 4.0 %fusion.22 = f32[2,256,1,512]{3,0,1,2:T(2,128)S(1)} fusion(f32[2,256,512]{2,1,0:T(8,128)S(1)} %bitcast.75, f32[256,2,512]{2,1,0:T(2,128)} %gather_fusion.1, pred[256]{0:T(512)(128)(4,1)S(1)} %compare_and_fusion, pred[256]{0:T(512)(128)(4,1)S(1)} %gt.18, f32[2]{0:T(128)S(1)} %neg.4, f32[2,256,1,512]{3,2,1,0:T(1,128)S(1)} %copy-done), kind=kLoop, calls=%fused_computation.40 | loop fusion | flops 1310720 | bytes 4194824 | tf_op jit(solution)/shard_map/add | solution.py:185
  100.1 2.0 %copy.185 = f32[2,256,1,512]{3,2,1,0:T(1,128)} copy(f32[2,256,1,512]{3,0,1,2:T(2,128)S(1)} %fusion.22) | data formatting | bytes 2097152 | tf_op jit(solution)/shard_map/add | solution.py:185
  (50 shorter events, 5.1 us)
Async XLA Ops:
  8.9 15.1 %copy-start.3 = (s32[120]{0:T(128)S(1)}, s32[120]{0:T(128)}, u32[]{:S(2)}) copy-start(s32[120]{0:T(128)} %param.9) | copy-start | bytes 1444
  8.9 15.9 %copy-start.4 = (f32[2]{0:T(128)S(1)}, f32[2]{0:T(128)}, u32[]{:S(2)}) copy-start(f32[2]{0:T(128)} %param.10) | copy-start | bytes 28
  9.7 20.5 %collective-permute-start.1 = (f32[2,1,8,8,1,2,256]{6,3,5,4,2,1,0:T(8,128)}, f32[2,1,8,8,1,2,256]{6,3,5,4,2,1,0:T(8,128)}, u32[]{:S(2)}, u32[]{:S(2)}) collective-permute-start(f32[2,1,8,8,1,2,256]{6,3,5,4,2,1,0:T(8,128)} %get-tuple-element.24), channel_id=1, source_target_pairs={{0,16},{16,32},{32,48},{1,17},{17,33},{33,49},{2,18},{18,34},{34,5... | collective-permute-start | bytes 786440 | tf_op jit(solution)/shard_map/ppermute | solution.py:119
  13.9 16.3 %collective-permute-start = (f32[2,1,8,8,1,2,256]{6,3,5,4,2,1,0:T(8,128)}, f32[2,1,8,8,1,2,256]{6,3,5,4,2,1,0:T(8,128)}, u32[]{:S(2)}, u32[]{:S(2)}) collective-permute-start(f32[2,1,8,8,1,2,256]{6,3,5,4,2,1,0:T(8,128)} %get-tuple-element.23), channel_id=1, source_target_pairs={{16,0},{32,16},{48,32},{17,1},{33,17},{49,33},{18,2},{34,18},{50,3... | collective-permute-start | bytes 786440 | tf_op jit(solution)/shard_map/ppermute | solution.py:122
  15.2 30.0 %all-to-all-start = ((bf16[2,120,4,128]{3,0,1,2:T(2,128)(2,1)}), bf16[2,120,4,128]{3,0,1,2:T(2,128)(2,1)S(1)}, u32[]{:S(2)}, u32[]{:S(2)}) async-start(bf16[2,120,4,128]{3,0,1,2:T(2,128)(2,1)} %fusion.26), calls=%async_computation | async-start | bytes 491520 | tf_op jit(solution)/shard_map/all_to_all | solution.py:117
  22.4 4.5 %copy-start.2 = (s32[8,8]{1,0:T(8,128)S(1)}, s32[8,8]{1,0:T(8,128)}, u32[]{:S(2)}) copy-start(s32[8,8]{1,0:T(8,128)} %param.8) | copy-start | bytes 772
  22.4 4.8 %copy-start.5 = (f32[2]{0:T(128)S(1)}, f32[2]{0:T(128)}, u32[]{:S(2)}) copy-start(f32[2]{0:T(128)} %param.11) | copy-start | bytes 28
  33.2 49.9 %collective-permute-start.3 = (f16[2,4,8,8,1,2,256]{6,3,5,4,2,1,0:T(8,128)(2,1)}, f16[2,4,8,8,1,2,256]{6,3,5,4,2,1,0:T(8,128)(2,1)}, u32[]{:S(2)}, u32[]{:S(2)}) collective-permute-start(f16[2,4,8,8,1,2,256]{6,3,5,4,2,1,0:T(8,128)(2,1)} %get-tuple-element.18), channel_id=1, source_target_pairs={{0,1},{1,2},{2,3},{3,4},{4,5},{5,6},{6,7},{7,8},{8,9},{9,10},{10,1... | collective-permute-start | bytes 1572872 | tf_op jit(solution)/shard_map/ppermute | solution.py:131
  35.1 48.0 %collective-permute-start.2 = (f16[2,4,8,8,1,2,256]{6,3,5,4,2,1,0:T(8,128)(2,1)}, f16[2,4,8,8,1,2,256]{6,3,5,4,2,1,0:T(8,128)(2,1)}, u32[]{:S(2)}, u32[]{:S(2)}) collective-permute-start(f16[2,4,8,8,1,2,256]{6,3,5,4,2,1,0:T(8,128)(2,1)} %get-tuple-element.17), channel_id=1, source_target_pairs={{1,0},{2,1},{3,2},{4,3},{5,4},{6,5},{7,6},{8,7},{9,8},{10,9},{11,1... | collective-permute-start | bytes 1572872 | tf_op jit(solution)/shard_map/ppermute | solution.py:126
  45.3 14.9 %collective-permute-start.6 = (bf16[8,120,1,128]{3,1,0,2:T(8,128)(2,1)S(1)}, bf16[8,120,1,128]{3,1,0,2:T(8,128)(2,1)S(1)}, u32[]{:S(2)}, u32[]{:S(2)}) collective-permute-start(bf16[8,120,1,128]{3,1,0,2:T(8,128)(2,1)S(1)} %bitcast.81), channel_id=1, source_target_pairs={{0,48},{16,0},{1,49},{17,1},{2,50},{18,2},{3,51},{19,3},{4,52},{20... | collective-permute-start | bytes 737288 | tf_op jit(solution)/shard_map/ppermute | solution.py:90
  51.3 8.9 %collective-permute-start.5 = (bf16[8,120,1,128]{3,1,0,2:T(8,128)(2,1)S(1)}, bf16[8,120,1,128]{3,1,0,2:T(8,128)(2,1)S(1)}, u32[]{:S(2)}, u32[]{:S(2)}) collective-permute-start(bf16[8,120,1,128]{3,1,0,2:T(8,128)(2,1)S(1)} %bitcast.82), channel_id=1, source_target_pairs={{0,32},{16,48},{1,33},{17,49},{2,34},{18,50},{3,35},{19,51},{4,36}... | collective-permute-start | bytes 737288 | tf_op jit(solution)/shard_map/ppermute | solution.py:90
  52.6 8.9 %collective-permute-start.4 = (bf16[8,120,1,128]{3,1,0,2:T(8,128)(2,1)S(1)}, bf16[8,120,1,128]{3,1,0,2:T(8,128)(2,1)S(1)}, u32[]{:S(2)}, u32[]{:S(2)}) collective-permute-start(bf16[8,120,1,128]{3,1,0,2:T(8,128)(2,1)S(1)} %bitcast.83), channel_id=1, source_target_pairs={{0,16},{16,32},{1,17},{17,33},{2,18},{18,34},{3,19},{19,35},{4,20}... | collective-permute-start | bytes 737288 | tf_op jit(solution)/shard_map/ppermute | solution.py:90
  64.6 18.5 %copy-start.1 = (f32[2,4,8,8,1,2,255]{6,3,5,4,2,1,0:T(8,128)S(1)}, f32[2,4,8,8,1,2,255]{6,3,5,4,2,1,0:T(8,128)}, u32[]{:S(2)}) copy-start(f32[2,4,8,8,1,2,255]{6,3,5,4,2,1,0:T(8,128)} %get-tuple-element.31) | copy-start | bytes 3133444
  74.3 18.4 %all-to-all-start.1 = ((bf16[30,16,2,128]{3,2,0,1:T(2,128)(2,1)}), bf16[30,16,2,128]{3,2,0,1:T(2,128)(2,1)S(1)}, u32[]{:S(2)}, u32[]{:S(2)}) async-start(bf16[30,16,2,128]{3,2,0,1:T(2,128)(2,1)} %bitcast.85), calls=%async_computation.1 | async-start | bytes 491520 | tf_op jit(solution)/shard_map/all_to_all | solution.py:167
  87.4 8.7 %copy-start = (f32[2,256,1,512]{3,2,1,0:T(1,128)S(1)}, f32[2,256,1,512]{3,2,1,0:T(1,128)}, u32[]{:S(2)}) copy-start(f32[2,256,1,512]{3,2,1,0:T(1,128)} %param.6) | copy-start | bytes 3145732

commit v11 on v9

--- a/solution.py
+++ b/solution.py
@@ -105,9 +105,13 @@
 
     phase_field = distribution.reshape(own_count, per_vx, NVY, NVZ, row_count, NZ, NY)
     below = lax.ppermute(
-        phase_field[:, per_vx - 1 :], "mode", [(i, i + 1) for i in range(mode_devs - 1)]
-    )
-    above = lax.ppermute(phase_field[:, :1], "mode", [(i + 1, i) for i in range(mode_devs - 1)])
+        phase_field[:, per_vx - 1 :].astype(jnp.float16),
+        "mode",
+        [(i, i + 1) for i in range(mode_devs - 1)],
+    ).astype(jnp.float32)
+    above = lax.ppermute(
+        phase_field[:, :1].astype(jnp.float16), "mode", [(i + 1, i) for i in range(mode_devs - 1)]
+    ).astype(jnp.float32)
     flux_x = flux_from_padded(jnp.concatenate([below, phase_field, above], axis=1), 1, first_vx)
     up_part = 0.5 * flux_x - 0.5 * bound_x * phase_field
     down_part = -0.5 * flux_x - 0.5 * bound_x * phase_field

time: 102 us -> 101 us (level)
  other arithmetic: 21.3 us -> 22.8 us
  local copies, waits for them, and re-layouts: 20.9 us -> 19.6 us
    unnamed x15 -> x17, local copies, waits for them, and re-layouts: 3.5 us -> 2.34 us
  transfers between devices with their start and end apart: 9 -> 9, of which waited for: 3 -> 3; matrix products, arithmetic and copies ran while one was open for 28% -> 29% of each run, Pallas kernels for 8% -> 8%
where the time goes in v11:
time: 101 us
  starting transfers between devices  39.7 us (39%)
  other arithmetic  22.8 us (23%)
  local copies, waits for them, and re-layouts  19.6 us (19%)
  waiting for transfers between devices  10 us (10%)
  Pallas kernels  7.81 us (8%)
    ppermute x3, starting transfers between devices, shift_permutes(): received.append((shift, lax.ppermute(values, axis, pairs)))  10.1 us
    all_to_all x1, starting transfers between devices, per_device(): lax.all_to_all(gained.astype(jnp.bfloat16), ('species', 'mode'), 1, 1, ti...  8.58 us
    ppermute x1, starting transfers between devices, per_device(): lax.ppermute(up_part[:, :, :, :, :1].astype(jnp.float16), 'space', [(i +...  8.45 us
    pallas_call x1, Pallas kernels, collide_call(): pl.pallas_call(collide_body, out_shape=jax.ShapeDtypeStruct((kcat.shape[0...  7.81 us
    all_to_all x1, starting transfers between devices, per_device(): spread = lax.all_to_all(picked, 'species', 2, 0, tiled=True)  5.89 us
    all_to_all x1, waiting for transfers between devices, per_device(): lax.all_to_all(gained.astype(jnp.bfloat16), ('species', 'mode'), 1, 1, ti...  5.09 us
    ppermute x3, waiting for transfers between devices, shift_permutes(): received.append((shift, lax.ppermute(values, axis, pairs)))  4.92 us
    sub x1, other arithmetic, per_device(): phase_field - nu_step * thermal_speed.reshape(own_count, 1, 1, 1, 1, 1, 1...  4.59 us
  transfers between devices with their start and end apart: 9, of which 3 were waited for; matrix products, arithmetic and copies ran while one was open for 29% of the time, Pallas kernels for 8%

profile of v11, /device:TPU:2, one launch (start us, length us, event | category | flops | bytes accessed | tf_op | source)
XLA Modules:
  0.0 100.6 jit_solution(6370014370682064122)
XLA Ops:
  0.0 3.8 %reduce.18 = f32[2,256,512]{2,1,0:T(8,128)S(1)} reduce(f32[2,256,1,512]{3,2,1,0:T(1,128)} %param.6, f32[]{:T(128)} %constant.93), dimensions={2}, to_apply=%param.6.reduce_sub_computation | reduce | bytes 2097156 | tf_op args[0]
  4.6 3.5 %collective-permute-start.1 = (f16[2,1,8,8,1,2,256]{6,3,5,4,2,1,0:T(8,128)(2,1)}, f16[2,1,8,8,1,2,256]{6,3,5,4,2,1,0:T(8,128)(2,1)S(1)}, u32[]{:S(2)}, u32[]{:S(2)}) collective-permute-start(f16[2,1,8,8,1,2,256]{6,3,5,4,2,1,0:T(8,128)(2,1)} %get-tuple-element.32), channel_id=1, source_target_pairs={{0,16},{16,32},{32,48},{1,17},{17,33},{33,49},{2,18},{18,34},{34,5... | collective-permute-start | bytes 393224 | tf_op jit(solution)/shard_map/ppermute | solution.py:107
  8.1 1.3 %collective-permute-start = (f16[2,1,8,8,1,2,256]{6,3,5,4,2,1,0:T(8,128)(2,1)S(1)}, f16[2,1,8,8,1,2,256]{6,3,5,4,2,1,0:T(8,128)(2,1)S(1)}, u32[]{:S(2)}, u32[]{:S(2)}) collective-permute-start(f16[2,1,8,8,1,2,256]{6,3,5,4,2,1,0:T(8,128)(2,1)S(1)} %get-tuple-element.31), channel_id=1, source_target_pairs={{16,0},{32,16},{48,32},{17,1},{33,17},{49,33},{18,2},{34,18},{50,3... | collective-permute-start | bytes 393224 | tf_op jit(solution)/shard_map/ppermute | solution.py:112
  10.3 1.1 %gather_fusion = bf16[120,2,512]{2,1,0:T(2,128)(2,1)S(1)} fusion(bf16[2,256,512]{2,0,1:T(2,128)(2,1)S(1)} %bitcast.80, s32[1024]{0:T(1024)S(1)} %pad_clamp_fusion.1), kind=kCustom, calls=%fused_computation | custom fusion | bytes 492000 | tf_op jit(solution)/shard_map/jit(_take)/gather | solution.py:142
  11.4 1.4 %fusion.26 = bf16[2,120,4,128]{3,0,1,2:T(2,128)(2,1)} fusion(pred[120]{0:T(512)(128)(4,1)S(1)} %get-tuple-element.9, pred[120]{0:T(512)(128)(4,1)S(1)} %get-tuple-element.39, bf16[120,2,512]{2,1,0:T(2,128)(2,1)S(1)} %gather_fusion), kind=kLoop, calls=%fused_computation.52 | loop fusion | flops 245760 | bytes 491760 | tf_op jit(solution)/shard_map/convert_element_type | solution.py:142
  12.8 5.9 %all-to-all-start = ((bf16[2,120,4,128]{3,0,1,2:T(2,128)(2,1)}), bf16[2,120,4,128]{3,0,1,2:T(2,128)(2,1)S(1)}, u32[]{:S(2)}, u32[]{:S(2)}) async-start(bf16[2,120,4,128]{3,0,1,2:T(2,128)(2,1)} %fusion.26), calls=%async_computation | async-start | bytes 491520 | tf_op jit(solution)/shard_map/all_to_all | solution.py:146
  18.6 1.1 %fusion.33 = (f32[2,4,8,8,1,2,1]{6,3,5,4,2,1,0:T(8,128)}, f32[2,4,8,8,1,2,1]{6,3,5,4,2,1,0:T(8,128)}) fusion(f32[2,4,8,8,1,2,256]{6,3,5,4,2,1,0:T(8,128)S(1)} %bitcast.70), kind=kLoop, calls=%fused_computation.81 | loop fusion | bytes 16384 | tf_op jit(solution)/shard_map/jit(_roll_static)/slice | solution.py:52
  19.8 1.7 %fusion.34 = (f32[2,4,8,8,1,2,255]{6,3,5,4,2,1,0:T(8,128)}, f32[2,4,8,8,1,2,255]{6,3,5,4,2,1,0:T(8,128)}) fusion(f32[2,4,8,8,1,2,256]{6,3,5,4,2,1,0:T(8,128)S(1)} %bitcast.71), kind=kLoop, calls=%fused_computation.82 | loop fusion | bytes 4177920 | tf_op jit(solution)/shard_map/jit(_roll_static)/slice | solution.py:52
  21.4 1.1 %fusion.31 = (f32[2,4,8,8,1,1,256]{6,3,5,4,2,1,0:T(8,128)}, f32[2,4,8,8,1,1,256]{6,3,5,4,2,1,0:T(8,128)}) fusion(f32[2,4,8,8,1,2,256]{6,3,5,4,2,1,0:T(8,128)S(1)} %bitcast.72), kind=kLoop, calls=%fused_computation.79 | loop fusion | bytes 2097152 | tf_op jit(solution)/shard_map/jit(_roll_static)/slice | solution.py:51
  24.3 2.0 %fusion.23 = (bf16[30,128,128]{2,1,0:T(8,128)(2,1)S(1)}, bf16[30,128,128]{2,1,0:T(8,128)(2,1)S(1)}) fusion(bf16[2,30,120,120]{3,2,1,0:T(8,128)(2,1)} %param.7), kind=kLoop, calls=%fused_computation.44 | loop fusion | bytes 3694080 | tf_op jit(solution)/shard_map/squeeze | solution.py:163
  26.5 2.0 %pad_maximum_fusion.k_ref = bf16[30,128,512]{2,1,0:T(8,128)(2,1)} fusion(bf16[30,128,128]{2,1,0:T(8,128)(2,1)S(1)} %get-tuple-element.12, bf16[30,128,128]{2,1,0:T(8,128)(2,1)S(1)} %get-tuple-element.11), kind=kLoop, calls=%fused_computation.2 | loop fusion | flops 15728640 | bytes 5898240 | tf_op jit(solution)/shard_map/concatenate | solution.py:163
  28.8 2.8 %subtract_convert_fusion.1 = (f16[2,4,8,8,1,2,256]{6,3,5,4,2,1,0:T(8,128)(2,1)}, f16[2,4,8,8,1,2,256]{6,3,5,4,2,1,0:T(8,128)(2,1)}, f32[2,4,8,8,1,2,256]{6,3,5,4,2,1,0:T(8,128)S(1)}, f32[2,4,8,8,1,2,256]{6,3,5,4,2,1,0:T(8,128)}) fusion(f32[2,4,8,8,1,2,256]{6,3,5,4,2,1,0:T(8,128)S(1)} %bitcast.73, f32[2,1,8,8,1,2,256]{6,3,5,4,2,1,0:T(8,128)S(1)} %convert_element_type.93, ...), kind=kLoop, calls=%fused_computation.43 | loop fusion | flops 4718592 | bytes 4720672 | tf_op jit(solution)/shard_map/convert_element_type | solution.py:119
  31.6 1.9 %collective-permute-start.3 = (f16[2,4,8,8,1,2,256]{6,3,5,4,2,1,0:T(8,128)(2,1)}, f16[2,4,8,8,1,2,256]{6,3,5,4,2,1,0:T(8,128)(2,1)}, u32[]{:S(2)}, u32[]{:S(2)}) collective-permute-start(f16[2,4,8,8,1,2,256]{6,3,5,4,2,1,0:T(8,128)(2,1)} %get-tuple-element.14), channel_id=1, source_target_pairs={{0,1},{1,2},{2,3},{3,4},{4,5},{5,6},{6,7},{7,8},{8,9},{9,10},{10,1... | collective-permute-start | bytes 1572872 | tf_op jit(solution)/shard_map/ppermute | solution.py:123
  33.5 8.4 %collective-permute-start.2 = (f16[2,4,8,8,1,2,256]{6,3,5,4,2,1,0:T(8,128)(2,1)}, f16[2,4,8,8,1,2,256]{6,3,5,4,2,1,0:T(8,128)(2,1)}, u32[]{:S(2)}, u32[]{:S(2)}) collective-permute-start(f16[2,4,8,8,1,2,256]{6,3,5,4,2,1,0:T(8,128)(2,1)} %get-tuple-element.13), channel_id=1, source_target_pairs={{1,0},{2,1},{3,2},{4,3},{5,4},{6,5},{7,6},{8,7},{9,8},{10,9},{11,1... | collective-permute-start | bytes 1572872 | tf_op jit(solution)/shard_map/ppermute | solution.py:118
  42.0 1.7 %fusion.36 = (f32[2,4,8,8,1,2,255]{6,3,5,4,2,1,0:T(8,128)}, f32[2,4,8,8,1,2,255]{6,3,5,4,2,1,0:T(8,128)}) fusion(f32[2,4,8,8,1,2,256]{6,3,5,4,2,1,0:T(8,128)S(1)} %get-tuple-element.17), kind=kLoop, calls=%fused_computation.84 | loop fusion | bytes 4177920 | tf_op jit(solution)/shard_map/jit(_roll_static)/slice | solution.py:54
  43.7 6.0 %collective-permute-start.6 = (bf16[8,120,1,128]{3,1,0,2:T(8,128)(2,1)S(1)}, bf16[8,120,1,128]{3,1,0,2:T(8,128)(2,1)S(1)}, u32[]{:S(2)}, u32[]{:S(2)}) collective-permute-start(bf16[8,120,1,128]{3,1,0,2:T(8,128)(2,1)S(1)} %bitcast.81), channel_id=1, source_target_pairs={{0,48},{16,0},{1,49},{17,1},{2,50},{18,2},{3,51},{19,3},{4,52},{20... | collective-permute-start | bytes 737288 | tf_op jit(solution)/shard_map/ppermute | solution.py:90
  49.7 1.3 %collective-permute-start.5 = (bf16[8,120,1,128]{3,1,0,2:T(8,128)(2,1)S(1)}, bf16[8,120,1,128]{3,1,0,2:T(8,128)(2,1)S(1)}, u32[]{:S(2)}, u32[]{:S(2)}) collective-permute-start(bf16[8,120,1,128]{3,1,0,2:T(8,128)(2,1)S(1)} %bitcast.82), channel_id=1, source_target_pairs={{0,32},{16,48},{1,33},{17,49},{2,34},{18,50},{3,35},{19,51},{4,36}... | collective-permute-start | bytes 737288 | tf_op jit(solution)/shard_map/ppermute | solution.py:90
  51.0 2.8 %collective-permute-start.4 = (bf16[8,120,1,128]{3,1,0,2:T(8,128)(2,1)S(1)}, bf16[8,120,1,128]{3,1,0,2:T(8,128)(2,1)S(1)}, u32[]{:S(2)}, u32[]{:S(2)}) collective-permute-start(bf16[8,120,1,128]{3,1,0,2:T(8,128)(2,1)S(1)} %bitcast.83), channel_id=1, source_target_pairs={{0,16},{16,32},{1,17},{17,33},{2,18},{18,34},{3,19},{19,35},{4,20}... | collective-permute-start | bytes 737288 | tf_op jit(solution)/shard_map/ppermute | solution.py:90
  53.8 1.2 %fusion.35 = (f32[2,4,8,8,1,2,1]{6,3,5,4,2,1,0:T(8,128)}, f32[2,4,8,8,1,2,1]{6,3,5,4,2,1,0:T(8,128)}) fusion(f32[2,4,8,8,1,2,256]{6,3,5,4,2,1,0:T(8,128)S(1)} %get-tuple-element.17), kind=kLoop, calls=%fused_computation.83 | loop fusion | bytes 16384 | tf_op jit(solution)/shard_map/jit(_roll_static)/slice | solution.py:54
  55.0 3.6 %collective-permute-done.6 = bf16[8,120,1,128]{3,1,0,2:T(8,128)(2,1)S(1)} collective-permute-done((bf16[8,120,1,128]{3,1,0,2:T(8,128)(2,1)S(1)}, bf16[8,120,1,128]{3,1,0,2:T(8,128)(2,1)S(1)}, u32[]{:S(2)}, u32[]{:S(2)}) %collective-permute-start.6) | collective-permute-done | bytes 245792 | tf_op jit(solution)/shard_map/ppermute | solution.py:90
  58.6 1.3 %collective-permute-done.4 = bf16[8,120,1,128]{3,1,0,2:T(8,128)(2,1)S(1)} collective-permute-done((bf16[8,120,1,128]{3,1,0,2:T(8,128)(2,1)S(1)}, bf16[8,120,1,128]{3,1,0,2:T(8,128)(2,1)S(1)}, u32[]{:S(2)}, u32[]{:S(2)}) %collective-permute-start.4) | collective-permute-done | bytes 245792 | tf_op jit(solution)/shard_map/ppermute | solution.py:90
  60.9 1.3 %copy.199 = bf16[64,8,8,128]{3,1,2,0:T(8,128)(2,1)} copy(bf16[64,8,8,128]{3,2,1,0:T(8,128)(2,1)S(1)} %bitcast.76) | data formatting | bytes 2097152
  62.3 0.9 copy_bitcast_fusion.2.l_ref
  63.1 7.8 %shard_map.64 = f32[30,1024]{1,0:T(8,128)} custom-call(bf16[30,128,512]{2,1,0:T(8,128)(2,1)} %pad_maximum_fusion.k_ref, bf16[512,1024]{1,0:T(8,128)(2,1)} %bitcast.77, f32[128,1024]{1,0:T(8,128)} %copy_bitcast_fusion.2.l_ref), custom_call_target="tpu_custom_call" | custom-call | tf_op jit(solution)/shard_map/pallas_call | solution.py:76
  70.9 0.9 convert_element_type.103
  71.9 0.8 broadcast_in_dim.62
  72.8 8.6 %all-to-all-start.1 = ((bf16[30,16,2,128]{3,2,0,1:T(2,128)(2,1)}), bf16[30,16,2,128]{3,2,0,1:T(2,128)(2,1)S(1)}, u32[]{:S(2)}, u32[]{:S(2)}) async-start(bf16[30,16,2,128]{3,2,0,1:T(2,128)(2,1)} %bitcast.85), calls=%async_computation.1 | async-start | bytes 491520 | tf_op jit(solution)/shard_map/all_to_all | solution.py:170
  81.5 4.6 %fusion.7 = f32[2,4,8,8,1,2,256]{6,3,5,4,2,1,0:T(8,128)S(1)} fusion(f32[2,4,8,8,1,2,256]{6,3,5,4,2,1,0:T(8,128)S(1)} %bitcast.74, f32[2,4,8,8,1,2,1]{6,3,5,4,2,1,0:T(8,128)} %get-tuple-element.28, f32[2,4,8,8,1,2,255]{6,3,5,4,2,1,0:T(8,128)} %get-tuple-element.30, f32[2,4,8,8,1,2,255]{6,3,5,4,2,1,0:T(8,128)} %get-tuple-element.29, ...), kind=kLoop, calls=%fused_computation.18 | loop fusion | flops 7340032 | bytes 9437192 | tf_op jit(solution)/shard_map/sub | solution.py:134
  86.1 5.1 %all-to-all-done.1 = bf16[30,16,2,128]{3,2,0,1:T(2,128)(2,1)S(1)} async-done(((bf16[30,16,2,128]{3,2,0,1:T(2,128)(2,1)}), bf16[30,16,2,128]{3,2,0,1:T(2,128)(2,1)S(1)}, u32[]{:S(2)}, u32[]{:S(2)}) %all-to-all-start.1) | async-done | bytes 245792 | tf_op jit(solution)/shard_map/all_to_all | solution.py:170
  91.8 2.7 %gather_fusion.1 = f32[256,2,512]{2,1,0:T(2,128)} fusion(f32[120,2,512]{2,1,0:T(2,128)S(1)} %reshape.456, s32[1024]{0:T(1024)S(1)} %pad_clamp_fusion), kind=kCustom, calls=%fused_computation.1 | custom fusion | bytes 2098176 | tf_op jit(solution)/shard_map/jit(_take)/gather | solution.py:180
  94.5 4.0 %fusion.22 = f32[2,256,1,512]{3,0,1,2:T(2,128)S(1)} fusion(f32[2,256,512]{2,1,0:T(8,128)S(1)} %bitcast.75, f32[256,2,512]{2,1,0:T(2,128)} %gather_fusion.1, pred[256]{0:T(512)(128)(4,1)S(1)} %compare_and_fusion.2, pred[256]{0:T(512)(128)(4,1)S(1)} %gt.18, f32[2]{0:T(128)S(1)} %neg.4, f32[2,256,1,512]{3,2,1,0:T(1,128)S(1)} %copy-done), kind=kLoop, calls=%fused_computation.40 | loop fusion | flops 1310720 | bytes 4194824 | tf_op jit(solution)/shard_map/add | solution.py:188
  98.5 2.0 %copy.178 = f32[2,256,1,512]{3,2,1,0:T(1,128)} copy(f32[2,256,1,512]{3,0,1,2:T(2,128)S(1)} %fusion.22) | data formatting | bytes 2097152 | tf_op jit(solution)/shard_map/add | solution.py:188
  (55 shorter events, 5.5 us)
Async XLA Ops:
  0.0 9.4 %copy-start = (f32[2,256,1,512]{3,2,1,0:T(1,128)S(1)}, f32[2,256,1,512]{3,2,1,0:T(1,128)}, u32[]{:S(2)}) copy-start(f32[2,256,1,512]{3,2,1,0:T(1,128)} %param.6) | copy-start | bytes 3145732
  0.0 10.3 %copy-start.3 = (s32[120]{0:T(128)S(1)}, s32[120]{0:T(128)}, u32[]{:S(2)}) copy-start(s32[120]{0:T(128)} %param.9) | copy-start | bytes 1444
  4.6 24.1 %collective-permute-start.1 = (f16[2,1,8,8,1,2,256]{6,3,5,4,2,1,0:T(8,128)(2,1)}, f16[2,1,8,8,1,2,256]{6,3,5,4,2,1,0:T(8,128)(2,1)S(1)}, u32[]{:S(2)}, u32[]{:S(2)}) collective-permute-start(f16[2,1,8,8,1,2,256]{6,3,5,4,2,1,0:T(8,128)(2,1)} %get-tuple-element.32), channel_id=1, source_target_pairs={{0,16},{16,32},{32,48},{1,17},{17,33},{33,49},{2,18},{18,34},{34,5... | collective-permute-start | bytes 393224 | tf_op jit(solution)/shard_map/ppermute | solution.py:107
  8.1 20.6 %collective-permute-start = (f16[2,1,8,8,1,2,256]{6,3,5,4,2,1,0:T(8,128)(2,1)S(1)}, f16[2,1,8,8,1,2,256]{6,3,5,4,2,1,0:T(8,128)(2,1)S(1)}, u32[]{:S(2)}, u32[]{:S(2)}) collective-permute-start(f16[2,1,8,8,1,2,256]{6,3,5,4,2,1,0:T(8,128)(2,1)S(1)} %get-tuple-element.31), channel_id=1, source_target_pairs={{16,0},{32,16},{48,32},{17,1},{33,17},{49,33},{18,2},{34,18},{50,3... | collective-permute-start | bytes 393224 | tf_op jit(solution)/shard_map/ppermute | solution.py:112
  12.8 30.9 %all-to-all-start = ((bf16[2,120,4,128]{3,0,1,2:T(2,128)(2,1)}), bf16[2,120,4,128]{3,0,1,2:T(2,128)(2,1)S(1)}, u32[]{:S(2)}, u32[]{:S(2)}) async-start(bf16[2,120,4,128]{3,0,1,2:T(2,128)(2,1)} %fusion.26), calls=%async_computation | async-start | bytes 491520 | tf_op jit(solution)/shard_map/all_to_all | solution.py:146
  18.6 5.1 %copy-start.5 = (f32[2]{0:T(128)S(1)}, f32[2]{0:T(128)}, u32[]{:S(2)}) copy-start(f32[2]{0:T(128)} %param.10) | copy-start | bytes 28
  21.4 4.9 %copy-start.2 = (s32[8,8]{1,0:T(8,128)S(1)}, s32[8,8]{1,0:T(8,128)}, u32[]{:S(2)}) copy-start(s32[8,8]{1,0:T(8,128)} %param.8) | copy-start | bytes 772
  24.3 4.3 %copy-start.6 = (f32[2]{0:T(128)S(1)}, f32[2]{0:T(128)}, u32[]{:S(2)}) copy-start(f32[2]{0:T(128)} %param.11) | copy-start | bytes 28
  31.6 49.9 %collective-permute-start.3 = (f16[2,4,8,8,1,2,256]{6,3,5,4,2,1,0:T(8,128)(2,1)}, f16[2,4,8,8,1,2,256]{6,3,5,4,2,1,0:T(8,128)(2,1)}, u32[]{:S(2)}, u32[]{:S(2)}) collective-permute-start(f16[2,4,8,8,1,2,256]{6,3,5,4,2,1,0:T(8,128)(2,1)} %get-tuple-element.14), channel_id=1, source_target_pairs={{0,1},{1,2},{2,3},{3,4},{4,5},{5,6},{6,7},{7,8},{8,9},{9,10},{10,1... | collective-permute-start | bytes 1572872 | tf_op jit(solution)/shard_map/ppermute | solution.py:123
  33.5 48.0 %collective-permute-start.2 = (f16[2,4,8,8,1,2,256]{6,3,5,4,2,1,0:T(8,128)(2,1)}, f16[2,4,8,8,1,2,256]{6,3,5,4,2,1,0:T(8,128)(2,1)}, u32[]{:S(2)}, u32[]{:S(2)}) collective-permute-start(f16[2,4,8,8,1,2,256]{6,3,5,4,2,1,0:T(8,128)(2,1)} %get-tuple-element.13), channel_id=1, source_target_pairs={{1,0},{2,1},{3,2},{4,3},{5,4},{6,5},{7,6},{8,7},{9,8},{10,9},{11,1... | collective-permute-start | bytes 1572872 | tf_op jit(solution)/shard_map/ppermute | solution.py:118
  43.7 14.9 %collective-permute-start.6 = (bf16[8,120,1,128]{3,1,0,2:T(8,128)(2,1)S(1)}, bf16[8,120,1,128]{3,1,0,2:T(8,128)(2,1)S(1)}, u32[]{:S(2)}, u32[]{:S(2)}) collective-permute-start(bf16[8,120,1,128]{3,1,0,2:T(8,128)(2,1)S(1)} %bitcast.81), channel_id=1, source_target_pairs={{0,48},{16,0},{1,49},{17,1},{2,50},{18,2},{3,51},{19,3},{4,52},{20... | collective-permute-start | bytes 737288 | tf_op jit(solution)/shard_map/ppermute | solution.py:90
  49.7 8.9 %collective-permute-start.5 = (bf16[8,120,1,128]{3,1,0,2:T(8,128)(2,1)S(1)}, bf16[8,120,1,128]{3,1,0,2:T(8,128)(2,1)S(1)}, u32[]{:S(2)}, u32[]{:S(2)}) collective-permute-start(bf16[8,120,1,128]{3,1,0,2:T(8,128)(2,1)S(1)} %bitcast.82), channel_id=1, source_target_pairs={{0,32},{16,48},{1,33},{17,49},{2,34},{18,50},{3,35},{19,51},{4,36}... | collective-permute-start | bytes 737288 | tf_op jit(solution)/shard_map/ppermute | solution.py:90
  51.0 8.9 %collective-permute-start.4 = (bf16[8,120,1,128]{3,1,0,2:T(8,128)(2,1)S(1)}, bf16[8,120,1,128]{3,1,0,2:T(8,128)(2,1)S(1)}, u32[]{:S(2)}, u32[]{:S(2)}) collective-permute-start(bf16[8,120,1,128]{3,1,0,2:T(8,128)(2,1)S(1)} %bitcast.83), channel_id=1, source_target_pairs={{0,16},{16,32},{1,17},{17,33},{2,18},{18,34},{3,19},{19,35},{4,20}... | collective-permute-start | bytes 737288 | tf_op jit(solution)/shard_map/ppermute | solution.py:90
  62.3 19.1 %copy-start.1 = (f32[2,4,8,8,1,2,256]{6,3,5,4,2,1,0:T(8,128)S(1)}, f32[2,4,8,8,1,2,256]{6,3,5,4,2,1,0:T(8,128)}, u32[]{:S(2)}) copy-start(f32[2,4,8,8,1,2,256]{6,3,5,4,2,1,0:T(8,128)} %get-tuple-element.18) | copy-start | bytes 3145732
  63.1 18.4 %copy-start.4 = (f32[2]{0:T(128)S(1)}, f32[2]{0:T(128)}, u32[]{:S(2)}) copy-start(f32[2]{0:T(128)} %broadcast_multiply_fusion) | copy-start | bytes 28
  72.8 18.4 %all-to-all-start.1 = ((bf16[30,16,2,128]{3,2,0,1:T(2,128)(2,1)}), bf16[30,16,2,128]{3,2,0,1:T(2,128)(2,1)S(1)}, u32[]{:S(2)}, u32[]{:S(2)}) async-start(bf16[30,16,2,128]{3,2,0,1:T(2,128)(2,1)} %bitcast.85), calls=%async_computation.1 | async-start | bytes 491520 | tf_op jit(solution)/shard_map/all_to_all | solution.py:170

commit v12 on v10

--- a/solution.py
+++ b/solution.py
@@ -103,6 +103,18 @@
     out_rows = kernel.shape[1]
     species_all = own_count * species_devs
 
+    phase_field = distribution.reshape(own_count, per_vx, NVY, NVZ, row_count, NZ, NY)
+    below = lax.ppermute(
+        phase_field[:, per_vx - 1 :].astype(jnp.float16),
+        "mode",
+        [(i, i + 1) for i in range(mode_devs - 1)],
+    ).astype(jnp.float32)
+    above = lax.ppermute(
+        phase_field[:, :1].astype(jnp.float16), "mode", [(i + 1, i) for i in range(mode_devs - 1)]
+    ).astype(jnp.float32)
+    flux_x = flux_from_padded(jnp.concatenate([below, phase_field, above], axis=1), 1, first_vx)
+    up_part = 0.5 * flux_x - 0.5 * bound_x * phase_field
+    down_part = -0.5 * flux_x - 0.5 * bound_x * phase_field
     cell_count = row_count * plane_cells
     block_cells = cell_count // species_devs
     flat_dist = distribution.reshape(own_count, mode_count, cell_count)
@@ -113,16 +125,8 @@
         jnp.bfloat16
     )
     picked = picked.reshape(own_count, low_count, species_devs, block_cells)
-    picked, distribution = lax.optimization_barrier((picked, distribution))
     spread = lax.all_to_all(picked, "species", 2, 0, tiled=True)
-    phase_field = distribution.reshape(own_count, per_vx, NVY, NVZ, row_count, NZ, NY)
-    below = lax.ppermute(
-        phase_field[:, per_vx - 1 :], "mode", [(i, i + 1) for i in range(mode_devs - 1)]
-    )
-    above = lax.ppermute(phase_field[:, :1], "mode", [(i + 1, i) for i in range(mode_devs - 1)])
-    flux_x = flux_from_padded(jnp.concatenate([below, phase_field, above], axis=1), 1, first_vx)
-    up_part = 0.5 * flux_x - 0.5 * bound_x * phase_field
-    down_part = -0.5 * flux_x - 0.5 * bound_x * phase_field
+    up_part, down_part, spread = lax.optimization_barrier((up_part, down_part, spread))
     from_next = lax.ppermute(
         up_part[:, :, :, :, :1].astype(jnp.float16),
         "space",
@@ -133,6 +137,7 @@
         "space",
         [(i, i + 1) for i in range(space_devs - 1)],
     ).astype(jnp.float32)
+    holders = [h for h in range(mode_devs) if h * per_vx <= DEG]
     up_all = jnp.concatenate([up_part[:, :, :, :, 1:], from_next], axis=4)
     down_all = jnp.concatenate([from_prev, down_part[:, :, :, :, : row_count - 1]], axis=4)
     x_term = up_all + down_all + bound_x * phase_field
@@ -141,7 +146,6 @@
     stream = x_term + y_term + z_term
     advected = phase_field - nu_step * thermal_speed.reshape(own_count, 1, 1, 1, 1, 1, 1) * stream
 
-    holders = [h for h in range(mode_devs) if h * per_vx <= DEG]
     low_all = spread
     for _, got in shift_permutes(spread, "mode", holders, mode_devs, False):
         low_all = low_all + got

time: 103 us -> 96.1 us (0.933)
  waiting for transfers between devices: 10.4 us -> 5.11 us
  other arithmetic: 22 us -> 26 us
  starting transfers between devices: 40.4 us -> 36.4 us
  local copies, waits for them, and re-layouts: 20.9 us -> 19.4 us
    ppermute x3, waiting for transfers between devices: 4.96 us -> 0.01 us  [shift_permutes(): received.append((shift, lax.ppermute(values, axis, pairs)))]
    unnamed x0 -> x1, other arithmetic: none -> 3.79 us
    optimization_barrier x1 -> x0, other arithmetic: 3.72 us -> none  [per_device(): picked, distribution = lax.optimization_barrier((picked, distribution))]
    all_to_all x1, starting transfers between devices: 8.59 us -> 5.21 us  [per_device(): lax.all_to_all(gained.astype(jnp.bfloat16), ('species', 'mode'), 1, 1, ti...]
    sub x0 -> x1, other arithmetic: none -> 2.93 us  [per_device(): down_part = -0.5 * flux_x - 0.5 * bound_x * phase_field]
    convert_element_type x0 -> x3, other arithmetic: none -> 2.17 us  [the longest x1 2.13 us: per_device(): down_part[:, :, :, :, row_count - 1:].astype(jnp.float16)]
    convert_element_type x1, other arithmetic: 2.89 us -> 0.9 us  [per_device(): up_part[:, :, :, :, :1].astype(jnp.float16)]
    unnamed x15 -> x19, local copies, waits for them, and re-layouts: 3.5 us -> 2.26 us
  transfers between devices with their start and end apart: 9 -> 9, of which waited for: 3 -> 1; matrix products, arithmetic and copies ran while one was open for 24% -> 33% of each run, Pallas kernels for 8% -> 8%
where the time goes in v12:
time: 96.1 us; the launch traced here: 95.4 us
  starting transfers between devices  36.4 us (38%)
  other arithmetic  26 us (27%)
  local copies, waits for them, and re-layouts  19.4 us (20%)
  Pallas kernels  7.81 us (8%)
  waiting for transfers between devices  5.11 us (5%)
    ppermute x3, starting transfers between devices, shift_permutes(): received.append((shift, lax.ppermute(values, axis, pairs)))  10.2 us
    ppermute x1, starting transfers between devices, per_device(): lax.ppermute(up_part[:, :, :, :, :1].astype(jnp.float16), 'space', [(i +...  8.44 us
    pallas_call x1, Pallas kernels, collide_call(): pl.pallas_call(collide_body, out_shape=jax.ShapeDtypeStruct((kcat.shape[0...  7.81 us
    all_to_all x1, starting transfers between devices, per_device(): spread = lax.all_to_all(picked, 'species', 2, 0, tiled=True)  5.89 us
    all_to_all x1, starting transfers between devices, per_device(): lax.all_to_all(gained.astype(jnp.bfloat16), ('species', 'mode'), 1, 1, ti...  5.21 us
    all_to_all x1, waiting for transfers between devices, per_device(): lax.all_to_all(gained.astype(jnp.bfloat16), ('species', 'mode'), 1, 1, ti...  5.09 us
    sub x1, other arithmetic, per_device(): phase_field - nu_step * thermal_speed.reshape(own_count, 1, 1, 1, 1, 1, 1...  4.59 us
    add x1, other arithmetic, per_device(): advected.reshape(own_count, mode_count, row_count, plane_cells)  4.05 us
  transfers between devices with their start and end apart: 9, of which 1 were waited for; matrix products, arithmetic and copies ran while one was open for 33% of the time, Pallas kernels for 8%

profile of v12, /device:TPU:2, one launch (start us, length us, event | category | flops | bytes accessed | tf_op | source)
XLA Modules:
  0.0 95.4 jit_solution(11490939401995738744)
XLA Ops:
  0.0 3.8 %reduce.18 = f32[2,256,512]{2,1,0:T(8,128)S(1)} reduce(f32[2,256,1,512]{3,2,1,0:T(1,128)} %param.6, f32[]{:T(128)} %constant.93), dimensions={2}, to_apply=%param.6.reduce_sub_computation | reduce | bytes 2097156 | tf_op args[0]
  4.6 3.5 %collective-permute-start.1 = (f16[2,1,8,8,1,2,256]{6,3,5,4,2,1,0:T(8,128)(2,1)}, f16[2,1,8,8,1,2,256]{6,3,5,4,2,1,0:T(8,128)(2,1)S(1)}, u32[]{:S(2)}, u32[]{:S(2)}) collective-permute-start(f16[2,1,8,8,1,2,256]{6,3,5,4,2,1,0:T(8,128)(2,1)} %get-tuple-element.38), channel_id=1, source_target_pairs={{0,16},{16,32},{32,48},{1,17},{17,33},{33,49},{2,18},{18,34},{34,5... | collective-permute-start | bytes 393224 | tf_op jit(solution)/shard_map/ppermute | solution.py:107
  8.1 1.3 %collective-permute-start = (f16[2,1,8,8,1,2,256]{6,3,5,4,2,1,0:T(8,128)(2,1)S(1)}, f16[2,1,8,8,1,2,256]{6,3,5,4,2,1,0:T(8,128)(2,1)S(1)}, u32[]{:S(2)}, u32[]{:S(2)}) collective-permute-start(f16[2,1,8,8,1,2,256]{6,3,5,4,2,1,0:T(8,128)(2,1)S(1)} %get-tuple-element.37), channel_id=1, source_target_pairs={{16,0},{32,16},{48,32},{17,1},{33,17},{49,33},{18,2},{34,18},{50,3... | collective-permute-start | bytes 393224 | tf_op jit(solution)/shard_map/ppermute | solution.py:112
  10.3 1.1 %gather_fusion = bf16[120,2,512]{2,1,0:T(2,128)(2,1)S(1)} fusion(bf16[2,256,512]{2,0,1:T(2,128)(2,1)S(1)} %bitcast.78, s32[1024]{0:T(1024)S(1)} %pad_clamp_fusion.1), kind=kCustom, calls=%fused_computation | custom fusion | bytes 492000 | tf_op jit(solution)/shard_map/jit(_take)/gather | solution.py:124
  11.4 1.3 %fusion.26 = bf16[2,120,4,128]{3,0,1,2:T(2,128)(2,1)} fusion(pred[120]{0:T(512)(128)(4,1)S(1)} %get-tuple-element.15, pred[120]{0:T(512)(128)(4,1)S(1)} %get-tuple-element.45, bf16[120,2,512]{2,1,0:T(2,128)(2,1)S(1)} %gather_fusion), kind=kLoop, calls=%fused_computation.52 | loop fusion | flops 245760 | bytes 491760 | tf_op jit(solution)/shard_map/convert_element_type | solution.py:124
  12.7 5.9 %all-to-all-start = ((bf16[2,120,4,128]{3,0,1,2:T(2,128)(2,1)}), bf16[2,120,4,128]{3,0,1,2:T(2,128)(2,1)S(1)}, u32[]{:S(2)}, u32[]{:S(2)}) async-start(bf16[2,120,4,128]{3,0,1,2:T(2,128)(2,1)} %fusion.26), calls=%async_computation | async-start | bytes 491520 | tf_op jit(solution)/shard_map/all_to_all | solution.py:128
  18.6 1.1 %fusion.33 = (f32[2,4,8,8,1,2,1]{6,3,5,4,2,1,0:T(8,128)}, f32[2,4,8,8,1,2,1]{6,3,5,4,2,1,0:T(8,128)}) fusion(f32[2,4,8,8,1,2,256]{6,3,5,4,2,1,0:T(8,128)S(1)} %bitcast.68), kind=kLoop, calls=%fused_computation.81 | loop fusion | bytes 16384 | tf_op jit(solution)/shard_map/jit(_roll_static)/slice | solution.py:52
  19.8 1.7 %fusion.34 = (f32[2,4,8,8,1,2,255]{6,3,5,4,2,1,0:T(8,128)}, f32[2,4,8,8,1,2,255]{6,3,5,4,2,1,0:T(8,128)}) fusion(f32[2,4,8,8,1,2,256]{6,3,5,4,2,1,0:T(8,128)S(1)} %bitcast.69), kind=kLoop, calls=%fused_computation.82 | loop fusion | bytes 4177920 | tf_op jit(solution)/shard_map/jit(_roll_static)/slice | solution.py:52
  21.5 1.1 %fusion.31 = (f32[2,4,8,8,1,1,256]{6,3,5,4,2,1,0:T(8,128)}, f32[2,4,8,8,1,1,256]{6,3,5,4,2,1,0:T(8,128)}) fusion(f32[2,4,8,8,1,2,256]{6,3,5,4,2,1,0:T(8,128)S(1)} %bitcast.70), kind=kLoop, calls=%fused_computation.79 | loop fusion | bytes 2097152 | tf_op jit(solution)/shard_map/jit(_roll_static)/slice | solution.py:51
  24.3 2.0 %fusion.23 = (bf16[30,128,128]{2,1,0:T(8,128)(2,1)S(1)}, bf16[30,128,128]{2,1,0:T(8,128)(2,1)S(1)}) fusion(bf16[2,30,120,120]{3,2,1,0:T(8,128)(2,1)} %param.7), kind=kLoop, calls=%fused_computation.44 | loop fusion | bytes 3694080 | tf_op jit(solution)/shard_map/squeeze | solution.py:164
  26.5 2.0 %pad_maximum_fusion.k_ref = bf16[30,128,512]{2,1,0:T(8,128)(2,1)} fusion(bf16[30,128,128]{2,1,0:T(8,128)(2,1)S(1)} %get-tuple-element.18, bf16[30,128,128]{2,1,0:T(8,128)(2,1)S(1)} %get-tuple-element.17), kind=kLoop, calls=%fused_computation.2 | loop fusion | flops 15728640 | bytes 5898240 | tf_op jit(solution)/shard_map/concatenate | solution.py:164
  28.8 2.9 %multiply_subtract_fusion = (f32[2,4,8,8,1,2,256]{6,3,5,4,2,1,0:T(8,128)}, f32[2,4,8,8,1,2,256]{6,3,5,4,2,1,0:T(8,128)}, f32[2,4,8,8,1,2,256]{6,3,5,4,2,1,0:T(8,128)S(1)}, f32[2,4,8,8,1,2,256]{6,3,5,4,2,1,0:T(8,128)}) fusion(f32[2,4,8,8,1,2,256]{6,3,5,4,2,1,0:T(8,128)S(1)} %bitcast.71, f32[2,1,8,8,1,2,256]{6,3,5,4,2,1,0:T(8,128)S(1)} %convert_element_type.93, ...), kind=kLoop, calls=%fused_computation.42 | loop fusion | flops 4194304 | bytes 5769248 | tf_op jit(solution)/shard_map/sub | solution.py:117
  31.7 1.7 %fusion.36 = (f32[2,4,8,8,1,2,255]{6,3,5,4,2,1,0:T(8,128)}, f32[2,4,8,8,1,2,255]{6,3,5,4,2,1,0:T(8,128)}) fusion(f32[2,4,8,8,1,2,256]{6,3,5,4,2,1,0:T(8,128)S(1)} %get-tuple-element.23), kind=kLoop, calls=%fused_computation.84 | loop fusion | bytes 4177920 | tf_op jit(solution)/shard_map/jit(_roll_static)/slice | solution.py:54
  33.5 6.1 %collective-permute-start.6 = (bf16[8,120,1,128]{3,1,0,2:T(8,128)(2,1)S(1)}, bf16[8,120,1,128]{3,1,0,2:T(8,128)(2,1)S(1)}, u32[]{:S(2)}, u32[]{:S(2)}) collective-permute-start(bf16[8,120,1,128]{3,1,0,2:T(8,128)(2,1)S(1)} %bitcast.79), channel_id=1, source_target_pairs={{0,48},{16,0},{1,49},{17,1},{2,50},{18,2},{3,51},{19,3},{4,52},{20... | collective-permute-start | bytes 737288 | tf_op jit(solution)/shard_map/ppermute | solution.py:90
  39.6 1.3 %collective-permute-start.5 = (bf16[8,120,1,128]{3,1,0,2:T(8,128)(2,1)S(1)}, bf16[8,120,1,128]{3,1,0,2:T(8,128)(2,1)S(1)}, u32[]{:S(2)}, u32[]{:S(2)}) collective-permute-start(bf16[8,120,1,128]{3,1,0,2:T(8,128)(2,1)S(1)} %bitcast.80), channel_id=1, source_target_pairs={{0,32},{16,48},{1,33},{17,49},{2,34},{18,50},{3,35},{19,51},{4,36}... | collective-permute-start | bytes 737288 | tf_op jit(solution)/shard_map/ppermute | solution.py:90
  40.9 2.8 %collective-permute-start.4 = (bf16[8,120,1,128]{3,1,0,2:T(8,128)(2,1)S(1)}, bf16[8,120,1,128]{3,1,0,2:T(8,128)(2,1)S(1)}, u32[]{:S(2)}, u32[]{:S(2)}) collective-permute-start(bf16[8,120,1,128]{3,1,0,2:T(8,128)(2,1)S(1)} %bitcast.81), channel_id=1, source_target_pairs={{0,16},{16,32},{1,17},{17,33},{2,18},{18,34},{3,19},{19,35},{4,20}... | collective-permute-start | bytes 737288 | tf_op jit(solution)/shard_map/ppermute | solution.py:90
  43.7 1.2 %fusion.35 = (f32[2,4,8,8,1,2,1]{6,3,5,4,2,1,0:T(8,128)}, f32[2,4,8,8,1,2,1]{6,3,5,4,2,1,0:T(8,128)}) fusion(f32[2,4,8,8,1,2,256]{6,3,5,4,2,1,0:T(8,128)S(1)} %get-tuple-element.23), kind=kLoop, calls=%fused_computation.83 | loop fusion | bytes 16384 | tf_op jit(solution)/shard_map/jit(_roll_static)/slice | solution.py:54
  44.9 2.1 %convert_element_type.97 = f16[2,4,8,8,1,2,256]{6,3,5,4,2,1,0:T(8,128)(2,1)} convert(f32[2,4,8,8,1,2,256]{6,3,5,4,2,1,0:T(8,128)} %get-tuple-element.10) | non-fusion elementwise | flops 262144 | bytes 1572864 | tf_op jit(solution)/shard_map/convert_element_type | solution.py:136
  47.0 1.9 %collective-permute-start.3 = (f16[2,4,8,8,1,2,256]{6,3,5,4,2,1,0:T(8,128)(2,1)}, f16[2,4,8,8,1,2,256]{6,3,5,4,2,1,0:T(8,128)(2,1)}, u32[]{:S(2)}, u32[]{:S(2)}) collective-permute-start(f16[2,4,8,8,1,2,256]{6,3,5,4,2,1,0:T(8,128)(2,1)} %convert_element_type.97), channel_id=1, source_target_pairs={{0,1},{1,2},{2,3},{3,4},{4,5},{5,6},{6,7},{7,8},{8,9},{9,10},{10,1... | collective-permute-start | bytes 1572872 | tf_op jit(solution)/shard_map/ppermute | solution.py:135
  48.9 0.9 convert_element_type.95
  49.8 8.4 %collective-permute-start.2 = (f16[2,4,8,8,1,2,256]{6,3,5,4,2,1,0:T(8,128)(2,1)}, f16[2,4,8,8,1,2,256]{6,3,5,4,2,1,0:T(8,128)(2,1)}, u32[]{:S(2)}, u32[]{:S(2)}) collective-permute-start(f16[2,4,8,8,1,2,256]{6,3,5,4,2,1,0:T(8,128)(2,1)} %convert_element_type.95), channel_id=1, source_target_pairs={{1,0},{2,1},{3,2},{4,3},{5,4},{6,5},{7,6},{8,7},{9,8},{10,9},{11,1... | collective-permute-start | bytes 1572872 | tf_op jit(solution)/shard_map/ppermute | solution.py:130
  59.2 1.2 %copy.199 = bf16[64,8,8,128]{3,1,2,0:T(8,128)(2,1)} copy(bf16[64,8,8,128]{3,2,1,0:T(8,128)(2,1)S(1)} %bitcast.74) | data formatting | bytes 2097152
  60.5 0.9 copy_bitcast_fusion.2.l_ref
  61.3 7.8 %shard_map.64 = f32[30,1024]{1,0:T(8,128)} custom-call(bf16[30,128,512]{2,1,0:T(8,128)(2,1)} %pad_maximum_fusion.k_ref, bf16[512,1024]{1,0:T(8,128)(2,1)} %bitcast.75, f32[128,1024]{1,0:T(8,128)} %copy_bitcast_fusion.2.l_ref), custom_call_target="tpu_custom_call" | custom-call | tf_op jit(solution)/shard_map/pallas_call | solution.py:76
  69.2 0.9 convert_element_type.103
  70.2 0.8 broadcast_in_dim.62
  71.0 5.2 %all-to-all-start.1 = ((bf16[30,16,2,128]{3,2,0,1:T(2,128)(2,1)}), bf16[30,16,2,128]{3,2,0,1:T(2,128)(2,1)S(1)}, u32[]{:S(2)}, u32[]{:S(2)}) async-start(bf16[30,16,2,128]{3,2,0,1:T(2,128)(2,1)} %bitcast.83), calls=%async_computation.1 | async-start | bytes 491520 | tf_op jit(solution)/shard_map/all_to_all | solution.py:171
  76.4 4.6 %fusion.7 = f32[2,4,8,8,1,2,256]{6,3,5,4,2,1,0:T(8,128)S(1)} fusion(f32[2,4,8,8,1,2,256]{6,3,5,4,2,1,0:T(8,128)S(1)} %bitcast.72, f32[2,4,8,8,1,2,1]{6,3,5,4,2,1,0:T(8,128)} %get-tuple-element.34, f32[2,4,8,8,1,2,255]{6,3,5,4,2,1,0:T(8,128)} %get-tuple-element.36, f32[2,4,8,8,1,2,255]{6,3,5,4,2,1,0:T(8,128)} %get-tuple-element.35, ...), kind=kLoop, calls=%fused_computation.18 | loop fusion | flops 7340032 | bytes 9437192 | tf_op jit(solution)/shard_map/sub | solution.py:147
  80.9 5.1 %all-to-all-done.1 = bf16[30,16,2,128]{3,2,0,1:T(2,128)(2,1)S(1)} async-done(((bf16[30,16,2,128]{3,2,0,1:T(2,128)(2,1)}), bf16[30,16,2,128]{3,2,0,1:T(2,128)(2,1)S(1)}, u32[]{:S(2)}, u32[]{:S(2)}) %all-to-all-start.1) | async-done | bytes 245792 | tf_op jit(solution)/shard_map/all_to_all | solution.py:171
  86.6 2.7 %gather_fusion.1 = f32[256,2,512]{2,1,0:T(2,128)} fusion(f32[120,2,512]{2,1,0:T(2,128)S(1)} %reshape.456, s32[1024]{0:T(1024)S(1)} %pad_clamp_fusion), kind=kCustom, calls=%fused_computation.1 | custom fusion | bytes 2098176 | tf_op jit(solution)/shard_map/jit(_take)/gather | solution.py:181
  89.3 4.0 %fusion.22 = f32[2,256,1,512]{3,0,1,2:T(2,128)S(1)} fusion(f32[2,256,512]{2,1,0:T(8,128)S(1)} %bitcast.73, f32[256,2,512]{2,1,0:T(2,128)} %gather_fusion.1, pred[256]{0:T(512)(128)(4,1)S(1)} %compare_and_fusion, pred[256]{0:T(512)(128)(4,1)S(1)} %gt.18, f32[2]{0:T(128)S(1)} %neg.4, f32[2,256,1,512]{3,2,1,0:T(1,128)S(1)} %copy-done), kind=kLoop, calls=%fused_computation.40 | loop fusion | flops 1310720 | bytes 4194824 | tf_op jit(solution)/shard_map/add | solution.py:189
  93.4 2.0 %copy.178 = f32[2,256,1,512]{3,2,1,0:T(1,128)} copy(f32[2,256,1,512]{3,0,1,2:T(2,128)S(1)} %fusion.22) | data formatting | bytes 2097152 | tf_op jit(solution)/shard_map/add | solution.py:189
  (60 shorter events, 5.4 us)
Async XLA Ops:
  0.0 9.4 %copy-start = (f32[2,256,1,512]{3,2,1,0:T(1,128)S(1)}, f32[2,256,1,512]{3,2,1,0:T(1,128)}, u32[]{:S(2)}) copy-start(f32[2,256,1,512]{3,2,1,0:T(1,128)} %param.6) | copy-start | bytes 3145732
  0.0 10.3 %copy-start.4 = (s32[120]{0:T(128)S(1)}, s32[120]{0:T(128)}, u32[]{:S(2)}) copy-start(s32[120]{0:T(128)} %param.9) | copy-start | bytes 1444
  4.6 24.1 %collective-permute-start.1 = (f16[2,1,8,8,1,2,256]{6,3,5,4,2,1,0:T(8,128)(2,1)}, f16[2,1,8,8,1,2,256]{6,3,5,4,2,1,0:T(8,128)(2,1)S(1)}, u32[]{:S(2)}, u32[]{:S(2)}) collective-permute-start(f16[2,1,8,8,1,2,256]{6,3,5,4,2,1,0:T(8,128)(2,1)} %get-tuple-element.38), channel_id=1, source_target_pairs={{0,16},{16,32},{32,48},{1,17},{17,33},{33,49},{2,18},{18,34},{34,5... | collective-permute-start | bytes 393224 | tf_op jit(solution)/shard_map/ppermute | solution.py:107
  8.1 20.6 %collective-permute-start = (f16[2,1,8,8,1,2,256]{6,3,5,4,2,1,0:T(8,128)(2,1)S(1)}, f16[2,1,8,8,1,2,256]{6,3,5,4,2,1,0:T(8,128)(2,1)S(1)}, u32[]{:S(2)}, u32[]{:S(2)}) collective-permute-start(f16[2,1,8,8,1,2,256]{6,3,5,4,2,1,0:T(8,128)(2,1)S(1)} %get-tuple-element.37), channel_id=1, source_target_pairs={{16,0},{32,16},{48,32},{17,1},{33,17},{49,33},{18,2},{34,18},{50,3... | collective-permute-start | bytes 393224 | tf_op jit(solution)/shard_map/ppermute | solution.py:112
  12.7 20.7 %all-to-all-start = ((bf16[2,120,4,128]{3,0,1,2:T(2,128)(2,1)}), bf16[2,120,4,128]{3,0,1,2:T(2,128)(2,1)S(1)}, u32[]{:S(2)}, u32[]{:S(2)}) async-start(bf16[2,120,4,128]{3,0,1,2:T(2,128)(2,1)} %fusion.26), calls=%async_computation | async-start | bytes 491520 | tf_op jit(solution)/shard_map/all_to_all | solution.py:128
  18.6 5.2 %copy-start.6 = (f32[2]{0:T(128)S(1)}, f32[2]{0:T(128)}, u32[]{:S(2)}) copy-start(f32[2]{0:T(128)} %param.10) | copy-start | bytes 28
  21.5 4.9 %copy-start.3 = (s32[8,8]{1,0:T(8,128)S(1)}, s32[8,8]{1,0:T(8,128)}, u32[]{:S(2)}) copy-start(s32[8,8]{1,0:T(8,128)} %param.8) | copy-start | bytes 772
  24.3 4.3 %copy-start.7 = (f32[2]{0:T(128)S(1)}, f32[2]{0:T(128)}, u32[]{:S(2)}) copy-start(f32[2]{0:T(128)} %param.11) | copy-start | bytes 28
  33.4 15.5 %copy-start.2 = (f32[2,4,8,8,1,2,256]{6,3,5,4,2,1,0:T(8,128)S(1)}, f32[2,4,8,8,1,2,256]{6,3,5,4,2,1,0:T(8,128)}, u32[]{:S(2)}) copy-start(f32[2,4,8,8,1,2,256]{6,3,5,4,2,1,0:T(8,128)} %get-tuple-element.9) | copy-start | bytes 3145732
  33.5 24.8 %collective-permute-start.6 = (bf16[8,120,1,128]{3,1,0,2:T(8,128)(2,1)S(1)}, bf16[8,120,1,128]{3,1,0,2:T(8,128)(2,1)S(1)}, u32[]{:S(2)}, u32[]{:S(2)}) collective-permute-start(bf16[8,120,1,128]{3,1,0,2:T(8,128)(2,1)S(1)} %bitcast.79), channel_id=1, source_target_pairs={{0,48},{16,0},{1,49},{17,1},{2,50},{18,2},{3,51},{19,3},{4,52},{20... | collective-permute-start | bytes 737288 | tf_op jit(solution)/shard_map/ppermute | solution.py:90
  39.6 18.7 %collective-permute-start.5 = (bf16[8,120,1,128]{3,1,0,2:T(8,128)(2,1)S(1)}, bf16[8,120,1,128]{3,1,0,2:T(8,128)(2,1)S(1)}, u32[]{:S(2)}, u32[]{:S(2)}) collective-permute-start(bf16[8,120,1,128]{3,1,0,2:T(8,128)(2,1)S(1)} %bitcast.80), channel_id=1, source_target_pairs={{0,32},{16,48},{1,33},{17,49},{2,34},{18,50},{3,35},{19,51},{4,36}... | collective-permute-start | bytes 737288 | tf_op jit(solution)/shard_map/ppermute | solution.py:90
  40.9 17.4 %collective-permute-start.4 = (bf16[8,120,1,128]{3,1,0,2:T(8,128)(2,1)S(1)}, bf16[8,120,1,128]{3,1,0,2:T(8,128)(2,1)S(1)}, u32[]{:S(2)}, u32[]{:S(2)}) collective-permute-start(bf16[8,120,1,128]{3,1,0,2:T(8,128)(2,1)S(1)} %bitcast.81), channel_id=1, source_target_pairs={{0,16},{16,32},{1,17},{17,33},{2,18},{18,34},{3,19},{19,35},{4,20}... | collective-permute-start | bytes 737288 | tf_op jit(solution)/shard_map/ppermute | solution.py:90
  47.0 29.3 %collective-permute-start.3 = (f16[2,4,8,8,1,2,256]{6,3,5,4,2,1,0:T(8,128)(2,1)}, f16[2,4,8,8,1,2,256]{6,3,5,4,2,1,0:T(8,128)(2,1)}, u32[]{:S(2)}, u32[]{:S(2)}) collective-permute-start(f16[2,4,8,8,1,2,256]{6,3,5,4,2,1,0:T(8,128)(2,1)} %convert_element_type.97), channel_id=1, source_target_pairs={{0,1},{1,2},{2,3},{3,4},{4,5},{5,6},{6,7},{7,8},{8,9},{9,10},{10,1... | collective-permute-start | bytes 1572872 | tf_op jit(solution)/shard_map/ppermute | solution.py:135
  49.8 26.5 %collective-permute-start.2 = (f16[2,4,8,8,1,2,256]{6,3,5,4,2,1,0:T(8,128)(2,1)}, f16[2,4,8,8,1,2,256]{6,3,5,4,2,1,0:T(8,128)(2,1)}, u32[]{:S(2)}, u32[]{:S(2)}) collective-permute-start(f16[2,4,8,8,1,2,256]{6,3,5,4,2,1,0:T(8,128)(2,1)} %convert_element_type.95), channel_id=1, source_target_pairs={{1,0},{2,1},{3,2},{4,3},{5,4},{6,5},{7,6},{8,7},{9,8},{10,9},{11,1... | collective-permute-start | bytes 1572872 | tf_op jit(solution)/shard_map/ppermute | solution.py:130
  60.5 15.7 %copy-start.1 = (f32[2,4,8,8,1,2,256]{6,3,5,4,2,1,0:T(8,128)S(1)}, f32[2,4,8,8,1,2,256]{6,3,5,4,2,1,0:T(8,128)}, u32[]{:S(2)}) copy-start(f32[2,4,8,8,1,2,256]{6,3,5,4,2,1,0:T(8,128)} %get-tuple-element.24) | copy-start | bytes 3145732
  61.3 15.0 %copy-start.5 = (f32[2]{0:T(128)S(1)}, f32[2]{0:T(128)}, u32[]{:S(2)}) copy-start(f32[2]{0:T(128)} %broadcast_multiply_fusion) | copy-start | bytes 28
  71.0 15.1 %all-to-all-start.1 = ((bf16[30,16,2,128]{3,2,0,1:T(2,128)(2,1)}), bf16[30,16,2,128]{3,2,0,1:T(2,128)(2,1)S(1)}, u32[]{:S(2)}, u32[]{:S(2)}) async-start(bf16[30,16,2,128]{3,2,0,1:T(2,128)(2,1)} %bitcast.83), calls=%async_computation.1 | async-start | bytes 491520 | tf_op jit(solution)/shard_map/all_to_all | solution.py:171

commit v13 on v12

--- a/solution.py
+++ b/solution.py
@@ -126,16 +126,14 @@
     )
     picked = picked.reshape(own_count, low_count, species_devs, block_cells)
     spread = lax.all_to_all(picked, "species", 2, 0, tiled=True)
-    up_part, down_part, spread = lax.optimization_barrier((up_part, down_part, spread))
+    up_edge = up_part[:, :, :, :, :1].astype(jnp.float16)
+    down_edge = down_part[:, :, :, :, row_count - 1 :].astype(jnp.float16)
+    up_edge, down_edge, spread = lax.optimization_barrier((up_edge, down_edge, spread))
     from_next = lax.ppermute(
-        up_part[:, :, :, :, :1].astype(jnp.float16),
-        "space",
-        [(i + 1, i) for i in range(space_devs - 1)],
+        up_edge, "space", [(i + 1, i) for i in range(space_devs - 1)]
     ).astype(jnp.float32)
     from_prev = lax.ppermute(
-        down_part[:, :, :, :, row_count - 1 :].astype(jnp.float16),
-        "space",
-        [(i, i + 1) for i in range(space_devs - 1)],
+        down_edge, "space", [(i, i + 1) for i in range(space_devs - 1)]
     ).astype(jnp.float32)
     holders = [h for h in range(mode_devs) if h * per_vx <= DEG]
     up_all = jnp.concatenate([up_part[:, :, :, :, 1:], from_next], axis=4)

time: 96.1 us -> 93.2 us (0.970)
  other arithmetic: 26 us -> 22.9 us
    sub x1 -> x0, other arithmetic: 2.93 us -> none  [per_device(): down_part = -0.5 * flux_x - 0.5 * bound_x * phase_field]
    convert_element_type x2 -> x1, other arithmetic: 3.04 us -> 2.84 us  [per_device(): down_edge = down_part[:, :, :, :, row_count - 1:].astype(jnp.float16)]
    unnamed x19 -> x17, local copies, waits for them, and re-layouts: 2.26 us -> 2.33 us
  transfers between devices with their start and end apart: 9 -> 9, of which waited for: 1 -> 1; matrix products, arithmetic and copies ran while one was open for 33% -> 31% of each run, Pallas kernels for 8% -> 8%
where the time goes in v13:
time: 93.2 us; the launch traced here: 92.3 us
  starting transfers between devices  36.3 us (39%)
  other arithmetic  22.9 us (25%)
  local copies, waits for them, and re-layouts  19.4 us (21%)
  Pallas kernels  7.8 us (8%)
  waiting for transfers between devices  5.11 us (5%)
    ppermute x3, starting transfers between devices, shift_permutes(): received.append((shift, lax.ppermute(values, axis, pairs)))  10.1 us
    ppermute x1, starting transfers between devices, per_device(): lax.ppermute(up_edge, 'space', [(i + 1, i) for i in range(space_devs - 1)])  8.45 us
    pallas_call x1, Pallas kernels, collide_call(): pl.pallas_call(collide_body, out_shape=jax.ShapeDtypeStruct((kcat.shape[0...  7.8 us
    all_to_all x1, starting transfers between devices, per_device(): spread = lax.all_to_all(picked, 'species', 2, 0, tiled=True)  5.89 us
    all_to_all x1, starting transfers between devices, per_device(): lax.all_to_all(gained.astype(jnp.bfloat16), ('species', 'mode'), 1, 1, ti...  5.21 us
    all_to_all x1, waiting for transfers between devices, per_device(): lax.all_to_all(gained.astype(jnp.bfloat16), ('species', 'mode'), 1, 1, ti...  5.09 us
    sub x1, other arithmetic, per_device(): phase_field - nu_step * thermal_speed.reshape(own_count, 1, 1, 1, 1, 1, 1...  4.59 us
    add x1, other arithmetic, per_device(): advected.reshape(own_count, mode_count, row_count, plane_cells)  4.05 us
  transfers between devices with their start and end apart: 9, of which 1 were waited for; matrix products, arithmetic and copies ran while one was open for 31% of the time, Pallas kernels for 8%

profile of v13, /device:TPU:2, one launch (start us, length us, event | category | flops | bytes accessed | tf_op | source)
XLA Modules:
  0.0 92.3 jit_solution(9435245279540677952)
XLA Ops:
  0.0 3.8 %reduce.18 = f32[2,256,512]{2,1,0:T(8,128)S(1)} reduce(f32[2,256,1,512]{3,2,1,0:T(1,128)} %param.6, f32[]{:T(128)} %constant.93), dimensions={2}, to_apply=%param.6.reduce_sub_computation | reduce | bytes 2097156 | tf_op args[0]
  3.9 0.7 fusion.37
  4.6 3.5 %collective-permute-start.1 = (f16[2,1,8,8,1,2,256]{6,3,5,4,2,1,0:T(8,128)(2,1)}, f16[2,1,8,8,1,2,256]{6,3,5,4,2,1,0:T(8,128)(2,1)S(1)}, u32[]{:S(2)}, u32[]{:S(2)}) collective-permute-start(f16[2,1,8,8,1,2,256]{6,3,5,4,2,1,0:T(8,128)(2,1)} %get-tuple-element.38), channel_id=1, source_target_pairs={{0,16},{16,32},{32,48},{1,17},{17,33},{33,49},{2,18},{18,34},{34,5... | collective-permute-start | bytes 393224 | tf_op jit(solution)/shard_map/ppermute | solution.py:107
  8.1 1.3 %collective-permute-start = (f16[2,1,8,8,1,2,256]{6,3,5,4,2,1,0:T(8,128)(2,1)S(1)}, f16[2,1,8,8,1,2,256]{6,3,5,4,2,1,0:T(8,128)(2,1)S(1)}, u32[]{:S(2)}, u32[]{:S(2)}) collective-permute-start(f16[2,1,8,8,1,2,256]{6,3,5,4,2,1,0:T(8,128)(2,1)S(1)} %get-tuple-element.37), channel_id=1, source_target_pairs={{16,0},{32,16},{48,32},{17,1},{33,17},{49,33},{18,2},{34,18},{50,3... | collective-permute-start | bytes 393224 | tf_op jit(solution)/shard_map/ppermute | solution.py:112
  9.4 0.8 copy.200
  10.3 1.1 %gather_fusion = bf16[120,2,512]{2,1,0:T(2,128)(2,1)S(1)} fusion(bf16[2,256,512]{2,0,1:T(2,128)(2,1)S(1)} %bitcast.78, s32[1024]{0:T(1024)S(1)} %pad_clamp_fusion.1), kind=kCustom, calls=%fused_computation | custom fusion | bytes 492000 | tf_op jit(solution)/shard_map/jit(_take)/gather | solution.py:124
  11.4 1.4 %fusion.26 = bf16[2,120,4,128]{3,0,1,2:T(2,128)(2,1)} fusion(pred[120]{0:T(512)(128)(4,1)S(1)} %get-tuple-element.15, pred[120]{0:T(512)(128)(4,1)S(1)} %get-tuple-element.45, bf16[120,2,512]{2,1,0:T(2,128)(2,1)S(1)} %gather_fusion), kind=kLoop, calls=%fused_computation.52 | loop fusion | flops 245760 | bytes 491760 | tf_op jit(solution)/shard_map/convert_element_type | solution.py:124
  12.8 5.9 %all-to-all-start = ((bf16[2,120,4,128]{3,0,1,2:T(2,128)(2,1)}), bf16[2,120,4,128]{3,0,1,2:T(2,128)(2,1)S(1)}, u32[]{:S(2)}, u32[]{:S(2)}) async-start(bf16[2,120,4,128]{3,0,1,2:T(2,128)(2,1)} %fusion.26), calls=%async_computation | async-start | bytes 491520 | tf_op jit(solution)/shard_map/all_to_all | solution.py:128
  18.7 1.1 %fusion.33 = (f32[2,4,8,8,1,2,1]{6,3,5,4,2,1,0:T(8,128)}, f32[2,4,8,8,1,2,1]{6,3,5,4,2,1,0:T(8,128)}) fusion(f32[2,4,8,8,1,2,256]{6,3,5,4,2,1,0:T(8,128)S(1)} %bitcast.68), kind=kLoop, calls=%fused_computation.81 | loop fusion | bytes 16384 | tf_op jit(solution)/shard_map/jit(_roll_static)/slice | solution.py:52
  19.8 1.7 %fusion.34 = (f32[2,4,8,8,1,2,255]{6,3,5,4,2,1,0:T(8,128)}, f32[2,4,8,8,1,2,255]{6,3,5,4,2,1,0:T(8,128)}) fusion(f32[2,4,8,8,1,2,256]{6,3,5,4,2,1,0:T(8,128)S(1)} %bitcast.69), kind=kLoop, calls=%fused_computation.82 | loop fusion | bytes 4177920 | tf_op jit(solution)/shard_map/jit(_roll_static)/slice | solution.py:52
  21.5 1.1 %fusion.31 = (f32[2,4,8,8,1,1,256]{6,3,5,4,2,1,0:T(8,128)}, f32[2,4,8,8,1,1,256]{6,3,5,4,2,1,0:T(8,128)}) fusion(f32[2,4,8,8,1,2,256]{6,3,5,4,2,1,0:T(8,128)S(1)} %bitcast.70), kind=kLoop, calls=%fused_computation.79 | loop fusion | bytes 2097152 | tf_op jit(solution)/shard_map/jit(_roll_static)/slice | solution.py:51
  24.4 2.0 %fusion.23 = (bf16[30,128,128]{2,1,0:T(8,128)(2,1)S(1)}, bf16[30,128,128]{2,1,0:T(8,128)(2,1)S(1)}) fusion(bf16[2,30,120,120]{3,2,1,0:T(8,128)(2,1)} %param.7), kind=kLoop, calls=%fused_computation.44 | loop fusion | bytes 3694080 | tf_op jit(solution)/shard_map/squeeze | solution.py:162
  26.6 2.0 %pad_maximum_fusion.k_ref = bf16[30,128,512]{2,1,0:T(8,128)(2,1)} fusion(bf16[30,128,128]{2,1,0:T(8,128)(2,1)S(1)} %get-tuple-element.18, bf16[30,128,128]{2,1,0:T(8,128)(2,1)S(1)} %get-tuple-element.17), kind=kLoop, calls=%fused_computation.2 | loop fusion | flops 15728640 | bytes 5898240 | tf_op jit(solution)/shard_map/concatenate | solution.py:162
  28.9 2.8 %subtract_convert_fusion = (f16[2,4,8,8,1,2,256]{6,3,5,4,2,1,0:T(8,128)(2,1)}, f16[2,4,8,8,1,2,256]{6,3,5,4,2,1,0:T(8,128)(2,1)}, f32[2,4,8,8,1,2,256]{6,3,5,4,2,1,0:T(8,128)S(1)}, f32[2,4,8,8,1,2,256]{6,3,5,4,2,1,0:T(8,128)}) fusion(f32[2,4,8,8,1,2,256]{6,3,5,4,2,1,0:T(8,128)S(1)} %bitcast.71, f32[2,1,8,8,1,2,256]{6,3,5,4,2,1,0:T(8,128)S(1)} %convert_element_type.93, ...), kind=kLoop, calls=%fused_computation.42 | loop fusion | flops 4718592 | bytes 4720672 | tf_op jit(solution)/shard_map/convert_element_type | solution.py:130
  31.7 1.7 %fusion.36 = (f32[2,4,8,8,1,2,255]{6,3,5,4,2,1,0:T(8,128)}, f32[2,4,8,8,1,2,255]{6,3,5,4,2,1,0:T(8,128)}) fusion(f32[2,4,8,8,1,2,256]{6,3,5,4,2,1,0:T(8,128)S(1)} %get-tuple-element.23), kind=kLoop, calls=%fused_computation.84 | loop fusion | bytes 4177920 | tf_op jit(solution)/shard_map/jit(_roll_static)/slice | solution.py:54
  33.5 6.0 %collective-permute-start.6 = (bf16[8,120,1,128]{3,1,0,2:T(8,128)(2,1)S(1)}, bf16[8,120,1,128]{3,1,0,2:T(8,128)(2,1)S(1)}, u32[]{:S(2)}, u32[]{:S(2)}) collective-permute-start(bf16[8,120,1,128]{3,1,0,2:T(8,128)(2,1)S(1)} %bitcast.79), channel_id=1, source_target_pairs={{0,48},{16,0},{1,49},{17,1},{2,50},{18,2},{3,51},{19,3},{4,52},{20... | collective-permute-start | bytes 737288 | tf_op jit(solution)/shard_map/ppermute | solution.py:90
  39.4 1.3 %collective-permute-start.5 = (bf16[8,120,1,128]{3,1,0,2:T(8,128)(2,1)S(1)}, bf16[8,120,1,128]{3,1,0,2:T(8,128)(2,1)S(1)}, u32[]{:S(2)}, u32[]{:S(2)}) collective-permute-start(bf16[8,120,1,128]{3,1,0,2:T(8,128)(2,1)S(1)} %bitcast.80), channel_id=1, source_target_pairs={{0,32},{16,48},{1,33},{17,49},{2,34},{18,50},{3,35},{19,51},{4,36}... | collective-permute-start | bytes 737288 | tf_op jit(solution)/shard_map/ppermute | solution.py:90
  40.8 2.8 %collective-permute-start.4 = (bf16[8,120,1,128]{3,1,0,2:T(8,128)(2,1)S(1)}, bf16[8,120,1,128]{3,1,0,2:T(8,128)(2,1)S(1)}, u32[]{:S(2)}, u32[]{:S(2)}) collective-permute-start(bf16[8,120,1,128]{3,1,0,2:T(8,128)(2,1)S(1)} %bitcast.81), channel_id=1, source_target_pairs={{0,16},{16,32},{1,17},{17,33},{2,18},{18,34},{3,19},{19,35},{4,20}... | collective-permute-start | bytes 737288 | tf_op jit(solution)/shard_map/ppermute | solution.py:90
  43.5 1.1 %fusion.35 = (f32[2,4,8,8,1,2,1]{6,3,5,4,2,1,0:T(8,128)}, f32[2,4,8,8,1,2,1]{6,3,5,4,2,1,0:T(8,128)}) fusion(f32[2,4,8,8,1,2,256]{6,3,5,4,2,1,0:T(8,128)S(1)} %get-tuple-element.23), kind=kLoop, calls=%fused_computation.83 | loop fusion | bytes 16384 | tf_op jit(solution)/shard_map/jit(_roll_static)/slice | solution.py:54
  44.7 1.9 %collective-permute-start.3 = (f16[2,4,8,8,1,2,256]{6,3,5,4,2,1,0:T(8,128)(2,1)}, f16[2,4,8,8,1,2,256]{6,3,5,4,2,1,0:T(8,128)(2,1)}, u32[]{:S(2)}, u32[]{:S(2)}) collective-permute-start(f16[2,4,8,8,1,2,256]{6,3,5,4,2,1,0:T(8,128)(2,1)} %get-tuple-element.10), channel_id=1, source_target_pairs={{0,1},{1,2},{2,3},{3,4},{4,5},{5,6},{6,7},{7,8},{8,9},{9,10},{10,1... | collective-permute-start | bytes 1572872 | tf_op jit(solution)/shard_map/ppermute | solution.py:135
  46.6 8.4 %collective-permute-start.2 = (f16[2,4,8,8,1,2,256]{6,3,5,4,2,1,0:T(8,128)(2,1)}, f16[2,4,8,8,1,2,256]{6,3,5,4,2,1,0:T(8,128)(2,1)}, u32[]{:S(2)}, u32[]{:S(2)}) collective-permute-start(f16[2,4,8,8,1,2,256]{6,3,5,4,2,1,0:T(8,128)(2,1)} %get-tuple-element.9), channel_id=1, source_target_pairs={{1,0},{2,1},{3,2},{4,3},{5,4},{6,5},{7,6},{8,7},{9,8},{10,9},{11,1... | collective-permute-start | bytes 1572872 | tf_op jit(solution)/shard_map/ppermute | solution.py:132
  56.0 1.3 %copy.199 = bf16[64,8,8,128]{3,1,2,0:T(8,128)(2,1)} copy(bf16[64,8,8,128]{3,2,1,0:T(8,128)(2,1)S(1)} %bitcast.74) | data formatting | bytes 2097152
  57.3 0.9 copy_bitcast_fusion.2.l_ref
  58.2 7.8 %shard_map.64 = f32[30,1024]{1,0:T(8,128)} custom-call(bf16[30,128,512]{2,1,0:T(8,128)(2,1)} %pad_maximum_fusion.k_ref, bf16[512,1024]{1,0:T(8,128)(2,1)} %bitcast.75, f32[128,1024]{1,0:T(8,128)} %copy_bitcast_fusion.2.l_ref), custom_call_target="tpu_custom_call" | custom-call | tf_op jit(solution)/shard_map/pallas_call | solution.py:76
  66.0 0.9 convert_element_type.103
  67.0 0.8 broadcast_in_dim.62
  67.8 5.2 %all-to-all-start.1 = ((bf16[30,16,2,128]{3,2,0,1:T(2,128)(2,1)}), bf16[30,16,2,128]{3,2,0,1:T(2,128)(2,1)S(1)}, u32[]{:S(2)}, u32[]{:S(2)}) async-start(bf16[30,16,2,128]{3,2,0,1:T(2,128)(2,1)} %bitcast.83), calls=%async_computation.1 | async-start | bytes 491520 | tf_op jit(solution)/shard_map/all_to_all | solution.py:169
  73.2 4.6 %fusion.7 = f32[2,4,8,8,1,2,256]{6,3,5,4,2,1,0:T(8,128)S(1)} fusion(f32[2,4,8,8,1,2,256]{6,3,5,4,2,1,0:T(8,128)S(1)} %bitcast.72, f32[2,4,8,8,1,2,1]{6,3,5,4,2,1,0:T(8,128)} %get-tuple-element.34, f32[2,4,8,8,1,2,255]{6,3,5,4,2,1,0:T(8,128)} %get-tuple-element.36, f32[2,4,8,8,1,2,255]{6,3,5,4,2,1,0:T(8,128)} %get-tuple-element.35, ...), kind=kLoop, calls=%fused_computation.18 | loop fusion | flops 7340032 | bytes 9437192 | tf_op jit(solution)/shard_map/sub | solution.py:145
  77.8 5.1 %all-to-all-done.1 = bf16[30,16,2,128]{3,2,0,1:T(2,128)(2,1)S(1)} async-done(((bf16[30,16,2,128]{3,2,0,1:T(2,128)(2,1)}), bf16[30,16,2,128]{3,2,0,1:T(2,128)(2,1)S(1)}, u32[]{:S(2)}, u32[]{:S(2)}) %all-to-all-start.1) | async-done | bytes 245792 | tf_op jit(solution)/shard_map/all_to_all | solution.py:169
  83.5 2.7 %gather_fusion.1 = f32[256,2,512]{2,1,0:T(2,128)} fusion(f32[120,2,512]{2,1,0:T(2,128)S(1)} %reshape.456, s32[1024]{0:T(1024)S(1)} %pad_clamp_fusion), kind=kCustom, calls=%fused_computation.1 | custom fusion | bytes 2098176 | tf_op jit(solution)/shard_map/jit(_take)/gather | solution.py:179
  86.2 4.0 %fusion.22 = f32[2,256,1,512]{3,0,1,2:T(2,128)S(1)} fusion(f32[2,256,512]{2,1,0:T(8,128)S(1)} %bitcast.73, f32[256,2,512]{2,1,0:T(2,128)} %gather_fusion.1, pred[256]{0:T(512)(128)(4,1)S(1)} %compare_and_fusion, pred[256]{0:T(512)(128)(4,1)S(1)} %gt.18, f32[2]{0:T(128)S(1)} %neg.4, f32[2,256,1,512]{3,2,1,0:T(1,128)S(1)} %copy-done), kind=kLoop, calls=%fused_computation.40 | loop fusion | flops 1310720 | bytes 4194824 | tf_op jit(solution)/shard_map/add | solution.py:187
  90.2 2.0 %copy.178 = f32[2,256,1,512]{3,2,1,0:T(1,128)} copy(f32[2,256,1,512]{3,0,1,2:T(2,128)S(1)} %fusion.22) | data formatting | bytes 2097152 | tf_op jit(solution)/shard_map/add | solution.py:187
  (56 shorter events, 4.0 us)
Async XLA Ops:
  0.0 9.4 %copy-start = (f32[2,256,1,512]{3,2,1,0:T(1,128)S(1)}, f32[2,256,1,512]{3,2,1,0:T(1,128)}, u32[]{:S(2)}) copy-start(f32[2,256,1,512]{3,2,1,0:T(1,128)} %param.6) | copy-start | bytes 3145732
  0.0 10.3 %copy-start.3 = (s32[120]{0:T(128)S(1)}, s32[120]{0:T(128)}, u32[]{:S(2)}) copy-start(s32[120]{0:T(128)} %param.9) | copy-start | bytes 1444
  4.6 24.2 %collective-permute-start.1 = (f16[2,1,8,8,1,2,256]{6,3,5,4,2,1,0:T(8,128)(2,1)}, f16[2,1,8,8,1,2,256]{6,3,5,4,2,1,0:T(8,128)(2,1)S(1)}, u32[]{:S(2)}, u32[]{:S(2)}) collective-permute-start(f16[2,1,8,8,1,2,256]{6,3,5,4,2,1,0:T(8,128)(2,1)} %get-tuple-element.38), channel_id=1, source_target_pairs={{0,16},{16,32},{32,48},{1,17},{17,33},{33,49},{2,18},{18,34},{34,5... | collective-permute-start | bytes 393224 | tf_op jit(solution)/shard_map/ppermute | solution.py:107
  8.1 20.7 %collective-permute-start = (f16[2,1,8,8,1,2,256]{6,3,5,4,2,1,0:T(8,128)(2,1)S(1)}, f16[2,1,8,8,1,2,256]{6,3,5,4,2,1,0:T(8,128)(2,1)S(1)}, u32[]{:S(2)}, u32[]{:S(2)}) collective-permute-start(f16[2,1,8,8,1,2,256]{6,3,5,4,2,1,0:T(8,128)(2,1)S(1)} %get-tuple-element.37), channel_id=1, source_target_pairs={{16,0},{32,16},{48,32},{17,1},{33,17},{49,33},{18,2},{34,18},{50,3... | collective-permute-start | bytes 393224 | tf_op jit(solution)/shard_map/ppermute | solution.py:112
  12.8 20.7 %all-to-all-start = ((bf16[2,120,4,128]{3,0,1,2:T(2,128)(2,1)}), bf16[2,120,4,128]{3,0,1,2:T(2,128)(2,1)S(1)}, u32[]{:S(2)}, u32[]{:S(2)}) async-start(bf16[2,120,4,128]{3,0,1,2:T(2,128)(2,1)} %fusion.26), calls=%async_computation | async-start | bytes 491520 | tf_op jit(solution)/shard_map/all_to_all | solution.py:128
  18.7 5.2 %copy-start.5 = (f32[2]{0:T(128)S(1)}, f32[2]{0:T(128)}, u32[]{:S(2)}) copy-start(f32[2]{0:T(128)} %param.10) | copy-start | bytes 28
  21.5 5.0 %copy-start.2 = (s32[8,8]{1,0:T(8,128)S(1)}, s32[8,8]{1,0:T(8,128)}, u32[]{:S(2)}) copy-start(s32[8,8]{1,0:T(8,128)} %param.8) | copy-start | bytes 772
  24.4 4.3 %copy-start.6 = (f32[2]{0:T(128)S(1)}, f32[2]{0:T(128)}, u32[]{:S(2)}) copy-start(f32[2]{0:T(128)} %param.11) | copy-start | bytes 28
  33.5 21.6 %collective-permute-start.6 = (bf16[8,120,1,128]{3,1,0,2:T(8,128)(2,1)S(1)}, bf16[8,120,1,128]{3,1,0,2:T(8,128)(2,1)S(1)}, u32[]{:S(2)}, u32[]{:S(2)}) collective-permute-start(bf16[8,120,1,128]{3,1,0,2:T(8,128)(2,1)S(1)} %bitcast.79), channel_id=1, source_target_pairs={{0,48},{16,0},{1,49},{17,1},{2,50},{18,2},{3,51},{19,3},{4,52},{20... | collective-permute-start | bytes 737288 | tf_op jit(solution)/shard_map/ppermute | solution.py:90
  39.4 15.6 %collective-permute-start.5 = (bf16[8,120,1,128]{3,1,0,2:T(8,128)(2,1)S(1)}, bf16[8,120,1,128]{3,1,0,2:T(8,128)(2,1)S(1)}, u32[]{:S(2)}, u32[]{:S(2)}) collective-permute-start(bf16[8,120,1,128]{3,1,0,2:T(8,128)(2,1)S(1)} %bitcast.80), channel_id=1, source_target_pairs={{0,32},{16,48},{1,33},{17,49},{2,34},{18,50},{3,35},{19,51},{4,36}... | collective-permute-start | bytes 737288 | tf_op jit(solution)/shard_map/ppermute | solution.py:90
  40.8 14.3 %collective-permute-start.4 = (bf16[8,120,1,128]{3,1,0,2:T(8,128)(2,1)S(1)}, bf16[8,120,1,128]{3,1,0,2:T(8,128)(2,1)S(1)}, u32[]{:S(2)}, u32[]{:S(2)}) collective-permute-start(bf16[8,120,1,128]{3,1,0,2:T(8,128)(2,1)S(1)} %bitcast.81), channel_id=1, source_target_pairs={{0,16},{16,32},{1,17},{17,33},{2,18},{18,34},{3,19},{19,35},{4,20}... | collective-permute-start | bytes 737288 | tf_op jit(solution)/shard_map/ppermute | solution.py:90
  44.7 28.5 %collective-permute-start.3 = (f16[2,4,8,8,1,2,256]{6,3,5,4,2,1,0:T(8,128)(2,1)}, f16[2,4,8,8,1,2,256]{6,3,5,4,2,1,0:T(8,128)(2,1)}, u32[]{:S(2)}, u32[]{:S(2)}) collective-permute-start(f16[2,4,8,8,1,2,256]{6,3,5,4,2,1,0:T(8,128)(2,1)} %get-tuple-element.10), channel_id=1, source_target_pairs={{0,1},{1,2},{2,3},{3,4},{4,5},{5,6},{6,7},{7,8},{8,9},{9,10},{10,1... | collective-permute-start | bytes 1572872 | tf_op jit(solution)/shard_map/ppermute | solution.py:135
  46.6 26.6 %collective-permute-start.2 = (f16[2,4,8,8,1,2,256]{6,3,5,4,2,1,0:T(8,128)(2,1)}, f16[2,4,8,8,1,2,256]{6,3,5,4,2,1,0:T(8,128)(2,1)}, u32[]{:S(2)}, u32[]{:S(2)}) collective-permute-start(f16[2,4,8,8,1,2,256]{6,3,5,4,2,1,0:T(8,128)(2,1)} %get-tuple-element.9), channel_id=1, source_target_pairs={{1,0},{2,1},{3,2},{4,3},{5,4},{6,5},{7,6},{8,7},{9,8},{10,9},{11,1... | collective-permute-start | bytes 1572872 | tf_op jit(solution)/shard_map/ppermute | solution.py:132
  57.3 15.7 %copy-start.1 = (f32[2,4,8,8,1,2,256]{6,3,5,4,2,1,0:T(8,128)S(1)}, f32[2,4,8,8,1,2,256]{6,3,5,4,2,1,0:T(8,128)}, u32[]{:S(2)}) copy-start(f32[2,4,8,8,1,2,256]{6,3,5,4,2,1,0:T(8,128)} %get-tuple-element.24) | copy-start | bytes 3145732
  58.2 15.0 %copy-start.4 = (f32[2]{0:T(128)S(1)}, f32[2]{0:T(128)}, u32[]{:S(2)}) copy-start(f32[2]{0:T(128)} %broadcast_multiply_fusion) | copy-start | bytes 28
  67.8 15.1 %all-to-all-start.1 = ((bf16[30,16,2,128]{3,2,0,1:T(2,128)(2,1)}), bf16[30,16,2,128]{3,2,0,1:T(2,128)(2,1)S(1)}, u32[]{:S(2)}, u32[]{:S(2)}) async-start(bf16[30,16,2,128]{3,2,0,1:T(2,128)(2,1)} %bitcast.83), calls=%async_computation.1 | async-start | bytes 491520 | tf_op jit(solution)/shard_map/all_to_all | solution.py:169

commit v14 on v13

--- a/solution.py
+++ b/solution.py
@@ -138,11 +138,13 @@
     holders = [h for h in range(mode_devs) if h * per_vx <= DEG]
     up_all = jnp.concatenate([up_part[:, :, :, :, 1:], from_next], axis=4)
     down_all = jnp.concatenate([from_prev, down_part[:, :, :, :, : row_count - 1]], axis=4)
-    x_term = up_all + down_all + bound_x * phase_field
     y_term = periodic_term(phase_field, 2, 6, bound_y)
     z_term = periodic_term(phase_field, 3, 5, bound_z)
-    stream = x_term + y_term + z_term
-    advected = phase_field - nu_step * thermal_speed.reshape(own_count, 1, 1, 1, 1, 1, 1) * stream
+    step_scale = nu_step * thermal_speed.reshape(own_count, 1, 1, 1, 1, 1, 1)
+    partial = lax.optimization_barrier(
+        phase_field - step_scale * (bound_x * phase_field + y_term + z_term)
+    )
+    advected = partial - step_scale * (up_all + down_all)
 
     low_all = spread
     for _, got in shift_permutes(spread, "mode", holders, mode_devs, False):

time: 93.2 us -> 94 us (level)
  local copies, waits for them, and re-layouts: 19.4 us -> 20.4 us
    sub x1 -> x2, other arithmetic: 4.59 us -> 5.62 us  [the longest x1 4.14 us: per_device(): phase_field - step_scale * (bound_x * phase_field + y_term + z_term)]
    slice x1, local copies, waits for them, and re-layouts: 0.11 us -> 1.09 us  [periodic_term(): jnp.roll(flux_dir, -1, axis_cell)]
  transfers between devices with their start and end apart: 9 -> 9, of which waited for: 1 -> 1; matrix products, arithmetic and copies ran while one was open for 31% -> 33% of each run, Pallas kernels for 8% -> 8%
where the time goes in v14:
time: 94 us; the launch traced here: 93 us
  starting transfers between devices  36.3 us (39%)
  other arithmetic  23.6 us (25%)
  local copies, waits for them, and re-layouts  20.4 us (22%)
  Pallas kernels  7.8 us (8%)
  waiting for transfers between devices  4.2 us (4%)
    ppermute x3, starting transfers between devices, shift_permutes(): received.append((shift, lax.ppermute(values, axis, pairs)))  10.1 us
    ppermute x1, starting transfers between devices, per_device(): lax.ppermute(up_edge, 'space', [(i + 1, i) for i in range(space_devs - 1)])  8.45 us
    pallas_call x1, Pallas kernels, collide_call(): pl.pallas_call(collide_body, out_shape=jax.ShapeDtypeStruct((kcat.shape[0...  7.8 us
    all_to_all x1, starting transfers between devices, per_device(): spread = lax.all_to_all(picked, 'species', 2, 0, tiled=True)  5.89 us
    all_to_all x1, starting transfers between devices, per_device(): lax.all_to_all(gained.astype(jnp.bfloat16), ('species', 'mode'), 1, 1, ti...  5.2 us
    all_to_all x1, waiting for transfers between devices, per_device(): lax.all_to_all(gained.astype(jnp.bfloat16), ('species', 'mode'), 1, 1, ti...  4.18 us
    sub x1, other arithmetic, per_device(): phase_field - step_scale * (bound_x * phase_field + y_term + z_term)  4.14 us
    add x1, other arithmetic, per_device(): advected.reshape(own_count, mode_count, row_count, plane_cells)  4.05 us
  transfers between devices with their start and end apart: 9, of which 1 were waited for; matrix products, arithmetic and copies ran while one was open for 33% of the time, Pallas kernels for 8%

profile of v14, /device:TPU:2, one launch (start us, length us, event | category | flops | bytes accessed | tf_op | source)
XLA Modules:
  0.0 93.0 jit_solution(10472687053882687025)
XLA Ops:
  0.0 3.8 %reduce.18 = f32[2,256,512]{2,1,0:T(8,128)S(1)} reduce(f32[2,256,1,512]{3,2,1,0:T(1,128)} %param.6, f32[]{:T(128)} %constant.93), dimensions={2}, to_apply=%param.6.reduce_sub_computation | reduce | bytes 2097156 | tf_op args[0]
  4.6 3.5 %collective-permute-start.1 = (f16[2,1,8,8,1,2,256]{6,3,5,4,2,1,0:T(8,128)(2,1)}, f16[2,1,8,8,1,2,256]{6,3,5,4,2,1,0:T(8,128)(2,1)S(1)}, u32[]{:S(2)}, u32[]{:S(2)}) collective-permute-start(f16[2,1,8,8,1,2,256]{6,3,5,4,2,1,0:T(8,128)(2,1)} %get-tuple-element.38), channel_id=1, source_target_pairs={{0,16},{16,32},{32,48},{1,17},{17,33},{33,49},{2,18},{18,34},{34,5... | collective-permute-start | bytes 393224 | tf_op jit(solution)/shard_map/ppermute | solution.py:107
  8.1 1.3 %collective-permute-start = (f16[2,1,8,8,1,2,256]{6,3,5,4,2,1,0:T(8,128)(2,1)S(1)}, f16[2,1,8,8,1,2,256]{6,3,5,4,2,1,0:T(8,128)(2,1)S(1)}, u32[]{:S(2)}, u32[]{:S(2)}) collective-permute-start(f16[2,1,8,8,1,2,256]{6,3,5,4,2,1,0:T(8,128)(2,1)S(1)} %get-tuple-element.37), channel_id=1, source_target_pairs={{16,0},{32,16},{48,32},{17,1},{33,17},{49,33},{18,2},{34,18},{50,3... | collective-permute-start | bytes 393224 | tf_op jit(solution)/shard_map/ppermute | solution.py:112
  10.3 1.1 %gather_fusion = bf16[120,2,512]{2,1,0:T(2,128)(2,1)S(1)} fusion(bf16[2,256,512]{2,0,1:T(2,128)(2,1)S(1)} %bitcast.78, s32[1024]{0:T(1024)S(1)} %pad_clamp_fusion.1), kind=kCustom, calls=%fused_computation | custom fusion | bytes 492000 | tf_op jit(solution)/shard_map/jit(_take)/gather | solution.py:124
  11.4 1.3 %fusion.26 = bf16[2,120,4,128]{3,0,1,2:T(2,128)(2,1)} fusion(pred[120]{0:T(512)(128)(4,1)S(1)} %get-tuple-element.15, pred[120]{0:T(512)(128)(4,1)S(1)} %get-tuple-element.45, bf16[120,2,512]{2,1,0:T(2,128)(2,1)S(1)} %gather_fusion), kind=kLoop, calls=%fused_computation.53 | loop fusion | flops 245760 | bytes 491760 | tf_op jit(solution)/shard_map/convert_element_type | solution.py:124
  12.7 5.9 %all-to-all-start = ((bf16[2,120,4,128]{3,0,1,2:T(2,128)(2,1)}), bf16[2,120,4,128]{3,0,1,2:T(2,128)(2,1)S(1)}, u32[]{:S(2)}, u32[]{:S(2)}) async-start(bf16[2,120,4,128]{3,0,1,2:T(2,128)(2,1)} %fusion.26), calls=%async_computation | async-start | bytes 491520 | tf_op jit(solution)/shard_map/all_to_all | solution.py:128
  18.6 1.2 %fusion.33 = (f32[2,4,8,8,1,2,1]{6,3,5,4,2,1,0:T(8,128)}, f32[2,4,8,8,1,2,1]{6,3,5,4,2,1,0:T(8,128)}) fusion(f32[2,4,8,8,1,2,256]{6,3,5,4,2,1,0:T(8,128)S(1)} %bitcast.68), kind=kLoop, calls=%fused_computation.82 | loop fusion | bytes 16384 | tf_op jit(solution)/shard_map/jit(_roll_static)/slice | solution.py:52
  19.8 1.7 %fusion.34 = (f32[2,4,8,8,1,2,255]{6,3,5,4,2,1,0:T(8,128)}, f32[2,4,8,8,1,2,255]{6,3,5,4,2,1,0:T(8,128)}) fusion(f32[2,4,8,8,1,2,256]{6,3,5,4,2,1,0:T(8,128)S(1)} %bitcast.69), kind=kLoop, calls=%fused_computation.83 | loop fusion | bytes 4177920 | tf_op jit(solution)/shard_map/jit(_roll_static)/slice | solution.py:52
  21.5 1.1 %fusion.31 = (f32[2,4,8,8,1,1,256]{6,3,5,4,2,1,0:T(8,128)}, f32[2,4,8,8,1,1,256]{6,3,5,4,2,1,0:T(8,128)}) fusion(f32[2,4,8,8,1,2,256]{6,3,5,4,2,1,0:T(8,128)S(1)} %bitcast.70), kind=kLoop, calls=%fused_computation.80 | loop fusion | bytes 2097152 | tf_op jit(solution)/shard_map/jit(_roll_static)/slice | solution.py:51
  23.9 2.0 %fusion.23 = (bf16[30,128,128]{2,1,0:T(8,128)(2,1)S(1)}, bf16[30,128,128]{2,1,0:T(8,128)(2,1)S(1)}) fusion(bf16[2,30,120,120]{3,2,1,0:T(8,128)(2,1)} %param.7), kind=kLoop, calls=%fused_computation.45 | loop fusion | bytes 3694080 | tf_op jit(solution)/shard_map/squeeze | solution.py:164
  26.1 2.0 %pad_maximum_fusion.k_ref = bf16[30,128,512]{2,1,0:T(8,128)(2,1)} fusion(bf16[30,128,128]{2,1,0:T(8,128)(2,1)S(1)} %get-tuple-element.18, bf16[30,128,128]{2,1,0:T(8,128)(2,1)S(1)} %get-tuple-element.17), kind=kLoop, calls=%fused_computation.2 | loop fusion | flops 15728640 | bytes 5898240 | tf_op jit(solution)/shard_map/concatenate | solution.py:164
  28.9 2.5 %subtract_convert_fusion = (f16[2,4,8,8,1,2,256]{6,3,5,4,2,1,0:T(8,128)(2,1)}, f16[2,4,8,8,1,2,256]{6,3,5,4,2,1,0:T(8,128)(2,1)}, f32[2,4,8,8,1,2,256]{6,3,5,4,2,1,0:T(8,128)S(1)}, f32[2,4,8,8,1,2,256]{6,3,5,4,2,1,0:T(8,128)S(1)}) fusion(f32[2,4,8,8,1,2,256]{6,3,5,4,2,1,0:T(8,128)S(1)} %bitcast.71, f32[2,1,8,8,1,2,256]{6,3,5,4,2,1,0:T(8,128)S(1)} %convert_element_type.94, ...), kind=kLoop, calls=%fused_computation.43 | loop fusion | flops 4718592 | bytes 4720672 | tf_op jit(solution)/shard_map/convert_element_type | solution.py:130
  31.3 1.2 %fusion.35 = (f32[2,4,8,8,1,2,1]{6,3,5,4,2,1,0:T(8,128)}, f32[2,4,8,8,1,2,1]{6,3,5,4,2,1,0:T(8,128)}) fusion(f32[2,4,8,8,1,2,256]{6,3,5,4,2,1,0:T(8,128)S(1)} %get-tuple-element.23), kind=kLoop, calls=%fused_computation.84 | loop fusion | bytes 16384 | tf_op jit(solution)/shard_map/jit(_roll_static)/slice | solution.py:54
  32.5 1.7 %fusion.36 = (f32[2,4,8,8,1,2,255]{6,3,5,4,2,1,0:T(8,128)}, f32[2,4,8,8,1,2,255]{6,3,5,4,2,1,0:T(8,128)}) fusion(f32[2,4,8,8,1,2,256]{6,3,5,4,2,1,0:T(8,128)S(1)} %get-tuple-element.23), kind=kLoop, calls=%fused_computation.85 | loop fusion | bytes 4177920 | tf_op jit(solution)/shard_map/jit(_roll_static)/slice | solution.py:54
  34.3 6.0 %collective-permute-start.6 = (bf16[8,120,1,128]{3,1,0,2:T(8,128)(2,1)S(1)}, bf16[8,120,1,128]{3,1,0,2:T(8,128)(2,1)S(1)}, u32[]{:S(2)}, u32[]{:S(2)}) collective-permute-start(bf16[8,120,1,128]{3,1,0,2:T(8,128)(2,1)S(1)} %bitcast.79), channel_id=1, source_target_pairs={{0,48},{16,0},{1,49},{17,1},{2,50},{18,2},{3,51},{19,3},{4,52},{20... | collective-permute-start | bytes 737288 | tf_op jit(solution)/shard_map/ppermute | solution.py:90
  40.3 1.3 %collective-permute-start.5 = (bf16[8,120,1,128]{3,1,0,2:T(8,128)(2,1)S(1)}, bf16[8,120,1,128]{3,1,0,2:T(8,128)(2,1)S(1)}, u32[]{:S(2)}, u32[]{:S(2)}) collective-permute-start(bf16[8,120,1,128]{3,1,0,2:T(8,128)(2,1)S(1)} %bitcast.80), channel_id=1, source_target_pairs={{0,32},{16,48},{1,33},{17,49},{2,34},{18,50},{3,35},{19,51},{4,36}... | collective-permute-start | bytes 737288 | tf_op jit(solution)/shard_map/ppermute | solution.py:90
  41.6 2.8 %collective-permute-start.4 = (bf16[8,120,1,128]{3,1,0,2:T(8,128)(2,1)S(1)}, bf16[8,120,1,128]{3,1,0,2:T(8,128)(2,1)S(1)}, u32[]{:S(2)}, u32[]{:S(2)}) collective-permute-start(bf16[8,120,1,128]{3,1,0,2:T(8,128)(2,1)S(1)} %bitcast.81), channel_id=1, source_target_pairs={{0,16},{16,32},{1,17},{17,33},{2,18},{18,34},{3,19},{19,35},{4,20}... | collective-permute-start | bytes 737288 | tf_op jit(solution)/shard_map/ppermute | solution.py:90
  44.4 1.1 %fusion.32 = (f32[2,4,8,8,1,1,256]{6,3,5,4,2,1,0:T(8,128)}, f32[2,4,8,8,1,1,256]{6,3,5,4,2,1,0:T(8,128)}) fusion(f32[2,4,8,8,1,2,256]{6,3,5,4,2,1,0:T(8,128)S(1)} %get-tuple-element.24), kind=kLoop, calls=%fused_computation.81 | loop fusion | bytes 2097152 | tf_op jit(solution)/shard_map/jit(_roll_static)/slice | solution.py:53
  45.5 1.9 %collective-permute-start.3 = (f16[2,4,8,8,1,2,256]{6,3,5,4,2,1,0:T(8,128)(2,1)}, f16[2,4,8,8,1,2,256]{6,3,5,4,2,1,0:T(8,128)(2,1)}, u32[]{:S(2)}, u32[]{:S(2)}) collective-permute-start(f16[2,4,8,8,1,2,256]{6,3,5,4,2,1,0:T(8,128)(2,1)} %get-tuple-element.10), channel_id=1, source_target_pairs={{0,1},{1,2},{2,3},{3,4},{4,5},{5,6},{6,7},{7,8},{8,9},{9,10},{10,1... | collective-permute-start | bytes 1572872 | tf_op jit(solution)/shard_map/ppermute | solution.py:135
  47.4 8.4 %collective-permute-start.2 = (f16[2,4,8,8,1,2,256]{6,3,5,4,2,1,0:T(8,128)(2,1)}, f16[2,4,8,8,1,2,256]{6,3,5,4,2,1,0:T(8,128)(2,1)}, u32[]{:S(2)}, u32[]{:S(2)}) collective-permute-start(f16[2,4,8,8,1,2,256]{6,3,5,4,2,1,0:T(8,128)(2,1)} %get-tuple-element.9), channel_id=1, source_target_pairs={{1,0},{2,1},{3,2},{4,3},{5,4},{6,5},{7,6},{8,7},{9,8},{10,9},{11,1... | collective-permute-start | bytes 1572872 | tf_op jit(solution)/shard_map/ppermute | solution.py:132
  56.8 1.3 %copy.199 = bf16[64,8,8,128]{3,1,2,0:T(8,128)(2,1)} copy(bf16[64,8,8,128]{3,2,1,0:T(8,128)(2,1)S(1)} %bitcast.74) | data formatting | bytes 2097152
  58.0 0.9 copy_bitcast_fusion.2.l_ref
  58.9 7.8 %shard_map.64 = f32[30,1024]{1,0:T(8,128)} custom-call(bf16[30,128,512]{2,1,0:T(8,128)(2,1)} %pad_maximum_fusion.k_ref, bf16[512,1024]{1,0:T(8,128)(2,1)} %bitcast.75, f32[128,1024]{1,0:T(8,128)} %copy_bitcast_fusion.2.l_ref), custom_call_target="tpu_custom_call" | custom-call | tf_op jit(solution)/shard_map/pallas_call | solution.py:76
  66.7 0.9 convert_element_type.103
  67.7 0.8 broadcast_in_dim.62
  68.5 5.2 %all-to-all-start.1 = ((bf16[30,16,2,128]{3,2,0,1:T(2,128)(2,1)}), bf16[30,16,2,128]{3,2,0,1:T(2,128)(2,1)S(1)}, u32[]{:S(2)}, u32[]{:S(2)}) async-start(bf16[30,16,2,128]{3,2,0,1:T(2,128)(2,1)} %bitcast.83), calls=%async_computation.1 | async-start | bytes 491520 | tf_op jit(solution)/shard_map/all_to_all | solution.py:171
  73.7 4.1 %fusion.7 = f32[2,4,8,8,1,2,256]{6,3,5,4,2,1,0:T(8,128)S(1)} fusion(f32[2,4,8,8,1,2,256]{6,3,5,4,2,1,0:T(8,128)S(1)} %bitcast.72, f32[2,4,8,8,1,2,1]{6,3,5,4,2,1,0:T(8,128)} %get-tuple-element.34, f32[2,4,8,8,1,2,255]{6,3,5,4,2,1,0:T(8,128)} %get-tuple-element.36, f32[2,4,8,8,1,2,255]{6,3,5,4,2,1,0:T(8,128)} %get-tuple-element.35, ...), kind=kLoop, calls=%fused_computation.18 | loop fusion | flops 6291456 | bytes 8388616 | tf_op jit(solution)/shard_map/sub | solution.py:145
  77.9 1.5 %multiply_subtract_fusion = f32[2,4,8,8,1,2,256]{6,3,5,4,2,1,0:T(8,128)S(1)} fusion(f32[2,4,8,8,1,2,256]{6,3,5,4,2,1,0:T(8,128)S(1)} %fusion.7, f16[2,4,8,8,1,2,256]{6,3,5,4,2,1,0:T(8,128)(2,1)} %collective-permute-done.3, f16[2,4,8,8,1,2,256]{6,3,5,4,2,1,0:T(8,128)(2,1)} %collective-permute-done.2, f32[2]{0:T(128)S(1)} %broadcast_multiply_fusion), kind=kLoop, calls=%fused_computation.42 | loop fusion | flops 1310720 | bytes 3145736 | tf_op jit(solution)/shard_map/sub | solution.py:147
  79.4 4.2 %all-to-all-done.1 = bf16[30,16,2,128]{3,2,0,1:T(2,128)(2,1)S(1)} async-done(((bf16[30,16,2,128]{3,2,0,1:T(2,128)(2,1)}), bf16[30,16,2,128]{3,2,0,1:T(2,128)(2,1)S(1)}, u32[]{:S(2)}, u32[]{:S(2)}) %all-to-all-start.1) | async-done | bytes 245792 | tf_op jit(solution)/shard_map/all_to_all | solution.py:171
  84.2 2.7 %gather_fusion.1 = f32[256,2,512]{2,1,0:T(2,128)} fusion(f32[120,2,512]{2,1,0:T(2,128)S(1)} %reshape.476, s32[1024]{0:T(1024)S(1)} %pad_clamp_fusion), kind=kCustom, calls=%fused_computation.1 | custom fusion | bytes 2098176 | tf_op jit(solution)/shard_map/jit(_take)/gather | solution.py:181
  86.8 4.0 %fusion.22 = f32[2,256,1,512]{3,0,1,2:T(2,128)S(1)} fusion(f32[2,256,512]{2,1,0:T(8,128)S(1)} %bitcast.73, f32[256,2,512]{2,1,0:T(2,128)} %gather_fusion.1, pred[256]{0:T(512)(128)(4,1)S(1)} %compare_and_fusion, pred[256]{0:T(512)(128)(4,1)S(1)} %gt.18, f32[2]{0:T(128)S(1)} %copy-done.4, f32[2,256,1,512]{3,2,1,0:T(1,128)S(1)} %copy-done), kind=kLoop, calls=%fused_computation.40 | loop fusion | flops 1310720 | bytes 4194824 | tf_op jit(solution)/shard_map/add | solution.py:189
  90.9 2.0 %copy.178 = f32[2,256,1,512]{3,2,1,0:T(1,128)} copy(f32[2,256,1,512]{3,0,1,2:T(2,128)S(1)} %fusion.22) | data formatting | bytes 2097152 | tf_op jit(solution)/shard_map/add | solution.py:189
  (57 shorter events, 5.4 us)
Async XLA Ops:
  0.0 9.4 %copy-start = (f32[2,256,1,512]{3,2,1,0:T(1,128)S(1)}, f32[2,256,1,512]{3,2,1,0:T(1,128)}, u32[]{:S(2)}) copy-start(f32[2,256,1,512]{3,2,1,0:T(1,128)} %param.6) | copy-start | bytes 3145732
  0.0 10.3 %copy-start.3 = (s32[120]{0:T(128)S(1)}, s32[120]{0:T(128)}, u32[]{:S(2)}) copy-start(s32[120]{0:T(128)} %param.9) | copy-start | bytes 1444
  4.6 24.2 %collective-permute-start.1 = (f16[2,1,8,8,1,2,256]{6,3,5,4,2,1,0:T(8,128)(2,1)}, f16[2,1,8,8,1,2,256]{6,3,5,4,2,1,0:T(8,128)(2,1)S(1)}, u32[]{:S(2)}, u32[]{:S(2)}) collective-permute-start(f16[2,1,8,8,1,2,256]{6,3,5,4,2,1,0:T(8,128)(2,1)} %get-tuple-element.38), channel_id=1, source_target_pairs={{0,16},{16,32},{32,48},{1,17},{17,33},{33,49},{2,18},{18,34},{34,5... | collective-permute-start | bytes 393224 | tf_op jit(solution)/shard_map/ppermute | solution.py:107
  8.1 20.7 %collective-permute-start = (f16[2,1,8,8,1,2,256]{6,3,5,4,2,1,0:T(8,128)(2,1)S(1)}, f16[2,1,8,8,1,2,256]{6,3,5,4,2,1,0:T(8,128)(2,1)S(1)}, u32[]{:S(2)}, u32[]{:S(2)}) collective-permute-start(f16[2,1,8,8,1,2,256]{6,3,5,4,2,1,0:T(8,128)(2,1)S(1)} %get-tuple-element.37), channel_id=1, source_target_pairs={{16,0},{32,16},{48,32},{17,1},{33,17},{49,33},{18,2},{34,18},{50,3... | collective-permute-start | bytes 393224 | tf_op jit(solution)/shard_map/ppermute | solution.py:112
  12.7 21.5 %all-to-all-start = ((bf16[2,120,4,128]{3,0,1,2:T(2,128)(2,1)}), bf16[2,120,4,128]{3,0,1,2:T(2,128)(2,1)S(1)}, u32[]{:S(2)}, u32[]{:S(2)}) async-start(bf16[2,120,4,128]{3,0,1,2:T(2,128)(2,1)} %fusion.26), calls=%async_computation | async-start | bytes 491520 | tf_op jit(solution)/shard_map/all_to_all | solution.py:128
  18.6 5.2 %copy-start.5 = (f32[2]{0:T(128)S(1)}, f32[2]{0:T(128)}, u32[]{:S(2)}) copy-start(f32[2]{0:T(128)} %param.10) | copy-start | bytes 28
  21.5 4.4 %copy-start.2 = (s32[8,8]{1,0:T(8,128)S(1)}, s32[8,8]{1,0:T(8,128)}, u32[]{:S(2)}) copy-start(s32[8,8]{1,0:T(8,128)} %param.8) | copy-start | bytes 772
  23.9 4.3 %copy-start.6 = (f32[2]{0:T(128)S(1)}, f32[2]{0:T(128)}, u32[]{:S(2)}) copy-start(f32[2]{0:T(128)} %param.11) | copy-start | bytes 28
  34.3 21.6 %collective-permute-start.6 = (bf16[8,120,1,128]{3,1,0,2:T(8,128)(2,1)S(1)}, bf16[8,120,1,128]{3,1,0,2:T(8,128)(2,1)S(1)}, u32[]{:S(2)}, u32[]{:S(2)}) collective-permute-start(bf16[8,120,1,128]{3,1,0,2:T(8,128)(2,1)S(1)} %bitcast.79), channel_id=1, source_target_pairs={{0,48},{16,0},{1,49},{17,1},{2,50},{18,2},{3,51},{19,3},{4,52},{20... | collective-permute-start | bytes 737288 | tf_op jit(solution)/shard_map/ppermute | solution.py:90
  40.3 15.6 %collective-permute-start.5 = (bf16[8,120,1,128]{3,1,0,2:T(8,128)(2,1)S(1)}, bf16[8,120,1,128]{3,1,0,2:T(8,128)(2,1)S(1)}, u32[]{:S(2)}, u32[]{:S(2)}) collective-permute-start(bf16[8,120,1,128]{3,1,0,2:T(8,128)(2,1)S(1)} %bitcast.80), channel_id=1, source_target_pairs={{0,32},{16,48},{1,33},{17,49},{2,34},{18,50},{3,35},{19,51},{4,36}... | collective-permute-start | bytes 737288 | tf_op jit(solution)/shard_map/ppermute | solution.py:90
  41.6 14.3 %collective-permute-start.4 = (bf16[8,120,1,128]{3,1,0,2:T(8,128)(2,1)S(1)}, bf16[8,120,1,128]{3,1,0,2:T(8,128)(2,1)S(1)}, u32[]{:S(2)}, u32[]{:S(2)}) collective-permute-start(bf16[8,120,1,128]{3,1,0,2:T(8,128)(2,1)S(1)} %bitcast.81), channel_id=1, source_target_pairs={{0,16},{16,32},{1,17},{17,33},{2,18},{18,34},{3,19},{19,35},{4,20}... | collective-permute-start | bytes 737288 | tf_op jit(solution)/shard_map/ppermute | solution.py:90
  45.5 32.5 %collective-permute-start.3 = (f16[2,4,8,8,1,2,256]{6,3,5,4,2,1,0:T(8,128)(2,1)}, f16[2,4,8,8,1,2,256]{6,3,5,4,2,1,0:T(8,128)(2,1)}, u32[]{:S(2)}, u32[]{:S(2)}) collective-permute-start(f16[2,4,8,8,1,2,256]{6,3,5,4,2,1,0:T(8,128)(2,1)} %get-tuple-element.10), channel_id=1, source_target_pairs={{0,1},{1,2},{2,3},{3,4},{4,5},{5,6},{6,7},{7,8},{8,9},{9,10},{10,1... | collective-permute-start | bytes 1572872 | tf_op jit(solution)/shard_map/ppermute | solution.py:135
  47.4 30.5 %collective-permute-start.2 = (f16[2,4,8,8,1,2,256]{6,3,5,4,2,1,0:T(8,128)(2,1)}, f16[2,4,8,8,1,2,256]{6,3,5,4,2,1,0:T(8,128)(2,1)}, u32[]{:S(2)}, u32[]{:S(2)}) collective-permute-start(f16[2,4,8,8,1,2,256]{6,3,5,4,2,1,0:T(8,128)(2,1)} %get-tuple-element.9), channel_id=1, source_target_pairs={{1,0},{2,1},{3,2},{4,3},{5,4},{6,5},{7,6},{8,7},{9,8},{10,9},{11,1... | collective-permute-start | bytes 1572872 | tf_op jit(solution)/shard_map/ppermute | solution.py:132
  58.0 15.7 %copy-start.1 = (f32[2,4,8,8,1,2,255]{6,3,5,4,2,1,0:T(8,128)S(1)}, f32[2,4,8,8,1,2,255]{6,3,5,4,2,1,0:T(8,128)}, u32[]{:S(2)}) copy-start(f32[2,4,8,8,1,2,255]{6,3,5,4,2,1,0:T(8,128)} %get-tuple-element.31) | copy-start | bytes 3133444
  68.5 15.1 %all-to-all-start.1 = ((bf16[30,16,2,128]{3,2,0,1:T(2,128)(2,1)}), bf16[30,16,2,128]{3,2,0,1:T(2,128)(2,1)S(1)}, u32[]{:S(2)}, u32[]{:S(2)}) async-start(bf16[30,16,2,128]{3,2,0,1:T(2,128)(2,1)} %bitcast.83), calls=%async_computation.1 | async-start | bytes 491520 | tf_op jit(solution)/shard_map/all_to_all | solution.py:171
  77.9 9.0 %copy-start.4 = (f32[2]{0:T(128)S(1)}, f32[2]{0:T(128)}, u32[]{:S(2)}) copy-start(f32[2]{0:T(128)} %neg.4) | copy-start | bytes 28

commit v15 on v13

--- a/solution.py
+++ b/solution.py
@@ -151,15 +151,12 @@
 
     chooser = jnp.stack([(pair_kind == k).astype(jnp.float32) for k in range(NKIND)])
     partner = jnp.einsum("ksr,rlc->klsc", chooser, low_all, precision=lax.Precision.HIGHEST)
-    part_hi = partner.astype(jnp.bfloat16)
-    part_lo = (partner - part_hi.astype(jnp.float32)).astype(jnp.bfloat16)
-    rhs = jnp.stack([piece for k in range(NKIND) for piece in (part_hi[k], part_lo[k])])
-    rhs = jnp.pad(rhs, ((0, 0), (0, PAD - low_count), (0, 0), (0, 0)))
-    rhs = rhs.reshape(2 * NKIND * PAD, species_all * block_cells)
+    rhs = jnp.pad(partner.astype(jnp.bfloat16), ((0, 0), (0, PAD - low_count), (0, 0), (0, 0)))
+    rhs = rhs.reshape(NKIND * PAD, species_all * block_cells)
     lmat = jnp.pad(jnp.moveaxis(low_all, 1, 0), ((0, PAD - low_count), (0, 0), (0, 0)))
     lmat = lmat.reshape(PAD, species_all * block_cells)
     kpad = jnp.pad(kernel, ((0, 0), (0, 0), (0, PAD - low_count), (0, PAD - low_count)))
-    kcat = jnp.concatenate([kpad[k] for k in range(NKIND) for _ in range(2)], axis=-1)
+    kcat = jnp.concatenate([kpad[k] for k in range(NKIND)], axis=-1)
     gained = collide_call(kcat, rhs, lmat)
 
     gained = gained.reshape(out_rows, species_devs, 1, own_count, block_cells)

time: 93.2 us -> 94.4 us (1.013)
  the two profiles are of different devices: /device:TPU:2 before, /device:TPU:33 now
where the time goes in v15:
time: 94.4 us; the launch traced here: 93.8 us
  starting transfers between devices  34.2 us (36%)
  other arithmetic  21.8 us (23%)
  local copies, waits for them, and re-layouts  18.9 us (20%)
  waiting for transfers between devices  13.1 us (14%)
  Pallas kernels  5.11 us (5%)
    ppermute x1, waiting for transfers between devices, per_device(): lax.ppermute(up_edge, 'space', [(i + 1, i) for i in range(space_devs - 1)])  13.1 us
    ppermute x3, starting transfers between devices, shift_permutes(): received.append((shift, lax.ppermute(values, axis, pairs)))  9.23 us
    ppermute x1, starting transfers between devices, per_device(): lax.ppermute(down_edge, 'space', [(i, i + 1) for i in range(space_devs -...  8.52 us
    all_to_all x1, starting transfers between devices, per_device(): spread = lax.all_to_all(picked, 'species', 2, 0, tiled=True)  5.44 us
    pallas_call x1, Pallas kernels, collide_call(): pl.pallas_call(collide_body, out_shape=jax.ShapeDtypeStruct((kcat.shape[0...  5.11 us
    all_to_all x1, starting transfers between devices, per_device(): lax.all_to_all(gained.astype(jnp.bfloat16), ('species', 'mode'), 1, 1, ti...  4.56 us
    sub x1, other arithmetic, per_device(): phase_field - nu_step * thermal_speed.reshape(own_count, 1, 1, 1, 1, 1, 1...  4.06 us
    add x1, other arithmetic, per_device(): advected.reshape(own_count, mode_count, row_count, plane_cells)  4.05 us
  transfers between devices with their start and end apart: 9, of which 1 were waited for; matrix products, arithmetic and copies ran while one was open for 29% of the time, Pallas kernels for 5%

profile of v15, /device:TPU:33, one launch (start us, length us, event | category | flops | bytes accessed | tf_op | source)
XLA Modules:
  0.0 93.8 jit_solution(15222227096199469876)
XLA Ops:
  0.0 3.8 %reduce.18 = f32[2,256,512]{2,1,0:T(8,128)S(1)} reduce(f32[2,256,1,512]{3,2,1,0:T(1,128)} %param.6, f32[]{:T(128)} %constant.93), dimensions={2}, to_apply=%param.6.reduce_sub_computation | reduce | bytes 2097156 | tf_op args[0]
  3.9 0.7 fusion.38
  4.6 3.2 %collective-permute-start.1 = (f16[2,1,8,8,1,2,256]{6,3,5,4,2,1,0:T(8,128)(2,1)}, f16[2,1,8,8,1,2,256]{6,3,5,4,2,1,0:T(8,128)(2,1)S(1)}, u32[]{:S(2)}, u32[]{:S(2)}) collective-permute-start(f16[2,1,8,8,1,2,256]{6,3,5,4,2,1,0:T(8,128)(2,1)} %get-tuple-element.36), channel_id=1, source_target_pairs={{0,16},{16,32},{32,48},{1,17},{17,33},{33,49},{2,18},{18,34},{34,5... | collective-permute-start | bytes 393224 | tf_op jit(solution)/shard_map/ppermute | solution.py:107
  7.9 1.3 %collective-permute-start = (f16[2,1,8,8,1,2,256]{6,3,5,4,2,1,0:T(8,128)(2,1)S(1)}, f16[2,1,8,8,1,2,256]{6,3,5,4,2,1,0:T(8,128)(2,1)S(1)}, u32[]{:S(2)}, u32[]{:S(2)}) collective-permute-start(f16[2,1,8,8,1,2,256]{6,3,5,4,2,1,0:T(8,128)(2,1)S(1)} %get-tuple-element.35), channel_id=1, source_target_pairs={{16,0},{32,16},{48,32},{17,1},{33,17},{49,33},{18,2},{34,18},{50,3... | collective-permute-start | bytes 393224 | tf_op jit(solution)/shard_map/ppermute | solution.py:112
  9.2 0.8 copy.197
  10.0 1.1 %gather_fusion = bf16[120,2,512]{2,1,0:T(2,128)(2,1)S(1)} fusion(bf16[2,256,512]{2,0,1:T(2,128)(2,1)S(1)} %bitcast.76, s32[1024]{0:T(1024)S(1)} %pad_clamp_fusion.1), kind=kCustom, calls=%fused_computation | custom fusion | bytes 492000 | tf_op jit(solution)/shard_map/jit(_take)/gather | solution.py:124
  11.1 1.4 %fusion.27 = bf16[2,120,4,128]{3,0,1,2:T(2,128)(2,1)} fusion(pred[120]{0:T(512)(128)(4,1)S(1)} %get-tuple-element.13, pred[120]{0:T(512)(128)(4,1)S(1)} %get-tuple-element.39, bf16[120,2,512]{2,1,0:T(2,128)(2,1)S(1)} %gather_fusion), kind=kLoop, calls=%fused_computation.51 | loop fusion | flops 245760 | bytes 491760 | tf_op jit(solution)/shard_map/convert_element_type | solution.py:124
  12.5 5.4 %all-to-all-start = ((bf16[2,120,4,128]{3,0,1,2:T(2,128)(2,1)}), bf16[2,120,4,128]{3,0,1,2:T(2,128)(2,1)S(1)}, u32[]{:S(2)}, u32[]{:S(2)}) async-start(bf16[2,120,4,128]{3,0,1,2:T(2,128)(2,1)} %fusion.27), calls=%async_computation | async-start | bytes 491520 | tf_op jit(solution)/shard_map/all_to_all | solution.py:128
  17.9 1.2 %fusion.34 = (f32[2,4,8,8,1,2,1]{6,3,5,4,2,1,0:T(8,128)}, f32[2,4,8,8,1,2,1]{6,3,5,4,2,1,0:T(8,128)}) fusion(f32[2,4,8,8,1,2,256]{6,3,5,4,2,1,0:T(8,128)S(1)} %bitcast.66), kind=kLoop, calls=%fused_computation.80 | loop fusion | bytes 16384 | tf_op jit(solution)/shard_map/jit(_roll_static)/slice | solution.py:52
  19.1 1.7 %fusion.35 = (f32[2,4,8,8,1,2,255]{6,3,5,4,2,1,0:T(8,128)}, f32[2,4,8,8,1,2,255]{6,3,5,4,2,1,0:T(8,128)}) fusion(f32[2,4,8,8,1,2,256]{6,3,5,4,2,1,0:T(8,128)S(1)} %bitcast.67), kind=kLoop, calls=%fused_computation.81 | loop fusion | bytes 4177920 | tf_op jit(solution)/shard_map/jit(_roll_static)/slice | solution.py:52
  20.8 1.1 %fusion.32 = (f32[2,4,8,8,1,1,256]{6,3,5,4,2,1,0:T(8,128)}, f32[2,4,8,8,1,1,256]{6,3,5,4,2,1,0:T(8,128)}) fusion(f32[2,4,8,8,1,2,256]{6,3,5,4,2,1,0:T(8,128)S(1)} %bitcast.68), kind=kLoop, calls=%fused_computation.78 | loop fusion | bytes 2097152 | tf_op jit(solution)/shard_map/jit(_roll_static)/slice | solution.py:51
  23.9 2.0 %fusion.24 = (bf16[30,128,128]{2,1,0:T(8,128)(2,1)S(1)}, bf16[30,128,128]{2,1,0:T(8,128)(2,1)S(1)}) fusion(bf16[2,30,120,120]{3,2,1,0:T(8,128)(2,1)} %param.7), kind=kLoop, calls=%fused_computation.44 | loop fusion | bytes 3694080 | tf_op jit(solution)/shard_map/squeeze | solution.py:159
  26.1 1.5 %pad_maximum_fusion.k_ref = bf16[30,128,256]{2,1,0:T(8,128)(2,1)} fusion(bf16[30,128,128]{2,1,0:T(8,128)(2,1)S(1)} %get-tuple-element.16, bf16[30,128,128]{2,1,0:T(8,128)(2,1)S(1)} %get-tuple-element.15), kind=kLoop, calls=%fused_computation.4 | loop fusion | flops 3932160 | bytes 3932160 | tf_op jit(solution)/shard_map/concatenate | solution.py:159
  27.8 2.9 %subtract_convert_fusion = (f16[2,4,8,8,1,2,256]{6,3,5,4,2,1,0:T(8,128)(2,1)}, f16[2,4,8,8,1,2,256]{6,3,5,4,2,1,0:T(8,128)(2,1)}, f32[2,4,8,8,1,2,256]{6,3,5,4,2,1,0:T(8,128)S(1)}, f32[2,4,8,8,1,2,256]{6,3,5,4,2,1,0:T(8,128)}) fusion(f32[2,4,8,8,1,2,256]{6,3,5,4,2,1,0:T(8,128)S(1)} %bitcast.69, f32[2,1,8,8,1,2,256]{6,3,5,4,2,1,0:T(8,128)S(1)} %convert_element_type.90, ...), kind=kLoop, calls=%fused_computation.42 | loop fusion | flops 4718592 | bytes 4720672 | tf_op jit(solution)/shard_map/convert_element_type | solution.py:130
  30.7 1.7 %fusion.37 = (f32[2,4,8,8,1,2,255]{6,3,5,4,2,1,0:T(8,128)}, f32[2,4,8,8,1,2,255]{6,3,5,4,2,1,0:T(8,128)}) fusion(f32[2,4,8,8,1,2,256]{6,3,5,4,2,1,0:T(8,128)S(1)} %get-tuple-element.21), kind=kLoop, calls=%fused_computation.83 | loop fusion | bytes 4177920 | tf_op jit(solution)/shard_map/jit(_roll_static)/slice | solution.py:54
  32.4 5.4 %collective-permute-start.6 = (bf16[8,120,1,128]{3,1,0,2:T(8,128)(2,1)S(1)}, bf16[8,120,1,128]{3,1,0,2:T(8,128)(2,1)S(1)}, u32[]{:S(2)}, u32[]{:S(2)}) collective-permute-start(bf16[8,120,1,128]{3,1,0,2:T(8,128)(2,1)S(1)} %bitcast.77), channel_id=1, source_target_pairs={{0,48},{16,0},{1,49},{17,1},{2,50},{18,2},{3,51},{19,3},{4,52},{20... | collective-permute-start | bytes 737288 | tf_op jit(solution)/shard_map/ppermute | solution.py:90
  37.9 1.3 %collective-permute-start.5 = (bf16[8,120,1,128]{3,1,0,2:T(8,128)(2,1)S(1)}, bf16[8,120,1,128]{3,1,0,2:T(8,128)(2,1)S(1)}, u32[]{:S(2)}, u32[]{:S(2)}) collective-permute-start(bf16[8,120,1,128]{3,1,0,2:T(8,128)(2,1)S(1)} %bitcast.78), channel_id=1, source_target_pairs={{0,32},{16,48},{1,33},{17,49},{2,34},{18,50},{3,35},{19,51},{4,36}... | collective-permute-start | bytes 737288 | tf_op jit(solution)/shard_map/ppermute | solution.py:90
  39.2 2.5 %collective-permute-start.4 = (bf16[8,120,1,128]{3,1,0,2:T(8,128)(2,1)S(1)}, bf16[8,120,1,128]{3,1,0,2:T(8,128)(2,1)S(1)}, u32[]{:S(2)}, u32[]{:S(2)}) collective-permute-start(bf16[8,120,1,128]{3,1,0,2:T(8,128)(2,1)S(1)} %bitcast.79), channel_id=1, source_target_pairs={{0,16},{16,32},{1,17},{17,33},{2,18},{18,34},{3,19},{19,35},{4,20}... | collective-permute-start | bytes 737288 | tf_op jit(solution)/shard_map/ppermute | solution.py:90
  41.7 1.2 %fusion.36 = (f32[2,4,8,8,1,2,1]{6,3,5,4,2,1,0:T(8,128)}, f32[2,4,8,8,1,2,1]{6,3,5,4,2,1,0:T(8,128)}) fusion(f32[2,4,8,8,1,2,256]{6,3,5,4,2,1,0:T(8,128)S(1)} %get-tuple-element.21), kind=kLoop, calls=%fused_computation.82 | loop fusion | bytes 16384 | tf_op jit(solution)/shard_map/jit(_roll_static)/slice | solution.py:54
  42.9 8.5 %collective-permute-start.3 = (f16[2,4,8,8,1,2,256]{6,3,5,4,2,1,0:T(8,128)(2,1)}, f16[2,4,8,8,1,2,256]{6,3,5,4,2,1,0:T(8,128)(2,1)}, u32[]{:S(2)}, u32[]{:S(2)}) collective-permute-start(f16[2,4,8,8,1,2,256]{6,3,5,4,2,1,0:T(8,128)(2,1)} %get-tuple-element.10), channel_id=1, source_target_pairs={{0,1},{1,2},{2,3},{3,4},{4,5},{5,6},{6,7},{7,8},{8,9},{9,10},{10,1... | collective-permute-start | bytes 1572872 | tf_op jit(solution)/shard_map/ppermute | solution.py:135
  51.4 1.9 %collective-permute-start.2 = (f16[2,4,8,8,1,2,256]{6,3,5,4,2,1,0:T(8,128)(2,1)}, f16[2,4,8,8,1,2,256]{6,3,5,4,2,1,0:T(8,128)(2,1)}, u32[]{:S(2)}, u32[]{:S(2)}) collective-permute-start(f16[2,4,8,8,1,2,256]{6,3,5,4,2,1,0:T(8,128)(2,1)} %get-tuple-element.9), channel_id=1, source_target_pairs={{1,0},{2,1},{3,2},{4,3},{5,4},{6,5},{7,6},{8,7},{9,8},{10,9},{11,1... | collective-permute-start | bytes 1572872 | tf_op jit(solution)/shard_map/ppermute | solution.py:132
  53.8 0.9 copy.198
  54.7 0.9 copy_bitcast_fusion.2.l_ref
  55.5 5.1 %shard_map.64 = f32[30,1024]{1,0:T(8,128)} custom-call(bf16[30,128,256]{2,1,0:T(8,128)(2,1)} %pad_maximum_fusion.k_ref, bf16[256,1024]{1,0:T(8,128)(2,1)} %bitcast.75, f32[128,1024]{1,0:T(8,128)} %copy_bitcast_fusion.2.l_ref), custom_call_target="tpu_custom_call" | custom-call | tf_op jit(solution)/shard_map/pallas_call | solution.py:76
  60.7 0.9 convert_element_type.99
  61.7 0.8 broadcast_in_dim.62
  62.5 4.6 %all-to-all-start.1 = ((bf16[30,16,2,128]{3,2,0,1:T(2,128)(2,1)}), bf16[30,16,2,128]{3,2,0,1:T(2,128)(2,1)S(1)}, u32[]{:S(2)}, u32[]{:S(2)}) async-start(bf16[30,16,2,128]{3,2,0,1:T(2,128)(2,1)} %bitcast.81), calls=%async_computation.1 | async-start | bytes 491520 | tf_op jit(solution)/shard_map/all_to_all | solution.py:166
  67.2 13.1 %collective-permute-done.2 = f16[2,4,8,8,1,2,256]{6,3,5,4,2,1,0:T(8,128)(2,1)} collective-permute-done((f16[2,4,8,8,1,2,256]{6,3,5,4,2,1,0:T(8,128)(2,1)}, f16[2,4,8,8,1,2,256]{6,3,5,4,2,1,0:T(8,128)(2,1)}, u32[]{:S(2)}, u32[]{:S(2)}) %collective-permute-start.2) | collective-permute-done | bytes 524320 | tf_op jit(solution)/shard_map/ppermute | solution.py:132
  80.3 4.1 %fusion.8 = f32[2,4,8,8,1,2,256]{6,3,5,4,2,1,0:T(8,128)S(1)} fusion(f32[2,4,8,8,1,2,256]{6,3,5,4,2,1,0:T(8,128)S(1)} %bitcast.70, f32[2,4,8,8,1,2,1]{6,3,5,4,2,1,0:T(8,128)} %get-tuple-element.32, f32[2,4,8,8,1,2,255]{6,3,5,4,2,1,0:T(8,128)} %get-tuple-element.34, f32[2,4,8,8,1,2,255]{6,3,5,4,2,1,0:T(8,128)} %get-tuple-element.33, ...), kind=kLoop, calls=%fused_computation.19 | loop fusion | flops 7340032 | bytes 9437192 | tf_op jit(solution)/shard_map/sub | solution.py:145
  85.0 2.7 %gather_fusion.1 = f32[256,2,512]{2,1,0:T(2,128)} fusion(f32[120,2,512]{2,1,0:T(2,128)S(1)} %reshape.456, s32[1024]{0:T(1024)S(1)} %pad_clamp_fusion), kind=kCustom, calls=%fused_computation.1 | custom fusion | bytes 2098176 | tf_op jit(solution)/shard_map/jit(_take)/gather | solution.py:176
  87.7 4.0 %fusion.23 = f32[2,256,1,512]{3,0,1,2:T(2,128)S(1)} fusion(f32[2,256,512]{2,1,0:T(8,128)S(1)} %bitcast.71, f32[256,2,512]{2,1,0:T(2,128)} %gather_fusion.1, pred[256]{0:T(512)(128)(4,1)S(1)} %compare_and_fusion, pred[256]{0:T(512)(128)(4,1)S(1)} %gt.18, f32[2]{0:T(128)S(1)} %neg.4, f32[2,256,1,512]{3,2,1,0:T(1,128)S(1)} %copy-done), kind=kLoop, calls=%fused_computation.40 | loop fusion | flops 1310720 | bytes 4194824 | tf_op jit(solution)/shard_map/add | solution.py:184
  91.7 2.0 %copy.178 = f32[2,256,1,512]{3,2,1,0:T(1,128)} copy(f32[2,256,1,512]{3,0,1,2:T(2,128)S(1)} %fusion.23) | data formatting | bytes 2097152 | tf_op jit(solution)/shard_map/add | solution.py:184
  (57 shorter events, 3.6 us)
Async XLA Ops:
  0.0 9.2 %copy-start = (f32[2,256,1,512]{3,2,1,0:T(1,128)S(1)}, f32[2,256,1,512]{3,2,1,0:T(1,128)}, u32[]{:S(2)}) copy-start(f32[2,256,1,512]{3,2,1,0:T(1,128)} %param.6) | copy-start | bytes 3145732
  3.8 6.2 %copy-start.5 = (s32[120]{0:T(128)S(1)}, s32[120]{0:T(128)}, u32[]{:S(2)}) copy-start(s32[120]{0:T(128)} %param.9) | copy-start | bytes 1444
  4.6 23.1 %collective-permute-start.1 = (f16[2,1,8,8,1,2,256]{6,3,5,4,2,1,0:T(8,128)(2,1)}, f16[2,1,8,8,1,2,256]{6,3,5,4,2,1,0:T(8,128)(2,1)S(1)}, u32[]{:S(2)}, u32[]{:S(2)}) collective-permute-start(f16[2,1,8,8,1,2,256]{6,3,5,4,2,1,0:T(8,128)(2,1)} %get-tuple-element.36), channel_id=1, source_target_pairs={{0,16},{16,32},{32,48},{1,17},{17,33},{33,49},{2,18},{18,34},{34,5... | collective-permute-start | bytes 393224 | tf_op jit(solution)/shard_map/ppermute | solution.py:107
  7.9 19.9 %collective-permute-start = (f16[2,1,8,8,1,2,256]{6,3,5,4,2,1,0:T(8,128)(2,1)S(1)}, f16[2,1,8,8,1,2,256]{6,3,5,4,2,1,0:T(8,128)(2,1)S(1)}, u32[]{:S(2)}, u32[]{:S(2)}) collective-permute-start(f16[2,1,8,8,1,2,256]{6,3,5,4,2,1,0:T(8,128)(2,1)S(1)} %get-tuple-element.35), channel_id=1, source_target_pairs={{16,0},{32,16},{48,32},{17,1},{33,17},{49,33},{18,2},{34,18},{50,3... | collective-permute-start | bytes 393224 | tf_op jit(solution)/shard_map/ppermute | solution.py:112
  12.5 19.9 %all-to-all-start = ((bf16[2,120,4,128]{3,0,1,2:T(2,128)(2,1)}), bf16[2,120,4,128]{3,0,1,2:T(2,128)(2,1)S(1)}, u32[]{:S(2)}, u32[]{:S(2)}) async-start(bf16[2,120,4,128]{3,0,1,2:T(2,128)(2,1)} %fusion.27), calls=%async_computation | async-start | bytes 491520 | tf_op jit(solution)/shard_map/all_to_all | solution.py:128
  20.8 2.5 %copy-start.7 = (f32[2]{0:T(128)S(1)}, f32[2]{0:T(128)}, u32[]{:S(2)}) copy-start(f32[2]{0:T(128)} %param.10) | copy-start | bytes 28
  21.9 3.9 %copy-start.4 = (s32[8,8]{1,0:T(8,128)S(1)}, s32[8,8]{1,0:T(8,128)}, u32[]{:S(2)}) copy-start(s32[8,8]{1,0:T(8,128)} %param.8) | copy-start | bytes 772
  26.1 1.7 %copy-start.8 = (f32[2]{0:T(128)S(1)}, f32[2]{0:T(128)}, u32[]{:S(2)}) copy-start(f32[2]{0:T(128)} %param.11) | copy-start | bytes 28
  32.4 20.9 %collective-permute-start.6 = (bf16[8,120,1,128]{3,1,0,2:T(8,128)(2,1)S(1)}, bf16[8,120,1,128]{3,1,0,2:T(8,128)(2,1)S(1)}, u32[]{:S(2)}, u32[]{:S(2)}) collective-permute-start(bf16[8,120,1,128]{3,1,0,2:T(8,128)(2,1)S(1)} %bitcast.77), channel_id=1, source_target_pairs={{0,48},{16,0},{1,49},{17,1},{2,50},{18,2},{3,51},{19,3},{4,52},{20... | collective-permute-start | bytes 737288 | tf_op jit(solution)/shard_map/ppermute | solution.py:90
  37.9 15.5 %collective-permute-start.5 = (bf16[8,120,1,128]{3,1,0,2:T(8,128)(2,1)S(1)}, bf16[8,120,1,128]{3,1,0,2:T(8,128)(2,1)S(1)}, u32[]{:S(2)}, u32[]{:S(2)}) collective-permute-start(bf16[8,120,1,128]{3,1,0,2:T(8,128)(2,1)S(1)} %bitcast.78), channel_id=1, source_target_pairs={{0,32},{16,48},{1,33},{17,49},{2,34},{18,50},{3,35},{19,51},{4,36}... | collective-permute-start | bytes 737288 | tf_op jit(solution)/shard_map/ppermute | solution.py:90
  39.2 14.2 %collective-permute-start.4 = (bf16[8,120,1,128]{3,1,0,2:T(8,128)(2,1)S(1)}, bf16[8,120,1,128]{3,1,0,2:T(8,128)(2,1)S(1)}, u32[]{:S(2)}, u32[]{:S(2)}) collective-permute-start(bf16[8,120,1,128]{3,1,0,2:T(8,128)(2,1)S(1)} %bitcast.79), channel_id=1, source_target_pairs={{0,16},{16,32},{1,17},{17,33},{2,18},{18,34},{3,19},{19,35},{4,20}... | collective-permute-start | bytes 737288 | tf_op jit(solution)/shard_map/ppermute | solution.py:90
  42.9 24.3 %collective-permute-start.3 = (f16[2,4,8,8,1,2,256]{6,3,5,4,2,1,0:T(8,128)(2,1)}, f16[2,4,8,8,1,2,256]{6,3,5,4,2,1,0:T(8,128)(2,1)}, u32[]{:S(2)}, u32[]{:S(2)}) collective-permute-start(f16[2,4,8,8,1,2,256]{6,3,5,4,2,1,0:T(8,128)(2,1)} %get-tuple-element.10), channel_id=1, source_target_pairs={{0,1},{1,2},{2,3},{3,4},{4,5},{5,6},{6,7},{7,8},{8,9},{9,10},{10,1... | collective-permute-start | bytes 1572872 | tf_op jit(solution)/shard_map/ppermute | solution.py:135
  51.4 28.9 %collective-permute-start.2 = (f16[2,4,8,8,1,2,256]{6,3,5,4,2,1,0:T(8,128)(2,1)}, f16[2,4,8,8,1,2,256]{6,3,5,4,2,1,0:T(8,128)(2,1)}, u32[]{:S(2)}, u32[]{:S(2)}) collective-permute-start(f16[2,4,8,8,1,2,256]{6,3,5,4,2,1,0:T(8,128)(2,1)} %get-tuple-element.9), channel_id=1, source_target_pairs={{1,0},{2,1},{3,2},{4,3},{5,4},{6,5},{7,6},{8,7},{9,8},{10,9},{11,1... | collective-permute-start | bytes 1572872 | tf_op jit(solution)/shard_map/ppermute | solution.py:132
  55.5 11.5 %copy-start.1 = (f32[2,4,8,8,1,2,256]{6,3,5,4,2,1,0:T(8,128)S(1)}, f32[2,4,8,8,1,2,256]{6,3,5,4,2,1,0:T(8,128)}, u32[]{:S(2)}) copy-start(f32[2,4,8,8,1,2,256]{6,3,5,4,2,1,0:T(8,128)} %get-tuple-element.22) | copy-start | bytes 3145732
  60.7 19.7 %copy-start.6 = (f32[2]{0:T(128)S(1)}, f32[2]{0:T(128)}, u32[]{:S(2)}) copy-start(f32[2]{0:T(128)} %broadcast_multiply_fusion) | copy-start | bytes 28
  62.5 21.9 %all-to-all-start.1 = ((bf16[30,16,2,128]{3,2,0,1:T(2,128)(2,1)}), bf16[30,16,2,128]{3,2,0,1:T(2,128)(2,1)S(1)}, u32[]{:S(2)}, u32[]{:S(2)}) async-start(bf16[30,16,2,128]{3,2,0,1:T(2,128)(2,1)} %bitcast.81), calls=%async_computation.1 | async-start | bytes 491520 | tf_op jit(solution)/shard_map/all_to_all | solution.py:166
  67.0 13.3 %copy-start.2 = (f32[2,4,8,8,1,2,255]{6,3,5,4,2,1,0:T(8,128)S(1)}, f32[2,4,8,8,1,2,255]{6,3,5,4,2,1,0:T(8,128)}, u32[]{:S(2)}) copy-start(f32[2,4,8,8,1,2,255]{6,3,5,4,2,1,0:T(8,128)} %get-tuple-element.29) | copy-start | bytes 3133444
  67.1 13.3 %copy-start.3 = (f32[2,4,8,8,1,2,255]{6,3,5,4,2,1,0:T(8,128)S(1)}, f32[2,4,8,8,1,2,255]{6,3,5,4,2,1,0:T(8,128)}, u32[]{:S(2)}) copy-start(f32[2,4,8,8,1,2,255]{6,3,5,4,2,1,0:T(8,128)} %get-tuple-element.30) | copy-start | bytes 3133444

commit v16 on v13

--- a/solution.py
+++ b/solution.py
@@ -138,11 +138,6 @@
     holders = [h for h in range(mode_devs) if h * per_vx <= DEG]
     up_all = jnp.concatenate([up_part[:, :, :, :, 1:], from_next], axis=4)
     down_all = jnp.concatenate([from_prev, down_part[:, :, :, :, : row_count - 1]], axis=4)
-    x_term = up_all + down_all + bound_x * phase_field
-    y_term = periodic_term(phase_field, 2, 6, bound_y)
-    z_term = periodic_term(phase_field, 3, 5, bound_z)
-    stream = x_term + y_term + z_term
-    advected = phase_field - nu_step * thermal_speed.reshape(own_count, 1, 1, 1, 1, 1, 1) * stream
 
     low_all = spread
     for _, got in shift_permutes(spread, "mode", holders, mode_devs, False):
@@ -184,6 +179,12 @@
     collide = jnp.where(
         degree_total > DEG, -relax_rate.reshape(own_count, 1, 1) * flat_dist, coll_low
     )
+    collide, phase_field = lax.optimization_barrier((collide, phase_field))
+    x_term = up_all + down_all + bound_x * phase_field
+    y_term = periodic_term(phase_field, 2, 6, bound_y)
+    z_term = periodic_term(phase_field, 3, 5, bound_z)
+    stream = x_term + y_term + z_term
+    advected = phase_field - nu_step * thermal_speed.reshape(own_count, 1, 1, 1, 1, 1, 1) * stream
     return advected.reshape(
         own_count, mode_count, row_count, plane_cells
     ) + dt_step * collide.reshape(own_count, mode_count, row_count, plane_cells)

time: 93.2 us -> 102 us (1.094)
  the two profiles are of different devices: /device:TPU:2 before, /device:TPU:34 now
where the time goes in v16:
time: 102 us; the launch traced here: 101 us
  starting transfers between devices  37 us (36%)
  waiting for transfers between devices  21.8 us (21%)
  other arithmetic  19.7 us (19%)
  local copies, waits for them, and re-layouts  14.4 us (14%)
  Pallas kernels  7.84 us (8%)
    ppermute x1, waiting for transfers between devices, per_device(): lax.ppermute(down_edge, 'space', [(i, i + 1) for i in range(space_devs -...  9.5 us
    ppermute x3, starting transfers between devices, shift_permutes(): received.append((shift, lax.ppermute(values, axis, pairs)))  9.18 us
    all_to_all x1, starting transfers between devices, per_device(): lax.all_to_all(gained.astype(jnp.bfloat16), ('species', 'mode'), 1, 1, ti...  8.66 us
    pallas_call x1, Pallas kernels, collide_call(): pl.pallas_call(collide_body, out_shape=jax.ShapeDtypeStruct((kcat.shape[0...  7.84 us
    ppermute x1, waiting for transfers between devices, per_device(): lax.ppermute(up_edge, 'space', [(i + 1, i) for i in range(space_devs - 1)])  6.35 us
    all_to_all x1, starting transfers between devices, per_device(): spread = lax.all_to_all(picked, 'species', 2, 0, tiled=True)  6 us
    ppermute x3, waiting for transfers between devices, shift_permutes(): received.append((shift, lax.ppermute(values, axis, pairs)))  5.89 us
    ppermute x1, starting transfers between devices, per_device(): lax.ppermute(up_edge, 'space', [(i + 1, i) for i in range(space_devs - 1)])  5.26 us
  transfers between devices with their start and end apart: 9, of which 4 were waited for; matrix products, arithmetic and copies ran while one was open for 18% of the time, Pallas kernels for 0%

profile of v16, /device:TPU:34, one launch (start us, length us, event | category | flops | bytes accessed | tf_op | source)
XLA Modules:
  0.0 101.5 jit_solution(11691932270048627768)
XLA Ops:
  0.0 0.8 compare_and_fusion
  0.8 2.0 %copy.203 = bf16[2,256,1,512]{3,0,1,2:T(2,128)(2,1)S(1)} copy(f32[2,256,1,512]{3,2,1,0:T(1,128)} %param.6) | data formatting | bytes 1572864 | tf_op args[0]
  2.9 1.1 %gather_fusion = bf16[120,2,512]{2,1,0:T(2,128)(2,1)S(1)} fusion(bf16[2,256,512]{2,0,1:T(2,128)(2,1)S(1)} %bitcast.68, s32[1024]{0:T(1024)S(1)} %pad_clamp_fusion.1), kind=kCustom, calls=%fused_computation | custom fusion | bytes 492000 | tf_op jit(solution)/shard_map/jit(_take)/gather | solution.py:124
  4.0 1.4 %fusion.24 = bf16[2,120,4,128]{3,0,1,2:T(2,128)(2,1)} fusion(pred[120]{0:T(512)(128)(4,1)S(1)} %get-tuple-element.19, pred[120]{0:T(512)(128)(4,1)S(1)} %get-tuple-element.47, bf16[120,2,512]{2,1,0:T(2,128)(2,1)S(1)} %gather_fusion), kind=kLoop, calls=%fused_computation.51 | loop fusion | flops 245760 | bytes 491760 | tf_op jit(solution)/shard_map/convert_element_type | solution.py:124
  5.3 6.0 %all-to-all-start = ((bf16[2,120,4,128]{3,0,1,2:T(2,128)(2,1)}), bf16[2,120,4,128]{3,0,1,2:T(2,128)(2,1)S(1)}, u32[]{:S(2)}, u32[]{:S(2)}) async-start(bf16[2,120,4,128]{3,0,1,2:T(2,128)(2,1)} %fusion.24), calls=%async_computation | async-start | bytes 491520 | tf_op jit(solution)/shard_map/all_to_all | solution.py:128
  11.3 3.7 %reduce.18 = f32[2,256,512]{2,1,0:T(8,128)S(1)} reduce(f32[2,256,1,512]{3,2,1,0:T(1,128)} %param.6, f32[]{:T(128)} %constant.93), dimensions={2}, to_apply=%param.6.reduce_sub_computation | reduce | bytes 2097156 | tf_op args[0]
  15.2 0.7 fusion.35
  15.9 1.3 %collective-permute-start = (f16[2,1,8,8,1,2,256]{6,3,5,4,2,1,0:T(8,128)(2,1)}, f16[2,1,8,8,1,2,256]{6,3,5,4,2,1,0:T(8,128)(2,1)S(1)}, u32[]{:S(2)}, u32[]{:S(2)}) collective-permute-start(f16[2,1,8,8,1,2,256]{6,3,5,4,2,1,0:T(8,128)(2,1)} %get-tuple-element.39), channel_id=1, source_target_pairs={{16,0},{32,16},{48,32},{17,1},{33,17},{49,33},{18,2},{34,18},{50,3... | collective-permute-start | bytes 393224 | tf_op jit(solution)/shard_map/ppermute | solution.py:112
  17.1 4.6 %collective-permute-start.1 = (f16[2,1,8,8,1,2,256]{6,3,5,4,2,1,0:T(8,128)(2,1)S(1)}, f16[2,1,8,8,1,2,256]{6,3,5,4,2,1,0:T(8,128)(2,1)S(1)}, u32[]{:S(2)}, u32[]{:S(2)}) collective-permute-start(f16[2,1,8,8,1,2,256]{6,3,5,4,2,1,0:T(8,128)(2,1)S(1)} %get-tuple-element.40), channel_id=1, source_target_pairs={{0,16},{16,32},{32,48},{1,17},{17,33},{33,49},{2,18},{18,34},{34,5... | collective-permute-start | bytes 393224 | tf_op jit(solution)/shard_map/ppermute | solution.py:107
  23.1 2.0 %pad_maximum_fusion.k_ref = bf16[30,128,512]{2,1,0:T(8,128)(2,1)} fusion(bf16[30,128,128]{2,1,0:T(8,128)(2,1)S(1)} %get-tuple-element.22, bf16[30,128,128]{2,1,0:T(8,128)(2,1)S(1)} %get-tuple-element.21), kind=kLoop, calls=%fused_computation.2 | loop fusion | flops 15728640 | bytes 5898240 | tf_op jit(solution)/shard_map/concatenate | solution.py:157
  25.2 1.5 %subtract_convert_fusion = (f16[2,4,8,8,1,2,256]{6,3,5,4,2,1,0:T(8,128)(2,1)}, f16[2,4,8,8,1,2,256]{6,3,5,4,2,1,0:T(8,128)(2,1)}) fusion(f32[2,4,8,8,1,2,256]{6,3,5,4,2,1,0:T(8,128)S(1)} %bitcast.62, f32[2,1,8,8,1,2,256]{6,3,5,4,2,1,0:T(8,128)S(1)} %convert_element_type.93, f32[4]{0:T(128)S(1)} %get-tuple-element.49, ...), kind=kLoop, calls=%fused_computation.41 | loop fusion | flops 3145728 | bytes 2621472 | tf_op jit(solution)/shard_map/convert_element_type | solution.py:130
  26.7 5.1 %collective-permute-start.4 = (bf16[8,120,1,128]{3,1,0,2:T(8,128)(2,1)S(1)}, bf16[8,120,1,128]{3,1,0,2:T(8,128)(2,1)S(1)}, u32[]{:S(2)}, u32[]{:S(2)}) collective-permute-start(bf16[8,120,1,128]{3,1,0,2:T(8,128)(2,1)S(1)} %bitcast.69), channel_id=1, source_target_pairs={{0,48},{16,0},{1,49},{17,1},{2,50},{18,2},{3,51},{19,3},{4,52},{20... | collective-permute-start | bytes 737288 | tf_op jit(solution)/shard_map/ppermute | solution.py:90
  31.8 1.3 %collective-permute-start.3 = (bf16[8,120,1,128]{3,1,0,2:T(8,128)(2,1)S(1)}, bf16[8,120,1,128]{3,1,0,2:T(8,128)(2,1)S(1)}, u32[]{:S(2)}, u32[]{:S(2)}) collective-permute-start(bf16[8,120,1,128]{3,1,0,2:T(8,128)(2,1)S(1)} %bitcast.70), channel_id=1, source_target_pairs={{0,32},{16,48},{1,33},{17,49},{2,34},{18,50},{3,35},{19,51},{4,36}... | collective-permute-start | bytes 737288 | tf_op jit(solution)/shard_map/ppermute | solution.py:90
  33.1 2.8 %collective-permute-start.2 = (bf16[8,120,1,128]{3,1,0,2:T(8,128)(2,1)S(1)}, bf16[8,120,1,128]{3,1,0,2:T(8,128)(2,1)S(1)}, u32[]{:S(2)}, u32[]{:S(2)}) collective-permute-start(bf16[8,120,1,128]{3,1,0,2:T(8,128)(2,1)S(1)} %bitcast.71), channel_id=1, source_target_pairs={{0,16},{16,32},{1,17},{17,33},{2,18},{18,34},{3,19},{19,35},{4,20}... | collective-permute-start | bytes 737288 | tf_op jit(solution)/shard_map/ppermute | solution.py:90
  36.0 4.4 %collective-permute-done.4 = bf16[8,120,1,128]{3,1,0,2:T(8,128)(2,1)S(1)} collective-permute-done((bf16[8,120,1,128]{3,1,0,2:T(8,128)(2,1)S(1)}, bf16[8,120,1,128]{3,1,0,2:T(8,128)(2,1)S(1)}, u32[]{:S(2)}, u32[]{:S(2)}) %collective-permute-start.4) | collective-permute-done | bytes 245792 | tf_op jit(solution)/shard_map/ppermute | solution.py:90
  40.3 1.5 %collective-permute-done.2 = bf16[8,120,1,128]{3,1,0,2:T(8,128)(2,1)S(1)} collective-permute-done((bf16[8,120,1,128]{3,1,0,2:T(8,128)(2,1)S(1)}, bf16[8,120,1,128]{3,1,0,2:T(8,128)(2,1)S(1)}, u32[]{:S(2)}, u32[]{:S(2)}) %collective-permute-start.2) | collective-permute-done | bytes 245792 | tf_op jit(solution)/shard_map/ppermute | solution.py:90
  41.9 0.9 copy_bitcast_fusion.2.l_ref
  43.6 1.2 %copy.202 = bf16[64,8,8,128]{3,1,2,0:T(8,128)(2,1)} copy(bf16[64,8,8,128]{3,2,1,0:T(8,128)(2,1)S(1)} %bitcast.64) | data formatting | bytes 2097152
  44.9 7.8 %shard_map.64 = f32[30,1024]{1,0:T(8,128)} custom-call(bf16[30,128,512]{2,1,0:T(8,128)(2,1)} %pad_maximum_fusion.k_ref, bf16[512,1024]{1,0:T(8,128)(2,1)} %bitcast.65, f32[128,1024]{1,0:T(8,128)} %copy_bitcast_fusion.2.l_ref), custom_call_target="tpu_custom_call" | custom-call | tf_op jit(solution)/shard_map/pallas_call | solution.py:76
  52.7 0.9 convert_element_type.100
  53.7 0.8 broadcast_in_dim.62
  54.5 8.7 %all-to-all-start.1 = ((bf16[30,16,2,128]{3,2,0,1:T(2,128)(2,1)}), bf16[30,16,2,128]{3,2,0,1:T(2,128)(2,1)S(1)}, u32[]{:S(2)}, u32[]{:S(2)}) async-start(bf16[30,16,2,128]{3,2,0,1:T(2,128)(2,1)} %bitcast.14), calls=%async_computation.1 | async-start | bytes 491520 | tf_op jit(solution)/shard_map/all_to_all | solution.py:164
  63.2 0.7 reshape.264
  64.1 5.3 %collective-permute-start.5 = (f16[2,4,8,8,1,2,256]{6,3,5,4,2,1,0:T(8,128)(2,1)}, f16[2,4,8,8,1,2,256]{6,3,5,4,2,1,0:T(8,128)(2,1)}, u32[]{:S(2)}, u32[]{:S(2)}) collective-permute-start(f16[2,4,8,8,1,2,256]{6,3,5,4,2,1,0:T(8,128)(2,1)} %get-tuple-element.14), channel_id=1, source_target_pairs={{1,0},{2,1},{3,2},{4,3},{5,4},{6,5},{7,6},{8,7},{9,8},{10,9},{11,1... | collective-permute-start | bytes 1572872 | tf_op jit(solution)/shard_map/ppermute | solution.py:132
  69.3 2.1 %collective-permute-start.6 = (f16[2,4,8,8,1,2,256]{6,3,5,4,2,1,0:T(8,128)(2,1)}, f16[2,4,8,8,1,2,256]{6,3,5,4,2,1,0:T(8,128)(2,1)}, u32[]{:S(2)}, u32[]{:S(2)}) collective-permute-start(f16[2,4,8,8,1,2,256]{6,3,5,4,2,1,0:T(8,128)(2,1)} %get-tuple-element.15), channel_id=1, source_target_pairs={{0,1},{1,2},{2,3},{3,4},{4,5},{5,6},{6,7},{7,8},{8,9},{9,10},{10,1... | collective-permute-start | bytes 1572872 | tf_op jit(solution)/shard_map/ppermute | solution.py:135
  72.1 2.7 %gather_fusion.1 = f32[256,2,512]{2,1,0:T(2,128)} fusion(f32[120,2,512]{2,1,0:T(2,128)S(1)} %reshape.300, s32[1024]{0:T(1024)S(1)} %pad_clamp_fusion), kind=kCustom, calls=%fused_computation.1 | custom fusion | bytes 2098176 | tf_op jit(solution)/shard_map/jit(_take)/gather | solution.py:174
  74.7 3.3 %bitcast_select_fusion = f32[2,256,512]{2,0,1:T(2,128)S(1)} fusion(f32[256,2,512]{2,1,0:T(2,128)} %gather_fusion.1, pred[256]{0:T(512)(128)(4,1)S(1)} %compare_and_fusion.2, pred[256]{0:T(512)(128)(4,1)S(1)} %gt.18, f32[2]{0:T(128)S(1)} %neg.4, f32[2,256,1,512]{3,2,1,0:T(1,128)S(1)} %copy-done), kind=kLoop, calls=%fused_computation.37 | loop fusion | flops 786432 | bytes 3146248 | tf_op jit(solution)/shard_map/jit(_where)/select_n | solution.py:179
  80.0 6.3 %collective-permute-done.5 = f16[2,4,8,8,1,2,256]{6,3,5,4,2,1,0:T(8,128)(2,1)} collective-permute-done((f16[2,4,8,8,1,2,256]{6,3,5,4,2,1,0:T(8,128)(2,1)}, f16[2,4,8,8,1,2,256]{6,3,5,4,2,1,0:T(8,128)(2,1)}, u32[]{:S(2)}, u32[]{:S(2)}) %collective-permute-start.5) | collective-permute-done | bytes 524320 | tf_op jit(solution)/shard_map/ppermute | solution.py:132
  86.4 9.5 %collective-permute-done.6 = f16[2,4,8,8,1,2,256]{6,3,5,4,2,1,0:T(8,128)(2,1)} collective-permute-done((f16[2,4,8,8,1,2,256]{6,3,5,4,2,1,0:T(8,128)(2,1)}, f16[2,4,8,8,1,2,256]{6,3,5,4,2,1,0:T(8,128)(2,1)}, u32[]{:S(2)}, u32[]{:S(2)}) %collective-permute-start.6) | collective-permute-done | bytes 524320 | tf_op jit(solution)/shard_map/ppermute | solution.py:135
  95.9 2.5 %fusion.7 = f32[2,4,8,8,1,2,256]{6,3,5,4,2,1,0:T(8,128)S(1)} fusion(f32[2,4,8,8,1,2,1]{6,3,5,4,2,1,0:T(8,128)S(1)} %get-tuple-element.36, f32[2,4,8,8,1,2,255]{6,3,5,4,2,1,0:T(8,128)S(1)} %get-tuple-element.38, f32[2,4,8,8,1,2,255]{6,3,5,4,2,1,0:T(8,128)S(1)} %get-tuple-element.37, f32[2,4,8,8,1,2,1]{6,3,5,4,2,1,0:T(8,128)S(1)} %get-tuple-element.35, ...), kind=kLoop, calls=%fused_computation.18 | loop fusion | flops 7340032 | bytes 9437192 | tf_op jit(solution)/shard_map/sub | solution.py:187
  98.3 1.1 %fusion.20 = f32[2,256,1,512]{3,0,1,2:T(2,128)S(1)} fusion(f32[2,256,512]{2,1,0:T(8,128)S(1)} %bitcast.63, f32[2,256,512]{2,0,1:T(2,128)S(1)} %bitcast_select_fusion), kind=kLoop, calls=%fused_computation.39 | loop fusion | flops 524288 | bytes 3145728 | tf_op jit(solution)/shard_map/add | solution.py:188
  99.4 2.0 %copy.178 = f32[2,256,1,512]{3,2,1,0:T(1,128)} copy(f32[2,256,1,512]{3,0,1,2:T(2,128)S(1)} %fusion.20) | data formatting | bytes 2097152 | tf_op jit(solution)/shard_map/add | solution.py:188
  (58 shorter events, 5.2 us)
Async XLA Ops:
  0.0 21.7 %copy-start.3 = (s32[120]{0:T(128)S(1)}, s32[120]{0:T(128)}, u32[]{:S(2)}) copy-start(s32[120]{0:T(128)} %param.9) | copy-start | bytes 1444
  0.0 22.5 %copy-start.1 = (bf16[2,30,120,120]{3,2,1,0:T(8,128)(2,1)S(1)}, bf16[2,30,120,120]{3,2,1,0:T(8,128)(2,1)}, u32[]{:S(2)}) copy-start(bf16[2,30,120,120]{3,2,1,0:T(8,128)(2,1)} %param.7) | copy-start | bytes 5184004
  5.3 21.4 %all-to-all-start = ((bf16[2,120,4,128]{3,0,1,2:T(2,128)(2,1)}), bf16[2,120,4,128]{3,0,1,2:T(2,128)(2,1)S(1)}, u32[]{:S(2)}, u32[]{:S(2)}) async-start(bf16[2,120,4,128]{3,0,1,2:T(2,128)(2,1)} %fusion.24), calls=%async_computation | async-start | bytes 491520 | tf_op jit(solution)/shard_map/all_to_all | solution.py:128
  15.9 9.3 %collective-permute-start = (f16[2,1,8,8,1,2,256]{6,3,5,4,2,1,0:T(8,128)(2,1)}, f16[2,1,8,8,1,2,256]{6,3,5,4,2,1,0:T(8,128)(2,1)S(1)}, u32[]{:S(2)}, u32[]{:S(2)}) collective-permute-start(f16[2,1,8,8,1,2,256]{6,3,5,4,2,1,0:T(8,128)(2,1)} %get-tuple-element.39), channel_id=1, source_target_pairs={{16,0},{32,16},{48,32},{17,1},{33,17},{49,33},{18,2},{34,18},{50,3... | collective-permute-start | bytes 393224 | tf_op jit(solution)/shard_map/ppermute | solution.py:112
  17.1 8.0 %collective-permute-start.1 = (f16[2,1,8,8,1,2,256]{6,3,5,4,2,1,0:T(8,128)(2,1)S(1)}, f16[2,1,8,8,1,2,256]{6,3,5,4,2,1,0:T(8,128)(2,1)S(1)}, u32[]{:S(2)}, u32[]{:S(2)}) collective-permute-start(f16[2,1,8,8,1,2,256]{6,3,5,4,2,1,0:T(8,128)(2,1)S(1)} %get-tuple-element.40), channel_id=1, source_target_pairs={{0,16},{16,32},{32,48},{1,17},{17,33},{33,49},{2,18},{18,34},{34,5... | collective-permute-start | bytes 393224 | tf_op jit(solution)/shard_map/ppermute | solution.py:107
  23.1 12.9 %copy-start.2 = (s32[8,8]{1,0:T(8,128)S(1)}, s32[8,8]{1,0:T(8,128)}, u32[]{:S(2)}) copy-start(s32[8,8]{1,0:T(8,128)} %param.8) | copy-start | bytes 772
  26.7 13.6 %collective-permute-start.4 = (bf16[8,120,1,128]{3,1,0,2:T(8,128)(2,1)S(1)}, bf16[8,120,1,128]{3,1,0,2:T(8,128)(2,1)S(1)}, u32[]{:S(2)}, u32[]{:S(2)}) collective-permute-start(bf16[8,120,1,128]{3,1,0,2:T(8,128)(2,1)S(1)} %bitcast.69), channel_id=1, source_target_pairs={{0,48},{16,0},{1,49},{17,1},{2,50},{18,2},{3,51},{19,3},{4,52},{20... | collective-permute-start | bytes 737288 | tf_op jit(solution)/shard_map/ppermute | solution.py:90
  31.8 8.5 %collective-permute-start.3 = (bf16[8,120,1,128]{3,1,0,2:T(8,128)(2,1)S(1)}, bf16[8,120,1,128]{3,1,0,2:T(8,128)(2,1)S(1)}, u32[]{:S(2)}, u32[]{:S(2)}) collective-permute-start(bf16[8,120,1,128]{3,1,0,2:T(8,128)(2,1)S(1)} %bitcast.70), channel_id=1, source_target_pairs={{0,32},{16,48},{1,33},{17,49},{2,34},{18,50},{3,35},{19,51},{4,36}... | collective-permute-start | bytes 737288 | tf_op jit(solution)/shard_map/ppermute | solution.py:90
  33.1 8.7 %collective-permute-start.2 = (bf16[8,120,1,128]{3,1,0,2:T(8,128)(2,1)S(1)}, bf16[8,120,1,128]{3,1,0,2:T(8,128)(2,1)S(1)}, u32[]{:S(2)}, u32[]{:S(2)}) collective-permute-start(bf16[8,120,1,128]{3,1,0,2:T(8,128)(2,1)S(1)} %bitcast.71), channel_id=1, source_target_pairs={{0,16},{16,32},{1,17},{17,33},{2,18},{18,34},{3,19},{19,35},{4,20}... | collective-permute-start | bytes 737288 | tf_op jit(solution)/shard_map/ppermute | solution.py:90
  44.9 19.0 %copy-start.4 = (f32[2]{0:T(128)S(1)}, f32[2]{0:T(128)}, u32[]{:S(2)}) copy-start(f32[2]{0:T(128)} %param.11) | copy-start | bytes 28
  44.9 19.2 %copy-start.5 = (f32[2]{0:T(128)S(1)}, f32[2]{0:T(128)}, u32[]{:S(2)}) copy-start(f32[2]{0:T(128)} %param.10) | copy-start | bytes 28
  54.5 20.2 %copy-start = (f32[2,256,1,512]{3,2,1,0:T(1,128)S(1)}, f32[2,256,1,512]{3,2,1,0:T(1,128)}, u32[]{:S(2)}) copy-start(f32[2,256,1,512]{3,2,1,0:T(1,128)} %param.6) | copy-start | bytes 3145732
  54.5 16.9 %all-to-all-start.1 = ((bf16[30,16,2,128]{3,2,0,1:T(2,128)(2,1)}), bf16[30,16,2,128]{3,2,0,1:T(2,128)(2,1)S(1)}, u32[]{:S(2)}, u32[]{:S(2)}) async-start(bf16[30,16,2,128]{3,2,0,1:T(2,128)(2,1)} %bitcast.14), calls=%async_computation.1 | async-start | bytes 491520 | tf_op jit(solution)/shard_map/all_to_all | solution.py:164
  64.1 22.3 %collective-permute-start.5 = (f16[2,4,8,8,1,2,256]{6,3,5,4,2,1,0:T(8,128)(2,1)}, f16[2,4,8,8,1,2,256]{6,3,5,4,2,1,0:T(8,128)(2,1)}, u32[]{:S(2)}, u32[]{:S(2)}) collective-permute-start(f16[2,4,8,8,1,2,256]{6,3,5,4,2,1,0:T(8,128)(2,1)} %get-tuple-element.14), channel_id=1, source_target_pairs={{1,0},{2,1},{3,2},{4,3},{5,4},{6,5},{7,6},{8,7},{9,8},{10,9},{11,1... | collective-permute-start | bytes 1572872 | tf_op jit(solution)/shard_map/ppermute | solution.py:132
  69.3 26.5 %collective-permute-start.6 = (f16[2,4,8,8,1,2,256]{6,3,5,4,2,1,0:T(8,128)(2,1)}, f16[2,4,8,8,1,2,256]{6,3,5,4,2,1,0:T(8,128)(2,1)}, u32[]{:S(2)}, u32[]{:S(2)}) collective-permute-start(f16[2,4,8,8,1,2,256]{6,3,5,4,2,1,0:T(8,128)(2,1)} %get-tuple-element.15), channel_id=1, source_target_pairs={{0,1},{1,2},{2,3},{3,4},{4,5},{5,6},{6,7},{7,8},{8,9},{9,10},{10,1... | collective-permute-start | bytes 1572872 | tf_op jit(solution)/shard_map/ppermute | solution.py:135

commit v17 on v13

--- a/solution.py
+++ b/solution.py
@@ -162,16 +162,15 @@
     kcat = jnp.concatenate([kpad[k] for k in range(NKIND) for _ in range(2)], axis=-1)
     gained = collide_call(kcat, rhs, lmat)
 
-    gained = gained.reshape(out_rows, species_devs, 1, own_count, block_cells)
-    gained = jnp.broadcast_to(
-        gained, (out_rows, species_devs, mode_devs, own_count, block_cells)
-    ).reshape(out_rows, species_devs * mode_devs, own_count, block_cells)
-    gathered = lax.all_to_all(gained.astype(jnp.bfloat16), ("species", "mode"), 1, 1, tiled=True)
-    gathered = gathered.astype(jnp.float32)
-    gathered = gathered.reshape(out_rows, species_devs, mode_devs, own_count, block_cells)
-    all_gained = jnp.transpose(gathered, (2, 0, 3, 1, 4)).reshape(
-        mode_devs * out_rows, own_count, cell_count
-    )
+    gained = gained.astype(jnp.bfloat16).reshape(out_rows, species_devs, own_count, block_cells)
+    gathered = lax.all_to_all(gained, "species", 1, 3, tiled=True)
+    gathered = gathered.reshape(out_rows, own_count, cell_count)
+    pieces = [gathered]
+    for _, got in shift_permutes(gathered, "mode", holders, mode_devs, True):
+        pieces.append(got)
+    stacked = jnp.stack(pieces)
+    by_source = jnp.take(stacked, (mode_id - jnp.arange(mode_devs)) % mode_devs, axis=0)
+    all_gained = by_source.reshape(mode_devs * out_rows, own_count, cell_count).astype(jnp.float32)
 
     local_modes = mode_id * mode_count + jnp.arange(mode_count)
     match = low_map[None, :] == local_modes[:, None]

time: 93.2 us -> 112 us (1.20)
  the two profiles are of different devices: /device:TPU:2 before, /device:TPU:41 now
where the time goes in v17:
time: 112 us
  starting transfers between devices  37.9 us (34%)
  other arithmetic  23.1 us (21%)
  local copies, waits for them, and re-layouts  22.8 us (20%)
  waiting for transfers between devices  19.6 us (18%)
  Pallas kernels  7.81 us (7%)
    ppermute x6, starting transfers between devices, shift_permutes(): received.append((shift, lax.ppermute(values, axis, pairs)))  11.8 us
    ppermute x1, waiting for transfers between devices, per_device(): lax.ppermute(up_edge, 'space', [(i + 1, i) for i in range(space_devs - 1)])  10.5 us
    ppermute x6, waiting for transfers between devices, shift_permutes(): received.append((shift, lax.ppermute(values, axis, pairs)))  9.03 us
    ppermute x1, starting transfers between devices, per_device(): lax.ppermute(down_edge, 'space', [(i, i + 1) for i in range(space_devs -...  8.93 us
    pallas_call x1, Pallas kernels, collide_call(): pl.pallas_call(collide_body, out_shape=jax.ShapeDtypeStruct((kcat.shape[0...  7.81 us
    all_to_all x1, starting transfers between devices, per_device(): spread = lax.all_to_all(picked, 'species', 2, 0, tiled=True)  5.44 us
    sub x1, other arithmetic, per_device(): phase_field - nu_step * thermal_speed.reshape(own_count, 1, 1, 1, 1, 1, 1...  4.77 us
    all_to_all x1, starting transfers between devices, per_device(): gathered = lax.all_to_all(gained, 'species', 1, 3, tiled=True)  4.52 us
  transfers between devices with their start and end apart: 12, of which 4 were waited for; matrix products, arithmetic and copies ran while one was open for 24% of the time, Pallas kernels for 0%

profile of v17, /device:TPU:41, one launch (start us, length us, event | category | flops | bytes accessed | tf_op | source)
XLA Modules:
  0.0 111.9 jit_solution(1917614952733252224)
XLA Ops:
  0.0 3.8 %reduce.18 = f32[2,256,512]{2,1,0:T(8,128)S(1)} reduce(f32[2,256,1,512]{3,2,1,0:T(1,128)} %param.6, f32[]{:T(128)} %constant.120), dimensions={2}, to_apply=%param.6.reduce_sub_computation | reduce | bytes 2097156 | tf_op args[0]
  4.6 3.2 %collective-permute-start.1 = (f16[2,1,8,8,1,2,256]{6,3,5,4,2,1,0:T(8,128)(2,1)}, f16[2,1,8,8,1,2,256]{6,3,5,4,2,1,0:T(8,128)(2,1)S(1)}, u32[]{:S(2)}, u32[]{:S(2)}) collective-permute-start(f16[2,1,8,8,1,2,256]{6,3,5,4,2,1,0:T(8,128)(2,1)} %get-tuple-element.38), channel_id=1, source_target_pairs={{0,16},{16,32},{32,48},{1,17},{17,33},{33,49},{2,18},{18,34},{34,5... | collective-permute-start | bytes 393224 | tf_op jit(solution)/shard_map/ppermute | solution.py:107
  7.8 2.1 %collective-permute-start = (f16[2,1,8,8,1,2,256]{6,3,5,4,2,1,0:T(8,128)(2,1)S(1)}, f16[2,1,8,8,1,2,256]{6,3,5,4,2,1,0:T(8,128)(2,1)S(1)}, u32[]{:S(2)}, u32[]{:S(2)}) collective-permute-start(f16[2,1,8,8,1,2,256]{6,3,5,4,2,1,0:T(8,128)(2,1)S(1)} %get-tuple-element.37), channel_id=1, source_target_pairs={{16,0},{32,16},{48,32},{17,1},{33,17},{49,33},{18,2},{34,18},{50,3... | collective-permute-start | bytes 393224 | tf_op jit(solution)/shard_map/ppermute | solution.py:112
  11.9 1.4 %fusion.26 = bf16[2,120,4,128]{3,0,1,2:T(2,128)(2,1)} fusion(pred[120]{0:T(512)(128)(4,1)S(1)} %get-tuple-element.15, pred[120]{0:T(512)(128)(4,1)S(1)} %get-tuple-element.45, bf16[120,2,512]{2,1,0:T(2,128)(2,1)S(1)} %gather_fusion), kind=kLoop, calls=%fused_computation.53 | loop fusion | flops 245760 | bytes 491760 | tf_op jit(solution)/shard_map/convert_element_type | solution.py:124
  13.3 5.4 %all-to-all-start = ((bf16[2,120,4,128]{3,0,1,2:T(2,128)(2,1)}), bf16[2,120,4,128]{3,0,1,2:T(2,128)(2,1)S(1)}, u32[]{:S(2)}, u32[]{:S(2)}) async-start(bf16[2,120,4,128]{3,0,1,2:T(2,128)(2,1)} %fusion.26), calls=%async_computation | async-start | bytes 491520 | tf_op jit(solution)/shard_map/all_to_all | solution.py:128
  18.7 1.1 %fusion.37 = (f32[2,4,8,8,1,2,1]{6,3,5,4,2,1,0:T(8,128)}, f32[2,4,8,8,1,2,1]{6,3,5,4,2,1,0:T(8,128)}) fusion(f32[2,4,8,8,1,2,256]{6,3,5,4,2,1,0:T(8,128)S(1)} %bitcast.77), kind=kLoop, calls=%fused_computation.97 | loop fusion | bytes 16384 | tf_op jit(solution)/shard_map/jit(_roll_static)/slice | solution.py:52
  19.8 1.7 %fusion.38 = (f32[2,4,8,8,1,2,255]{6,3,5,4,2,1,0:T(8,128)}, f32[2,4,8,8,1,2,255]{6,3,5,4,2,1,0:T(8,128)}) fusion(f32[2,4,8,8,1,2,256]{6,3,5,4,2,1,0:T(8,128)S(1)} %bitcast.78), kind=kLoop, calls=%fused_computation.98 | loop fusion | bytes 4177920 | tf_op jit(solution)/shard_map/jit(_roll_static)/slice | solution.py:52
  24.4 2.0 %fusion.23 = (bf16[30,128,128]{2,1,0:T(8,128)(2,1)S(1)}, bf16[30,128,128]{2,1,0:T(8,128)(2,1)S(1)}) fusion(bf16[2,30,120,120]{3,2,1,0:T(8,128)(2,1)} %param.7), kind=kLoop, calls=%fused_computation.45 | loop fusion | bytes 3694080 | tf_op jit(solution)/shard_map/squeeze | solution.py:162
  26.7 2.0 %pad_maximum_fusion.k_ref = bf16[30,128,512]{2,1,0:T(8,128)(2,1)} fusion(bf16[30,128,128]{2,1,0:T(8,128)(2,1)S(1)} %get-tuple-element.18, bf16[30,128,128]{2,1,0:T(8,128)(2,1)S(1)} %get-tuple-element.17), kind=kLoop, calls=%fused_computation.3 | loop fusion | flops 15728640 | bytes 5898240 | tf_op jit(solution)/shard_map/concatenate | solution.py:162
  30.2 2.8 %subtract_convert_fusion = (f16[2,4,8,8,1,2,256]{6,3,5,4,2,1,0:T(8,128)(2,1)}, f16[2,4,8,8,1,2,256]{6,3,5,4,2,1,0:T(8,128)(2,1)}, f32[2,4,8,8,1,2,256]{6,3,5,4,2,1,0:T(8,128)S(1)}, f32[2,4,8,8,1,2,256]{6,3,5,4,2,1,0:T(8,128)}) fusion(f32[2,4,8,8,1,2,256]{6,3,5,4,2,1,0:T(8,128)S(1)} %bitcast.80, f32[2,1,8,8,1,2,256]{6,3,5,4,2,1,0:T(8,128)S(1)} %convert_element_type.88, ...), kind=kLoop, calls=%fused_computation.43 | loop fusion | flops 4718592 | bytes 4720672 | tf_op jit(solution)/shard_map/convert_element_type | solution.py:130
  33.0 1.3 %collective-permute-start.6 = (bf16[8,120,1,128]{3,1,0,2:T(8,128)(2,1)S(1)}, bf16[8,120,1,128]{3,1,0,2:T(8,128)(2,1)S(1)}, u32[]{:S(2)}, u32[]{:S(2)}) collective-permute-start(bf16[8,120,1,128]{3,1,0,2:T(8,128)(2,1)S(1)} %bitcast.88), channel_id=1, source_target_pairs={{0,48},{16,0},{1,49},{17,1},{2,50},{18,2},{3,51},{19,3},{4,52},{20... | collective-permute-start | bytes 737288 | tf_op jit(solution)/shard_map/ppermute | solution.py:90
  34.4 3.9 %collective-permute-start.5 = (bf16[8,120,1,128]{3,1,0,2:T(8,128)(2,1)S(1)}, bf16[8,120,1,128]{3,1,0,2:T(8,128)(2,1)S(1)}, u32[]{:S(2)}, u32[]{:S(2)}) collective-permute-start(bf16[8,120,1,128]{3,1,0,2:T(8,128)(2,1)S(1)} %bitcast.89), channel_id=1, source_target_pairs={{0,32},{16,48},{1,33},{17,49},{2,34},{18,50},{3,35},{19,51},{4,36}... | collective-permute-start | bytes 737288 | tf_op jit(solution)/shard_map/ppermute | solution.py:90
  38.3 1.9 %collective-permute-start.4 = (bf16[8,120,1,128]{3,1,0,2:T(8,128)(2,1)S(1)}, bf16[8,120,1,128]{3,1,0,2:T(8,128)(2,1)S(1)}, u32[]{:S(2)}, u32[]{:S(2)}) collective-permute-start(bf16[8,120,1,128]{3,1,0,2:T(8,128)(2,1)S(1)} %bitcast.90), channel_id=1, source_target_pairs={{0,16},{16,32},{1,17},{17,33},{2,18},{18,34},{3,19},{19,35},{4,20}... | collective-permute-start | bytes 737288 | tf_op jit(solution)/shard_map/ppermute | solution.py:90
  40.2 1.7 %fusion.40 = (f32[2,4,8,8,1,2,255]{6,3,5,4,2,1,0:T(8,128)}, f32[2,4,8,8,1,2,255]{6,3,5,4,2,1,0:T(8,128)}) fusion(f32[2,4,8,8,1,2,256]{6,3,5,4,2,1,0:T(8,128)S(1)} %get-tuple-element.23), kind=kLoop, calls=%fused_computation.100 | loop fusion | bytes 4177920 | tf_op jit(solution)/shard_map/jit(_roll_static)/slice | solution.py:54
  41.9 2.2 %collective-permute-done.5 = bf16[8,120,1,128]{3,1,0,2:T(8,128)(2,1)S(1)} collective-permute-done((bf16[8,120,1,128]{3,1,0,2:T(8,128)(2,1)S(1)}, bf16[8,120,1,128]{3,1,0,2:T(8,128)(2,1)S(1)}, u32[]{:S(2)}, u32[]{:S(2)}) %collective-permute-start.5) | collective-permute-done | bytes 245792 | tf_op jit(solution)/shard_map/ppermute | solution.py:90
  44.1 5.4 %collective-permute-done.4 = bf16[8,120,1,128]{3,1,0,2:T(8,128)(2,1)S(1)} collective-permute-done((bf16[8,120,1,128]{3,1,0,2:T(8,128)(2,1)S(1)}, bf16[8,120,1,128]{3,1,0,2:T(8,128)(2,1)S(1)}, u32[]{:S(2)}, u32[]{:S(2)}) %collective-permute-start.4) | collective-permute-done | bytes 245792 | tf_op jit(solution)/shard_map/ppermute | solution.py:90
  50.5 1.3 %copy.167 = bf16[64,8,8,128]{3,1,2,0:T(8,128)(2,1)} copy(bf16[64,8,8,128]{3,2,1,0:T(8,128)(2,1)S(1)} %bitcast.83) | data formatting | bytes 2097152
  52.7 7.8 %shard_map.64 = f32[30,1024]{1,0:T(8,128)} custom-call(bf16[30,128,512]{2,1,0:T(8,128)(2,1)} %pad_maximum_fusion.k_ref, bf16[512,1024]{1,0:T(8,128)(2,1)} %bitcast.84, f32[128,1024]{1,0:T(8,128)} %copy_bitcast_fusion.2.l_ref), custom_call_target="tpu_custom_call" | custom-call | tf_op jit(solution)/shard_map/pallas_call | solution.py:76
  62.1 4.5 %all-to-all-start.1 = ((bf16[30,4,2,128]{3,2,0,1:T(2,128)(2,1)}), bf16[30,4,2,128]{3,2,0,1:T(2,128)(2,1)S(1)}, u32[]{:S(2)}, u32[]{:S(2)}) async-start(bf16[30,4,2,128]{3,2,0,1:T(2,128)(2,1)} %copy.144), calls=%async_computation.1 | async-start | bytes 122880 | tf_op jit(solution)/shard_map/all_to_all | solution.py:166
  66.6 1.2 %fusion.39 = (f32[2,4,8,8,1,2,1]{6,3,5,4,2,1,0:T(8,128)}, f32[2,4,8,8,1,2,1]{6,3,5,4,2,1,0:T(8,128)}) fusion(f32[2,4,8,8,1,2,256]{6,3,5,4,2,1,0:T(8,128)S(1)} %get-tuple-element.23), kind=kLoop, calls=%fused_computation.99 | loop fusion | bytes 16384 | tf_op jit(solution)/shard_map/jit(_roll_static)/slice | solution.py:54
  67.8 8.9 %collective-permute-start.3 = (f16[2,4,8,8,1,2,256]{6,3,5,4,2,1,0:T(8,128)(2,1)}, f16[2,4,8,8,1,2,256]{6,3,5,4,2,1,0:T(8,128)(2,1)}, u32[]{:S(2)}, u32[]{:S(2)}) collective-permute-start(f16[2,4,8,8,1,2,256]{6,3,5,4,2,1,0:T(8,128)(2,1)} %get-tuple-element.10), channel_id=1, source_target_pairs={{0,1},{1,2},{2,3},{3,4},{4,5},{5,6},{6,7},{7,8},{8,9},{9,10},{10,1... | collective-permute-start | bytes 1572872 | tf_op jit(solution)/shard_map/ppermute | solution.py:135
  76.8 1.9 %collective-permute-start.2 = (f16[2,4,8,8,1,2,256]{6,3,5,4,2,1,0:T(8,128)(2,1)}, f16[2,4,8,8,1,2,256]{6,3,5,4,2,1,0:T(8,128)(2,1)}, u32[]{:S(2)}, u32[]{:S(2)}) collective-permute-start(f16[2,4,8,8,1,2,256]{6,3,5,4,2,1,0:T(8,128)(2,1)} %get-tuple-element.9), channel_id=1, source_target_pairs={{1,0},{2,1},{3,2},{4,3},{5,4},{6,5},{7,6},{8,7},{9,8},{10,9},{11,1... | collective-permute-start | bytes 1572872 | tf_op jit(solution)/shard_map/ppermute | solution.py:132
  78.8 1.9 %collective-permute-start.9 = (bf16[30,2,512]{2,1,0:T(2,128)(2,1)S(1)}, bf16[30,2,512]{2,1,0:T(2,128)(2,1)S(1)}, u32[]{:S(2)}, u32[]{:S(2)}) collective-permute-start(bf16[30,2,512]{2,1,0:T(2,128)(2,1)S(1)} %reshape.477), channel_id=1, source_target_pairs={{16,0},{32,16},{17,1},{33,17},{18,2},{34,18},{19,3},{35,19},{20,4}... | collective-permute-start | bytes 184328 | tf_op jit(solution)/shard_map/ppermute | solution.py:90
  80.7 1.3 %collective-permute-start.8 = (bf16[30,2,512]{2,1,0:T(2,128)(2,1)S(1)}, bf16[30,2,512]{2,1,0:T(2,128)(2,1)S(1)}, u32[]{:S(2)}, u32[]{:S(2)}) collective-permute-start(bf16[30,2,512]{2,1,0:T(2,128)(2,1)S(1)} %reshape.477), channel_id=1, source_target_pairs={{32,0},{48,16},{33,1},{49,17},{34,2},{50,18},{35,3},{51,19},{36,4}... | collective-permute-start | bytes 184328 | tf_op jit(solution)/shard_map/ppermute | solution.py:90
  82.0 1.5 %collective-permute-start.7 = (bf16[30,2,512]{2,1,0:T(2,128)(2,1)S(1)}, bf16[30,2,512]{2,1,0:T(2,128)(2,1)S(1)}, u32[]{:S(2)}, u32[]{:S(2)}) collective-permute-start(bf16[30,2,512]{2,1,0:T(2,128)(2,1)S(1)} %reshape.477), channel_id=1, source_target_pairs={{48,0},{0,16},{49,1},{1,17},{50,2},{2,18},{51,3},{3,19},{52,4},{4,... | collective-permute-start | bytes 184328 | tf_op jit(solution)/shard_map/ppermute | solution.py:90
  83.5 2.3 %fusion.36 = (f32[2,4,8,8,1,1,256]{6,3,5,4,2,1,0:T(8,128)}, f32[2,4,8,8,1,1,256]{6,3,5,4,2,1,0:T(8,128)}) fusion(f32[2,4,8,8,1,2,256]{6,3,5,4,2,1,0:T(8,128)} %get-tuple-element.24), kind=kLoop, calls=%fused_computation.96 | loop fusion | bytes 2097152 | tf_op jit(solution)/shard_map/jit(_roll_static)/slice | solution.py:53
  85.8 1.4 %collective-permute-done.8 = bf16[30,2,512]{2,1,0:T(2,128)(2,1)S(1)} collective-permute-done((bf16[30,2,512]{2,1,0:T(2,128)(2,1)S(1)}, bf16[30,2,512]{2,1,0:T(2,128)(2,1)S(1)}, u32[]{:S(2)}, u32[]{:S(2)}) %collective-permute-start.8) | collective-permute-done | bytes 61472 | tf_op jit(solution)/shard_map/ppermute | solution.py:90
  89.0 2.7 %gather_fusion.2 = f32[256,2,512]{2,1,0:T(2,128)} fusion(f32[120,2,512]{2,1,0:T(2,128)S(1)} %fusion.27, s32[1024]{0:T(1024)S(1)} %pad_clamp_fusion), kind=kCustom, calls=%fused_computation.2 | custom fusion | bytes 2098176 | tf_op jit(solution)/shard_map/jit(_take)/gather | solution.py:178
  91.7 10.5 %collective-permute-done.2 = f16[2,4,8,8,1,2,256]{6,3,5,4,2,1,0:T(8,128)(2,1)} collective-permute-done((f16[2,4,8,8,1,2,256]{6,3,5,4,2,1,0:T(8,128)(2,1)}, f16[2,4,8,8,1,2,256]{6,3,5,4,2,1,0:T(8,128)(2,1)}, u32[]{:S(2)}, u32[]{:S(2)}) %collective-permute-start.2) | collective-permute-done | bytes 524320 | tf_op jit(solution)/shard_map/ppermute | solution.py:132
  102.2 4.8 %fusion.7 = f32[2,4,8,8,1,2,256]{6,3,5,4,2,1,0:T(8,128)S(1)} fusion(f32[2,4,8,8,1,2,256]{6,3,5,4,2,1,0:T(8,128)S(1)} %bitcast.81, f32[2,4,8,8,1,2,1]{6,3,5,4,2,1,0:T(8,128)} %get-tuple-element.34, f32[2,4,8,8,1,2,255]{6,3,5,4,2,1,0:T(8,128)} %get-tuple-element.36, f32[2,4,8,8,1,2,255]{6,3,5,4,2,1,0:T(8,128)} %get-tuple-element.35, ...), kind=kLoop, calls=%fused_computation.19 | loop fusion | flops 7340032 | bytes 9437192 | tf_op jit(solution)/shard_map/sub | solution.py:145
  107.0 2.8 %fusion.22 = f32[2,256,1,512]{3,0,1,2:T(2,128)S(1)} fusion(f32[2,256,512]{2,1,0:T(8,128)S(1)} %bitcast.82, f32[256,2,512]{2,1,0:T(2,128)S(1)} %copy-done.1, pred[256]{0:T(512)(128)(4,1)S(1)} %compare_and_fusion.1, pred[256]{0:T(512)(128)(4,1)S(1)} %gt.18, f32[2]{0:T(128)S(1)} %copy-done.6, f32[2,256,1,512]{3,2,1,0:T(1,128)S(1)} %copy-done), kind=kLoop, calls=%fused_computation.41 | loop fusion | flops 1310720 | bytes 4194824 | tf_op jit(solution)/shard_map/add | solution.py:186
  109.8 2.0 %copy.148 = f32[2,256,1,512]{3,2,1,0:T(1,128)} copy(f32[2,256,1,512]{3,0,1,2:T(2,128)S(1)} %fusion.22) | data formatting | bytes 2097152 | tf_op jit(solution)/shard_map/add | solution.py:186
  (74 shorter events, 12.6 us)
Async XLA Ops:
  0.0 9.9 %copy-start = (f32[2,256,1,512]{3,2,1,0:T(1,128)S(1)}, f32[2,256,1,512]{3,2,1,0:T(1,128)}, u32[]{:S(2)}) copy-start(f32[2,256,1,512]{3,2,1,0:T(1,128)} %param.6) | copy-start | bytes 3145732
  0.0 10.8 %copy-start.4 = (s32[120]{0:T(128)S(1)}, s32[120]{0:T(128)}, u32[]{:S(2)}) copy-start(s32[120]{0:T(128)} %param.9) | copy-start | bytes 1444
  4.6 25.5 %collective-permute-start.1 = (f16[2,1,8,8,1,2,256]{6,3,5,4,2,1,0:T(8,128)(2,1)}, f16[2,1,8,8,1,2,256]{6,3,5,4,2,1,0:T(8,128)(2,1)S(1)}, u32[]{:S(2)}, u32[]{:S(2)}) collective-permute-start(f16[2,1,8,8,1,2,256]{6,3,5,4,2,1,0:T(8,128)(2,1)} %get-tuple-element.38), channel_id=1, source_target_pairs={{0,16},{16,32},{32,48},{1,17},{17,33},{33,49},{2,18},{18,34},{34,5... | collective-permute-start | bytes 393224 | tf_op jit(solution)/shard_map/ppermute | solution.py:107
  7.8 22.3 %collective-permute-start = (f16[2,1,8,8,1,2,256]{6,3,5,4,2,1,0:T(8,128)(2,1)S(1)}, f16[2,1,8,8,1,2,256]{6,3,5,4,2,1,0:T(8,128)(2,1)S(1)}, u32[]{:S(2)}, u32[]{:S(2)}) collective-permute-start(f16[2,1,8,8,1,2,256]{6,3,5,4,2,1,0:T(8,128)(2,1)S(1)} %get-tuple-element.37), channel_id=1, source_target_pairs={{16,0},{32,16},{48,32},{17,1},{33,17},{49,33},{18,2},{34,18},{50,3... | collective-permute-start | bytes 393224 | tf_op jit(solution)/shard_map/ppermute | solution.py:112
  13.3 19.7 %all-to-all-start = ((bf16[2,120,4,128]{3,0,1,2:T(2,128)(2,1)}), bf16[2,120,4,128]{3,0,1,2:T(2,128)(2,1)S(1)}, u32[]{:S(2)}, u32[]{:S(2)}) async-start(bf16[2,120,4,128]{3,0,1,2:T(2,128)(2,1)} %fusion.26), calls=%async_computation | async-start | bytes 491520 | tf_op jit(solution)/shard_map/all_to_all | solution.py:128
  18.7 5.2 %copy-start.8 = (f32[2]{0:T(128)S(1)}, f32[2]{0:T(128)}, u32[]{:S(2)}) copy-start(f32[2]{0:T(128)} %param.10) | copy-start | bytes 28
  21.5 4.9 %copy-start.3 = (s32[8,8]{1,0:T(8,128)S(1)}, s32[8,8]{1,0:T(8,128)}, u32[]{:S(2)}) copy-start(s32[8,8]{1,0:T(8,128)} %param.8) | copy-start | bytes 772
  24.4 5.1 %copy-start.9 = (f32[2]{0:T(128)S(1)}, f32[2]{0:T(128)}, u32[]{:S(2)}) copy-start(f32[2]{0:T(128)} %param.11) | copy-start | bytes 28
  33.0 8.9 %collective-permute-start.6 = (bf16[8,120,1,128]{3,1,0,2:T(8,128)(2,1)S(1)}, bf16[8,120,1,128]{3,1,0,2:T(8,128)(2,1)S(1)}, u32[]{:S(2)}, u32[]{:S(2)}) collective-permute-start(bf16[8,120,1,128]{3,1,0,2:T(8,128)(2,1)S(1)} %bitcast.88), channel_id=1, source_target_pairs={{0,48},{16,0},{1,49},{17,1},{2,50},{18,2},{3,51},{19,3},{4,52},{20... | collective-permute-start | bytes 737288 | tf_op jit(solution)/shard_map/ppermute | solution.py:90
  34.4 9.8 %collective-permute-start.5 = (bf16[8,120,1,128]{3,1,0,2:T(8,128)(2,1)S(1)}, bf16[8,120,1,128]{3,1,0,2:T(8,128)(2,1)S(1)}, u32[]{:S(2)}, u32[]{:S(2)}) collective-permute-start(bf16[8,120,1,128]{3,1,0,2:T(8,128)(2,1)S(1)} %bitcast.89), channel_id=1, source_target_pairs={{0,32},{16,48},{1,33},{17,49},{2,34},{18,50},{3,35},{19,51},{4,36}... | collective-permute-start | bytes 737288 | tf_op jit(solution)/shard_map/ppermute | solution.py:90
  38.3 11.3 %collective-permute-start.4 = (bf16[8,120,1,128]{3,1,0,2:T(8,128)(2,1)S(1)}, bf16[8,120,1,128]{3,1,0,2:T(8,128)(2,1)S(1)}, u32[]{:S(2)}, u32[]{:S(2)}) collective-permute-start(bf16[8,120,1,128]{3,1,0,2:T(8,128)(2,1)S(1)} %bitcast.90), channel_id=1, source_target_pairs={{0,16},{16,32},{1,17},{17,33},{2,18},{18,34},{3,19},{19,35},{4,20}... | collective-permute-start | bytes 737288 | tf_op jit(solution)/shard_map/ppermute | solution.py:90
  60.5 28.2 %copy-start.7 = (pred[120]{0:T(512)(128)(4,1)S(1)}, pred[120]{0:T(512)(128)(4,1)}, u32[]{:S(2)}) copy-start(pred[120]{0:T(512)(128)(4,1)} %broadcast_in_dim.72) | copy-start | bytes 364
  62.1 16.6 %all-to-all-start.1 = ((bf16[30,4,2,128]{3,2,0,1:T(2,128)(2,1)}), bf16[30,4,2,128]{3,2,0,1:T(2,128)(2,1)S(1)}, u32[]{:S(2)}, u32[]{:S(2)}) async-start(bf16[30,4,2,128]{3,2,0,1:T(2,128)(2,1)} %copy.144), calls=%async_computation.1 | async-start | bytes 122880 | tf_op jit(solution)/shard_map/all_to_all | solution.py:166
  66.6 35.5 %copy-start.5 = (f32[2]{0:T(128)S(1)}, f32[2]{0:T(128)}, u32[]{:S(2)}) copy-start(f32[2]{0:T(128)} %broadcast_multiply_fusion) | copy-start | bytes 28
  67.8 34.3 %copy-start.2 = (f32[2,4,8,8,1,2,1]{6,3,5,4,2,1,0:T(8,128)S(1)}, f32[2,4,8,8,1,2,1]{6,3,5,4,2,1,0:T(8,128)}, u32[]{:S(2)}) copy-start(f32[2,4,8,8,1,2,1]{6,3,5,4,2,1,0:T(8,128)} %get-tuple-element.29) | copy-start | bytes 12292
  67.8 23.8 %collective-permute-start.3 = (f16[2,4,8,8,1,2,256]{6,3,5,4,2,1,0:T(8,128)(2,1)}, f16[2,4,8,8,1,2,256]{6,3,5,4,2,1,0:T(8,128)(2,1)}, u32[]{:S(2)}, u32[]{:S(2)}) collective-permute-start(f16[2,4,8,8,1,2,256]{6,3,5,4,2,1,0:T(8,128)(2,1)} %get-tuple-element.10), channel_id=1, source_target_pairs={{0,1},{1,2},{2,3},{3,4},{4,5},{5,6},{6,7},{7,8},{8,9},{9,10},{10,1... | collective-permute-start | bytes 1572872 | tf_op jit(solution)/shard_map/ppermute | solution.py:135
  76.8 25.4 %collective-permute-start.2 = (f16[2,4,8,8,1,2,256]{6,3,5,4,2,1,0:T(8,128)(2,1)}, f16[2,4,8,8,1,2,256]{6,3,5,4,2,1,0:T(8,128)(2,1)}, u32[]{:S(2)}, u32[]{:S(2)}) collective-permute-start(f16[2,4,8,8,1,2,256]{6,3,5,4,2,1,0:T(8,128)(2,1)} %get-tuple-element.9), channel_id=1, source_target_pairs={{1,0},{2,1},{3,2},{4,3},{5,4},{6,5},{7,6},{8,7},{9,8},{10,9},{11,1... | collective-permute-start | bytes 1572872 | tf_op jit(solution)/shard_map/ppermute | solution.py:132
  78.8 7.0 %collective-permute-start.9 = (bf16[30,2,512]{2,1,0:T(2,128)(2,1)S(1)}, bf16[30,2,512]{2,1,0:T(2,128)(2,1)S(1)}, u32[]{:S(2)}, u32[]{:S(2)}) collective-permute-start(bf16[30,2,512]{2,1,0:T(2,128)(2,1)S(1)} %reshape.477), channel_id=1, source_target_pairs={{16,0},{32,16},{17,1},{33,17},{18,2},{34,18},{19,3},{35,19},{20,4}... | collective-permute-start | bytes 184328 | tf_op jit(solution)/shard_map/ppermute | solution.py:90
  80.7 6.5 %collective-permute-start.8 = (bf16[30,2,512]{2,1,0:T(2,128)(2,1)S(1)}, bf16[30,2,512]{2,1,0:T(2,128)(2,1)S(1)}, u32[]{:S(2)}, u32[]{:S(2)}) collective-permute-start(bf16[30,2,512]{2,1,0:T(2,128)(2,1)S(1)} %reshape.477), channel_id=1, source_target_pairs={{32,0},{48,16},{33,1},{49,17},{34,2},{50,18},{35,3},{51,19},{36,4}... | collective-permute-start | bytes 184328 | tf_op jit(solution)/shard_map/ppermute | solution.py:90
  82.0 5.2 %collective-permute-start.7 = (bf16[30,2,512]{2,1,0:T(2,128)(2,1)S(1)}, bf16[30,2,512]{2,1,0:T(2,128)(2,1)S(1)}, u32[]{:S(2)}, u32[]{:S(2)}) collective-permute-start(bf16[30,2,512]{2,1,0:T(2,128)(2,1)S(1)} %reshape.477), channel_id=1, source_target_pairs={{48,0},{0,16},{49,1},{1,17},{50,2},{2,18},{51,3},{3,19},{52,4},{4,... | collective-permute-start | bytes 184328 | tf_op jit(solution)/shard_map/ppermute | solution.py:90
  102.2 4.8 %copy-start.1 = (f32[256,2,512]{2,1,0:T(2,128)S(1)}, f32[256,2,512]{2,1,0:T(2,128)}, u32[]{:S(2)}) copy-start(f32[256,2,512]{2,1,0:T(2,128)} %gather_fusion.2) | copy-start | bytes 3145732
  102.2 4.8 %copy-start.6 = (f32[2]{0:T(128)S(1)}, f32[2]{0:T(128)}, u32[]{:S(2)}) copy-start(f32[2]{0:T(128)} %neg.4) | copy-start | bytes 28
